TPU v7x, 1024 devices: a whole 8x8x8 slice. The times are simulated.
1024 devices in a mesh: row: 128 (over z, x, core), vec: 8 (over y).
Axes of the slice: x: 8, y: 8, z: 8, core: 2. Of those that a mesh axis runs over, the one named last changes fastest.
Arguments:
- vectors: bfloat16 [131072, 1024], P(('row', 'vec')), may hold values from -6 to 6
- rotation: bfloat16 [1024, 1024], replicated, may hold values from -0.1875 to 0.1875
- blocks: bfloat16 [1024, 8, 128, 128], P('row'), may hold values from -0.1875 to 0.1875
- columns: int32 [1024, 8], P('row'), may hold values from 0 to 1023, as said below
Outputs:
- filtered: bfloat16 [131072, 1024], P('row', 'vec')
Inputs may be any that keep to these rules, and one draw needn't show every extreme that they name: `columns`: block row i stores its own block first, then block max(i - 6, 0), then block min(i + 2, 1023); every other entry lies between i - 6 and i + 2, clipped to the grid.
All inputs are finite; a program needn't handle non-finite values.
Results may differ from a plain program's by a relative error of at most 0.0065.
Values may be sent and summed in bfloat16 or wider, within the bound.
No kernel may reach another device: no remote copies, remote signals or barrier semaphores. Data moves between devices by JAX's collectives and lax.ppermute only.
A program may use at most 32 MiB of HBM per device.

v0:
```python
import jax
import jax.numpy as jnp
from jax import lax
from jax.sharding import PartitionSpec as P

DEG = 4
REACH_LO = 6
REACH_HI = 2


def extended_2(cells, sides, width):
    for axis, dim in sides:
        count = lax.axis_size(axis)
        ends = count - 1
        head = lax.slice_in_dim(cells, 0, width, axis=dim)
        tail = lax.slice_in_dim(cells, cells.shape[dim] - width, cells.shape[dim], axis=dim)
        cells = jnp.concatenate(
            [
                lax.ppermute(tail, axis, [(i, (i + 1) % count) for i in range(ends)]),
                cells,
                lax.ppermute(head, axis, [((i + 1) % count, i) for i in range(ends)]),
            ],
            axis=dim,
        )
    return cells


def per_device(vectors, rotation, blocks, columns):
    rotated = jnp.dot(vectors, rotation, preferred_element_type=jnp.float32).astype(jnp.bfloat16)
    panel = lax.all_to_all(rotated, "vec", split_axis=1, concat_axis=0, tiled=True)
    local_blocks = blocks.shape[0]
    block_rows = blocks.shape[2]
    group_width = panel.shape[1]
    first_block = lax.axis_index("row") * local_blocks

    def extend(state_bf):
        reach_blocks = max(REACH_LO, REACH_HI)
        wider = extended_2(state_bf, (("row", 0),), reach_blocks * block_rows)
        return (wider, reach_blocks)

    def apply_operator(state_bf):
        extended, offset = extend(state_bf)
        tiles = extended.reshape(-1, block_rows, group_width)
        local_index = columns - first_block + offset
        picked = tiles[local_index]
        result = jnp.einsum("bjrc,bjcv->brv", blocks, picked, preferred_element_type=jnp.float32)
        return result.reshape(local_blocks * block_rows, group_width)

    prev = panel.astype(jnp.float32)
    cur = (apply_operator(panel) - 0.25 * prev) / 2.0
    for degree in range(DEG - 1):
        sent = cur.astype(jnp.bfloat16)
        nxt = 2.0 * (apply_operator(sent) - 0.25 * cur) / 2.0 - prev
        prev = cur
        cur = nxt
    return cur.astype(jnp.bfloat16)


def solution(mesh):
    return jax.shard_map(
        per_device,
        mesh=mesh,
        in_specs=(P(("row", "vec"), None), P(), P("row", None, None, None), P("row", None)),
        out_specs=P("row", "vec"),
        check_vma=False,
    )
```

profile of v0, /device:TPU:399, one launch (start us, length us, event | category | flops | bytes accessed | tf_op | source)
XLA Modules:
  0.0 99.5 jit_solution(17108480388819630249)
XLA Ops:
  0.0 0.0 copy-start
  0.0 0.0 copy-start.3
  0.0 2.3 %fusion = bf16[16,8,8,128]{3,2,1,0:T(8,128)(2,1)S(1)} fusion(bf16[128,1024]{1,0:T(8,128)(2,1)} %param.4, bf16[1024,1024]{1,0:T(8,128)(2,1)} %param.5), kind=kOutput, calls=%fused_computation.5 | convolution fusion | flops 268566528 | bytes 2621440 | tf_op jit(solution)/shard_map/dot_general | solution.py:29
  2.3 0.8 copy.15
  3.0 7.3 %all-to-all-start = ((bf16[128,8,128]{2,0,1:T(8,128)(2,1)}), bf16[128,8,128]{2,0,1:T(8,128)(2,1)S(1)}, u32[]{:S(2)}, u32[]{:S(2)}) async-start(bf16[128,8,128]{2,0,1:T(8,128)(2,1)} %bitcast.102), calls=%async_computation | async-start | bytes 524288 | tf_op jit(solution)/shard_map/all_to_all | solution.py:30
  10.3 10.4 %all-to-all-done = bf16[128,8,128]{2,0,1:T(8,128)(2,1)S(1)} async-done(((bf16[128,8,128]{2,0,1:T(8,128)(2,1)}), bf16[128,8,128]{2,0,1:T(8,128)(2,1)S(1)}, u32[]{:S(2)}, u32[]{:S(2)}) %all-to-all-start) | async-done | bytes 262176 | tf_op jit(solution)/shard_map/all_to_all | solution.py:30
  20.7 4.4 %collective-permute-start.1 = (bf16[768,128]{1,0:T(8,128)(2,1)S(1)}, bf16[768,128]{1,0:T(8,128)(2,1)S(1)}, u32[]{:S(2)}, u32[]{:S(2)}) collective-permute-start(bf16[768,128]{1,0:T(8,128)(2,1)S(1)} %bitcast.114), channel_id=1, source_target_pairs={{8,0},{16,8},{24,16},{32,24},{40,32},{48,40},{56,48},{64,56},{72,6... | collective-permute-start | bytes 589832 | tf_op jit(solution)/shard_map/ppermute | solution.py:21
  25.1 5.8 %collective-permute-start = (bf16[768,128]{1,0:T(8,128)(2,1)S(1)}, bf16[768,128]{1,0:T(8,128)(2,1)S(1)}, u32[]{:S(2)}, u32[]{:S(2)}) collective-permute-start(bf16[768,128]{1,0:T(8,128)(2,1)S(1)} %bitcast.113), channel_id=1, source_target_pairs={{0,8},{8,16},{16,24},{24,32},{32,40},{40,48},{48,56},{56,64},{64,7... | collective-permute-start | bytes 589832 | tf_op jit(solution)/shard_map/ppermute | solution.py:19
  30.9 0.0 copy-done.3
  31.0 0.1 reshape.39
  31.1 1.3 %collective-permute-done.1 = bf16[768,128]{1,0:T(8,128)(2,1)S(1)} collective-permute-done((bf16[768,128]{1,0:T(8,128)(2,1)S(1)}, bf16[768,128]{1,0:T(8,128)(2,1)S(1)}, u32[]{:S(2)}, u32[]{:S(2)}) %collective-permute-start.1) | collective-permute-done | bytes 196640 | tf_op jit(solution)/shard_map/ppermute | solution.py:21
  32.4 1.2 %collective-permute-done = bf16[768,128]{1,0:T(8,128)(2,1)S(1)} collective-permute-done((bf16[768,128]{1,0:T(8,128)(2,1)S(1)}, bf16[768,128]{1,0:T(8,128)(2,1)S(1)}, u32[]{:S(2)}, u32[]{:S(2)}) %collective-permute-start) | collective-permute-done | bytes 196640 | tf_op jit(solution)/shard_map/ppermute | solution.py:19
  33.6 2.2 %gather_fusion = bf16[64,128,128]{2,1,0:T(8,128)(2,1)} fusion(bf16[20,128,128]{2,1,0:T(8,128)(2,1)S(1)} %bitcast.112, s32[1024]{0:T(1024)S(1)} %pad_clamp_fusion), kind=kCustom, calls=%fused_computation | custom fusion | bytes 4194560 | tf_op jit(solution)/shard_map/gather | solution.py:45
  35.7 0.0 copy-done
  35.8 2.3 %fusion.11 = f32[8,128,128,1]{1,2,3,0:T(8,128)S(1)} fusion(bf16[8,8,128,128]{3,2,1,0:T(8,128)(2,1)S(1)} %copy-done, bf16[8,8,128,128]{3,2,1,0:T(8,128)(2,1)} %bitcast.104), kind=kOutput, calls=%fused_computation.29 | convolution fusion | flops 268435456 | bytes 4718592 | tf_op jit(solution)/shard_map/bjrc,bjcv->brv/dot_general | solution.py:46
  38.0 0.1 multiply_convert_fusion
  38.2 7.7 %collective-permute-start.2 = (bf16[768,128]{1,0:T(8,128)(2,1)S(1)}, bf16[768,128]{1,0:T(8,128)(2,1)S(1)}, u32[]{:S(2)}, u32[]{:S(2)}) collective-permute-start(bf16[768,128]{1,0:T(8,128)(2,1)S(1)} %get-tuple-element.9), channel_id=1, source_target_pairs={{0,8},{8,16},{16,24},{24,32},{32,40},{40,48},{48,56},{56,64},{64,7... | collective-permute-start | bytes 589832 | tf_op jit(solution)/shard_map/ppermute | solution.py:19
  45.9 1.9 %collective-permute-start.3 = (bf16[768,128]{1,0:T(8,128)(2,1)S(1)}, bf16[768,128]{1,0:T(8,128)(2,1)S(1)}, u32[]{:S(2)}, u32[]{:S(2)}) collective-permute-start(bf16[768,128]{1,0:T(8,128)(2,1)S(1)} %get-tuple-element.10), channel_id=1, source_target_pairs={{8,0},{16,8},{24,16},{32,24},{40,32},{48,40},{56,48},{64,56},{72,6... | collective-permute-start | bytes 589832 | tf_op jit(solution)/shard_map/ppermute | solution.py:21
  47.8 0.7 collective-permute-done.2
  48.5 7.7 %collective-permute-done.3 = bf16[768,128]{1,0:T(8,128)(2,1)S(1)} collective-permute-done((bf16[768,128]{1,0:T(8,128)(2,1)S(1)}, bf16[768,128]{1,0:T(8,128)(2,1)S(1)}, u32[]{:S(2)}, u32[]{:S(2)}) %collective-permute-start.3) | collective-permute-done | bytes 196640 | tf_op jit(solution)/shard_map/ppermute | solution.py:21
  56.3 2.2 %gather_fusion.1 = bf16[64,128,128]{2,1,0:T(8,128)(2,1)} fusion(bf16[20,128,128]{2,1,0:T(8,128)(2,1)S(1)} %bitcast.110, s32[1024]{0:T(1024)S(1)} %pad_clamp_fusion), kind=kCustom, calls=%fused_computation.1 | custom fusion | bytes 4194560 | tf_op jit(solution)/shard_map/gather | solution.py:45
  58.4 2.3 %fusion.12 = f32[8,128,128,1]{1,2,3,0:T(8,128)S(1)} fusion(bf16[8,8,128,128]{3,2,1,0:T(8,128)(2,1)S(1)} %copy-done, bf16[8,8,128,128]{3,2,1,0:T(8,128)(2,1)} %bitcast.105), kind=kOutput, calls=%fused_computation.30 | convolution fusion | flops 268435456 | bytes 4718592 | tf_op jit(solution)/shard_map/bjrc,bjcv->brv/dot_general | solution.py:46
  60.7 0.1 fusion.6
  60.9 1.9 %collective-permute-start.4 = (bf16[768,128]{1,0:T(8,128)(2,1)S(1)}, bf16[768,128]{1,0:T(8,128)(2,1)S(1)}, u32[]{:S(2)}, u32[]{:S(2)}) collective-permute-start(bf16[768,128]{1,0:T(8,128)(2,1)S(1)} %get-tuple-element.7), channel_id=1, source_target_pairs={{0,8},{8,16},{16,24},{24,32},{32,40},{40,48},{48,56},{56,64},{64,7... | collective-permute-start | bytes 589832 | tf_op jit(solution)/shard_map/ppermute | solution.py:19
  62.8 2.4 %collective-permute-start.5 = (bf16[768,128]{1,0:T(8,128)(2,1)S(1)}, bf16[768,128]{1,0:T(8,128)(2,1)S(1)}, u32[]{:S(2)}, u32[]{:S(2)}) collective-permute-start(bf16[768,128]{1,0:T(8,128)(2,1)S(1)} %get-tuple-element.8), channel_id=1, source_target_pairs={{8,0},{16,8},{24,16},{32,24},{40,32},{48,40},{56,48},{64,56},{72,6... | collective-permute-start | bytes 589832 | tf_op jit(solution)/shard_map/ppermute | solution.py:21
  65.2 0.2 collective-permute-done.4
  65.4 7.7 %collective-permute-done.5 = bf16[768,128]{1,0:T(8,128)(2,1)S(1)} collective-permute-done((bf16[768,128]{1,0:T(8,128)(2,1)S(1)}, bf16[768,128]{1,0:T(8,128)(2,1)S(1)}, u32[]{:S(2)}, u32[]{:S(2)}) %collective-permute-start.5) | collective-permute-done | bytes 196640 | tf_op jit(solution)/shard_map/ppermute | solution.py:21
  73.1 0.9 pad_maximum_fusion.2
  74.0 3.2 %gather_fusion.2 = bf16[64,128,128]{2,1,0:T(8,128)(2,1)} fusion(bf16[20,128,128]{2,1,0:T(8,128)(2,1)} %bitcast.111, s32[1024]{0:T(1024)S(1)} %pad_clamp_fusion), kind=kCustom, calls=%fused_computation.2 | custom fusion | bytes 4194560 | tf_op jit(solution)/shard_map/gather | solution.py:45
  77.3 2.3 %fusion.13 = f32[8,128,128,1]{1,2,3,0:T(8,128)S(1)} fusion(bf16[8,8,128,128]{3,2,1,0:T(8,128)(2,1)S(1)} %copy-done, bf16[8,8,128,128]{3,2,1,0:T(8,128)(2,1)} %bitcast.106), kind=kOutput, calls=%fused_computation.31 | convolution fusion | flops 268435456 | bytes 4718592 | tf_op jit(solution)/shard_map/bjrc,bjcv->brv/dot_general | solution.py:46
  79.5 0.0 copy-start.1
  79.6 0.2 fusion.5
  79.8 1.9 %collective-permute-start.6 = (bf16[768,128]{1,0:T(8,128)(2,1)S(1)}, bf16[768,128]{1,0:T(8,128)(2,1)S(1)}, u32[]{:S(2)}, u32[]{:S(2)}) collective-permute-start(bf16[768,128]{1,0:T(8,128)(2,1)S(1)} %get-tuple-element.5), channel_id=1, source_target_pairs={{0,8},{8,16},{16,24},{24,32},{32,40},{40,48},{48,56},{56,64},{64,7... | collective-permute-start | bytes 589832 | tf_op jit(solution)/shard_map/ppermute | solution.py:19
  81.8 2.4 %collective-permute-start.7 = (bf16[768,128]{1,0:T(8,128)(2,1)S(1)}, bf16[768,128]{1,0:T(8,128)(2,1)S(1)}, u32[]{:S(2)}, u32[]{:S(2)}) collective-permute-start(bf16[768,128]{1,0:T(8,128)(2,1)S(1)} %get-tuple-element.6), channel_id=1, source_target_pairs={{8,0},{16,8},{24,16},{32,24},{40,32},{48,40},{56,48},{64,56},{72,6... | collective-permute-start | bytes 589832 | tf_op jit(solution)/shard_map/ppermute | solution.py:21
  84.2 0.2 collective-permute-done.6
  84.3 7.7 %collective-permute-done.7 = bf16[768,128]{1,0:T(8,128)(2,1)S(1)} collective-permute-done((bf16[768,128]{1,0:T(8,128)(2,1)S(1)}, bf16[768,128]{1,0:T(8,128)(2,1)S(1)}, u32[]{:S(2)}, u32[]{:S(2)}) %collective-permute-start.7) | collective-permute-done | bytes 196640 | tf_op jit(solution)/shard_map/ppermute | solution.py:21
  92.1 0.9 pad_maximum_fusion.3
  92.9 0.0 copy-done.1
  92.9 3.2 %gather_fusion.3 = bf16[64,128,128]{2,1,0:T(8,128)(2,1)} fusion(bf16[20,128,128]{2,1,0:T(8,128)(2,1)} %bitcast.109, s32[1024]{0:T(1024)S(1)} %pad_clamp_fusion), kind=kCustom, calls=%fused_computation.3 | custom fusion | bytes 4194560 | tf_op jit(solution)/shard_map/gather | solution.py:45
  96.2 0.0 copy-start.2
  96.2 2.3 %fusion.14 = f32[8,128,128,1]{1,2,3,0:T(8,128)S(1)} fusion(bf16[8,8,128,128]{3,2,1,0:T(8,128)(2,1)S(1)} %copy-done, bf16[8,8,128,128]{3,2,1,0:T(8,128)(2,1)} %bitcast.103), kind=kOutput, calls=%fused_computation.32 | convolution fusion | flops 268435456 | bytes 4718592 | tf_op jit(solution)/shard_map/bjrc,bjcv->brv/dot_general | solution.py:46
  98.5 0.0 copy-done.2
  98.5 1.0 fusion.3
  (8 shorter events, 0.2 us)
Async XLA Ops:
  0.0 35.7 %copy-start = (bf16[8,8,128,128]{3,2,1,0:T(8,128)(2,1)S(1)}, bf16[8,8,128,128]{3,2,1,0:T(8,128)(2,1)}, u32[]{:S(2)}) copy-start(bf16[8,8,128,128]{3,2,1,0:T(8,128)(2,1)} %param.6) | copy-start | bytes 6291460
  0.0 30.9 %copy-start.3 = (s32[8,8]{1,0:T(8,128)S(1)}, s32[8,8]{1,0:T(8,128)}, u32[]{:S(2)}) copy-start(s32[8,8]{1,0:T(8,128)} %param.7) | copy-start | bytes 772
  3.0 17.6 %all-to-all-start = ((bf16[128,8,128]{2,0,1:T(8,128)(2,1)}), bf16[128,8,128]{2,0,1:T(8,128)(2,1)S(1)}, u32[]{:S(2)}, u32[]{:S(2)}) async-start(bf16[128,8,128]{2,0,1:T(8,128)(2,1)} %bitcast.102), calls=%async_computation | async-start | bytes 524288 | tf_op jit(solution)/shard_map/all_to_all | solution.py:30
  20.7 11.6 %collective-permute-start.1 = (bf16[768,128]{1,0:T(8,128)(2,1)S(1)}, bf16[768,128]{1,0:T(8,128)(2,1)S(1)}, u32[]{:S(2)}, u32[]{:S(2)}) collective-permute-start(bf16[768,128]{1,0:T(8,128)(2,1)S(1)} %bitcast.114), channel_id=1, source_target_pairs={{8,0},{16,8},{24,16},{32,24},{40,32},{48,40},{56,48},{64,56},{72,6... | collective-permute-start | bytes 589832 | tf_op jit(solution)/shard_map/ppermute | solution.py:21
  25.1 8.4 %collective-permute-start = (bf16[768,128]{1,0:T(8,128)(2,1)S(1)}, bf16[768,128]{1,0:T(8,128)(2,1)S(1)}, u32[]{:S(2)}, u32[]{:S(2)}) collective-permute-start(bf16[768,128]{1,0:T(8,128)(2,1)S(1)} %bitcast.113), channel_id=1, source_target_pairs={{0,8},{8,16},{16,24},{24,32},{32,40},{40,48},{48,56},{56,64},{64,7... | collective-permute-start | bytes 589832 | tf_op jit(solution)/shard_map/ppermute | solution.py:19
  38.2 10.3 %collective-permute-start.2 = (bf16[768,128]{1,0:T(8,128)(2,1)S(1)}, bf16[768,128]{1,0:T(8,128)(2,1)S(1)}, u32[]{:S(2)}, u32[]{:S(2)}) collective-permute-start(bf16[768,128]{1,0:T(8,128)(2,1)S(1)} %get-tuple-element.9), channel_id=1, source_target_pairs={{0,8},{8,16},{16,24},{24,32},{32,40},{40,48},{48,56},{56,64},{64,7... | collective-permute-start | bytes 589832 | tf_op jit(solution)/shard_map/ppermute | solution.py:19
  45.9 10.3 %collective-permute-start.3 = (bf16[768,128]{1,0:T(8,128)(2,1)S(1)}, bf16[768,128]{1,0:T(8,128)(2,1)S(1)}, u32[]{:S(2)}, u32[]{:S(2)}) collective-permute-start(bf16[768,128]{1,0:T(8,128)(2,1)S(1)} %get-tuple-element.10), channel_id=1, source_target_pairs={{8,0},{16,8},{24,16},{32,24},{40,32},{48,40},{56,48},{64,56},{72,6... | collective-permute-start | bytes 589832 | tf_op jit(solution)/shard_map/ppermute | solution.py:21
  60.9 4.5 %collective-permute-start.4 = (bf16[768,128]{1,0:T(8,128)(2,1)S(1)}, bf16[768,128]{1,0:T(8,128)(2,1)S(1)}, u32[]{:S(2)}, u32[]{:S(2)}) collective-permute-start(bf16[768,128]{1,0:T(8,128)(2,1)S(1)} %get-tuple-element.7), channel_id=1, source_target_pairs={{0,8},{8,16},{16,24},{24,32},{32,40},{40,48},{48,56},{56,64},{64,7... | collective-permute-start | bytes 589832 | tf_op jit(solution)/shard_map/ppermute | solution.py:19
  62.8 10.3 %collective-permute-start.5 = (bf16[768,128]{1,0:T(8,128)(2,1)S(1)}, bf16[768,128]{1,0:T(8,128)(2,1)S(1)}, u32[]{:S(2)}, u32[]{:S(2)}) collective-permute-start(bf16[768,128]{1,0:T(8,128)(2,1)S(1)} %get-tuple-element.8), channel_id=1, source_target_pairs={{8,0},{16,8},{24,16},{32,24},{40,32},{48,40},{56,48},{64,56},{72,6... | collective-permute-start | bytes 589832 | tf_op jit(solution)/shard_map/ppermute | solution.py:21
  79.5 13.4 %copy-start.1 = (f32[8,128,128,1]{1,2,3,0:T(8,128)}, f32[8,128,128,1]{1,2,3,0:T(8,128)S(1)}, u32[]{:S(2)}) copy-start(f32[8,128,128,1]{1,2,3,0:T(8,128)S(1)} %fusion.13) | copy-start | bytes 1572868
  79.8 4.5 %collective-permute-start.6 = (bf16[768,128]{1,0:T(8,128)(2,1)S(1)}, bf16[768,128]{1,0:T(8,128)(2,1)S(1)}, u32[]{:S(2)}, u32[]{:S(2)}) collective-permute-start(bf16[768,128]{1,0:T(8,128)(2,1)S(1)} %get-tuple-element.5), channel_id=1, source_target_pairs={{0,8},{8,16},{16,24},{24,32},{32,40},{40,48},{48,56},{56,64},{64,7... | collective-permute-start | bytes 589832 | tf_op jit(solution)/shard_map/ppermute | solution.py:19
  81.8 10.3 %collective-permute-start.7 = (bf16[768,128]{1,0:T(8,128)(2,1)S(1)}, bf16[768,128]{1,0:T(8,128)(2,1)S(1)}, u32[]{:S(2)}, u32[]{:S(2)}) collective-permute-start(bf16[768,128]{1,0:T(8,128)(2,1)S(1)} %get-tuple-element.6), channel_id=1, source_target_pairs={{8,0},{16,8},{24,16},{32,24},{40,32},{48,40},{56,48},{64,56},{72,6... | collective-permute-start | bytes 589832 | tf_op jit(solution)/shard_map/ppermute | solution.py:21
  96.2 2.4 %copy-start.2 = (f32[8,128,128,1]{1,2,3,0:T(8,128)S(1)}, f32[8,128,128,1]{1,2,3,0:T(8,128)}, u32[]{:S(2)}) copy-start(f32[8,128,128,1]{1,2,3,0:T(8,128)} %copy-done.1) | copy-start | bytes 1572868
where the time goes:
time: 100 us; the launch traced here: 99.5 us
  waiting for transfers between devices  37 us (37%)
  starting transfers between devices  35.8 us (36%)
  local copies, waits for them, and re-layouts  11.8 us (12%)
  matrix products  11.5 us (12%)
  other arithmetic  3.32 us (3%)
    ppermute x4, waiting for transfers between devices, extended_2(): lax.ppermute(head, axis, [((i + 1) % count, i) for i in range(ends)])  24.4 us
    ppermute x4, starting transfers between devices, extended_2(): lax.ppermute(tail, axis, [(i, (i + 1) % count) for i in range(ends)])  17.4 us
    ppermute x4, starting transfers between devices, extended_2(): lax.ppermute(head, axis, [((i + 1) % count, i) for i in range(ends)])  11.1 us
    gather x4, local copies, waits for them, and re-layouts, apply_operator(): picked = tiles[local_index]  10.8 us
    all_to_all x1, waiting for transfers between devices, per_device(): lax.all_to_all(rotated, 'vec', split_axis=1, concat_axis=0, tiled=True)  10.4 us
    dot_general x4, matrix products, apply_operator(): jnp.einsum('bjrc,bjcv->brv', blocks, picked, preferred_element_type=jnp.f...  9.2 us
    all_to_all x1, starting transfers between devices, per_device(): lax.all_to_all(rotated, 'vec', split_axis=1, concat_axis=0, tiled=True)  7.27 us
    dot_general x1, matrix products, per_device(): jnp.dot(vectors, rotation, preferred_element_type=jnp.float32)  2.28 us
  transfers between devices with their start and end apart: 9, of which 9 were waited for; matrix products, arithmetic and copies ran while one was open for 0% of the time, Pallas kernels for 0%

commit v1 on v0

v1 whole, which is shorter than its diff:
```python
import jax
import jax.numpy as jnp
from jax import lax
from jax.experimental import pallas as pl
from jax.experimental.pallas import tpu as pltpu
from jax.sharding import PartitionSpec as P

DEG = 4
REACH_LO = 6
REACH_HI = 2


def shift_up(cells, axis):
    count = lax.axis_size(axis)
    return lax.ppermute(cells, axis, [(i, i + 1) for i in range(count - 1)])


def shift_down(cells, axis):
    count = lax.axis_size(axis)
    return lax.ppermute(cells, axis, [(i + 1, i) for i in range(count - 1)])


def halo_extend(state_bf, block_rows):
    lo = shift_up(state_bf[state_bf.shape[0] - REACH_LO * block_rows:], "row")
    hi = shift_down(state_bf[: REACH_HI * block_rows], "row")
    return jnp.concatenate([lo, state_bf, hi], axis=0)


def make_apply(local_blocks, nnz, block_rows, width, n_tiles, first):
    def kernel(idx_ref, ext_ref, blk_ref, *rest):
        if first:
            cur_out, sent_out = rest
        else:
            cur_ref, prev_ref, cur_out, sent_out = rest

        def row_body(b, carry):
            acc = jnp.zeros((block_rows, width), jnp.float32)
            for j in range(nnz):
                t = idx_ref[b * nnz + j]
                acc = acc + jnp.dot(blk_ref[b, j], ext_ref[t], preferred_element_type=jnp.float32)
            if first:
                p = ext_ref[b + REACH_LO].astype(jnp.float32)
                nxt = (acc - 0.25 * p) / 2.0
            else:
                c = cur_ref[b]
                nxt = 2.0 * (acc - 0.25 * c) / 2.0 - prev_ref[b]
            cur_out[b] = nxt
            sent_out[b] = nxt.astype(jnp.bfloat16)
            return carry

        lax.fori_loop(0, local_blocks, row_body, 0)

    vmem = pl.BlockSpec(memory_space=pltpu.VMEM)
    smem = pl.BlockSpec(memory_space=pltpu.SMEM)
    n_in = 3 if first else 5
    shape3 = (local_blocks, block_rows, width)
    return pl.pallas_call(
        kernel,
        in_specs=[smem] + [vmem] * (n_in - 1),
        out_specs=(vmem, vmem),
        out_shape=(
            jax.ShapeDtypeStruct(shape3, jnp.float32),
            jax.ShapeDtypeStruct(shape3, jnp.bfloat16),
        ),
    )


def per_device(vectors, rotation, blocks, columns):
    rotated = jnp.dot(vectors, rotation, preferred_element_type=jnp.float32).astype(jnp.bfloat16)
    panel = lax.all_to_all(rotated, "vec", split_axis=1, concat_axis=0, tiled=True)
    local_blocks, nnz, block_rows, _ = blocks.shape
    width = panel.shape[1]
    n_tiles = local_blocks + REACH_LO + REACH_HI
    first_block = lax.axis_index("row") * local_blocks
    local_index = jnp.clip(columns - first_block + REACH_LO, 0, n_tiles - 1).reshape(-1).astype(jnp.int32)

    first_apply = make_apply(local_blocks, nnz, block_rows, width, n_tiles, True)
    next_apply = make_apply(local_blocks, nnz, block_rows, width, n_tiles, False)

    def tiles_of(state_bf):
        return halo_extend(state_bf, block_rows).reshape(n_tiles, block_rows, width)

    prev = panel.astype(jnp.float32).reshape(local_blocks, block_rows, width)
    cur, sent = first_apply(local_index, tiles_of(panel), blocks)
    for degree in range(DEG - 1):
        nxt, sent = next_apply(local_index, tiles_of(sent.reshape(-1, width)), blocks, cur, prev)
        prev = cur
        cur = nxt
    return sent.reshape(local_blocks * block_rows, width)


def solution(mesh):
    return jax.shard_map(
        per_device,
        mesh=mesh,
        in_specs=(P(("row", "vec"), None), P(), P("row", None, None, None), P("row", None)),
        out_specs=P("row", "vec"),
        check_vma=False,
    )
```

time: 100 us -> 105 us (1.050)
  Pallas kernels: 0 us -> 18.6 us
  matrix products: 11.5 us -> 1.39 us
  waiting for transfers between devices: 37 us -> 27.6 us
  starting transfers between devices: 35.8 us -> 41 us
  other arithmetic: 3.32 us -> 7.07 us
  local copies, waits for them, and re-layouts: 11.8 us -> 8.58 us
    pallas_call x0 -> x4, Pallas kernels: none -> 18.6 us  [the longest x3 14.1 us: per_device(): next_apply(local_index, tiles_of(sent.reshape(-1, width)), blocks, cur, p...]
    gather x4 -> x0, local copies, waits for them, and re-layouts: 10.8 us -> none  [apply_operator(): picked = tiles[local_index]]
    ppermute x8, waiting for transfers between devices: 26.6 us -> 17.2 us  [the longest x4 13.5 us: shift_down(): return lax.ppermute(cells, axis, [(i + 1, i) for i in range(count - 1)])]
    dot_general x4 -> x0, matrix products: 9.2 us -> none  [apply_operator(): jnp.einsum('bjrc,bjcv->brv', blocks, picked, preferred_element_type=jnp.f...]
    ppermute x8, starting transfers between devices: 28.5 us -> 33.7 us  [the longest x4 23.2 us: shift_up(): return lax.ppermute(cells, axis, [(i, i + 1) for i in range(count - 1)])]
    slice x4 -> x8, local copies, waits for them, and re-layouts: 0.13 us -> 5.38 us  [the longest x4 2.83 us: halo_extend(): lo = shift_up(state_bf[state_bf.shape[0] - REACH_LO * block_rows:], 'row')]
    concatenate x4, other arithmetic: 1.84 us -> 6.21 us  [halo_extend(): return jnp.concatenate([lo, state_bf, hi], axis=0)]
    unnamed x8 -> x4, local copies, waits for them, and re-layouts: 0.02 us -> 1.59 us
  transfers between devices with their start and end apart: 9 -> 9, of which waited for: 9 -> 5; matrix products, arithmetic and copies ran while one was open for 0% -> 3% of each run, Pallas kernels for 0% -> 0%
where the time goes in v1:
time: 105 us; the launch traced here: 104 us
  starting transfers between devices  41 us (39%)
  waiting for transfers between devices  27.6 us (26%)
  Pallas kernels  18.6 us (18%)
  local copies, waits for them, and re-layouts  8.58 us (8%)
  other arithmetic  7.07 us (7%)
  matrix products  1.39 us (1%)
    ppermute x4, starting transfers between devices, shift_up(): return lax.ppermute(cells, axis, [(i, i + 1) for i in range(count - 1)])  23.2 us
    pallas_call x3, Pallas kernels, per_device(): next_apply(local_index, tiles_of(sent.reshape(-1, width)), blocks, cur, p...  14.1 us
    ppermute x4, waiting for transfers between devices, shift_down(): return lax.ppermute(cells, axis, [(i + 1, i) for i in range(count - 1)])  13.5 us
    ppermute x4, starting transfers between devices, shift_down(): return lax.ppermute(cells, axis, [(i + 1, i) for i in range(count - 1)])  10.6 us
    all_to_all x1, waiting for transfers between devices, per_device(): lax.all_to_all(rotated, 'vec', split_axis=1, concat_axis=0, tiled=True)  10.4 us
    all_to_all x1, starting transfers between devices, per_device(): lax.all_to_all(rotated, 'vec', split_axis=1, concat_axis=0, tiled=True)  7.28 us
    concatenate x4, other arithmetic, halo_extend(): return jnp.concatenate([lo, state_bf, hi], axis=0)  6.21 us
    pallas_call x1, Pallas kernels, per_device(): cur, sent = first_apply(local_index, tiles_of(panel), blocks)  4.47 us
  transfers between devices with their start and end apart: 9, of which 5 were waited for; matrix products, arithmetic and copies ran while one was open for 3% of the time, Pallas kernels for 0%

profile of v1, /device:TPU:399, one launch (start us, length us, event | category | flops | bytes accessed | tf_op | source)
XLA Modules:
  0.0 104.3 jit_solution(16430365727166499478)
XLA Ops:
  0.0 0.0 copy-start
  0.0 0.0 copy-start.1
  0.0 1.6 %copy-done = bf16[1024,1024]{1,0:T(8,128)(2,1)S(1)} copy-done((bf16[1024,1024]{1,0:T(8,128)(2,1)S(1)}, bf16[1024,1024]{1,0:T(8,128)(2,1)}, u32[]{:S(2)}) %copy-start) | copy-done | bytes 2097176
  1.6 1.4 %convolution_convert_fusion = bf16[128,1024]{1,0:T(8,128)(2,1)S(1)} fusion(bf16[128,1024]{1,0:T(8,128)(2,1)} %param.4, bf16[1024,1024]{1,0:T(8,128)(2,1)S(1)} %copy-done), kind=kOutput, calls=%fused_computation | convolution fusion | flops 268566528 | bytes 2621440 | tf_op jit(solution)/shard_map/dot_general | solution.py:69
  3.0 0.2 copy.5
  3.2 0.9 copy.6
  4.0 7.3 %all-to-all-start = ((bf16[128,8,128]{2,0,1:T(8,128)(2,1)}), bf16[128,8,128]{2,0,1:T(8,128)(2,1)S(1)}, u32[]{:S(2)}, u32[]{:S(2)}) async-start(bf16[128,8,128]{2,0,1:T(8,128)(2,1)} %copy.6), calls=%async_computation | async-start | bytes 524288 | tf_op jit(solution)/shard_map/all_to_all | solution.py:70
  11.3 10.4 %all-to-all-done = bf16[128,8,128]{2,0,1:T(8,128)(2,1)S(1)} async-done(((bf16[128,8,128]{2,0,1:T(8,128)(2,1)}), bf16[128,8,128]{2,0,1:T(8,128)(2,1)S(1)}, u32[]{:S(2)}, u32[]{:S(2)}) %all-to-all-start) | async-done | bytes 262176 | tf_op jit(solution)/shard_map/all_to_all | solution.py:70
  21.7 4.4 %collective-permute-start.1 = (bf16[256,128]{1,0:T(8,128)(2,1)S(1)}, bf16[256,128]{1,0:T(8,128)(2,1)S(1)}, u32[]{:S(2)}, u32[]{:S(2)}) collective-permute-start(bf16[256,128]{1,0:T(8,128)(2,1)S(1)} %bitcast.38), channel_id=1, source_target_pairs={{8,0},{16,8},{24,16},{32,24},{40,32},{48,40},{56,48},{64,56},{72,6... | collective-permute-start | bytes 196616 | tf_op jit(solution)/shard_map/ppermute | solution.py:20
  26.1 5.8 %collective-permute-start = (bf16[768,128]{1,0:T(8,128)(2,1)S(1)}, bf16[768,128]{1,0:T(8,128)(2,1)S(1)}, u32[]{:S(2)}, u32[]{:S(2)}) collective-permute-start(bf16[768,128]{1,0:T(8,128)(2,1)S(1)} %bitcast.34), channel_id=1, source_target_pairs={{0,8},{8,16},{16,24},{24,32},{32,40},{40,48},{48,56},{56,64},{64,7... | collective-permute-start | bytes 589832 | tf_op jit(solution)/shard_map/ppermute | solution.py:15
  31.9 0.0 copy-done.1
  31.9 0.6 reshape.39.idx_ref
  32.5 0.0 collective-permute-done.1
  32.5 2.0 %collective-permute-done = bf16[768,128]{1,0:T(8,128)(2,1)S(1)} collective-permute-done((bf16[768,128]{1,0:T(8,128)(2,1)S(1)}, bf16[768,128]{1,0:T(8,128)(2,1)S(1)}, u32[]{:S(2)}, u32[]{:S(2)}) %collective-permute-start) | collective-permute-done | bytes 196640 | tf_op jit(solution)/shard_map/ppermute | solution.py:15
  34.5 0.8 pad_maximum_fusion
  35.3 4.5 %shard_map.46 = (f32[8,128,128]{2,1,0:T(8,128)}, bf16[8,128,128]{2,1,0:T(8,128)(2,1)}) custom-call(s32[64]{0:T(128)} %reshape.39.idx_ref, bf16[16,128,128]{2,1,0:T(8,128)(2,1)} %bitcast.29, bf16[8,8,128,128]{3,2,1,0:T(8,128)(2,1)} %blk_ref.7), custom_call_target="tpu_custom_call" | custom-call | tf_op jit(solution)/shard_map/pallas_call | solution.py:84
  39.8 0.8 slice.54
  40.6 0.9 slice.52
  41.6 1.9 %collective-permute-start.3 = (bf16[256,128]{1,0:T(8,128)(2,1)S(1)}, bf16[256,128]{1,0:T(8,128)(2,1)S(1)}, u32[]{:S(2)}, u32[]{:S(2)}) collective-permute-start(bf16[256,128]{1,0:T(8,128)(2,1)S(1)} %bitcast.39), channel_id=1, source_target_pairs={{8,0},{16,8},{24,16},{32,24},{40,32},{48,40},{56,48},{64,56},{72,6... | collective-permute-start | bytes 196616 | tf_op jit(solution)/shard_map/ppermute | solution.py:20
  43.5 7.7 %collective-permute-start.2 = (bf16[768,128]{1,0:T(8,128)(2,1)S(1)}, bf16[768,128]{1,0:T(8,128)(2,1)S(1)}, u32[]{:S(2)}, u32[]{:S(2)}) collective-permute-start(bf16[768,128]{1,0:T(8,128)(2,1)S(1)} %bitcast.35), channel_id=1, source_target_pairs={{0,8},{8,16},{16,24},{24,32},{32,40},{40,48},{48,56},{56,64},{64,7... | collective-permute-start | bytes 589832 | tf_op jit(solution)/shard_map/ppermute | solution.py:15
  51.2 0.8 bitcast_convert_fusion.rest_1_
  52.1 0.0 collective-permute-done.3
  52.1 1.7 %collective-permute-done.2 = bf16[768,128]{1,0:T(8,128)(2,1)S(1)} collective-permute-done((bf16[768,128]{1,0:T(8,128)(2,1)S(1)}, bf16[768,128]{1,0:T(8,128)(2,1)S(1)}, u32[]{:S(2)}, u32[]{:S(2)}) %collective-permute-start.2) | collective-permute-done | bytes 196640 | tf_op jit(solution)/shard_map/ppermute | solution.py:15
  53.8 1.8 %pad_maximum_fusion.1 = bf16[2048,128]{1,0:T(8,128)(2,1)} fusion(bf16[256,128]{1,0:T(8,128)(2,1)S(1)} %collective-permute-done.3, bf16[1024,128]{1,0:T(8,128)(2,1)} %bitcast.31, bf16[768,128]{1,0:T(8,128)(2,1)S(1)} %collective-permute-done.2), kind=kLoop, calls=%fused_computation.2 | loop fusion | flops 1572864 | bytes 1048576 | tf_op jit(solution)/shard_map/concatenate | solution.py:26
  55.6 4.7 %shard_map.47 = (f32[8,128,128]{2,1,0:T(8,128)}, bf16[8,128,128]{2,1,0:T(8,128)(2,1)}) custom-call(s32[64]{0:T(128)} %reshape.39.idx_ref, bf16[16,128,128]{2,1,0:T(8,128)(2,1)} %bitcast.27, bf16[8,8,128,128]{3,2,1,0:T(8,128)(2,1)} %blk_ref.7, f32[8,128,128]{2,1,0:T(8,128)} %get-tuple-element.13.rest_0_.rest_1_, f32[8,128,128]{2,1,0:T(8,128)} %bitcast_convert_fusion.rest_1_), custom_call_target="tpu_custom_call" | custom-call | tf_op jit(solution)/shard_map/pallas_call | solution.py:86
  60.3 0.9 slice.56
  61.3 7.7 %collective-permute-start.4 = (bf16[768,128]{1,0:T(8,128)(2,1)S(1)}, bf16[768,128]{1,0:T(8,128)(2,1)S(1)}, u32[]{:S(2)}, u32[]{:S(2)}) collective-permute-start(bf16[768,128]{1,0:T(8,128)(2,1)S(1)} %bitcast.36), channel_id=1, source_target_pairs={{0,8},{8,16},{16,24},{24,32},{32,40},{40,48},{48,56},{56,64},{64,7... | collective-permute-start | bytes 589832 | tf_op jit(solution)/shard_map/ppermute | solution.py:15
  69.0 0.8 slice.58
  69.8 1.9 %collective-permute-start.5 = (bf16[256,128]{1,0:T(8,128)(2,1)S(1)}, bf16[256,128]{1,0:T(8,128)(2,1)S(1)}, u32[]{:S(2)}, u32[]{:S(2)}) collective-permute-start(bf16[256,128]{1,0:T(8,128)(2,1)S(1)} %bitcast.40), channel_id=1, source_target_pairs={{8,0},{16,8},{24,16},{32,24},{40,32},{48,40},{56,48},{64,56},{72,6... | collective-permute-start | bytes 196616 | tf_op jit(solution)/shard_map/ppermute | solution.py:20
  71.8 7.0 %collective-permute-done.5 = bf16[256,128]{1,0:T(8,128)(2,1)S(1)} collective-permute-done((bf16[256,128]{1,0:T(8,128)(2,1)S(1)}, bf16[256,128]{1,0:T(8,128)(2,1)S(1)}, u32[]{:S(2)}, u32[]{:S(2)}) %collective-permute-start.5) | collective-permute-done | bytes 65568 | tf_op jit(solution)/shard_map/ppermute | solution.py:20
  78.7 0.0 collective-permute-done.4
  78.7 1.8 %pad_maximum_fusion.2 = bf16[2048,128]{1,0:T(8,128)(2,1)} fusion(bf16[256,128]{1,0:T(8,128)(2,1)S(1)} %collective-permute-done.5, bf16[1024,128]{1,0:T(8,128)(2,1)} %bitcast.32, bf16[768,128]{1,0:T(8,128)(2,1)S(1)} %collective-permute-done.4), kind=kLoop, calls=%fused_computation.3 | loop fusion | flops 1572864 | bytes 1048576 | tf_op jit(solution)/shard_map/concatenate | solution.py:26
  80.5 4.7 %shard_map.48 = (f32[8,128,128]{2,1,0:T(8,128)}, bf16[8,128,128]{2,1,0:T(8,128)(2,1)}) custom-call(s32[64]{0:T(128)} %reshape.39.idx_ref, bf16[16,128,128]{2,1,0:T(8,128)(2,1)} %bitcast.28, bf16[8,8,128,128]{3,2,1,0:T(8,128)(2,1)} %blk_ref.7, f32[8,128,128]{2,1,0:T(8,128)} %get-tuple-element.15.rest_0_.rest_1_, f32[8,128,128]{2,1,0:T(8,128)} %get-tuple-element.13.rest_0_.rest_1_), custom_call_target="tpu_custom_call" | custom-call | tf_op jit(solution)/shard_map/pallas_call | solution.py:86
  85.2 0.9 slice.60
  86.2 1.9 %collective-permute-start.6 = (bf16[768,128]{1,0:T(8,128)(2,1)S(1)}, bf16[768,128]{1,0:T(8,128)(2,1)S(1)}, u32[]{:S(2)}, u32[]{:S(2)}) collective-permute-start(bf16[768,128]{1,0:T(8,128)(2,1)S(1)} %bitcast.37), channel_id=1, source_target_pairs={{0,8},{8,16},{16,24},{24,32},{32,40},{40,48},{48,56},{56,64},{64,7... | collective-permute-start | bytes 589832 | tf_op jit(solution)/shard_map/ppermute | solution.py:15
  88.1 0.8 slice.62
  89.0 2.4 %collective-permute-start.7 = (bf16[256,128]{1,0:T(8,128)(2,1)S(1)}, bf16[256,128]{1,0:T(8,128)(2,1)S(1)}, u32[]{:S(2)}, u32[]{:S(2)}) collective-permute-start(bf16[256,128]{1,0:T(8,128)(2,1)S(1)} %bitcast.41), channel_id=1, source_target_pairs={{8,0},{16,8},{24,16},{32,24},{40,32},{48,40},{56,48},{64,56},{72,6... | collective-permute-start | bytes 196616 | tf_op jit(solution)/shard_map/ppermute | solution.py:20
  91.4 6.5 %collective-permute-done.7 = bf16[256,128]{1,0:T(8,128)(2,1)S(1)} collective-permute-done((bf16[256,128]{1,0:T(8,128)(2,1)S(1)}, bf16[256,128]{1,0:T(8,128)(2,1)S(1)}, u32[]{:S(2)}, u32[]{:S(2)}) %collective-permute-start.7) | collective-permute-done | bytes 65568 | tf_op jit(solution)/shard_map/ppermute | solution.py:20
  97.9 0.0 collective-permute-done.6
  97.9 1.8 %pad_maximum_fusion.3 = bf16[2048,128]{1,0:T(8,128)(2,1)} fusion(bf16[256,128]{1,0:T(8,128)(2,1)S(1)} %collective-permute-done.7, bf16[1024,128]{1,0:T(8,128)(2,1)} %bitcast.33, bf16[768,128]{1,0:T(8,128)(2,1)S(1)} %collective-permute-done.6), kind=kLoop, calls=%fused_computation.4 | loop fusion | flops 1572864 | bytes 1048576 | tf_op jit(solution)/shard_map/concatenate | solution.py:26
  99.6 4.7 %shard_map.49 = (f32[8,128,128]{2,1,0:T(8,128)}, bf16[8,128,128]{2,1,0:T(8,128)(2,1)}) custom-call(s32[64]{0:T(128)} %reshape.39.idx_ref, bf16[16,128,128]{2,1,0:T(8,128)(2,1)} %bitcast.26, bf16[8,8,128,128]{3,2,1,0:T(8,128)(2,1)} %blk_ref.7, f32[8,128,128]{2,1,0:T(8,128)} %get-tuple-element.17.rest_0_, f32[8,128,128]{2,1,0:T(8,128)} %get-tuple-element.15.rest_0_.rest_1_), custom_call_target="tpu_custom_call" | custom-call | tf_op jit(solution)/shard_map/pallas_call | solution.py:86
  (3 shorter events, 0.0 us)
Async XLA Ops:
  0.0 1.6 %copy-start = (bf16[1024,1024]{1,0:T(8,128)(2,1)S(1)}, bf16[1024,1024]{1,0:T(8,128)(2,1)}, u32[]{:S(2)}) copy-start(bf16[1024,1024]{1,0:T(8,128)(2,1)} %param.5) | copy-start | bytes 6291460
  0.0 31.9 %copy-start.1 = (s32[8,8]{1,0:T(8,128)S(1)}, s32[8,8]{1,0:T(8,128)}, u32[]{:S(2)}) copy-start(s32[8,8]{1,0:T(8,128)} %param.7) | copy-start | bytes 772
  4.0 17.7 %all-to-all-start = ((bf16[128,8,128]{2,0,1:T(8,128)(2,1)}), bf16[128,8,128]{2,0,1:T(8,128)(2,1)S(1)}, u32[]{:S(2)}, u32[]{:S(2)}) async-start(bf16[128,8,128]{2,0,1:T(8,128)(2,1)} %copy.6), calls=%async_computation | async-start | bytes 524288 | tf_op jit(solution)/shard_map/all_to_all | solution.py:70
  21.7 10.8 %collective-permute-start.1 = (bf16[256,128]{1,0:T(8,128)(2,1)S(1)}, bf16[256,128]{1,0:T(8,128)(2,1)S(1)}, u32[]{:S(2)}, u32[]{:S(2)}) collective-permute-start(bf16[256,128]{1,0:T(8,128)(2,1)S(1)} %bitcast.38), channel_id=1, source_target_pairs={{8,0},{16,8},{24,16},{32,24},{40,32},{48,40},{56,48},{64,56},{72,6... | collective-permute-start | bytes 196616 | tf_op jit(solution)/shard_map/ppermute | solution.py:20
  26.1 8.4 %collective-permute-start = (bf16[768,128]{1,0:T(8,128)(2,1)S(1)}, bf16[768,128]{1,0:T(8,128)(2,1)S(1)}, u32[]{:S(2)}, u32[]{:S(2)}) collective-permute-start(bf16[768,128]{1,0:T(8,128)(2,1)S(1)} %bitcast.34), channel_id=1, source_target_pairs={{0,8},{8,16},{16,24},{24,32},{32,40},{40,48},{48,56},{56,64},{64,7... | collective-permute-start | bytes 589832 | tf_op jit(solution)/shard_map/ppermute | solution.py:15
  41.6 10.5 %collective-permute-start.3 = (bf16[256,128]{1,0:T(8,128)(2,1)S(1)}, bf16[256,128]{1,0:T(8,128)(2,1)S(1)}, u32[]{:S(2)}, u32[]{:S(2)}) collective-permute-start(bf16[256,128]{1,0:T(8,128)(2,1)S(1)} %bitcast.39), channel_id=1, source_target_pairs={{8,0},{16,8},{24,16},{32,24},{40,32},{48,40},{56,48},{64,56},{72,6... | collective-permute-start | bytes 196616 | tf_op jit(solution)/shard_map/ppermute | solution.py:20
  43.5 10.3 %collective-permute-start.2 = (bf16[768,128]{1,0:T(8,128)(2,1)S(1)}, bf16[768,128]{1,0:T(8,128)(2,1)S(1)}, u32[]{:S(2)}, u32[]{:S(2)}) collective-permute-start(bf16[768,128]{1,0:T(8,128)(2,1)S(1)} %bitcast.35), channel_id=1, source_target_pairs={{0,8},{8,16},{16,24},{24,32},{32,40},{40,48},{48,56},{56,64},{64,7... | collective-permute-start | bytes 589832 | tf_op jit(solution)/shard_map/ppermute | solution.py:15
  61.3 17.5 %collective-permute-start.4 = (bf16[768,128]{1,0:T(8,128)(2,1)S(1)}, bf16[768,128]{1,0:T(8,128)(2,1)S(1)}, u32[]{:S(2)}, u32[]{:S(2)}) collective-permute-start(bf16[768,128]{1,0:T(8,128)(2,1)S(1)} %bitcast.36), channel_id=1, source_target_pairs={{0,8},{8,16},{16,24},{24,32},{32,40},{40,48},{48,56},{56,64},{64,7... | collective-permute-start | bytes 589832 | tf_op jit(solution)/shard_map/ppermute | solution.py:15
  69.8 8.9 %collective-permute-start.5 = (bf16[256,128]{1,0:T(8,128)(2,1)S(1)}, bf16[256,128]{1,0:T(8,128)(2,1)S(1)}, u32[]{:S(2)}, u32[]{:S(2)}) collective-permute-start(bf16[256,128]{1,0:T(8,128)(2,1)S(1)} %bitcast.40), channel_id=1, source_target_pairs={{8,0},{16,8},{24,16},{32,24},{40,32},{48,40},{56,48},{64,56},{72,6... | collective-permute-start | bytes 196616 | tf_op jit(solution)/shard_map/ppermute | solution.py:20
  86.2 11.7 %collective-permute-start.6 = (bf16[768,128]{1,0:T(8,128)(2,1)S(1)}, bf16[768,128]{1,0:T(8,128)(2,1)S(1)}, u32[]{:S(2)}, u32[]{:S(2)}) collective-permute-start(bf16[768,128]{1,0:T(8,128)(2,1)S(1)} %bitcast.37), channel_id=1, source_target_pairs={{0,8},{8,16},{16,24},{24,32},{32,40},{40,48},{48,56},{56,64},{64,7... | collective-permute-start | bytes 589832 | tf_op jit(solution)/shard_map/ppermute | solution.py:15
  89.0 8.9 %collective-permute-start.7 = (bf16[256,128]{1,0:T(8,128)(2,1)S(1)}, bf16[256,128]{1,0:T(8,128)(2,1)S(1)}, u32[]{:S(2)}, u32[]{:S(2)}) collective-permute-start(bf16[256,128]{1,0:T(8,128)(2,1)S(1)} %bitcast.41), channel_id=1, source_target_pairs={{8,0},{16,8},{24,16},{32,24},{40,32},{48,40},{56,48},{64,56},{72,6... | collective-permute-start | bytes 196616 | tf_op jit(solution)/shard_map/ppermute | solution.py:20

commit v2 on v1

v2 whole, which is shorter than its diff:
```python
import jax
import jax.numpy as jnp
from jax import lax
from jax.experimental import pallas as pl
from jax.experimental.pallas import tpu as pltpu
from jax.sharding import PartitionSpec as P

DEG = 4
REACH_LO = 6
REACH_HI = 2


def shift_up(cells, axis):
    count = lax.axis_size(axis)
    return lax.ppermute(cells, axis, [(i, i + 1) for i in range(count - 1)])


def shift_down(cells, axis):
    count = lax.axis_size(axis)
    return lax.ppermute(cells, axis, [(i + 1, i) for i in range(count - 1)])


def make_apply(local_blocks, nnz, block_rows, width, piece_sizes, first, last):
    n_pieces = len(piece_sizes)
    n_tiles = sum(piece_sizes)
    n_in = n_pieces + 1 + (0 if first else 2)
    out_split = (local_blocks,) if last else (REACH_HI, local_blocks - REACH_HI)
    n_out = len(out_split) + (0 if last else 1)
    f32, bf16 = jnp.float32, jnp.bfloat16

    def kernel(idx_ref, *refs):
        ins = refs[:n_in]
        outs = refs[n_in:n_in + n_out]
        ext_v, blk_v, cp_v, res_v, sent_v, in_sem, blk_sem, cp_sem, out_sem = refs[n_in + n_out:]
        pieces = ins[:n_pieces]
        blk_hbm = ins[n_pieces]

        ext_copies = []
        start = 0
        for k, size in enumerate(piece_sizes):
            ext_copies.append(pltpu.make_async_copy(pieces[k], ext_v.at[start:start + size], in_sem.at[k]))
            start += size
        blk_copies = [pltpu.make_async_copy(blk_hbm.at[b], blk_v.at[b], blk_sem.at[b]) for b in range(local_blocks)]
        cp_copies = []
        if not first:
            cp_copies = [pltpu.make_async_copy(ins[n_pieces + 1 + k], cp_v.at[k], cp_sem.at[k]) for k in range(2)]
        for c in ext_copies:
            c.start()
        for c in blk_copies:
            c.start()
        for c in cp_copies:
            c.start()
        for c in ext_copies:
            c.wait()
        for c in cp_copies:
            c.wait()

        out_copies = []
        for b in range(local_blocks):
            blk_copies[b].wait()
            acc = jnp.zeros((block_rows, width), f32)
            for j in range(nnz):
                t = idx_ref[b * nnz + j]
                acc = acc + jnp.dot(blk_v[b, j], ext_v[t], preferred_element_type=f32)
            if first:
                p = ext_v[b + REACH_LO].astype(f32)
                nxt = (acc - 0.25 * p) / 2.0
            else:
                nxt = 2.0 * (acc - 0.25 * cp_v[0, b]) / 2.0 - cp_v[1, b]
            sent_v[b] = nxt.astype(bf16)
            if not last:
                res_v[b] = nxt
                c = pltpu.make_async_copy(res_v.at[b], outs[0].at[b], out_sem.at[b])
                c.start()
                out_copies.append(c)
        base = 0 if last else 1
        start = 0
        for k, size in enumerate(out_split):
            c = pltpu.make_async_copy(sent_v.at[start:start + size], outs[base + k], out_sem.at[local_blocks + k])
            c.start()
            out_copies.append(c)
            start += size
        for c in out_copies:
            c.wait()

    any_spec = pl.BlockSpec(memory_space=pl.ANY)
    smem = pl.BlockSpec(memory_space=pltpu.SMEM)
    out_shape = []
    if not last:
        out_shape.append(jax.ShapeDtypeStruct((local_blocks, block_rows, width), f32))
    for size in out_split:
        out_shape.append(jax.ShapeDtypeStruct((size, block_rows, width), bf16))
    return pl.pallas_call(
        kernel,
        in_specs=[smem] + [any_spec] * n_in,
        out_specs=tuple([any_spec] * n_out),
        out_shape=tuple(out_shape),
        scratch_shapes=[
            pltpu.VMEM((n_tiles, block_rows, width), bf16),
            pltpu.VMEM((local_blocks, nnz, block_rows, block_rows), bf16),
            pltpu.VMEM((2, local_blocks, block_rows, width), f32),
            pltpu.VMEM((local_blocks, block_rows, width), f32),
            pltpu.VMEM((local_blocks, block_rows, width), bf16),
            pltpu.SemaphoreType.DMA((n_pieces,)),
            pltpu.SemaphoreType.DMA((local_blocks,)),
            pltpu.SemaphoreType.DMA((2,)),
            pltpu.SemaphoreType.DMA((local_blocks + 2,)),
        ],
    )


def per_device(vectors, rotation, blocks, columns):
    rotated = jnp.dot(vectors, rotation, preferred_element_type=jnp.float32).astype(jnp.bfloat16)
    panel = lax.all_to_all(rotated, "vec", split_axis=1, concat_axis=0, tiled=True)
    local_blocks, nnz, block_rows, _ = blocks.shape
    width = panel.shape[1]
    n_tiles = local_blocks + REACH_LO + REACH_HI
    first_block = lax.axis_index("row") * local_blocks
    local_index = jnp.clip(columns - first_block + REACH_LO, 0, n_tiles - 1).reshape(-1).astype(jnp.int32)

    tiles = panel.reshape(local_blocks, block_rows, width)
    head = tiles[:REACH_HI]
    tail = tiles[local_blocks - REACH_LO:]
    sizes_first = (REACH_LO, local_blocks, REACH_HI)
    sizes_next = (REACH_LO, REACH_HI, local_blocks - REACH_HI, REACH_HI)
    first_apply = make_apply(local_blocks, nnz, block_rows, width, sizes_first, True, False)
    next_apply = make_apply(local_blocks, nnz, block_rows, width, sizes_next, False, False)
    last_apply = make_apply(local_blocks, nnz, block_rows, width, sizes_next, False, True)

    prev = tiles.astype(jnp.float32)
    cur, head, rest = first_apply(local_index, shift_up(tail, "row"), tiles, shift_down(head, "row"), blocks)
    for degree in range(DEG - 1):
        tail = rest[rest.shape[0] - REACH_LO:]
        lo = shift_up(tail, "row")
        hi = shift_down(head, "row")
        if degree < DEG - 2:
            nxt, head, rest = next_apply(local_index, lo, head, rest, hi, blocks, cur, prev)
            prev = cur
            cur = nxt
        else:
            (out,) = last_apply(local_index, lo, head, rest, hi, blocks, cur, prev)
    return out.reshape(local_blocks * block_rows, width)


def solution(mesh):
    return jax.shard_map(
        per_device,
        mesh=mesh,
        in_specs=(P(("row", "vec"), None), P(), P("row", None, None, None), P("row", None)),
        out_specs=P("row", "vec"),
        check_vma=False,
    )
```

time: 105 us -> 101 us (0.962)
  other arithmetic: 7.07 us -> 1.79 us
  Pallas kernels: 18.6 us -> 22.7 us
  local copies, waits for them, and re-layouts: 8.58 us -> 6.02 us
    concatenate x4 -> x0, other arithmetic: 6.21 us -> none  [halo_extend(): return jnp.concatenate([lo, state_bf, hi], axis=0)]
    slice x8 -> x2, local copies, waits for them, and re-layouts: 5.38 us -> 0.02 us  [the longest x1 0.01 us: per_device(): tail = tiles[local_blocks - REACH_LO:]]
    pallas_call x4, Pallas kernels: 18.6 us -> 22.7 us  [the longest x2 11.6 us: per_device(): next_apply(local_index, lo, head, rest, hi, blocks, cur, prev)]
    unnamed x4 -> x22, local copies, waits for them, and re-layouts: 1.59 us -> 4.35 us
  transfers between devices with their start and end apart: 9 -> 9, of which waited for: 5 -> 5; matrix products, arithmetic and copies ran while one was open for 3% -> 2% of each run, Pallas kernels for 0% -> 0%
where the time goes in v2:
time: 101 us; the launch traced here: 100 us
  starting transfers between devices  40.9 us (40%)
  waiting for transfers between devices  27.4 us (27%)
  Pallas kernels  22.7 us (22%)
  local copies, waits for them, and re-layouts  6.02 us (6%)
  other arithmetic  1.79 us (2%)
  matrix products  1.39 us (1%)
    ppermute x4, starting transfers between devices, shift_up(): return lax.ppermute(cells, axis, [(i, i + 1) for i in range(count - 1)])  23.1 us
    ppermute x4, waiting for transfers between devices, shift_down(): return lax.ppermute(cells, axis, [(i + 1, i) for i in range(count - 1)])  13.9 us
    pallas_call x2, Pallas kernels, per_device(): next_apply(local_index, lo, head, rest, hi, blocks, cur, prev)  11.6 us
    ppermute x4, starting transfers between devices, shift_down(): return lax.ppermute(cells, axis, [(i + 1, i) for i in range(count - 1)])  10.6 us
    all_to_all x1, waiting for transfers between devices, per_device(): lax.all_to_all(rotated, 'vec', split_axis=1, concat_axis=0, tiled=True)  10.4 us
    all_to_all x1, starting transfers between devices, per_device(): lax.all_to_all(rotated, 'vec', split_axis=1, concat_axis=0, tiled=True)  7.28 us
    pallas_call x1, Pallas kernels, per_device(): out, = last_apply(local_index, lo, head, rest, hi, blocks, cur, prev)  5.79 us
    pallas_call x1, Pallas kernels, per_device(): first_apply(local_index, shift_up(tail, 'row'), tiles, shift_down(head, '...  5.31 us
  transfers between devices with their start and end apart: 9, of which 5 were waited for; matrix products, arithmetic and copies ran while one was open for 2% of the time, Pallas kernels for 0%

profile of v2, /device:TPU:399, one launch (start us, length us, event | category | flops | bytes accessed | tf_op | source)
XLA Modules:
  0.0 100.4 jit_solution(10999383296858061730)
XLA Ops:
  0.0 0.0 copy-start
  0.0 0.0 copy-start.10
  0.0 1.6 %copy-done = bf16[1024,1024]{1,0:T(8,128)(2,1)S(1)} copy-done((bf16[1024,1024]{1,0:T(8,128)(2,1)S(1)}, bf16[1024,1024]{1,0:T(8,128)(2,1)}, u32[]{:S(2)}) %copy-start) | copy-done | bytes 2097176
  1.6 1.4 %convolution_convert_fusion = bf16[128,1024]{1,0:T(8,128)(2,1)S(1)} fusion(bf16[128,1024]{1,0:T(8,128)(2,1)} %param.4, bf16[1024,1024]{1,0:T(8,128)(2,1)S(1)} %copy-done), kind=kOutput, calls=%fused_computation | convolution fusion | flops 268566528 | bytes 2621440 | tf_op jit(solution)/shard_map/dot_general | solution.py:113
  3.0 0.2 copy.5
  3.2 0.9 copy.6
  4.0 7.3 %all-to-all-start = ((bf16[128,8,128]{2,0,1:T(8,128)(2,1)}), bf16[128,8,128]{2,0,1:T(8,128)(2,1)S(1)}, u32[]{:S(2)}, u32[]{:S(2)}) async-start(bf16[128,8,128]{2,0,1:T(8,128)(2,1)} %copy.6), calls=%async_computation | async-start | bytes 524288 | tf_op jit(solution)/shard_map/all_to_all | solution.py:114
  11.3 10.4 %all-to-all-done = bf16[128,8,128]{2,0,1:T(8,128)(2,1)S(1)} async-done(((bf16[128,8,128]{2,0,1:T(8,128)(2,1)}), bf16[128,8,128]{2,0,1:T(8,128)(2,1)S(1)}, u32[]{:S(2)}, u32[]{:S(2)}) %all-to-all-start) | async-done | bytes 262176 | tf_op jit(solution)/shard_map/all_to_all | solution.py:114
  21.7 0.0 copy-start.1
  21.7 4.4 %collective-permute-start.1 = (bf16[2,128,128]{2,1,0:T(8,128)(2,1)S(1)}, bf16[2,128,128]{2,1,0:T(8,128)(2,1)S(1)}, u32[]{:S(2)}, u32[]{:S(2)}) collective-permute-start(bf16[2,128,128]{2,1,0:T(8,128)(2,1)S(1)} %slice.10), channel_id=1, source_target_pairs={{8,0},{16,8},{24,16},{32,24},{40,32},{48,40},{56,48},{64,56},{72,6... | collective-permute-start | bytes 196616 | tf_op jit(solution)/shard_map/ppermute | solution.py:20
  26.1 5.8 %collective-permute-start = (bf16[6,128,128]{2,1,0:T(8,128)(2,1)S(1)}, bf16[6,128,128]{2,1,0:T(8,128)(2,1)S(1)}, u32[]{:S(2)}, u32[]{:S(2)}) collective-permute-start(bf16[6,128,128]{2,1,0:T(8,128)(2,1)S(1)} %slice.9), channel_id=1, source_target_pairs={{0,8},{8,16},{16,24},{24,32},{32,40},{40,48},{48,56},{56,64},{64,7... | collective-permute-start | bytes 589832 | tf_op jit(solution)/shard_map/ppermute | solution.py:15
  31.9 0.0 copy-done.10
  31.9 0.6 reshape.12.idx_ref
  32.6 0.0 collective-permute-done.1.refs_2_
  32.6 0.0 copy-start.9
  32.6 1.9 %collective-permute-done.refs_0_ = bf16[6,128,128]{2,1,0:T(8,128)(2,1)S(1)} collective-permute-done((bf16[6,128,128]{2,1,0:T(8,128)(2,1)S(1)}, bf16[6,128,128]{2,1,0:T(8,128)(2,1)S(1)}, u32[]{:S(2)}, u32[]{:S(2)}) %collective-permute-start) | collective-permute-done | bytes 196640 | tf_op jit(solution)/shard_map/ppermute | solution.py:15
  34.5 0.0 copy-done.1
  34.5 0.0 copy-done.9
  34.5 0.0 copy-start.3
  34.5 0.7 copy-done.3
  35.2 5.3 %shard_map.46 = (f32[8,128,128]{2,1,0:T(8,128)}, bf16[2,128,128]{2,1,0:T(8,128)(2,1)}, bf16[6,128,128]{2,1,0:T(8,128)(2,1)}) custom-call(s32[64]{0:T(128)} %reshape.12.idx_ref, bf16[6,128,128]{2,1,0:T(8,128)(2,1)} %copy-done.3, bf16[8,128,128]{2,1,0:T(8,128)(2,1)} %bitcast.8, bf16[2,128,128]{2,1,0:T(8,128)(2,1)} %copy-done.9, bf16[8,8,128,128]{3,2,1,0:T(8,128)(2,1)} %refs_4_.5), custom_call_target="tpu_custom_call" | custom-call | tf_op jit(solution)/shard_map/pallas_call | solution.py:131
  40.5 1.9 %collective-permute-start.3 = (bf16[2,128,128]{2,1,0:T(8,128)(2,1)}, bf16[2,128,128]{2,1,0:T(8,128)(2,1)S(1)}, u32[]{:S(2)}, u32[]{:S(2)}) collective-permute-start(bf16[2,128,128]{2,1,0:T(8,128)(2,1)} %get-tuple-element.15.refs_1_), channel_id=1, source_target_pairs={{8,0},{16,8},{24,16},{32,24},{40,32},{48,40},{56,48},{64,56},{72,6... | collective-permute-start | bytes 196616 | tf_op jit(solution)/shard_map/ppermute | solution.py:20
  42.4 7.7 %collective-permute-start.2 = (bf16[6,128,128]{2,1,0:T(8,128)(2,1)}, bf16[6,128,128]{2,1,0:T(8,128)(2,1)S(1)}, u32[]{:S(2)}, u32[]{:S(2)}) collective-permute-start(bf16[6,128,128]{2,1,0:T(8,128)(2,1)} %get-tuple-element.14.refs_2_), channel_id=1, source_target_pairs={{0,8},{8,16},{16,24},{24,32},{32,40},{40,48},{48,56},{56,64},{64,7... | collective-permute-start | bytes 589832 | tf_op jit(solution)/shard_map/ppermute | solution.py:15
  50.2 1.8 %bitcast_convert_fusion.refs_6_ = f32[8,128,128]{2,1,0:T(8,128)} fusion(bf16[128,8,128]{2,0,1:T(8,128)(2,1)} %copy-done.1), kind=kLoop, calls=%fused_computation.2 | loop fusion | flops 131072 | bytes 786432 | tf_op jit(solution)/shard_map/convert_element_type | solution.py:130
  51.9 0.0 collective-permute-done.3.refs_3_
  51.9 0.0 copy-start.6
  51.9 1.1 %collective-permute-done.2.refs_0_ = bf16[6,128,128]{2,1,0:T(8,128)(2,1)S(1)} collective-permute-done((bf16[6,128,128]{2,1,0:T(8,128)(2,1)}, bf16[6,128,128]{2,1,0:T(8,128)(2,1)S(1)}, u32[]{:S(2)}, u32[]{:S(2)}) %collective-permute-start.2) | collective-permute-done | bytes 196640 | tf_op jit(solution)/shard_map/ppermute | solution.py:15
  53.1 0.0 copy-start.5
  53.1 0.0 copy-done.6
  53.1 0.7 copy-done.5
  53.7 5.8 %shard_map.47 = (f32[8,128,128]{2,1,0:T(8,128)}, bf16[2,128,128]{2,1,0:T(8,128)(2,1)}, bf16[6,128,128]{2,1,0:T(8,128)(2,1)}) custom-call(s32[64]{0:T(128)} %reshape.12.idx_ref, bf16[6,128,128]{2,1,0:T(8,128)(2,1)} %copy-done.5, bf16[2,128,128]{2,1,0:T(8,128)(2,1)} %get-tuple-element.15.refs_1_, bf16[6,128,128]{2,1,0:T(8,128)(2,1)} %get-tuple-element.14.refs_2_, ...), custom_call_target="tpu_custom_call" | custom-call | tf_op jit(solution)/shard_map/pallas_call | solution.py:137
  59.6 7.6 %collective-permute-start.4 = (bf16[6,128,128]{2,1,0:T(8,128)(2,1)}, bf16[6,128,128]{2,1,0:T(8,128)(2,1)S(1)}, u32[]{:S(2)}, u32[]{:S(2)}) collective-permute-start(bf16[6,128,128]{2,1,0:T(8,128)(2,1)} %get-tuple-element.17.refs_2_), channel_id=1, source_target_pairs={{0,8},{8,16},{16,24},{24,32},{32,40},{40,48},{48,56},{56,64},{64,7... | collective-permute-start | bytes 589832 | tf_op jit(solution)/shard_map/ppermute | solution.py:15
  67.2 1.9 %collective-permute-start.5 = (bf16[2,128,128]{2,1,0:T(8,128)(2,1)}, bf16[2,128,128]{2,1,0:T(8,128)(2,1)S(1)}, u32[]{:S(2)}, u32[]{:S(2)}) collective-permute-start(bf16[2,128,128]{2,1,0:T(8,128)(2,1)} %get-tuple-element.18.refs_1_), channel_id=1, source_target_pairs={{8,0},{16,8},{24,16},{32,24},{40,32},{48,40},{56,48},{64,56},{72,6... | collective-permute-start | bytes 196616 | tf_op jit(solution)/shard_map/ppermute | solution.py:20
  69.1 7.2 %collective-permute-done.5.refs_3_ = bf16[2,128,128]{2,1,0:T(8,128)(2,1)S(1)} collective-permute-done((bf16[2,128,128]{2,1,0:T(8,128)(2,1)}, bf16[2,128,128]{2,1,0:T(8,128)(2,1)S(1)}, u32[]{:S(2)}, u32[]{:S(2)}) %collective-permute-start.5) | collective-permute-done | bytes 65568 | tf_op jit(solution)/shard_map/ppermute | solution.py:20
  76.3 0.0 copy-start.7
  76.3 0.0 collective-permute-done.4.refs_0_
  76.3 0.0 copy-start.4
  76.3 0.6 copy-done.7
  76.9 0.1 copy-done.4
  77.0 5.8 %shard_map.48 = (f32[8,128,128]{2,1,0:T(8,128)}, bf16[2,128,128]{2,1,0:T(8,128)(2,1)}, bf16[6,128,128]{2,1,0:T(8,128)(2,1)}) custom-call(s32[64]{0:T(128)} %reshape.12.idx_ref, bf16[6,128,128]{2,1,0:T(8,128)(2,1)} %copy-done.4, bf16[2,128,128]{2,1,0:T(8,128)(2,1)} %get-tuple-element.18.refs_1_, bf16[6,128,128]{2,1,0:T(8,128)(2,1)} %get-tuple-element.17.refs_2_, ...), custom_call_target="tpu_custom_call" | custom-call | tf_op jit(solution)/shard_map/pallas_call | solution.py:137
  82.8 2.0 %collective-permute-start.6 = (bf16[6,128,128]{2,1,0:T(8,128)(2,1)}, bf16[6,128,128]{2,1,0:T(8,128)(2,1)S(1)}, u32[]{:S(2)}, u32[]{:S(2)}) collective-permute-start(bf16[6,128,128]{2,1,0:T(8,128)(2,1)} %get-tuple-element.20.refs_2_), channel_id=1, source_target_pairs={{0,8},{8,16},{16,24},{24,32},{32,40},{40,48},{48,56},{56,64},{64,7... | collective-permute-start | bytes 589832 | tf_op jit(solution)/shard_map/ppermute | solution.py:15
  84.8 2.4 %collective-permute-start.7 = (bf16[2,128,128]{2,1,0:T(8,128)(2,1)}, bf16[2,128,128]{2,1,0:T(8,128)(2,1)S(1)}, u32[]{:S(2)}, u32[]{:S(2)}) collective-permute-start(bf16[2,128,128]{2,1,0:T(8,128)(2,1)} %get-tuple-element.21.refs_1_), channel_id=1, source_target_pairs={{8,0},{16,8},{24,16},{32,24},{40,32},{48,40},{56,48},{64,56},{72,6... | collective-permute-start | bytes 196616 | tf_op jit(solution)/shard_map/ppermute | solution.py:20
  87.1 6.8 %collective-permute-done.7.refs_3_ = bf16[2,128,128]{2,1,0:T(8,128)(2,1)S(1)} collective-permute-done((bf16[2,128,128]{2,1,0:T(8,128)(2,1)}, bf16[2,128,128]{2,1,0:T(8,128)(2,1)S(1)}, u32[]{:S(2)}, u32[]{:S(2)}) %collective-permute-start.7) | collective-permute-done | bytes 65568 | tf_op jit(solution)/shard_map/ppermute | solution.py:20
  93.9 0.0 copy-start.8
  93.9 0.0 collective-permute-done.6.refs_0_
  93.9 0.0 copy-start.2
  93.9 0.6 copy-done.8
  94.5 0.1 copy-done.2
  94.6 5.8 %shard_map.49 = bf16[8,128,128]{2,1,0:T(8,128)(2,1)} custom-call(s32[64]{0:T(128)} %reshape.12.idx_ref, bf16[6,128,128]{2,1,0:T(8,128)(2,1)} %copy-done.2, bf16[2,128,128]{2,1,0:T(8,128)(2,1)} %get-tuple-element.21.refs_1_, bf16[6,128,128]{2,1,0:T(8,128)(2,1)} %get-tuple-element.20.refs_2_, bf16[2,128,128]{2,1,0:T(8,128)(2,1)} %copy-done.8, ...), custom_call_target="tpu_custom_call" | custom-call | tf_op jit(solution)/shard_map/pallas_call | solution.py:141
  (3 shorter events, 0.0 us)
Async XLA Ops:
  0.0 1.6 %copy-start = (bf16[1024,1024]{1,0:T(8,128)(2,1)S(1)}, bf16[1024,1024]{1,0:T(8,128)(2,1)}, u32[]{:S(2)}) copy-start(bf16[1024,1024]{1,0:T(8,128)(2,1)} %param.5) | copy-start | bytes 6291460
  0.0 31.9 %copy-start.10 = (s32[8,8]{1,0:T(8,128)S(1)}, s32[8,8]{1,0:T(8,128)}, u32[]{:S(2)}) copy-start(s32[8,8]{1,0:T(8,128)} %param.7) | copy-start | bytes 772
  4.0 17.7 %all-to-all-start = ((bf16[128,8,128]{2,0,1:T(8,128)(2,1)}), bf16[128,8,128]{2,0,1:T(8,128)(2,1)S(1)}, u32[]{:S(2)}, u32[]{:S(2)}) async-start(bf16[128,8,128]{2,0,1:T(8,128)(2,1)} %copy.6), calls=%async_computation | async-start | bytes 524288 | tf_op jit(solution)/shard_map/all_to_all | solution.py:114
  21.7 12.8 %copy-start.1 = (bf16[128,8,128]{2,0,1:T(8,128)(2,1)}, bf16[128,8,128]{2,0,1:T(8,128)(2,1)S(1)}, u32[]{:S(2)}) copy-start(bf16[128,8,128]{2,0,1:T(8,128)(2,1)S(1)} %all-to-all-done) | copy-start | bytes 786436
  21.7 10.9 %collective-permute-start.1 = (bf16[2,128,128]{2,1,0:T(8,128)(2,1)S(1)}, bf16[2,128,128]{2,1,0:T(8,128)(2,1)S(1)}, u32[]{:S(2)}, u32[]{:S(2)}) collective-permute-start(bf16[2,128,128]{2,1,0:T(8,128)(2,1)S(1)} %slice.10), channel_id=1, source_target_pairs={{8,0},{16,8},{24,16},{32,24},{40,32},{48,40},{56,48},{64,56},{72,6... | collective-permute-start | bytes 196616 | tf_op jit(solution)/shard_map/ppermute | solution.py:20
  26.1 8.4 %collective-permute-start = (bf16[6,128,128]{2,1,0:T(8,128)(2,1)S(1)}, bf16[6,128,128]{2,1,0:T(8,128)(2,1)S(1)}, u32[]{:S(2)}, u32[]{:S(2)}) collective-permute-start(bf16[6,128,128]{2,1,0:T(8,128)(2,1)S(1)} %slice.9), channel_id=1, source_target_pairs={{0,8},{8,16},{16,24},{24,32},{32,40},{40,48},{48,56},{56,64},{64,7... | collective-permute-start | bytes 589832 | tf_op jit(solution)/shard_map/ppermute | solution.py:15
  32.6 1.9 %copy-start.9 = (bf16[2,128,128]{2,1,0:T(8,128)(2,1)}, bf16[2,128,128]{2,1,0:T(8,128)(2,1)S(1)}, u32[]{:S(2)}) copy-start(bf16[2,128,128]{2,1,0:T(8,128)(2,1)S(1)} %collective-permute-done.1.refs_2_) | copy-start | bytes 196612
  34.5 0.7 copy-start.3
  40.5 11.4 %collective-permute-start.3 = (bf16[2,128,128]{2,1,0:T(8,128)(2,1)}, bf16[2,128,128]{2,1,0:T(8,128)(2,1)S(1)}, u32[]{:S(2)}, u32[]{:S(2)}) collective-permute-start(bf16[2,128,128]{2,1,0:T(8,128)(2,1)} %get-tuple-element.15.refs_1_), channel_id=1, source_target_pairs={{8,0},{16,8},{24,16},{32,24},{40,32},{48,40},{56,48},{64,56},{72,6... | collective-permute-start | bytes 196616 | tf_op jit(solution)/shard_map/ppermute | solution.py:20
  42.4 10.6 %collective-permute-start.2 = (bf16[6,128,128]{2,1,0:T(8,128)(2,1)}, bf16[6,128,128]{2,1,0:T(8,128)(2,1)S(1)}, u32[]{:S(2)}, u32[]{:S(2)}) collective-permute-start(bf16[6,128,128]{2,1,0:T(8,128)(2,1)} %get-tuple-element.14.refs_2_), channel_id=1, source_target_pairs={{0,8},{8,16},{16,24},{24,32},{32,40},{40,48},{48,56},{56,64},{64,7... | collective-permute-start | bytes 589832 | tf_op jit(solution)/shard_map/ppermute | solution.py:15
  51.9 1.1 %copy-start.6 = (bf16[2,128,128]{2,1,0:T(8,128)(2,1)}, bf16[2,128,128]{2,1,0:T(8,128)(2,1)S(1)}, u32[]{:S(2)}) copy-start(bf16[2,128,128]{2,1,0:T(8,128)(2,1)S(1)} %collective-permute-done.3.refs_3_) | copy-start | bytes 196612
  53.1 0.7 copy-start.5
  59.6 16.7 %collective-permute-start.4 = (bf16[6,128,128]{2,1,0:T(8,128)(2,1)}, bf16[6,128,128]{2,1,0:T(8,128)(2,1)S(1)}, u32[]{:S(2)}, u32[]{:S(2)}) collective-permute-start(bf16[6,128,128]{2,1,0:T(8,128)(2,1)} %get-tuple-element.17.refs_2_), channel_id=1, source_target_pairs={{0,8},{8,16},{16,24},{24,32},{32,40},{40,48},{48,56},{56,64},{64,7... | collective-permute-start | bytes 589832 | tf_op jit(solution)/shard_map/ppermute | solution.py:15
  67.2 9.1 %collective-permute-start.5 = (bf16[2,128,128]{2,1,0:T(8,128)(2,1)}, bf16[2,128,128]{2,1,0:T(8,128)(2,1)S(1)}, u32[]{:S(2)}, u32[]{:S(2)}) collective-permute-start(bf16[2,128,128]{2,1,0:T(8,128)(2,1)} %get-tuple-element.18.refs_1_), channel_id=1, source_target_pairs={{8,0},{16,8},{24,16},{32,24},{40,32},{48,40},{56,48},{64,56},{72,6... | collective-permute-start | bytes 196616 | tf_op jit(solution)/shard_map/ppermute | solution.py:20
  76.3 0.6 copy-start.7
  76.3 0.7 copy-start.4
  82.8 11.1 %collective-permute-start.6 = (bf16[6,128,128]{2,1,0:T(8,128)(2,1)}, bf16[6,128,128]{2,1,0:T(8,128)(2,1)S(1)}, u32[]{:S(2)}, u32[]{:S(2)}) collective-permute-start(bf16[6,128,128]{2,1,0:T(8,128)(2,1)} %get-tuple-element.20.refs_2_), channel_id=1, source_target_pairs={{0,8},{8,16},{16,24},{24,32},{32,40},{40,48},{48,56},{56,64},{64,7... | collective-permute-start | bytes 589832 | tf_op jit(solution)/shard_map/ppermute | solution.py:15
  84.8 9.1 %collective-permute-start.7 = (bf16[2,128,128]{2,1,0:T(8,128)(2,1)}, bf16[2,128,128]{2,1,0:T(8,128)(2,1)S(1)}, u32[]{:S(2)}, u32[]{:S(2)}) collective-permute-start(bf16[2,128,128]{2,1,0:T(8,128)(2,1)} %get-tuple-element.21.refs_1_), channel_id=1, source_target_pairs={{8,0},{16,8},{24,16},{32,24},{40,32},{48,40},{56,48},{64,56},{72,6... | collective-permute-start | bytes 196616 | tf_op jit(solution)/shard_map/ppermute | solution.py:20
  93.9 0.6 copy-start.8
  93.9 0.7 copy-start.2

commit v3 on v2

--- a/solution.py
+++ b/solution.py
@@ -20,7 +20,7 @@
     return lax.ppermute(cells, axis, [(i + 1, i) for i in range(count - 1)])
 
 
-def make_apply(local_blocks, nnz, block_rows, width, piece_sizes, first, last):
+def make_apply(local_blocks, nnz, block_rows, width, piece_sizes, first, last, prev_bf16=False):
     n_pieces = len(piece_sizes)
     n_tiles = sum(piece_sizes)
     n_in = n_pieces + 1 + (0 if first else 2)
@@ -31,7 +31,7 @@
     def kernel(idx_ref, *refs):
         ins = refs[:n_in]
         outs = refs[n_in:n_in + n_out]
-        ext_v, blk_v, cp_v, res_v, sent_v, in_sem, blk_sem, cp_sem, out_sem = refs[n_in + n_out:]
+        ext_v, blk_v, cur_v, prev_v, res_v, sent_v, in_sem, blk_sem, cp_sem, out_sem = refs[n_in + n_out:]
         pieces = ins[:n_pieces]
         blk_hbm = ins[n_pieces]
 
@@ -43,7 +43,10 @@
         blk_copies = [pltpu.make_async_copy(blk_hbm.at[b], blk_v.at[b], blk_sem.at[b]) for b in range(local_blocks)]
         cp_copies = []
         if not first:
-            cp_copies = [pltpu.make_async_copy(ins[n_pieces + 1 + k], cp_v.at[k], cp_sem.at[k]) for k in range(2)]
+            cp_copies = [
+                pltpu.make_async_copy(ins[n_pieces + 1], cur_v, cp_sem.at[0]),
+                pltpu.make_async_copy(ins[n_pieces + 2], prev_v, cp_sem.at[1]),
+            ]
         for c in ext_copies:
             c.start()
         for c in blk_copies:
@@ -58,15 +61,14 @@
         out_copies = []
         for b in range(local_blocks):
             blk_copies[b].wait()
-            acc = jnp.zeros((block_rows, width), f32)
-            for j in range(nnz):
-                t = idx_ref[b * nnz + j]
-                acc = acc + jnp.dot(blk_v[b, j], ext_v[t], preferred_element_type=f32)
+            lhs = jnp.concatenate([blk_v[b, j] for j in range(nnz)], axis=1)
+            rhs = jnp.concatenate([ext_v[idx_ref[b * nnz + j]] for j in range(nnz)], axis=0)
+            acc = jnp.dot(lhs, rhs, preferred_element_type=f32)
             if first:
                 p = ext_v[b + REACH_LO].astype(f32)
                 nxt = (acc - 0.25 * p) / 2.0
             else:
-                nxt = 2.0 * (acc - 0.25 * cp_v[0, b]) / 2.0 - cp_v[1, b]
+                nxt = 2.0 * (acc - 0.25 * cur_v[b]) / 2.0 - prev_v[b].astype(f32)
             sent_v[b] = nxt.astype(bf16)
             if not last:
                 res_v[b] = nxt
@@ -98,7 +100,8 @@
         scratch_shapes=[
             pltpu.VMEM((n_tiles, block_rows, width), bf16),
             pltpu.VMEM((local_blocks, nnz, block_rows, block_rows), bf16),
-            pltpu.VMEM((2, local_blocks, block_rows, width), f32),
+            pltpu.VMEM((local_blocks, block_rows, width), f32),
+            pltpu.VMEM((local_blocks, block_rows, width), bf16 if prev_bf16 else f32),
             pltpu.VMEM((local_blocks, block_rows, width), f32),
             pltpu.VMEM((local_blocks, block_rows, width), bf16),
             pltpu.SemaphoreType.DMA((n_pieces,)),
@@ -110,10 +113,12 @@
 
 
 def per_device(vectors, rotation, blocks, columns):
-    rotated = jnp.dot(vectors, rotation, preferred_element_type=jnp.float32).astype(jnp.bfloat16)
-    panel = lax.all_to_all(rotated, "vec", split_axis=1, concat_axis=0, tiled=True)
+    groups = lax.axis_size("vec")
+    width = rotation.shape[1] // groups
+    rot3 = rotation.reshape(rotation.shape[0], groups, width)
+    rotated = jnp.einsum("rk,kgc->grc", vectors, rot3, preferred_element_type=jnp.float32).astype(jnp.bfloat16)
+    panel = lax.all_to_all(rotated, "vec", split_axis=0, concat_axis=0, tiled=True)
     local_blocks, nnz, block_rows, _ = blocks.shape
-    width = panel.shape[1]
     n_tiles = local_blocks + REACH_LO + REACH_HI
     first_block = lax.axis_index("row") * local_blocks
     local_index = jnp.clip(columns - first_block + REACH_LO, 0, n_tiles - 1).reshape(-1).astype(jnp.int32)
@@ -124,17 +129,19 @@
     sizes_first = (REACH_LO, local_blocks, REACH_HI)
     sizes_next = (REACH_LO, REACH_HI, local_blocks - REACH_HI, REACH_HI)
     first_apply = make_apply(local_blocks, nnz, block_rows, width, sizes_first, True, False)
+    second_apply = make_apply(local_blocks, nnz, block_rows, width, sizes_next, False, False, True)
     next_apply = make_apply(local_blocks, nnz, block_rows, width, sizes_next, False, False)
     last_apply = make_apply(local_blocks, nnz, block_rows, width, sizes_next, False, True)
 
-    prev = tiles.astype(jnp.float32)
+    prev = tiles
     cur, head, rest = first_apply(local_index, shift_up(tail, "row"), tiles, shift_down(head, "row"), blocks)
     for degree in range(DEG - 1):
         tail = rest[rest.shape[0] - REACH_LO:]
         lo = shift_up(tail, "row")
         hi = shift_down(head, "row")
         if degree < DEG - 2:
-            nxt, head, rest = next_apply(local_index, lo, head, rest, hi, blocks, cur, prev)
+            step = second_apply if degree == 0 else next_apply
+            nxt, head, rest = step(local_index, lo, head, rest, hi, blocks, cur, prev)
             prev = cur
             cur = nxt
         else:

time: 101 us -> 98.5 us (0.975)
  waiting for transfers between devices: 27.4 us -> 33 us
  starting transfers between devices: 40.9 us -> 35.8 us
  other arithmetic: 1.79 us -> 0.01 us
  Pallas kernels: 22.7 us -> 21.1 us
    ppermute x4, waiting for transfers between devices: 13.9 us -> 20.7 us  [shift_down(): return lax.ppermute(cells, axis, [(i + 1, i) for i in range(count - 1)])]
    ppermute x4, starting transfers between devices: 23.1 us -> 17.5 us  [shift_up(): return lax.ppermute(cells, axis, [(i, i + 1) for i in range(count - 1)])]
    reshape x0 -> x1, local copies, waits for them, and re-layouts: none -> 2.9 us  [per_device(): rot3 = rotation.reshape(rotation.shape[0], groups, width)]
    convert_element_type x1 -> x0, other arithmetic: 1.79 us -> none  [per_device(): prev = tiles.astype(jnp.float32)]
    unnamed x22, local copies, waits for them, and re-layouts: 4.35 us -> 2.8 us
    ppermute x4, waiting for transfers between devices: 3.06 us -> 1.95 us  [shift_up(): return lax.ppermute(cells, axis, [(i, i + 1) for i in range(count - 1)])]
  transfers between devices with their start and end apart: 9 -> 9, of which waited for: 5 -> 5; matrix products, arithmetic and copies ran while one was open for 2% -> 1% of each run, Pallas kernels for 0% -> 0%
where the time goes in v3:
time: 98.5 us; the launch traced here: 97.9 us
  starting transfers between devices  35.8 us (36%)
  waiting for transfers between devices  33 us (34%)
  Pallas kernels  21.1 us (21%)
  local copies, waits for them, and re-layouts  6.34 us (6%)
  matrix products  1.54 us (2%)
    ppermute x4, waiting for transfers between devices, shift_down(): return lax.ppermute(cells, axis, [(i + 1, i) for i in range(count - 1)])  20.7 us
    ppermute x4, starting transfers between devices, shift_up(): return lax.ppermute(cells, axis, [(i, i + 1) for i in range(count - 1)])  17.5 us
    ppermute x4, starting transfers between devices, shift_down(): return lax.ppermute(cells, axis, [(i + 1, i) for i in range(count - 1)])  11 us
    pallas_call x2, Pallas kernels, per_device(): nxt, head, rest = step(local_index, lo, head, rest, hi, blocks, cur, prev)  10.7 us
    all_to_all x1, waiting for transfers between devices, per_device(): lax.all_to_all(rotated, 'vec', split_axis=0, concat_axis=0, tiled=True)  10.4 us
    all_to_all x1, starting transfers between devices, per_device(): lax.all_to_all(rotated, 'vec', split_axis=0, concat_axis=0, tiled=True)  7.27 us
    pallas_call x1, Pallas kernels, per_device(): out, = last_apply(local_index, lo, head, rest, hi, blocks, cur, prev)  5.4 us
    pallas_call x1, Pallas kernels, per_device(): first_apply(local_index, shift_up(tail, 'row'), tiles, shift_down(head, '...  4.97 us
  transfers between devices with their start and end apart: 9, of which 5 were waited for; matrix products, arithmetic and copies ran while one was open for 1% of the time, Pallas kernels for 0%

profile of v3, /device:TPU:399, one launch (start us, length us, event | category | flops | bytes accessed | tf_op | source)
XLA Modules:
  0.0 97.9 jit_solution(12749343066050673100)
XLA Ops:
  0.0 0.0 copy-start
  0.0 2.9 %copy.8 = bf16[1024,1024]{0,1:T(8,128)(2,1)S(1)} copy(bf16[1024,1024]{1,0:T(8,128)(2,1)} %param.5) | data formatting | bytes 4194304 | tf_op jit(solution)/shard_map/reshape | solution.py:118
  2.9 0.0 copy-start.10
  2.9 0.0 copy-done
  2.9 1.5 %fusion = bf16[8,128,128]{2,1,0:T(8,128)(2,1)} fusion(bf16[1024,8,128]{0,2,1:T(8,128)(2,1)S(1)} %bitcast.8, bf16[128,1024]{1,0:T(8,128)(2,1)S(1)} %copy-done), kind=kOutput, calls=%fused_computation.1 | convolution fusion | flops 268566528 | bytes 2621440 | tf_op jit(solution)/shard_map/rk,kgc->grc/dot_general | solution.py:119
  4.5 7.3 %all-to-all-start = ((bf16[8,128,128]{2,1,0:T(8,128)(2,1)}), bf16[8,128,128]{2,1,0:T(8,128)(2,1)S(1)}, u32[]{:S(2)}, u32[]{:S(2)}) async-start(bf16[8,128,128]{2,1,0:T(8,128)(2,1)} %fusion), calls=%async_computation | async-start | bytes 524288 | tf_op jit(solution)/shard_map/all_to_all | solution.py:120
  11.7 10.4 %all-to-all-done.refs_1_.refs_6_ = bf16[8,128,128]{2,1,0:T(8,128)(2,1)S(1)} async-done(((bf16[8,128,128]{2,1,0:T(8,128)(2,1)}), bf16[8,128,128]{2,1,0:T(8,128)(2,1)S(1)}, u32[]{:S(2)}, u32[]{:S(2)}) %all-to-all-start) | async-done | bytes 262176 | tf_op jit(solution)/shard_map/all_to_all | solution.py:120
  22.1 0.0 copy-start.1
  22.1 4.4 %collective-permute-start.1 = (bf16[2,128,128]{2,1,0:T(8,128)(2,1)S(1)}, bf16[2,128,128]{2,1,0:T(8,128)(2,1)S(1)}, u32[]{:S(2)}, u32[]{:S(2)}) collective-permute-start(bf16[2,128,128]{2,1,0:T(8,128)(2,1)S(1)} %slice.9), channel_id=1, source_target_pairs={{8,0},{16,8},{24,16},{32,24},{40,32},{48,40},{56,48},{64,56},{72,6... | collective-permute-start | bytes 196616 | tf_op jit(solution)/shard_map/ppermute | solution.py:20
  26.5 5.8 %collective-permute-start = (bf16[6,128,128]{2,1,0:T(8,128)(2,1)S(1)}, bf16[6,128,128]{2,1,0:T(8,128)(2,1)S(1)}, u32[]{:S(2)}, u32[]{:S(2)}) collective-permute-start(bf16[6,128,128]{2,1,0:T(8,128)(2,1)S(1)} %slice.8), channel_id=1, source_target_pairs={{0,8},{8,16},{16,24},{24,32},{32,40},{40,48},{48,56},{56,64},{64,7... | collective-permute-start | bytes 589832 | tf_op jit(solution)/shard_map/ppermute | solution.py:15
  32.4 0.0 copy-done.10
  32.4 0.6 reshape.9.idx_ref
  33.0 0.0 collective-permute-done.1.refs_2_
  33.0 0.0 copy-start.8
  33.0 1.9 %collective-permute-done.refs_0_ = bf16[6,128,128]{2,1,0:T(8,128)(2,1)S(1)} collective-permute-done((bf16[6,128,128]{2,1,0:T(8,128)(2,1)S(1)}, bf16[6,128,128]{2,1,0:T(8,128)(2,1)S(1)}, u32[]{:S(2)}, u32[]{:S(2)}) %collective-permute-start) | collective-permute-done | bytes 196640 | tf_op jit(solution)/shard_map/ppermute | solution.py:15
  34.9 0.0 copy-done.1
  34.9 0.0 copy-done.8
  34.9 0.0 copy-start.4
  35.0 0.7 copy-done.4
  35.6 5.0 %shard_map.46 = (f32[8,128,128]{2,1,0:T(8,128)}, bf16[2,128,128]{2,1,0:T(8,128)(2,1)}, bf16[6,128,128]{2,1,0:T(8,128)(2,1)}) custom-call(s32[64]{0:T(128)} %reshape.9.idx_ref, bf16[6,128,128]{2,1,0:T(8,128)(2,1)} %copy-done.4, bf16[8,128,128]{2,1,0:T(8,128)(2,1)} %copy-done.1, bf16[2,128,128]{2,1,0:T(8,128)(2,1)} %copy-done.8, bf16[8,8,128,128]{3,2,1,0:T(8,128)(2,1)} %refs_4_.5), custom_call_target="tpu_custom_call" | custom-call | tf_op jit(solution)/shard_map/pallas_call | solution.py:137
  40.6 7.7 %collective-permute-start.2 = (bf16[6,128,128]{2,1,0:T(8,128)(2,1)}, bf16[6,128,128]{2,1,0:T(8,128)(2,1)S(1)}, u32[]{:S(2)}, u32[]{:S(2)}) collective-permute-start(bf16[6,128,128]{2,1,0:T(8,128)(2,1)} %get-tuple-element.14.refs_2_), channel_id=1, source_target_pairs={{0,8},{8,16},{16,24},{24,32},{32,40},{40,48},{48,56},{56,64},{64,7... | collective-permute-start | bytes 589832 | tf_op jit(solution)/shard_map/ppermute | solution.py:15
  48.3 1.9 %collective-permute-start.3 = (bf16[2,128,128]{2,1,0:T(8,128)(2,1)}, bf16[2,128,128]{2,1,0:T(8,128)(2,1)S(1)}, u32[]{:S(2)}, u32[]{:S(2)}) collective-permute-start(bf16[2,128,128]{2,1,0:T(8,128)(2,1)} %get-tuple-element.15.refs_1_), channel_id=1, source_target_pairs={{8,0},{16,8},{24,16},{32,24},{40,32},{48,40},{56,48},{64,56},{72,6... | collective-permute-start | bytes 196616 | tf_op jit(solution)/shard_map/ppermute | solution.py:20
  50.2 7.2 %collective-permute-done.3.refs_3_ = bf16[2,128,128]{2,1,0:T(8,128)(2,1)S(1)} collective-permute-done((bf16[2,128,128]{2,1,0:T(8,128)(2,1)}, bf16[2,128,128]{2,1,0:T(8,128)(2,1)S(1)}, u32[]{:S(2)}, u32[]{:S(2)}) %collective-permute-start.3) | collective-permute-done | bytes 65568 | tf_op jit(solution)/shard_map/ppermute | solution.py:20
  57.4 0.0 copy-start.9
  57.4 0.0 collective-permute-done.2.refs_0_
  57.4 0.0 copy-start.3
  57.4 0.6 copy-done.9
  58.0 0.1 copy-done.3
  58.1 5.3 %shard_map.47 = (f32[8,128,128]{2,1,0:T(8,128)}, bf16[2,128,128]{2,1,0:T(8,128)(2,1)}, bf16[6,128,128]{2,1,0:T(8,128)(2,1)}) custom-call(s32[64]{0:T(128)} %reshape.9.idx_ref, bf16[6,128,128]{2,1,0:T(8,128)(2,1)} %copy-done.3, bf16[2,128,128]{2,1,0:T(8,128)(2,1)} %get-tuple-element.15.refs_1_, bf16[6,128,128]{2,1,0:T(8,128)(2,1)} %get-tuple-element.14.refs_2_, ...), custom_call_target="tpu_custom_call" | custom-call | tf_op jit(solution)/shard_map/pallas_call | solution.py:144
  63.5 2.0 %collective-permute-start.4 = (bf16[6,128,128]{2,1,0:T(8,128)(2,1)}, bf16[6,128,128]{2,1,0:T(8,128)(2,1)S(1)}, u32[]{:S(2)}, u32[]{:S(2)}) collective-permute-start(bf16[6,128,128]{2,1,0:T(8,128)(2,1)} %get-tuple-element.17.refs_2_), channel_id=1, source_target_pairs={{0,8},{8,16},{16,24},{24,32},{32,40},{40,48},{48,56},{56,64},{64,7... | collective-permute-start | bytes 589832 | tf_op jit(solution)/shard_map/ppermute | solution.py:15
  65.5 2.4 %collective-permute-start.5 = (bf16[2,128,128]{2,1,0:T(8,128)(2,1)}, bf16[2,128,128]{2,1,0:T(8,128)(2,1)S(1)}, u32[]{:S(2)}, u32[]{:S(2)}) collective-permute-start(bf16[2,128,128]{2,1,0:T(8,128)(2,1)} %get-tuple-element.18.refs_1_), channel_id=1, source_target_pairs={{8,0},{16,8},{24,16},{32,24},{40,32},{48,40},{56,48},{64,56},{72,6... | collective-permute-start | bytes 196616 | tf_op jit(solution)/shard_map/ppermute | solution.py:20
  67.8 6.8 %collective-permute-done.5.refs_3_ = bf16[2,128,128]{2,1,0:T(8,128)(2,1)S(1)} collective-permute-done((bf16[2,128,128]{2,1,0:T(8,128)(2,1)}, bf16[2,128,128]{2,1,0:T(8,128)(2,1)S(1)}, u32[]{:S(2)}, u32[]{:S(2)}) %collective-permute-start.5) | collective-permute-done | bytes 65568 | tf_op jit(solution)/shard_map/ppermute | solution.py:20
  74.6 0.0 copy-start.6
  74.6 0.0 collective-permute-done.4.refs_0_
  74.6 0.0 copy-start.5
  74.6 0.6 copy-done.6
  75.2 0.1 copy-done.5
  75.3 5.4 %shard_map.48 = (f32[8,128,128]{2,1,0:T(8,128)}, bf16[2,128,128]{2,1,0:T(8,128)(2,1)}, bf16[6,128,128]{2,1,0:T(8,128)(2,1)}) custom-call(s32[64]{0:T(128)} %reshape.9.idx_ref, bf16[6,128,128]{2,1,0:T(8,128)(2,1)} %copy-done.5, bf16[2,128,128]{2,1,0:T(8,128)(2,1)} %get-tuple-element.18.refs_1_, bf16[6,128,128]{2,1,0:T(8,128)(2,1)} %get-tuple-element.17.refs_2_, ...), custom_call_target="tpu_custom_call" | custom-call | tf_op jit(solution)/shard_map/pallas_call | solution.py:144
  80.7 2.0 %collective-permute-start.6 = (bf16[6,128,128]{2,1,0:T(8,128)(2,1)}, bf16[6,128,128]{2,1,0:T(8,128)(2,1)S(1)}, u32[]{:S(2)}, u32[]{:S(2)}) collective-permute-start(bf16[6,128,128]{2,1,0:T(8,128)(2,1)} %get-tuple-element.20.refs_2_), channel_id=1, source_target_pairs={{0,8},{8,16},{16,24},{24,32},{32,40},{40,48},{48,56},{56,64},{64,7... | collective-permute-start | bytes 589832 | tf_op jit(solution)/shard_map/ppermute | solution.py:15
  82.7 2.4 %collective-permute-start.7 = (bf16[2,128,128]{2,1,0:T(8,128)(2,1)}, bf16[2,128,128]{2,1,0:T(8,128)(2,1)S(1)}, u32[]{:S(2)}, u32[]{:S(2)}) collective-permute-start(bf16[2,128,128]{2,1,0:T(8,128)(2,1)} %get-tuple-element.21.refs_1_), channel_id=1, source_target_pairs={{8,0},{16,8},{24,16},{32,24},{40,32},{48,40},{56,48},{64,56},{72,6... | collective-permute-start | bytes 196616 | tf_op jit(solution)/shard_map/ppermute | solution.py:20
  85.0 6.8 %collective-permute-done.7.refs_3_ = bf16[2,128,128]{2,1,0:T(8,128)(2,1)S(1)} collective-permute-done((bf16[2,128,128]{2,1,0:T(8,128)(2,1)}, bf16[2,128,128]{2,1,0:T(8,128)(2,1)S(1)}, u32[]{:S(2)}, u32[]{:S(2)}) %collective-permute-start.7) | collective-permute-done | bytes 65568 | tf_op jit(solution)/shard_map/ppermute | solution.py:20
  91.8 0.0 copy-start.7
  91.8 0.0 collective-permute-done.6.refs_0_
  91.8 0.0 copy-start.2
  91.8 0.6 copy-done.7
  92.4 0.1 copy-done.2
  92.5 5.4 %shard_map.49 = bf16[8,128,128]{2,1,0:T(8,128)(2,1)} custom-call(s32[64]{0:T(128)} %reshape.9.idx_ref, bf16[6,128,128]{2,1,0:T(8,128)(2,1)} %copy-done.2, bf16[2,128,128]{2,1,0:T(8,128)(2,1)} %get-tuple-element.21.refs_1_, bf16[6,128,128]{2,1,0:T(8,128)(2,1)} %get-tuple-element.20.refs_2_, bf16[2,128,128]{2,1,0:T(8,128)(2,1)} %copy-done.7, ...), custom_call_target="tpu_custom_call" | custom-call | tf_op jit(solution)/shard_map/pallas_call | solution.py:148
  (3 shorter events, 0.0 us)
Async XLA Ops:
  0.0 2.9 %copy-start = (bf16[128,1024]{1,0:T(8,128)(2,1)S(1)}, bf16[128,1024]{1,0:T(8,128)(2,1)}, u32[]{:S(2)}) copy-start(bf16[128,1024]{1,0:T(8,128)(2,1)} %param.4) | copy-start | bytes 786436
  2.9 29.4 %copy-start.10 = (s32[8,8]{1,0:T(8,128)S(1)}, s32[8,8]{1,0:T(8,128)}, u32[]{:S(2)}) copy-start(s32[8,8]{1,0:T(8,128)} %param.7) | copy-start | bytes 772
  4.5 17.6 %all-to-all-start = ((bf16[8,128,128]{2,1,0:T(8,128)(2,1)}), bf16[8,128,128]{2,1,0:T(8,128)(2,1)S(1)}, u32[]{:S(2)}, u32[]{:S(2)}) async-start(bf16[8,128,128]{2,1,0:T(8,128)(2,1)} %fusion), calls=%async_computation | async-start | bytes 524288 | tf_op jit(solution)/shard_map/all_to_all | solution.py:120
  22.1 12.9 %copy-start.1 = (bf16[8,128,128]{2,1,0:T(8,128)(2,1)}, bf16[8,128,128]{2,1,0:T(8,128)(2,1)S(1)}, u32[]{:S(2)}) copy-start(bf16[8,128,128]{2,1,0:T(8,128)(2,1)S(1)} %all-to-all-done.refs_1_.refs_6_) | copy-start | bytes 786436
  22.1 10.9 %collective-permute-start.1 = (bf16[2,128,128]{2,1,0:T(8,128)(2,1)S(1)}, bf16[2,128,128]{2,1,0:T(8,128)(2,1)S(1)}, u32[]{:S(2)}, u32[]{:S(2)}) collective-permute-start(bf16[2,128,128]{2,1,0:T(8,128)(2,1)S(1)} %slice.9), channel_id=1, source_target_pairs={{8,0},{16,8},{24,16},{32,24},{40,32},{48,40},{56,48},{64,56},{72,6... | collective-permute-start | bytes 196616 | tf_op jit(solution)/shard_map/ppermute | solution.py:20
  26.5 8.4 %collective-permute-start = (bf16[6,128,128]{2,1,0:T(8,128)(2,1)S(1)}, bf16[6,128,128]{2,1,0:T(8,128)(2,1)S(1)}, u32[]{:S(2)}, u32[]{:S(2)}) collective-permute-start(bf16[6,128,128]{2,1,0:T(8,128)(2,1)S(1)} %slice.8), channel_id=1, source_target_pairs={{0,8},{8,16},{16,24},{24,32},{32,40},{40,48},{48,56},{56,64},{64,7... | collective-permute-start | bytes 589832 | tf_op jit(solution)/shard_map/ppermute | solution.py:15
  33.0 1.9 %copy-start.8 = (bf16[2,128,128]{2,1,0:T(8,128)(2,1)}, bf16[2,128,128]{2,1,0:T(8,128)(2,1)S(1)}, u32[]{:S(2)}) copy-start(bf16[2,128,128]{2,1,0:T(8,128)(2,1)S(1)} %collective-permute-done.1.refs_2_) | copy-start | bytes 196612
  34.9 0.7 copy-start.4
  40.6 16.8 %collective-permute-start.2 = (bf16[6,128,128]{2,1,0:T(8,128)(2,1)}, bf16[6,128,128]{2,1,0:T(8,128)(2,1)S(1)}, u32[]{:S(2)}, u32[]{:S(2)}) collective-permute-start(bf16[6,128,128]{2,1,0:T(8,128)(2,1)} %get-tuple-element.14.refs_2_), channel_id=1, source_target_pairs={{0,8},{8,16},{16,24},{24,32},{32,40},{40,48},{48,56},{56,64},{64,7... | collective-permute-start | bytes 589832 | tf_op jit(solution)/shard_map/ppermute | solution.py:15
  48.3 9.1 %collective-permute-start.3 = (bf16[2,128,128]{2,1,0:T(8,128)(2,1)}, bf16[2,128,128]{2,1,0:T(8,128)(2,1)S(1)}, u32[]{:S(2)}, u32[]{:S(2)}) collective-permute-start(bf16[2,128,128]{2,1,0:T(8,128)(2,1)} %get-tuple-element.15.refs_1_), channel_id=1, source_target_pairs={{8,0},{16,8},{24,16},{32,24},{40,32},{48,40},{56,48},{64,56},{72,6... | collective-permute-start | bytes 196616 | tf_op jit(solution)/shard_map/ppermute | solution.py:20
  57.4 0.6 copy-start.9
  57.4 0.7 copy-start.3
  63.5 11.1 %collective-permute-start.4 = (bf16[6,128,128]{2,1,0:T(8,128)(2,1)}, bf16[6,128,128]{2,1,0:T(8,128)(2,1)S(1)}, u32[]{:S(2)}, u32[]{:S(2)}) collective-permute-start(bf16[6,128,128]{2,1,0:T(8,128)(2,1)} %get-tuple-element.17.refs_2_), channel_id=1, source_target_pairs={{0,8},{8,16},{16,24},{24,32},{32,40},{40,48},{48,56},{56,64},{64,7... | collective-permute-start | bytes 589832 | tf_op jit(solution)/shard_map/ppermute | solution.py:15
  65.5 9.1 %collective-permute-start.5 = (bf16[2,128,128]{2,1,0:T(8,128)(2,1)}, bf16[2,128,128]{2,1,0:T(8,128)(2,1)S(1)}, u32[]{:S(2)}, u32[]{:S(2)}) collective-permute-start(bf16[2,128,128]{2,1,0:T(8,128)(2,1)} %get-tuple-element.18.refs_1_), channel_id=1, source_target_pairs={{8,0},{16,8},{24,16},{32,24},{40,32},{48,40},{56,48},{64,56},{72,6... | collective-permute-start | bytes 196616 | tf_op jit(solution)/shard_map/ppermute | solution.py:20
  74.6 0.6 copy-start.6
  74.6 0.7 copy-start.5
  80.7 11.1 %collective-permute-start.6 = (bf16[6,128,128]{2,1,0:T(8,128)(2,1)}, bf16[6,128,128]{2,1,0:T(8,128)(2,1)S(1)}, u32[]{:S(2)}, u32[]{:S(2)}) collective-permute-start(bf16[6,128,128]{2,1,0:T(8,128)(2,1)} %get-tuple-element.20.refs_2_), channel_id=1, source_target_pairs={{0,8},{8,16},{16,24},{24,32},{32,40},{40,48},{48,56},{56,64},{64,7... | collective-permute-start | bytes 589832 | tf_op jit(solution)/shard_map/ppermute | solution.py:15
  82.7 9.1 %collective-permute-start.7 = (bf16[2,128,128]{2,1,0:T(8,128)(2,1)}, bf16[2,128,128]{2,1,0:T(8,128)(2,1)S(1)}, u32[]{:S(2)}, u32[]{:S(2)}) collective-permute-start(bf16[2,128,128]{2,1,0:T(8,128)(2,1)} %get-tuple-element.21.refs_1_), channel_id=1, source_target_pairs={{8,0},{16,8},{24,16},{32,24},{40,32},{48,40},{56,48},{64,56},{72,6... | collective-permute-start | bytes 196616 | tf_op jit(solution)/shard_map/ppermute | solution.py:20
  91.8 0.6 copy-start.7
  91.8 0.7 copy-start.2

commit v4 on v0

v4 whole, which is shorter than its diff:
```python
import jax
import jax.numpy as jnp
from jax import lax
from jax.sharding import PartitionSpec as P

DEG = 4
REACH_LO = 6
REACH_HI = 2
CHUNKS = 1


def shift_up(cells, axis):
    count = lax.axis_size(axis)
    return lax.ppermute(cells, axis, [(i, i + 1) for i in range(count - 1)])


def shift_down(cells, axis):
    count = lax.axis_size(axis)
    return lax.ppermute(cells, axis, [(i + 1, i) for i in range(count - 1)])


def filter_chunk(panel, blocks, local_index):
    local_blocks, nnz, block_rows, _ = blocks.shape
    width = panel.shape[1]

    def apply_operator(state_bf):
        lo = shift_up(state_bf[state_bf.shape[0] - REACH_LO * block_rows:], "row")
        hi = shift_down(state_bf[: REACH_HI * block_rows], "row")
        tiles = jnp.concatenate([lo, state_bf, hi], axis=0).reshape(-1, block_rows, width)
        picked = tiles[local_index]
        result = jnp.einsum("bjrc,bjcv->brv", blocks, picked, preferred_element_type=jnp.float32)
        return result.reshape(local_blocks * block_rows, width)

    prev = panel.astype(jnp.float32)
    cur = (apply_operator(panel) - 0.25 * prev) / 2.0
    for degree in range(DEG - 1):
        sent = cur.astype(jnp.bfloat16)
        nxt = 2.0 * (apply_operator(sent) - 0.25 * cur) / 2.0 - prev
        prev = cur
        cur = nxt
    return cur.astype(jnp.bfloat16)


def per_device(vectors, rotation, blocks, columns):
    rotated = jnp.dot(vectors, rotation, preferred_element_type=jnp.float32).astype(jnp.bfloat16)
    panel = lax.all_to_all(rotated, "vec", split_axis=1, concat_axis=0, tiled=True)
    local_blocks = blocks.shape[0]
    n_tiles = local_blocks + REACH_LO + REACH_HI
    first_block = lax.axis_index("row") * local_blocks
    local_index = jnp.clip(columns - first_block + REACH_LO, 0, n_tiles - 1)
    width = panel.shape[1] // CHUNKS
    outs = [filter_chunk(panel[:, k * width:(k + 1) * width], blocks, local_index) for k in range(CHUNKS)]
    return outs[0] if CHUNKS == 1 else jnp.concatenate(outs, axis=1)


def solution(mesh):
    return jax.shard_map(
        per_device,
        mesh=mesh,
        in_specs=(P(("row", "vec"), None), P(), P("row", None, None, None), P("row", None)),
        out_specs=P("row", "vec"),
        check_vma=False,
    )
```

time: 100 us -> 90.7 us (0.907)
  starting transfers between devices: 35.8 us -> 30.5 us
  local copies, waits for them, and re-layouts: 11.8 us -> 9.52 us
  other arithmetic: 3.32 us -> 1.62 us
    ppermute x8, starting transfers between devices: 28.5 us -> 23.2 us  [the longest x4 14 us: shift_up(): return lax.ppermute(cells, axis, [(i, i + 1) for i in range(count - 1)])]
    gather x4, local copies, waits for them, and re-layouts: 10.8 us -> 8.58 us  [apply_operator(): picked = tiles[local_index]]
    concatenate x4, other arithmetic: 1.84 us -> 0.14 us  [apply_operator(): jnp.concatenate([lo, state_bf, hi], axis=0).reshape(-1, block_rows, width)]
  transfers between devices with their start and end apart: 9 -> 9, of which waited for: 9 -> 5; matrix products, arithmetic and copies ran while one was open for 0% -> 0% of each run, Pallas kernels for 0% -> 0%
where the time goes in v4:
time: 90.7 us; the launch traced here: 90.2 us
  waiting for transfers between devices  36.8 us (41%)
  starting transfers between devices  30.5 us (34%)
  matrix products  11.6 us (13%)
  local copies, waits for them, and re-layouts  9.52 us (10%)
  other arithmetic  1.62 us (2%)
    ppermute x4, waiting for transfers between devices, shift_down(): return lax.ppermute(cells, axis, [(i + 1, i) for i in range(count - 1)])  26.4 us
    ppermute x4, starting transfers between devices, shift_up(): return lax.ppermute(cells, axis, [(i, i + 1) for i in range(count - 1)])  14 us
    all_to_all x1, waiting for transfers between devices, per_device(): lax.all_to_all(rotated, 'vec', split_axis=1, concat_axis=0, tiled=True)  10.4 us
    dot_general x4, matrix products, apply_operator(): jnp.einsum('bjrc,bjcv->brv', blocks, picked, preferred_element_type=jnp.f...  9.29 us
    ppermute x4, starting transfers between devices, shift_down(): return lax.ppermute(cells, axis, [(i + 1, i) for i in range(count - 1)])  9.14 us
    gather x4, local copies, waits for them, and re-layouts, apply_operator(): picked = tiles[local_index]  8.58 us
    all_to_all x1, starting transfers between devices, per_device(): lax.all_to_all(rotated, 'vec', split_axis=1, concat_axis=0, tiled=True)  7.27 us
    dot_general x1, matrix products, per_device(): jnp.dot(vectors, rotation, preferred_element_type=jnp.float32)  2.28 us
  transfers between devices with their start and end apart: 9, of which 5 were waited for; matrix products, arithmetic and copies ran while one was open for 0% of the time, Pallas kernels for 0%

profile of v4, /device:TPU:399, one launch (start us, length us, event | category | flops | bytes accessed | tf_op | source)
XLA Modules:
  0.0 90.2 jit_solution(5348538426670396577)
XLA Ops:
  0.0 0.0 copy-start
  0.0 0.0 copy-start.6
  0.0 2.3 %fusion = bf16[16,8,8,128]{3,2,1,0:T(8,128)(2,1)S(1)} fusion(bf16[128,1024]{1,0:T(8,128)(2,1)} %param.4, bf16[1024,1024]{1,0:T(8,128)(2,1)} %param.5), kind=kOutput, calls=%fused_computation.5 | convolution fusion | flops 268566528 | bytes 2621440 | tf_op jit(solution)/shard_map/dot_general | solution.py:45
  2.3 0.8 copy.15
  3.0 7.3 %all-to-all-start = ((bf16[128,8,128]{2,0,1:T(8,128)(2,1)}), bf16[128,8,128]{2,0,1:T(8,128)(2,1)S(1)}, u32[]{:S(2)}, u32[]{:S(2)}) async-start(bf16[128,8,128]{2,0,1:T(8,128)(2,1)} %bitcast.102), calls=%async_computation | async-start | bytes 524288 | tf_op jit(solution)/shard_map/all_to_all | solution.py:46
  10.3 10.4 %all-to-all-done = bf16[128,8,128]{2,0,1:T(8,128)(2,1)S(1)} async-done(((bf16[128,8,128]{2,0,1:T(8,128)(2,1)}), bf16[128,8,128]{2,0,1:T(8,128)(2,1)S(1)}, u32[]{:S(2)}, u32[]{:S(2)}) %all-to-all-start) | async-done | bytes 262176 | tf_op jit(solution)/shard_map/all_to_all | solution.py:46
  20.7 8.3 %collective-permute-start = (bf16[768,128]{1,0:T(8,128)(2,1)S(1)}, bf16[768,128]{1,0:T(8,128)(2,1)S(1)}, u32[]{:S(2)}, u32[]{:S(2)}) collective-permute-start(bf16[768,128]{1,0:T(8,128)(2,1)S(1)} %bitcast.114), channel_id=1, source_target_pairs={{0,8},{8,16},{16,24},{24,32},{32,40},{40,48},{48,56},{56,64},{64,7... | collective-permute-start | bytes 589832 | tf_op jit(solution)/shard_map/ppermute | solution.py:14
  29.0 0.0 copy-done.6
  29.0 0.1 reshape.39
  29.1 1.9 %collective-permute-start.1 = (bf16[256,128]{1,0:T(8,128)(2,1)S(1)}, bf16[256,128]{1,0:T(8,128)(2,1)S(1)}, u32[]{:S(2)}, u32[]{:S(2)}) collective-permute-start(bf16[256,128]{1,0:T(8,128)(2,1)S(1)} %bitcast.115), channel_id=1, source_target_pairs={{8,0},{16,8},{24,16},{32,24},{40,32},{48,40},{56,48},{64,56},{72,6... | collective-permute-start | bytes 196616 | tf_op jit(solution)/shard_map/ppermute | solution.py:19
  31.0 7.0 %collective-permute-done.1 = bf16[256,128]{1,0:T(8,128)(2,1)S(1)} collective-permute-done((bf16[256,128]{1,0:T(8,128)(2,1)S(1)}, bf16[256,128]{1,0:T(8,128)(2,1)S(1)}, u32[]{:S(2)}, u32[]{:S(2)}) %collective-permute-start.1) | collective-permute-done | bytes 65568 | tf_op jit(solution)/shard_map/ppermute | solution.py:19
  38.0 0.0 collective-permute-done
  38.0 2.1 %gather_fusion = bf16[64,128,128]{2,1,0:T(8,128)(2,1)} fusion(bf16[16,128,128]{2,1,0:T(8,128)(2,1)S(1)} %bitcast.110, s32[1024]{0:T(1024)S(1)} %pad_clamp_fusion), kind=kCustom, calls=%fused_computation | custom fusion | bytes 4194560 | tf_op jit(solution)/shard_map/gather | solution.py:30
  40.2 0.0 copy-done
  40.2 2.3 %fusion.7 = f32[8,128,128,1]{1,2,3,0:T(8,128)S(1)} fusion(bf16[8,8,128,128]{3,2,1,0:T(8,128)(2,1)S(1)} %copy-done, bf16[8,8,128,128]{3,2,1,0:T(8,128)(2,1)} %bitcast.104), kind=kOutput, calls=%fused_computation.25 | convolution fusion | flops 268435456 | bytes 4718592 | tf_op jit(solution)/shard_map/bjrc,bjcv->brv/dot_general | solution.py:31
  42.5 0.1 multiply_convert_fusion
  42.6 1.9 %collective-permute-start.2 = (bf16[768,128]{1,0:T(8,128)(2,1)S(1)}, bf16[768,128]{1,0:T(8,128)(2,1)S(1)}, u32[]{:S(2)}, u32[]{:S(2)}) collective-permute-start(bf16[768,128]{1,0:T(8,128)(2,1)S(1)} %slice.50), channel_id=1, source_target_pairs={{0,8},{8,16},{16,24},{24,32},{32,40},{40,48},{48,56},{56,64},{64,7... | collective-permute-start | bytes 589832 | tf_op jit(solution)/shard_map/ppermute | solution.py:14
  44.6 2.4 %collective-permute-start.3 = (bf16[256,128]{1,0:T(8,128)(2,1)S(1)}, bf16[256,128]{1,0:T(8,128)(2,1)S(1)}, u32[]{:S(2)}, u32[]{:S(2)}) collective-permute-start(bf16[256,128]{1,0:T(8,128)(2,1)S(1)} %slice.51), channel_id=1, source_target_pairs={{8,0},{16,8},{24,16},{32,24},{40,32},{48,40},{56,48},{64,56},{72,6... | collective-permute-start | bytes 196616 | tf_op jit(solution)/shard_map/ppermute | solution.py:19
  47.0 6.5 %collective-permute-done.3 = bf16[256,128]{1,0:T(8,128)(2,1)S(1)} collective-permute-done((bf16[256,128]{1,0:T(8,128)(2,1)S(1)}, bf16[256,128]{1,0:T(8,128)(2,1)S(1)}, u32[]{:S(2)}, u32[]{:S(2)}) %collective-permute-start.3) | collective-permute-done | bytes 65568 | tf_op jit(solution)/shard_map/ppermute | solution.py:19
  53.5 0.0 collective-permute-done.2
  53.5 2.1 %gather_fusion.1 = bf16[64,128,128]{2,1,0:T(8,128)(2,1)} fusion(bf16[16,128,128]{2,1,0:T(8,128)(2,1)S(1)} %bitcast.108, s32[1024]{0:T(1024)S(1)} %pad_clamp_fusion), kind=kCustom, calls=%fused_computation.1 | custom fusion | bytes 4194560 | tf_op jit(solution)/shard_map/gather | solution.py:30
  55.7 2.3 %fusion.8 = f32[8,128,128,1]{1,2,3,0:T(8,128)S(1)} fusion(bf16[8,8,128,128]{3,2,1,0:T(8,128)(2,1)S(1)} %copy-done, bf16[8,8,128,128]{3,2,1,0:T(8,128)(2,1)} %bitcast.105), kind=kOutput, calls=%fused_computation.26 | convolution fusion | flops 268435456 | bytes 4718592 | tf_op jit(solution)/shard_map/bjrc,bjcv->brv/dot_general | solution.py:31
  57.9 0.0 copy-start.1
  58.0 0.1 fusion.6
  58.1 1.9 %collective-permute-start.4 = (bf16[768,128]{1,0:T(8,128)(2,1)S(1)}, bf16[768,128]{1,0:T(8,128)(2,1)S(1)}, u32[]{:S(2)}, u32[]{:S(2)}) collective-permute-start(bf16[768,128]{1,0:T(8,128)(2,1)S(1)} %slice.52), channel_id=1, source_target_pairs={{0,8},{8,16},{16,24},{24,32},{32,40},{40,48},{48,56},{56,64},{64,7... | collective-permute-start | bytes 589832 | tf_op jit(solution)/shard_map/ppermute | solution.py:14
  60.1 2.4 %collective-permute-start.5 = (bf16[256,128]{1,0:T(8,128)(2,1)S(1)}, bf16[256,128]{1,0:T(8,128)(2,1)S(1)}, u32[]{:S(2)}, u32[]{:S(2)}) collective-permute-start(bf16[256,128]{1,0:T(8,128)(2,1)S(1)} %slice.53), channel_id=1, source_target_pairs={{8,0},{16,8},{24,16},{32,24},{40,32},{48,40},{56,48},{64,56},{72,6... | collective-permute-start | bytes 196616 | tf_op jit(solution)/shard_map/ppermute | solution.py:19
  62.5 6.5 %collective-permute-done.5 = bf16[256,128]{1,0:T(8,128)(2,1)S(1)} collective-permute-done((bf16[256,128]{1,0:T(8,128)(2,1)S(1)}, bf16[256,128]{1,0:T(8,128)(2,1)S(1)}, u32[]{:S(2)}, u32[]{:S(2)}) %collective-permute-start.5) | collective-permute-done | bytes 65568 | tf_op jit(solution)/shard_map/ppermute | solution.py:19
  69.0 0.0 copy-done.1
  69.0 0.0 collective-permute-done.4
  69.0 2.1 %gather_fusion.2 = bf16[64,128,128]{2,1,0:T(8,128)(2,1)} fusion(bf16[16,128,128]{2,1,0:T(8,128)(2,1)S(1)} %bitcast.109, s32[1024]{0:T(1024)S(1)} %pad_clamp_fusion), kind=kCustom, calls=%fused_computation.2 | custom fusion | bytes 4194560 | tf_op jit(solution)/shard_map/gather | solution.py:30
  71.2 0.0 copy-start.2
  71.2 2.3 %fusion.9 = f32[8,128,128,1]{1,2,3,0:T(8,128)S(1)} fusion(bf16[8,8,128,128]{3,2,1,0:T(8,128)(2,1)S(1)} %copy-done, bf16[8,8,128,128]{3,2,1,0:T(8,128)(2,1)} %bitcast.106), kind=kOutput, calls=%fused_computation.27 | convolution fusion | flops 268435456 | bytes 4718592 | tf_op jit(solution)/shard_map/bjrc,bjcv->brv/dot_general | solution.py:31
  73.5 0.0 copy-done.2
  73.5 0.0 copy-start.4
  73.5 0.2 fusion.5
  73.8 1.9 %collective-permute-start.6 = (bf16[768,128]{1,0:T(8,128)(2,1)S(1)}, bf16[768,128]{1,0:T(8,128)(2,1)S(1)}, u32[]{:S(2)}, u32[]{:S(2)}) collective-permute-start(bf16[768,128]{1,0:T(8,128)(2,1)S(1)} %slice.54), channel_id=1, source_target_pairs={{0,8},{8,16},{16,24},{24,32},{32,40},{40,48},{48,56},{56,64},{64,7... | collective-permute-start | bytes 589832 | tf_op jit(solution)/shard_map/ppermute | solution.py:14
  75.7 2.4 %collective-permute-start.7 = (bf16[256,128]{1,0:T(8,128)(2,1)S(1)}, bf16[256,128]{1,0:T(8,128)(2,1)S(1)}, u32[]{:S(2)}, u32[]{:S(2)}) collective-permute-start(bf16[256,128]{1,0:T(8,128)(2,1)S(1)} %slice.55), channel_id=1, source_target_pairs={{8,0},{16,8},{24,16},{32,24},{40,32},{48,40},{56,48},{64,56},{72,6... | collective-permute-start | bytes 196616 | tf_op jit(solution)/shard_map/ppermute | solution.py:19
  78.1 6.5 %collective-permute-done.7 = bf16[256,128]{1,0:T(8,128)(2,1)S(1)} collective-permute-done((bf16[256,128]{1,0:T(8,128)(2,1)S(1)}, bf16[256,128]{1,0:T(8,128)(2,1)S(1)}, u32[]{:S(2)}, u32[]{:S(2)}) %collective-permute-start.7) | collective-permute-done | bytes 65568 | tf_op jit(solution)/shard_map/ppermute | solution.py:19
  84.6 0.0 copy-done.4
  84.6 0.0 collective-permute-done.6
  84.7 2.1 %gather_fusion.3 = bf16[64,128,128]{2,1,0:T(8,128)(2,1)} fusion(bf16[16,128,128]{2,1,0:T(8,128)(2,1)S(1)} %bitcast.107, s32[1024]{0:T(1024)S(1)} %pad_clamp_fusion), kind=kCustom, calls=%fused_computation.3 | custom fusion | bytes 4194560 | tf_op jit(solution)/shard_map/gather | solution.py:30
  86.8 0.0 copy-start.3
  86.8 0.0 copy-start.5
  86.8 2.4 %fusion.10 = f32[8,128,128,1]{1,2,3,0:T(8,128)S(1)} fusion(bf16[8,8,128,128]{3,2,1,0:T(8,128)(2,1)S(1)} %copy-done, bf16[8,8,128,128]{3,2,1,0:T(8,128)(2,1)} %bitcast.103), kind=kOutput, calls=%fused_computation.28 | convolution fusion | flops 268435456 | bytes 4718592 | tf_op jit(solution)/shard_map/bjrc,bjcv->brv/dot_general | solution.py:31
  89.2 0.0 copy-done.3
  89.2 0.0 copy-done.5
  89.2 1.0 %fusion.3 = bf16[1024,128]{1,0:T(8,128)(2,1)} fusion(f32[8,128,128,1]{1,2,3,0:T(8,128)S(1)} %fusion.10, bf16[128,8,128]{2,0,1:T(8,128)(2,1)S(1)} %all-to-all-done, f32[8,128,128,1]{1,2,3,0:T(8,128)S(1)} %fusion.7, f32[8,128,128,1]{1,2,3,0:T(8,128)S(1)} %copy-done.5, f32[8,128,128,1]{1,2,3,0:T(8,128)S(1)} %copy-done.3), kind=kLoop, calls=%fused_computation.15 | loop fusion | flops 1835008 | bytes 2621440 | tf_op jit(solution)/shard_map/convert_element_type | solution.py:41
  (14 shorter events, 0.2 us)
Async XLA Ops:
  0.0 40.2 %copy-start = (bf16[8,8,128,128]{3,2,1,0:T(8,128)(2,1)S(1)}, bf16[8,8,128,128]{3,2,1,0:T(8,128)(2,1)}, u32[]{:S(2)}) copy-start(bf16[8,8,128,128]{3,2,1,0:T(8,128)(2,1)} %param.6) | copy-start | bytes 6291460
  0.0 29.0 %copy-start.6 = (s32[8,8]{1,0:T(8,128)S(1)}, s32[8,8]{1,0:T(8,128)}, u32[]{:S(2)}) copy-start(s32[8,8]{1,0:T(8,128)} %param.7) | copy-start | bytes 772
  3.0 17.6 %all-to-all-start = ((bf16[128,8,128]{2,0,1:T(8,128)(2,1)}), bf16[128,8,128]{2,0,1:T(8,128)(2,1)S(1)}, u32[]{:S(2)}, u32[]{:S(2)}) async-start(bf16[128,8,128]{2,0,1:T(8,128)(2,1)} %bitcast.102), calls=%async_computation | async-start | bytes 524288 | tf_op jit(solution)/shard_map/all_to_all | solution.py:46
  20.7 17.3 %collective-permute-start = (bf16[768,128]{1,0:T(8,128)(2,1)S(1)}, bf16[768,128]{1,0:T(8,128)(2,1)S(1)}, u32[]{:S(2)}, u32[]{:S(2)}) collective-permute-start(bf16[768,128]{1,0:T(8,128)(2,1)S(1)} %bitcast.114), channel_id=1, source_target_pairs={{0,8},{8,16},{16,24},{24,32},{32,40},{40,48},{48,56},{56,64},{64,7... | collective-permute-start | bytes 589832 | tf_op jit(solution)/shard_map/ppermute | solution.py:14
  29.1 8.9 %collective-permute-start.1 = (bf16[256,128]{1,0:T(8,128)(2,1)S(1)}, bf16[256,128]{1,0:T(8,128)(2,1)S(1)}, u32[]{:S(2)}, u32[]{:S(2)}) collective-permute-start(bf16[256,128]{1,0:T(8,128)(2,1)S(1)} %bitcast.115), channel_id=1, source_target_pairs={{8,0},{16,8},{24,16},{32,24},{40,32},{48,40},{56,48},{64,56},{72,6... | collective-permute-start | bytes 196616 | tf_op jit(solution)/shard_map/ppermute | solution.py:19
  42.6 10.9 %collective-permute-start.2 = (bf16[768,128]{1,0:T(8,128)(2,1)S(1)}, bf16[768,128]{1,0:T(8,128)(2,1)S(1)}, u32[]{:S(2)}, u32[]{:S(2)}) collective-permute-start(bf16[768,128]{1,0:T(8,128)(2,1)S(1)} %slice.50), channel_id=1, source_target_pairs={{0,8},{8,16},{16,24},{24,32},{32,40},{40,48},{48,56},{56,64},{64,7... | collective-permute-start | bytes 589832 | tf_op jit(solution)/shard_map/ppermute | solution.py:14
  44.6 8.9 %collective-permute-start.3 = (bf16[256,128]{1,0:T(8,128)(2,1)S(1)}, bf16[256,128]{1,0:T(8,128)(2,1)S(1)}, u32[]{:S(2)}, u32[]{:S(2)}) collective-permute-start(bf16[256,128]{1,0:T(8,128)(2,1)S(1)} %slice.51), channel_id=1, source_target_pairs={{8,0},{16,8},{24,16},{32,24},{40,32},{48,40},{56,48},{64,56},{72,6... | collective-permute-start | bytes 196616 | tf_op jit(solution)/shard_map/ppermute | solution.py:19
  57.9 11.0 %copy-start.1 = (f32[8,128,128,1]{1,2,3,0:T(8,128)}, f32[8,128,128,1]{1,2,3,0:T(8,128)S(1)}, u32[]{:S(2)}) copy-start(f32[8,128,128,1]{1,2,3,0:T(8,128)S(1)} %fusion.8) | copy-start | bytes 1572868
  58.1 10.9 %collective-permute-start.4 = (bf16[768,128]{1,0:T(8,128)(2,1)S(1)}, bf16[768,128]{1,0:T(8,128)(2,1)S(1)}, u32[]{:S(2)}, u32[]{:S(2)}) collective-permute-start(bf16[768,128]{1,0:T(8,128)(2,1)S(1)} %slice.52), channel_id=1, source_target_pairs={{0,8},{8,16},{16,24},{24,32},{32,40},{40,48},{48,56},{56,64},{64,7... | collective-permute-start | bytes 589832 | tf_op jit(solution)/shard_map/ppermute | solution.py:14
  60.1 8.9 %collective-permute-start.5 = (bf16[256,128]{1,0:T(8,128)(2,1)S(1)}, bf16[256,128]{1,0:T(8,128)(2,1)S(1)}, u32[]{:S(2)}, u32[]{:S(2)}) collective-permute-start(bf16[256,128]{1,0:T(8,128)(2,1)S(1)} %slice.53), channel_id=1, source_target_pairs={{8,0},{16,8},{24,16},{32,24},{40,32},{48,40},{56,48},{64,56},{72,6... | collective-permute-start | bytes 196616 | tf_op jit(solution)/shard_map/ppermute | solution.py:19
  71.2 2.4 %copy-start.2 = (f32[8,128,128,1]{1,2,3,0:T(8,128)S(1)}, f32[8,128,128,1]{1,2,3,0:T(8,128)}, u32[]{:S(2)}) copy-start(f32[8,128,128,1]{1,2,3,0:T(8,128)} %copy-done.1) | copy-start | bytes 1572868
  73.5 11.1 %copy-start.4 = (f32[8,128,128,1]{1,2,3,0:T(8,128)}, f32[8,128,128,1]{1,2,3,0:T(8,128)S(1)}, u32[]{:S(2)}) copy-start(f32[8,128,128,1]{1,2,3,0:T(8,128)S(1)} %fusion.9) | copy-start | bytes 1572868
  73.8 10.9 %collective-permute-start.6 = (bf16[768,128]{1,0:T(8,128)(2,1)S(1)}, bf16[768,128]{1,0:T(8,128)(2,1)S(1)}, u32[]{:S(2)}, u32[]{:S(2)}) collective-permute-start(bf16[768,128]{1,0:T(8,128)(2,1)S(1)} %slice.54), channel_id=1, source_target_pairs={{0,8},{8,16},{16,24},{24,32},{32,40},{40,48},{48,56},{56,64},{64,7... | collective-permute-start | bytes 589832 | tf_op jit(solution)/shard_map/ppermute | solution.py:14
  75.7 8.9 %collective-permute-start.7 = (bf16[256,128]{1,0:T(8,128)(2,1)S(1)}, bf16[256,128]{1,0:T(8,128)(2,1)S(1)}, u32[]{:S(2)}, u32[]{:S(2)}) collective-permute-start(bf16[256,128]{1,0:T(8,128)(2,1)S(1)} %slice.55), channel_id=1, source_target_pairs={{8,0},{16,8},{24,16},{32,24},{40,32},{48,40},{56,48},{64,56},{72,6... | collective-permute-start | bytes 196616 | tf_op jit(solution)/shard_map/ppermute | solution.py:19
  86.8 2.4 %copy-start.3 = (f32[8,128,128,1]{1,2,3,0:T(8,128)S(1)}, f32[8,128,128,1]{1,2,3,0:T(8,128)}, u32[]{:S(2)}) copy-start(f32[8,128,128,1]{1,2,3,0:T(8,128)} %copy-done.1) | copy-start | bytes 1572868
  86.8 2.4 %copy-start.5 = (f32[8,128,128,1]{1,2,3,0:T(8,128)S(1)}, f32[8,128,128,1]{1,2,3,0:T(8,128)}, u32[]{:S(2)}) copy-start(f32[8,128,128,1]{1,2,3,0:T(8,128)} %copy-done.4) | copy-start | bytes 1572868

commit v5 on v4

--- a/solution.py
+++ b/solution.py
@@ -6,7 +6,7 @@
 DEG = 4
 REACH_LO = 6
 REACH_HI = 2
-CHUNKS = 1
+CHUNKS = 2
 
 
 def shift_up(cells, axis):

time: 90.7 us -> 130 us (1.43)
  starting transfers between devices: 30.5 us -> 79.5 us
  waiting for transfers between devices: 36.8 us -> 10.3 us
  local copies, waits for them, and re-layouts: 9.52 us -> 21.1 us
  other arithmetic: 1.62 us -> 8.26 us
  matrix products: 11.6 us -> 8.82 us
    ppermute x4 -> x8, starting transfers between devices: 14 us -> 54.5 us  [shift_up(): return lax.ppermute(cells, axis, [(i, i + 1) for i in range(count - 1)])]
    ppermute x4 -> x8, waiting for transfers between devices: 26.4 us -> 0.02 us  [shift_down(): return lax.ppermute(cells, axis, [(i + 1, i) for i in range(count - 1)])]
    ppermute x4 -> x8, starting transfers between devices: 9.14 us -> 17.7 us  [shift_down(): return lax.ppermute(cells, axis, [(i + 1, i) for i in range(count - 1)])]
    reshape x0 -> x8, other arithmetic: none -> 6.87 us  [apply_operator(): jnp.concatenate([lo, state_bf, hi], axis=0).reshape(-1, block_rows, width)]
    unnamed x14 -> x82, local copies, waits for them, and re-layouts: 0.03 us -> 5.08 us
    slice x4 -> x7, local copies, waits for them, and re-layouts: 0.02 us -> 4.22 us  [apply_operator(): hi = shift_down(state_bf[:REACH_HI * block_rows], 'row')]
    slice x4 -> x7, local copies, waits for them, and re-layouts: 0.06 us -> 3.99 us  [apply_operator(): lo = shift_up(state_bf[state_bf.shape[0] - REACH_LO * block_rows:], 'row')]
    dot_general x4 -> x8, matrix products: 9.29 us -> 6.55 us  [apply_operator(): jnp.einsum('bjrc,bjcv->brv', blocks, picked, preferred_element_type=jnp.f...]
  transfers between devices with their start and end apart: 9 -> 17, of which waited for: 5 -> 1; matrix products, arithmetic and copies ran while one was open for 0% -> 22% of each run, Pallas kernels for 0% -> 0%
where the time goes in v5:
time: 130 us; the launch traced here: 129 us
  starting transfers between devices  79.5 us (61%)
  local copies, waits for them, and re-layouts  21.1 us (16%)
  waiting for transfers between devices  10.3 us (8%)
  matrix products  8.82 us (7%)
  other arithmetic  8.26 us (6%)
    ppermute x8, starting transfers between devices, shift_up(): return lax.ppermute(cells, axis, [(i, i + 1) for i in range(count - 1)])  54.5 us
    ppermute x8, starting transfers between devices, shift_down(): return lax.ppermute(cells, axis, [(i + 1, i) for i in range(count - 1)])  17.7 us
    all_to_all x1, waiting for transfers between devices, per_device(): lax.all_to_all(rotated, 'vec', split_axis=1, concat_axis=0, tiled=True)  10.2 us
    all_to_all x1, starting transfers between devices, per_device(): lax.all_to_all(rotated, 'vec', split_axis=1, concat_axis=0, tiled=True)  7.27 us
    reshape x8, other arithmetic, apply_operator(): jnp.concatenate([lo, state_bf, hi], axis=0).reshape(-1, block_rows, width)  6.87 us
    dot_general x8, matrix products, apply_operator(): jnp.einsum('bjrc,bjcv->brv', blocks, picked, preferred_element_type=jnp.f...  6.55 us
    gather x8, local copies, waits for them, and re-layouts, apply_operator(): picked = tiles[local_index]  6 us
    unnamed x82, local copies, waits for them, and re-layouts  5.08 us
  transfers between devices with their start and end apart: 17, of which 1 were waited for; matrix products, arithmetic and copies ran while one was open for 22% of the time, Pallas kernels for 0%

profile of v5, /device:TPU:399, one launch (start us, length us, event | category | flops | bytes accessed | tf_op | source)
XLA Modules:
  0.0 128.9 jit_solution(17853985231135474239)
XLA Ops:
  0.0 2.3 %fusion = bf16[16,8,8,128]{3,2,1,0:T(8,128)(2,1)S(1)} fusion(bf16[128,1024]{1,0:T(8,128)(2,1)} %param.4, bf16[1024,1024]{1,0:T(8,128)(2,1)} %param.5), kind=kOutput, calls=%fused_computation.9 | convolution fusion | flops 268566528 | bytes 2621440 | tf_op jit(solution)/shard_map/dot_general | solution.py:45
  2.3 0.8 copy.180
  3.0 7.3 %all-to-all-start = ((bf16[128,8,128]{2,0,1:T(8,128)(2,1)}), bf16[128,8,128]{2,0,1:T(8,128)(2,1)S(1)}, u32[]{:S(2)}, u32[]{:S(2)}) async-start(bf16[128,8,128]{2,0,1:T(8,128)(2,1)} %bitcast.205), calls=%async_computation | async-start | bytes 524288 | tf_op jit(solution)/shard_map/all_to_all | solution.py:46
  10.4 10.2 %all-to-all-done = bf16[128,8,128]{2,0,1:T(8,128)(2,1)S(1)} async-done(((bf16[128,8,128]{2,0,1:T(8,128)(2,1)}), bf16[128,8,128]{2,0,1:T(8,128)(2,1)S(1)}, u32[]{:S(2)}, u32[]{:S(2)}) %all-to-all-start) | async-done | bytes 262176 | tf_op jit(solution)/shard_map/all_to_all | solution.py:46
  20.9 0.7 copy.90
  21.6 4.4 %collective-permute-start.1 = (bf16[256,64]{0,1:T(8,128)(2,1)}, bf16[256,64]{0,1:T(8,128)(2,1)S(1)}, u32[]{:S(2)}, u32[]{:S(2)}) collective-permute-start(bf16[256,64]{0,1:T(8,128)(2,1)} %copy.90), channel_id=1, source_target_pairs={{8,0},{16,8},{24,16},{32,24},{40,32},{48,40},{56,48},{64,56},{72,6... | collective-permute-start | bytes 98312 | tf_op jit(solution)/shard_map/ppermute | solution.py:19
  26.0 0.8 copy.88
  26.8 5.8 %collective-permute-start = (bf16[768,64]{0,1:T(8,128)(2,1)}, bf16[768,64]{0,1:T(8,128)(2,1)S(1)}, u32[]{:S(2)}, u32[]{:S(2)}) collective-permute-start(bf16[768,64]{0,1:T(8,128)(2,1)} %copy.88), channel_id=1, source_target_pairs={{0,8},{8,16},{16,24},{24,32},{32,40},{40,48},{48,56},{56,64},{64,7... | collective-permute-start | bytes 294920 | tf_op jit(solution)/shard_map/ppermute | solution.py:14
  32.6 0.1 fusion.15
  32.7 0.7 copy.93
  33.4 1.9 %collective-permute-start.9 = (bf16[256,64]{0,1:T(8,128)(2,1)}, bf16[256,64]{0,1:T(8,128)(2,1)}, u32[]{:S(2)}, u32[]{:S(2)}) collective-permute-start(bf16[256,64]{0,1:T(8,128)(2,1)} %copy.93), channel_id=1, source_target_pairs={{8,0},{16,8},{24,16},{32,24},{40,32},{48,40},{56,48},{64,56},{72,6... | collective-permute-start | bytes 98312 | tf_op jit(solution)/shard_map/ppermute | solution.py:19
  35.3 0.8 copy.91
  36.1 7.0 %collective-permute-start.8 = (bf16[768,64]{0,1:T(8,128)(2,1)}, bf16[768,64]{0,1:T(8,128)(2,1)}, u32[]{:S(2)}, u32[]{:S(2)}) collective-permute-start(bf16[768,64]{0,1:T(8,128)(2,1)} %copy.91), channel_id=1, source_target_pairs={{0,8},{8,16},{16,24},{24,32},{32,40},{40,48},{48,56},{56,64},{64,7... | collective-permute-start | bytes 294920 | tf_op jit(solution)/shard_map/ppermute | solution.py:14
  43.4 0.5 copy-done.9
  43.9 0.8 gather_fusion
  44.7 0.8 convolution_bitcast_fusion.7
  45.6 0.7 slice.96
  46.4 0.6 slice.95
  47.0 1.9 %collective-permute-start.3 = (bf16[256,64]{0,1:T(8,128)(2,1)}, bf16[256,64]{0,1:T(8,128)(2,1)}, u32[]{:S(2)}, u32[]{:S(2)}) collective-permute-start(bf16[256,64]{0,1:T(8,128)(2,1)} %slice.96), channel_id=1, source_target_pairs={{8,0},{16,8},{24,16},{32,24},{40,32},{48,40},{56,48},{64,56},{72,6... | collective-permute-start | bytes 98312 | tf_op jit(solution)/shard_map/ppermute | solution.py:19
  48.9 7.0 %collective-permute-start.2 = (bf16[768,64]{0,1:T(8,128)(2,1)}, bf16[768,64]{0,1:T(8,128)(2,1)}, u32[]{:S(2)}, u32[]{:S(2)}) collective-permute-start(bf16[768,64]{0,1:T(8,128)(2,1)} %slice.95), channel_id=1, source_target_pairs={{0,8},{8,16},{16,24},{24,32},{32,40},{40,48},{48,56},{56,64},{64,7... | collective-permute-start | bytes 294920 | tf_op jit(solution)/shard_map/ppermute | solution.py:14
  56.0 1.0 copy_bitcast_fusion.3
  56.9 0.8 gather_fusion.4
  57.7 0.8 convolution_bitcast_fusion.3
  58.6 0.7 slice.105
  59.3 0.7 slice.104
  59.9 1.9 %collective-permute-start.11 = (bf16[256,64]{0,1:T(8,128)(2,1)}, bf16[256,64]{0,1:T(8,128)(2,1)}, u32[]{:S(2)}, u32[]{:S(2)}) collective-permute-start(bf16[256,64]{0,1:T(8,128)(2,1)} %slice.105), channel_id=1, source_target_pairs={{8,0},{16,8},{24,16},{32,24},{40,32},{48,40},{56,48},{64,56},{72,6... | collective-permute-start | bytes 98312 | tf_op jit(solution)/shard_map/ppermute | solution.py:19
  61.8 7.0 %collective-permute-start.10 = (bf16[768,64]{0,1:T(8,128)(2,1)}, bf16[768,64]{0,1:T(8,128)(2,1)}, u32[]{:S(2)}, u32[]{:S(2)}) collective-permute-start(bf16[768,64]{0,1:T(8,128)(2,1)} %slice.104), channel_id=1, source_target_pairs={{0,8},{8,16},{16,24},{24,32},{32,40},{40,48},{48,56},{56,64},{64,7... | collective-permute-start | bytes 294920 | tf_op jit(solution)/shard_map/ppermute | solution.py:14
  68.9 1.0 copy_bitcast_fusion.6
  69.8 0.7 gather_fusion.1
  70.6 0.8 convolution_bitcast_fusion.6
  71.7 0.7 slice.98
  72.4 0.6 slice.97
  73.0 1.9 %collective-permute-start.5 = (bf16[256,64]{0,1:T(8,128)(2,1)}, bf16[256,64]{0,1:T(8,128)(2,1)}, u32[]{:S(2)}, u32[]{:S(2)}) collective-permute-start(bf16[256,64]{0,1:T(8,128)(2,1)} %slice.98), channel_id=1, source_target_pairs={{8,0},{16,8},{24,16},{32,24},{40,32},{48,40},{56,48},{64,56},{72,6... | collective-permute-start | bytes 98312 | tf_op jit(solution)/shard_map/ppermute | solution.py:19
  75.0 7.0 %collective-permute-start.4 = (bf16[768,64]{0,1:T(8,128)(2,1)}, bf16[768,64]{0,1:T(8,128)(2,1)}, u32[]{:S(2)}, u32[]{:S(2)}) collective-permute-start(bf16[768,64]{0,1:T(8,128)(2,1)} %slice.97), channel_id=1, source_target_pairs={{0,8},{8,16},{16,24},{24,32},{32,40},{40,48},{48,56},{56,64},{64,7... | collective-permute-start | bytes 294920 | tf_op jit(solution)/shard_map/ppermute | solution.py:14
  82.0 1.0 copy_bitcast_fusion.2
  83.0 0.7 gather_fusion.5
  83.7 0.8 convolution_bitcast_fusion.2
  84.8 0.7 slice.107
  85.4 0.7 slice.106
  86.1 1.9 %collective-permute-start.13 = (bf16[256,64]{0,1:T(8,128)(2,1)}, bf16[256,64]{0,1:T(8,128)(2,1)}, u32[]{:S(2)}, u32[]{:S(2)}) collective-permute-start(bf16[256,64]{0,1:T(8,128)(2,1)} %slice.107), channel_id=1, source_target_pairs={{8,0},{16,8},{24,16},{32,24},{40,32},{48,40},{56,48},{64,56},{72,6... | collective-permute-start | bytes 98312 | tf_op jit(solution)/shard_map/ppermute | solution.py:19
  88.0 7.0 %collective-permute-start.12 = (bf16[768,64]{0,1:T(8,128)(2,1)}, bf16[768,64]{0,1:T(8,128)(2,1)}, u32[]{:S(2)}, u32[]{:S(2)}) collective-permute-start(bf16[768,64]{0,1:T(8,128)(2,1)} %slice.106), channel_id=1, source_target_pairs={{0,8},{8,16},{16,24},{24,32},{32,40},{40,48},{48,56},{56,64},{64,7... | collective-permute-start | bytes 294920 | tf_op jit(solution)/shard_map/ppermute | solution.py:14
  95.0 1.0 copy_bitcast_fusion.5
  96.0 0.7 gather_fusion.2
  96.8 0.8 convolution_bitcast_fusion.5
  98.0 0.7 slice.100
  98.7 0.6 slice.99
  99.3 1.9 %collective-permute-start.7 = (bf16[256,64]{0,1:T(8,128)(2,1)}, bf16[256,64]{0,1:T(8,128)(2,1)}, u32[]{:S(2)}, u32[]{:S(2)}) collective-permute-start(bf16[256,64]{0,1:T(8,128)(2,1)} %slice.100), channel_id=1, source_target_pairs={{8,0},{16,8},{24,16},{32,24},{40,32},{48,40},{56,48},{64,56},{72,6... | collective-permute-start | bytes 98312 | tf_op jit(solution)/shard_map/ppermute | solution.py:19
  101.2 7.0 %collective-permute-start.6 = (bf16[768,64]{0,1:T(8,128)(2,1)}, bf16[768,64]{0,1:T(8,128)(2,1)}, u32[]{:S(2)}, u32[]{:S(2)}) collective-permute-start(bf16[768,64]{0,1:T(8,128)(2,1)} %slice.99), channel_id=1, source_target_pairs={{0,8},{8,16},{16,24},{24,32},{32,40},{40,48},{48,56},{56,64},{64,7... | collective-permute-start | bytes 294920 | tf_op jit(solution)/shard_map/ppermute | solution.py:14
  108.2 1.0 copy_bitcast_fusion.1
  109.2 0.7 gather_fusion.6
  110.0 0.8 convolution_bitcast_fusion.1
  111.1 0.6 slice.109
  111.8 0.6 slice.108
  112.4 1.9 %collective-permute-start.15 = (bf16[256,64]{0,1:T(8,128)(2,1)}, bf16[256,64]{0,1:T(8,128)(2,1)}, u32[]{:S(2)}, u32[]{:S(2)}) collective-permute-start(bf16[256,64]{0,1:T(8,128)(2,1)} %slice.109), channel_id=1, source_target_pairs={{8,0},{16,8},{24,16},{32,24},{40,32},{48,40},{56,48},{64,56},{72,6... | collective-permute-start | bytes 98312 | tf_op jit(solution)/shard_map/ppermute | solution.py:19
  114.3 7.0 %collective-permute-start.14 = (bf16[768,64]{0,1:T(8,128)(2,1)}, bf16[768,64]{0,1:T(8,128)(2,1)}, u32[]{:S(2)}, u32[]{:S(2)}) collective-permute-start(bf16[768,64]{0,1:T(8,128)(2,1)} %slice.108), channel_id=1, source_target_pairs={{0,8},{8,16},{16,24},{24,32},{32,40},{40,48},{48,56},{56,64},{64,7... | collective-permute-start | bytes 294920 | tf_op jit(solution)/shard_map/ppermute | solution.py:14
  121.4 1.0 copy_bitcast_fusion.4
  122.3 0.7 gather_fusion.3
  123.2 0.8 convolution_bitcast_fusion.4
  124.3 0.8 fusion.7
  125.1 1.0 copy_bitcast_fusion
  126.1 0.7 gather_fusion.7
  126.9 0.8 convolution_bitcast_fusion
  127.9 0.1 fusion.4
  128.1 0.8 copy.78
  (106 shorter events, 2.5 us)
Async XLA Ops:
  0.0 44.7 %copy-start = (bf16[8,8,128,128]{3,2,1,0:T(8,128)(2,1)S(1)}, bf16[8,8,128,128]{3,2,1,0:T(8,128)(2,1)}, u32[]{:S(2)}) copy-start(bf16[8,8,128,128]{3,2,1,0:T(8,128)(2,1)} %param.6) | copy-start | bytes 6291460
  0.0 10.3 %copy-start.37 = (s32[8,8]{1,0:T(8,128)S(1)}, s32[8,8]{1,0:T(8,128)}, u32[]{:S(2)}) copy-start(s32[8,8]{1,0:T(8,128)} %param.7) | copy-start | bytes 772
  3.0 17.6 %all-to-all-start = ((bf16[128,8,128]{2,0,1:T(8,128)(2,1)}), bf16[128,8,128]{2,0,1:T(8,128)(2,1)S(1)}, u32[]{:S(2)}, u32[]{:S(2)}) async-start(bf16[128,8,128]{2,0,1:T(8,128)(2,1)} %bitcast.205), calls=%async_computation | async-start | bytes 524288 | tf_op jit(solution)/shard_map/all_to_all | solution.py:46
  21.6 21.8 %collective-permute-start.1 = (bf16[256,64]{0,1:T(8,128)(2,1)}, bf16[256,64]{0,1:T(8,128)(2,1)S(1)}, u32[]{:S(2)}, u32[]{:S(2)}) collective-permute-start(bf16[256,64]{0,1:T(8,128)(2,1)} %copy.90), channel_id=1, source_target_pairs={{8,0},{16,8},{24,16},{32,24},{40,32},{48,40},{56,48},{64,56},{72,6... | collective-permute-start | bytes 98312 | tf_op jit(solution)/shard_map/ppermute | solution.py:19
  26.8 16.6 %collective-permute-start = (bf16[768,64]{0,1:T(8,128)(2,1)}, bf16[768,64]{0,1:T(8,128)(2,1)S(1)}, u32[]{:S(2)}, u32[]{:S(2)}) collective-permute-start(bf16[768,64]{0,1:T(8,128)(2,1)} %copy.88), channel_id=1, source_target_pairs={{0,8},{8,16},{16,24},{24,32},{32,40},{40,48},{48,56},{56,64},{64,7... | collective-permute-start | bytes 294920 | tf_op jit(solution)/shard_map/ppermute | solution.py:14
  33.4 22.5 %collective-permute-start.9 = (bf16[256,64]{0,1:T(8,128)(2,1)}, bf16[256,64]{0,1:T(8,128)(2,1)}, u32[]{:S(2)}, u32[]{:S(2)}) collective-permute-start(bf16[256,64]{0,1:T(8,128)(2,1)} %copy.93), channel_id=1, source_target_pairs={{8,0},{16,8},{24,16},{32,24},{40,32},{48,40},{56,48},{64,56},{72,6... | collective-permute-start | bytes 98312 | tf_op jit(solution)/shard_map/ppermute | solution.py:19
  36.1 19.8 %collective-permute-start.8 = (bf16[768,64]{0,1:T(8,128)(2,1)}, bf16[768,64]{0,1:T(8,128)(2,1)}, u32[]{:S(2)}, u32[]{:S(2)}) collective-permute-start(bf16[768,64]{0,1:T(8,128)(2,1)} %copy.91), channel_id=1, source_target_pairs={{0,8},{8,16},{16,24},{24,32},{32,40},{40,48},{48,56},{56,64},{64,7... | collective-permute-start | bytes 294920 | tf_op jit(solution)/shard_map/ppermute | solution.py:14
  43.2 0.7 copy-start.9
  44.7 0.9 copy-start.10
  45.6 10.3 %copy-start.1 = (f32[8,8,8,128]{3,2,1,0:T(8,128)}, f32[8,8,8,128]{3,2,1,0:T(8,128)S(1)}, u32[]{:S(2)}) copy-start(f32[8,8,8,128]{3,2,1,0:T(8,128)S(1)} %convolution_bitcast_fusion.7) | copy-start | bytes 786436
  45.6 10.3 %copy-start.30 = (bf16[1024,64]{0,1:T(8,128)(2,1)}, bf16[1024,64]{0,1:T(8,128)(2,1)S(1)}, u32[]{:S(2)}) copy-start(bf16[1024,64]{0,1:T(8,128)(2,1)S(1)} %multiply_convert_fusion.1) | copy-start | bytes 393220
  47.0 21.8 %collective-permute-start.3 = (bf16[256,64]{0,1:T(8,128)(2,1)}, bf16[256,64]{0,1:T(8,128)(2,1)}, u32[]{:S(2)}, u32[]{:S(2)}) collective-permute-start(bf16[256,64]{0,1:T(8,128)(2,1)} %slice.96), channel_id=1, source_target_pairs={{8,0},{16,8},{24,16},{32,24},{40,32},{48,40},{56,48},{64,56},{72,6... | collective-permute-start | bytes 98312 | tf_op jit(solution)/shard_map/ppermute | solution.py:19
  48.9 19.9 %collective-permute-start.2 = (bf16[768,64]{0,1:T(8,128)(2,1)}, bf16[768,64]{0,1:T(8,128)(2,1)}, u32[]{:S(2)}, u32[]{:S(2)}) collective-permute-start(bf16[768,64]{0,1:T(8,128)(2,1)} %slice.95), channel_id=1, source_target_pairs={{0,8},{8,16},{16,24},{24,32},{32,40},{40,48},{48,56},{56,64},{64,7... | collective-permute-start | bytes 294920 | tf_op jit(solution)/shard_map/ppermute | solution.py:14
  57.7 11.2 %copy-start.31 = (bf16[1024,64]{0,1:T(8,128)(2,1)S(1)}, bf16[1024,64]{0,1:T(8,128)(2,1)}, u32[]{:S(2)}) copy-start(bf16[1024,64]{0,1:T(8,128)(2,1)} %copy-done.30) | copy-start | bytes 393220
  58.5 10.3 %copy-start.5 = (f32[8,8,8,128]{3,2,1,0:T(8,128)}, f32[8,8,8,128]{3,2,1,0:T(8,128)S(1)}, u32[]{:S(2)}) copy-start(f32[8,8,8,128]{3,2,1,0:T(8,128)S(1)} %convolution_bitcast_fusion.3) | copy-start | bytes 786436
  58.6 10.3 %copy-start.24 = (bf16[1024,64]{0,1:T(8,128)(2,1)}, bf16[1024,64]{0,1:T(8,128)(2,1)S(1)}, u32[]{:S(2)}) copy-start(bf16[1024,64]{0,1:T(8,128)(2,1)S(1)} %multiply_convert_fusion) | copy-start | bytes 393220
  59.9 22.0 %collective-permute-start.11 = (bf16[256,64]{0,1:T(8,128)(2,1)}, bf16[256,64]{0,1:T(8,128)(2,1)}, u32[]{:S(2)}, u32[]{:S(2)}) collective-permute-start(bf16[256,64]{0,1:T(8,128)(2,1)} %slice.105), channel_id=1, source_target_pairs={{8,0},{16,8},{24,16},{32,24},{40,32},{48,40},{56,48},{64,56},{72,6... | collective-permute-start | bytes 98312 | tf_op jit(solution)/shard_map/ppermute | solution.py:19
  61.8 20.1 %collective-permute-start.10 = (bf16[768,64]{0,1:T(8,128)(2,1)}, bf16[768,64]{0,1:T(8,128)(2,1)}, u32[]{:S(2)}, u32[]{:S(2)}) collective-permute-start(bf16[768,64]{0,1:T(8,128)(2,1)} %slice.104), channel_id=1, source_target_pairs={{0,8},{8,16},{16,24},{24,32},{32,40},{40,48},{48,56},{56,64},{64,7... | collective-permute-start | bytes 294920 | tf_op jit(solution)/shard_map/ppermute | solution.py:14
  70.6 1.0 copy-start.2
  70.6 1.0 copy-start.11
  70.6 11.4 %copy-start.25 = (bf16[1024,64]{0,1:T(8,128)(2,1)S(1)}, bf16[1024,64]{0,1:T(8,128)(2,1)}, u32[]{:S(2)}) copy-start(bf16[1024,64]{0,1:T(8,128)(2,1)} %copy-done.24) | copy-start | bytes 393220
  71.6 10.4 %copy-start.14 = (f32[8,8,8,128]{3,2,1,0:T(8,128)}, f32[8,8,8,128]{3,2,1,0:T(8,128)S(1)}, u32[]{:S(2)}) copy-start(f32[8,8,8,128]{3,2,1,0:T(8,128)S(1)} %convolution_bitcast_fusion.6) | copy-start | bytes 786436
  71.7 10.3 %copy-start.26 = (bf16[1024,64]{0,1:T(8,128)(2,1)}, bf16[1024,64]{0,1:T(8,128)(2,1)S(1)}, u32[]{:S(2)}) copy-start(bf16[1024,64]{0,1:T(8,128)(2,1)S(1)} %fusion.11) | copy-start | bytes 393220
  73.0 21.9 %collective-permute-start.5 = (bf16[256,64]{0,1:T(8,128)(2,1)}, bf16[256,64]{0,1:T(8,128)(2,1)}, u32[]{:S(2)}, u32[]{:S(2)}) collective-permute-start(bf16[256,64]{0,1:T(8,128)(2,1)} %slice.98), channel_id=1, source_target_pairs={{8,0},{16,8},{24,16},{32,24},{40,32},{48,40},{56,48},{64,56},{72,6... | collective-permute-start | bytes 98312 | tf_op jit(solution)/shard_map/ppermute | solution.py:19
  75.0 20.0 %collective-permute-start.4 = (bf16[768,64]{0,1:T(8,128)(2,1)}, bf16[768,64]{0,1:T(8,128)(2,1)}, u32[]{:S(2)}, u32[]{:S(2)}) collective-permute-start(bf16[768,64]{0,1:T(8,128)(2,1)} %slice.97), channel_id=1, source_target_pairs={{0,8},{8,16},{16,24},{24,32},{32,40},{40,48},{48,56},{56,64},{64,7... | collective-permute-start | bytes 294920 | tf_op jit(solution)/shard_map/ppermute | solution.py:14
  83.7 1.0 copy-start.6
  83.7 11.3 %copy-start.27 = (bf16[1024,64]{0,1:T(8,128)(2,1)S(1)}, bf16[1024,64]{0,1:T(8,128)(2,1)}, u32[]{:S(2)}) copy-start(bf16[1024,64]{0,1:T(8,128)(2,1)} %copy-done.26) | copy-start | bytes 393220
  84.7 10.3 %copy-start.17 = (f32[8,8,8,128]{3,2,1,0:T(8,128)}, f32[8,8,8,128]{3,2,1,0:T(8,128)S(1)}, u32[]{:S(2)}) copy-start(f32[8,8,8,128]{3,2,1,0:T(8,128)S(1)} %convolution_bitcast_fusion.2) | copy-start | bytes 786436
  84.8 10.3 %copy-start.28 = (bf16[1024,64]{0,1:T(8,128)(2,1)}, bf16[1024,64]{0,1:T(8,128)(2,1)S(1)}, u32[]{:S(2)}) copy-start(bf16[1024,64]{0,1:T(8,128)(2,1)S(1)} %fusion.12) | copy-start | bytes 393220
  86.1 22.1 %collective-permute-start.13 = (bf16[256,64]{0,1:T(8,128)(2,1)}, bf16[256,64]{0,1:T(8,128)(2,1)}, u32[]{:S(2)}, u32[]{:S(2)}) collective-permute-start(bf16[256,64]{0,1:T(8,128)(2,1)} %slice.107), channel_id=1, source_target_pairs={{8,0},{16,8},{24,16},{32,24},{40,32},{48,40},{56,48},{64,56},{72,6... | collective-permute-start | bytes 98312 | tf_op jit(solution)/shard_map/ppermute | solution.py:19
  88.0 20.2 %collective-permute-start.12 = (bf16[768,64]{0,1:T(8,128)(2,1)}, bf16[768,64]{0,1:T(8,128)(2,1)}, u32[]{:S(2)}, u32[]{:S(2)}) collective-permute-start(bf16[768,64]{0,1:T(8,128)(2,1)} %slice.106), channel_id=1, source_target_pairs={{0,8},{8,16},{16,24},{24,32},{32,40},{40,48},{48,56},{56,64},{64,7... | collective-permute-start | bytes 294920 | tf_op jit(solution)/shard_map/ppermute | solution.py:14
  96.8 1.0 copy-start.3
  96.8 1.0 copy-start.12
  96.8 1.1 copy-start.15
  96.8 11.4 %copy-start.29 = (bf16[1024,64]{0,1:T(8,128)(2,1)S(1)}, bf16[1024,64]{0,1:T(8,128)(2,1)}, u32[]{:S(2)}) copy-start(bf16[1024,64]{0,1:T(8,128)(2,1)} %copy-done.28) | copy-start | bytes 393220
  97.9 10.3 %copy-start.20 = (f32[8,8,8,128]{3,2,1,0:T(8,128)}, f32[8,8,8,128]{3,2,1,0:T(8,128)S(1)}, u32[]{:S(2)}) copy-start(f32[8,8,8,128]{3,2,1,0:T(8,128)S(1)} %convolution_bitcast_fusion.5) | copy-start | bytes 786436
  98.0 10.2 %copy-start.32 = (bf16[1024,64]{0,1:T(8,128)(2,1)}, bf16[1024,64]{0,1:T(8,128)(2,1)S(1)}, u32[]{:S(2)}) copy-start(bf16[1024,64]{0,1:T(8,128)(2,1)S(1)} %fusion.9) | copy-start | bytes 393220
  99.3 22.0 %collective-permute-start.7 = (bf16[256,64]{0,1:T(8,128)(2,1)}, bf16[256,64]{0,1:T(8,128)(2,1)}, u32[]{:S(2)}, u32[]{:S(2)}) collective-permute-start(bf16[256,64]{0,1:T(8,128)(2,1)} %slice.100), channel_id=1, source_target_pairs={{8,0},{16,8},{24,16},{32,24},{40,32},{48,40},{56,48},{64,56},{72,6... | collective-permute-start | bytes 98312 | tf_op jit(solution)/shard_map/ppermute | solution.py:19
  101.2 20.1 %collective-permute-start.6 = (bf16[768,64]{0,1:T(8,128)(2,1)}, bf16[768,64]{0,1:T(8,128)(2,1)}, u32[]{:S(2)}, u32[]{:S(2)}) collective-permute-start(bf16[768,64]{0,1:T(8,128)(2,1)} %slice.99), channel_id=1, source_target_pairs={{0,8},{8,16},{16,24},{24,32},{32,40},{40,48},{48,56},{56,64},{64,7... | collective-permute-start | bytes 294920 | tf_op jit(solution)/shard_map/ppermute | solution.py:14
  110.0 1.0 copy-start.7
  110.0 1.0 copy-start.18
  110.0 11.4 %copy-start.33 = (bf16[1024,64]{0,1:T(8,128)(2,1)S(1)}, bf16[1024,64]{0,1:T(8,128)(2,1)}, u32[]{:S(2)}) copy-start(bf16[1024,64]{0,1:T(8,128)(2,1)} %copy-done.32) | copy-start | bytes 393220
  111.0 10.3 %copy-start.22 = (f32[8,8,8,128]{3,2,1,0:T(8,128)}, f32[8,8,8,128]{3,2,1,0:T(8,128)S(1)}, u32[]{:S(2)}) copy-start(f32[8,8,8,128]{3,2,1,0:T(8,128)S(1)} %convolution_bitcast_fusion.1) | copy-start | bytes 786436
  111.1 10.2 %copy-start.34 = (bf16[1024,64]{0,1:T(8,128)(2,1)}, bf16[1024,64]{0,1:T(8,128)(2,1)S(1)}, u32[]{:S(2)}) copy-start(bf16[1024,64]{0,1:T(8,128)(2,1)S(1)} %fusion.10) | copy-start | bytes 393220
  112.4 12.6 %collective-permute-start.15 = (bf16[256,64]{0,1:T(8,128)(2,1)}, bf16[256,64]{0,1:T(8,128)(2,1)}, u32[]{:S(2)}, u32[]{:S(2)}) collective-permute-start(bf16[256,64]{0,1:T(8,128)(2,1)} %slice.109), channel_id=1, source_target_pairs={{8,0},{16,8},{24,16},{32,24},{40,32},{48,40},{56,48},{64,56},{72,6... | collective-permute-start | bytes 98312 | tf_op jit(solution)/shard_map/ppermute | solution.py:19
  114.3 10.7 %collective-permute-start.14 = (bf16[768,64]{0,1:T(8,128)(2,1)}, bf16[768,64]{0,1:T(8,128)(2,1)}, u32[]{:S(2)}, u32[]{:S(2)}) collective-permute-start(bf16[768,64]{0,1:T(8,128)(2,1)} %slice.108), channel_id=1, source_target_pairs={{0,8},{8,16},{16,24},{24,32},{32,40},{40,48},{48,56},{56,64},{64,7... | collective-permute-start | bytes 294920 | tf_op jit(solution)/shard_map/ppermute | solution.py:14
  123.1 1.0 copy-start.4
  123.1 1.0 copy-start.13
  123.1 1.1 copy-start.16
  123.1 1.1 copy-start.21
  123.1 1.9 %copy-start.35 = (bf16[1024,64]{0,1:T(8,128)(2,1)S(1)}, bf16[1024,64]{0,1:T(8,128)(2,1)}, u32[]{:S(2)}) copy-start(bf16[1024,64]{0,1:T(8,128)(2,1)} %copy-done.34) | copy-start | bytes 393220
  126.8 1.0 copy-start.8
  126.8 1.0 copy-start.19
  126.8 1.1 copy-start.23
  126.8 1.2 copy-start.36

commit v6 on v5

v6 whole, which is shorter than its diff:
```python
import jax
import jax.numpy as jnp
from jax import lax
from jax.sharding import PartitionSpec as P

DEG = 4
REACH_LO = 6
REACH_HI = 2


def shift_up(cells, axis):
    count = lax.axis_size(axis)
    return lax.ppermute(cells, axis, [(i, i + 1) for i in range(count - 1)])


def shift_down(cells, axis):
    count = lax.axis_size(axis)
    return lax.ppermute(cells, axis, [(i + 1, i) for i in range(count - 1)])


def filter_chunk(panel, first_tiles, blocks, local_index):
    local_blocks, nnz, block_rows, _ = blocks.shape
    width = panel.shape[1]

    def product(tiles):
        picked = tiles[local_index]
        result = jnp.einsum("bjrc,bjcv->brv", blocks, picked, preferred_element_type=jnp.float32)
        return result.reshape(local_blocks * block_rows, width)

    def apply_operator(state_bf):
        lo = shift_up(state_bf[state_bf.shape[0] - REACH_LO * block_rows:], "row")
        hi = shift_down(state_bf[: REACH_HI * block_rows], "row")
        return product(jnp.concatenate([lo, state_bf, hi], axis=0).reshape(-1, block_rows, width))

    prev = panel.astype(jnp.float32)
    cur = (product(first_tiles) - 0.25 * prev) / 2.0
    for degree in range(DEG - 1):
        sent = cur.astype(jnp.bfloat16)
        nxt = 2.0 * (apply_operator(sent) - 0.25 * cur) / 2.0 - prev
        prev = cur
        cur = nxt
    return cur.astype(jnp.bfloat16)


def neighbour_rows(vectors, rows, groups, block_rows):
    pairs = []
    for r in range(rows):
        for t in range(groups):
            target = r + 1 if t >= REACH_HI else r - 1
            if 0 <= target < rows:
                pairs.append((r * groups + t, target * groups + t))
    return lax.ppermute(vectors, ("row", "vec"), pairs)


def per_device(vectors, rotation, blocks, columns):
    rows = lax.axis_size("row")
    groups = lax.axis_size("vec")
    local_blocks, nnz, block_rows, _ = blocks.shape
    width = rotation.shape[1] // groups
    both = jnp.concatenate([vectors, neighbour_rows(vectors, rows, groups, block_rows)], axis=0)
    rotated = jnp.dot(both, rotation, preferred_element_type=jnp.float32).astype(jnp.bfloat16)
    spread = rotated.reshape(2, block_rows, groups, width)
    got = lax.all_to_all(spread, "vec", split_axis=2, concat_axis=2, tiled=True)
    got = got.transpose(0, 2, 1, 3)
    panel = got[0].reshape(local_blocks * block_rows, width)
    first_tiles = jnp.concatenate([got[1, REACH_HI:], got[0], got[1, :REACH_HI]], axis=0)
    n_tiles = local_blocks + REACH_LO + REACH_HI
    first_block = lax.axis_index("row") * local_blocks
    local_index = jnp.clip(columns - first_block + REACH_LO, 0, n_tiles - 1)
    return filter_chunk(panel, first_tiles, blocks, local_index)


def solution(mesh):
    return jax.shard_map(
        per_device,
        mesh=mesh,
        in_specs=(P(("row", "vec"), None), P(), P("row", None, None, None), P("row", None)),
        out_specs=P("row", "vec"),
        check_vma=False,
    )
```

time: 130 us -> 93.4 us (0.72)
  starting transfers between devices: 79.5 us -> 23.7 us
  waiting for transfers between devices: 10.3 us -> 45.7 us
  local copies, waits for them, and re-layouts: 21.1 us -> 9.9 us
  other arithmetic: 8.26 us -> 1.65 us
  matrix products: 8.82 us -> 11.7 us
    ppermute x8 -> x3, starting transfers between devices: 54.5 us -> 8.1 us  [shift_up(): return lax.ppermute(cells, axis, [(i, i + 1) for i in range(count - 1)])]
    ppermute x8 -> x3, waiting for transfers between devices: 0.02 us -> 20 us  [shift_down(): return lax.ppermute(cells, axis, [(i + 1, i) for i in range(count - 1)])]
    ppermute x8 -> x3, starting transfers between devices: 17.7 us -> 6.73 us  [shift_down(): return lax.ppermute(cells, axis, [(i + 1, i) for i in range(count - 1)])]
    ppermute x0 -> x1, waiting for transfers between devices: none -> 8.63 us  [neighbour_rows(): return lax.ppermute(vectors, ('row', 'vec'), pairs)]
    reshape x8 -> x0, other arithmetic: 6.87 us -> none  [apply_operator(): jnp.concatenate([lo, state_bf, hi], axis=0).reshape(-1, block_rows, width)]
    all_to_all x1, waiting for transfers between devices: 10.2 us -> 17.1 us  [per_device(): got = lax.all_to_all(spread, 'vec', split_axis=2, concat_axis=2, tiled=True)]
    unnamed x82 -> x15, local copies, waits for them, and re-layouts: 5.08 us -> 0.12 us
    slice x7 -> x3, local copies, waits for them, and re-layouts: 4.22 us -> 0.02 us  [apply_operator(): hi = shift_down(state_bf[:REACH_HI * block_rows], 'row')]
  transfers between devices with their start and end apart: 17 -> 8, of which waited for: 1 -> 5; matrix products, arithmetic and copies ran while one was open for 22% -> 0% of each run, Pallas kernels for 0% -> 0%
where the time goes in v6:
time: 93.4 us; the launch traced here: 92.9 us
  waiting for transfers between devices  45.7 us (49%)
  starting transfers between devices  23.7 us (25%)
  matrix products  11.7 us (13%)
  local copies, waits for them, and re-layouts  9.9 us (11%)
  other arithmetic  1.65 us (2%)
    ppermute x3, waiting for transfers between devices, shift_down(): return lax.ppermute(cells, axis, [(i + 1, i) for i in range(count - 1)])  20 us
    all_to_all x1, waiting for transfers between devices, per_device(): got = lax.all_to_all(spread, 'vec', split_axis=2, concat_axis=2, tiled=True)  17.1 us
    dot_general x4, matrix products, product(): jnp.einsum('bjrc,bjcv->brv', blocks, picked, preferred_element_type=jnp.f...  9.29 us
    ppermute x1, waiting for transfers between devices, neighbour_rows(): return lax.ppermute(vectors, ('row', 'vec'), pairs)  8.63 us
    gather x4, local copies, waits for them, and re-layouts, product(): picked = tiles[local_index]  8.58 us
    ppermute x3, starting transfers between devices, shift_up(): return lax.ppermute(cells, axis, [(i, i + 1) for i in range(count - 1)])  8.1 us
    ppermute x3, starting transfers between devices, shift_down(): return lax.ppermute(cells, axis, [(i + 1, i) for i in range(count - 1)])  6.73 us
    all_to_all x1, starting transfers between devices, per_device(): got = lax.all_to_all(spread, 'vec', split_axis=2, concat_axis=2, tiled=True)  6.15 us
  transfers between devices with their start and end apart: 8, of which 5 were waited for; matrix products, arithmetic and copies ran while one was open for 0% of the time, Pallas kernels for 0%

profile of v6, /device:TPU:399, one launch (start us, length us, event | category | flops | bytes accessed | tf_op | source)
XLA Modules:
  0.0 92.9 jit_solution(1963265556014825020)
XLA Ops:
  0.0 0.0 copy-start
  0.0 2.7 %collective-permute-start = (bf16[128,1024]{1,0:T(8,128)(2,1)}, bf16[128,1024]{1,0:T(8,128)(2,1)S(1)}, u32[]{:S(2)}, u32[]{:S(2)}) collective-permute-start(bf16[128,1024]{1,0:T(8,128)(2,1)} %param.4), channel_id=1, source_target_pairs={{2,10},{3,11},{4,12},{5,13},{6,14},{7,15},{8,0},{9,1},{10,18},{11,... | collective-permute-start | bytes 786440 | tf_op jit(solution)/shard_map/ppermute | solution.py:52
  2.7 8.6 %collective-permute-done = bf16[128,1024]{1,0:T(8,128)(2,1)S(1)} collective-permute-done((bf16[128,1024]{1,0:T(8,128)(2,1)}, bf16[128,1024]{1,0:T(8,128)(2,1)S(1)}, u32[]{:S(2)}, u32[]{:S(2)}) %collective-permute-start) | collective-permute-done | bytes 262176 | tf_op jit(solution)/shard_map/ppermute | solution.py:52
  11.3 2.4 %fusion = bf16[32,8,8,128]{3,1,2,0:T(8,128)(2,1)S(1)} fusion(bf16[1024,1024]{1,0:T(8,128)(2,1)} %param.5, bf16[128,1024]{1,0:T(8,128)(2,1)S(1)} %collective-permute-done, bf16[128,1024]{1,0:T(8,128)(2,1)} %param.4), kind=kOutput, calls=%fused_computation.5 | convolution fusion | flops 538181632 | bytes 3145728 | tf_op jit(solution)/shard_map/dot_general | solution.py:61
  13.8 0.0 copy-start.6
  13.8 0.1 copy.14
  13.9 0.9 copy.8
  14.8 6.2 %all-to-all-start = ((bf16[2,128,8,128]{3,1,0,2:T(8,128)(2,1)}), bf16[2,128,8,128]{3,1,0,2:T(8,128)(2,1)S(1)}, u32[]{:S(2)}, u32[]{:S(2)}) async-start(bf16[2,128,8,128]{3,1,0,2:T(8,128)(2,1)} %copy.8), calls=%async_computation | async-start | bytes 1048576 | tf_op jit(solution)/shard_map/all_to_all | solution.py:63
  20.9 0.0 copy-done.6
  20.9 0.1 reshape.37
  21.0 17.1 %all-to-all-done = bf16[2,128,8,128]{3,1,0,2:T(8,128)(2,1)S(1)} async-done(((bf16[2,128,8,128]{3,1,0,2:T(8,128)(2,1)}), bf16[2,128,8,128]{3,1,0,2:T(8,128)(2,1)S(1)}, u32[]{:S(2)}, u32[]{:S(2)}) %all-to-all-start) | async-done | bytes 524320 | tf_op jit(solution)/shard_map/all_to_all | solution.py:63
  38.2 0.1 slice_bitcast_fusion.2
  38.3 0.1 pad_maximum_fusion
  38.4 2.1 %gather_fusion = bf16[64,128,128]{2,1,0:T(8,128)(2,1)} fusion(bf16[16,128,128]{2,1,0:T(8,128)(2,1)S(1)} %pad_maximum_fusion, s32[1024]{0:T(1024)S(1)} %pad_clamp_fusion), kind=kCustom, calls=%fused_computation | custom fusion | bytes 4194560 | tf_op jit(solution)/shard_map/gather | solution.py:26
  40.5 0.0 copy-done
  40.5 2.3 %fusion.11 = f32[8,128,128,1]{1,2,3,0:T(8,128)S(1)} fusion(bf16[8,8,128,128]{3,2,1,0:T(8,128)(2,1)S(1)} %copy-done, bf16[8,8,128,128]{3,2,1,0:T(8,128)(2,1)} %bitcast.107), kind=kOutput, calls=%fused_computation.32 | convolution fusion | flops 268435456 | bytes 4718592 | tf_op jit(solution)/shard_map/bjrc,bjcv->brv/dot_general | solution.py:27
  42.8 0.1 multiply_convert_fusion
  43.0 4.3 %collective-permute-start.1 = (bf16[768,128]{1,0:T(8,128)(2,1)S(1)}, bf16[768,128]{1,0:T(8,128)(2,1)S(1)}, u32[]{:S(2)}, u32[]{:S(2)}) collective-permute-start(bf16[768,128]{1,0:T(8,128)(2,1)S(1)} %slice.48), channel_id=1, source_target_pairs={{0,8},{8,16},{16,24},{24,32},{32,40},{40,48},{48,56},{56,64},{64,7... | collective-permute-start | bytes 589832 | tf_op jit(solution)/shard_map/ppermute | solution.py:13
  47.2 1.9 %collective-permute-start.2 = (bf16[256,128]{1,0:T(8,128)(2,1)S(1)}, bf16[256,128]{1,0:T(8,128)(2,1)S(1)}, u32[]{:S(2)}, u32[]{:S(2)}) collective-permute-start(bf16[256,128]{1,0:T(8,128)(2,1)S(1)} %slice.49), channel_id=1, source_target_pairs={{8,0},{16,8},{24,16},{32,24},{40,32},{48,40},{56,48},{64,56},{72,6... | collective-permute-start | bytes 196616 | tf_op jit(solution)/shard_map/ppermute | solution.py:18
  49.2 7.0 %collective-permute-done.2 = bf16[256,128]{1,0:T(8,128)(2,1)S(1)} collective-permute-done((bf16[256,128]{1,0:T(8,128)(2,1)S(1)}, bf16[256,128]{1,0:T(8,128)(2,1)S(1)}, u32[]{:S(2)}, u32[]{:S(2)}) %collective-permute-start.2) | collective-permute-done | bytes 65568 | tf_op jit(solution)/shard_map/ppermute | solution.py:18
  56.1 0.0 collective-permute-done.1
  56.2 2.1 %gather_fusion.1 = bf16[64,128,128]{2,1,0:T(8,128)(2,1)} fusion(bf16[16,128,128]{2,1,0:T(8,128)(2,1)S(1)} %bitcast.111, s32[1024]{0:T(1024)S(1)} %pad_clamp_fusion), kind=kCustom, calls=%fused_computation.1 | custom fusion | bytes 4194560 | tf_op jit(solution)/shard_map/gather | solution.py:26
  58.3 2.3 %fusion.12 = f32[8,128,128,1]{1,2,3,0:T(8,128)S(1)} fusion(bf16[8,8,128,128]{3,2,1,0:T(8,128)(2,1)S(1)} %copy-done, bf16[8,8,128,128]{3,2,1,0:T(8,128)(2,1)} %bitcast.108), kind=kOutput, calls=%fused_computation.33 | convolution fusion | flops 268435456 | bytes 4718592 | tf_op jit(solution)/shard_map/bjrc,bjcv->brv/dot_general | solution.py:27
  60.6 0.0 copy-start.1
  60.6 0.1 fusion.10
  60.8 1.9 %collective-permute-start.3 = (bf16[768,128]{1,0:T(8,128)(2,1)S(1)}, bf16[768,128]{1,0:T(8,128)(2,1)S(1)}, u32[]{:S(2)}, u32[]{:S(2)}) collective-permute-start(bf16[768,128]{1,0:T(8,128)(2,1)S(1)} %slice.50), channel_id=1, source_target_pairs={{0,8},{8,16},{16,24},{24,32},{32,40},{40,48},{48,56},{56,64},{64,7... | collective-permute-start | bytes 589832 | tf_op jit(solution)/shard_map/ppermute | solution.py:13
  62.7 2.4 %collective-permute-start.4 = (bf16[256,128]{1,0:T(8,128)(2,1)S(1)}, bf16[256,128]{1,0:T(8,128)(2,1)S(1)}, u32[]{:S(2)}, u32[]{:S(2)}) collective-permute-start(bf16[256,128]{1,0:T(8,128)(2,1)S(1)} %slice.51), channel_id=1, source_target_pairs={{8,0},{16,8},{24,16},{32,24},{40,32},{48,40},{56,48},{64,56},{72,6... | collective-permute-start | bytes 196616 | tf_op jit(solution)/shard_map/ppermute | solution.py:18
  65.2 6.5 %collective-permute-done.4 = bf16[256,128]{1,0:T(8,128)(2,1)S(1)} collective-permute-done((bf16[256,128]{1,0:T(8,128)(2,1)S(1)}, bf16[256,128]{1,0:T(8,128)(2,1)S(1)}, u32[]{:S(2)}, u32[]{:S(2)}) %collective-permute-start.4) | collective-permute-done | bytes 65568 | tf_op jit(solution)/shard_map/ppermute | solution.py:18
  71.6 0.0 copy-done.1
  71.6 0.0 collective-permute-done.3
  71.7 2.1 %gather_fusion.2 = bf16[64,128,128]{2,1,0:T(8,128)(2,1)} fusion(bf16[16,128,128]{2,1,0:T(8,128)(2,1)S(1)} %bitcast.112, s32[1024]{0:T(1024)S(1)} %pad_clamp_fusion), kind=kCustom, calls=%fused_computation.2 | custom fusion | bytes 4194560 | tf_op jit(solution)/shard_map/gather | solution.py:26
  73.8 0.0 copy-start.2
  73.8 2.3 %fusion.13 = f32[8,128,128,1]{1,2,3,0:T(8,128)S(1)} fusion(bf16[8,8,128,128]{3,2,1,0:T(8,128)(2,1)S(1)} %copy-done, bf16[8,8,128,128]{3,2,1,0:T(8,128)(2,1)} %bitcast.109), kind=kOutput, calls=%fused_computation.34 | convolution fusion | flops 268435456 | bytes 4718592 | tf_op jit(solution)/shard_map/bjrc,bjcv->brv/dot_general | solution.py:27
  76.2 0.0 copy-done.2
  76.2 0.0 copy-start.4
  76.2 0.2 fusion.9
  76.5 1.9 %collective-permute-start.5 = (bf16[768,128]{1,0:T(8,128)(2,1)S(1)}, bf16[768,128]{1,0:T(8,128)(2,1)S(1)}, u32[]{:S(2)}, u32[]{:S(2)}) collective-permute-start(bf16[768,128]{1,0:T(8,128)(2,1)S(1)} %slice.52), channel_id=1, source_target_pairs={{0,8},{8,16},{16,24},{24,32},{32,40},{40,48},{48,56},{56,64},{64,7... | collective-permute-start | bytes 589832 | tf_op jit(solution)/shard_map/ppermute | solution.py:13
  78.4 2.4 %collective-permute-start.6 = (bf16[256,128]{1,0:T(8,128)(2,1)S(1)}, bf16[256,128]{1,0:T(8,128)(2,1)S(1)}, u32[]{:S(2)}, u32[]{:S(2)}) collective-permute-start(bf16[256,128]{1,0:T(8,128)(2,1)S(1)} %slice.53), channel_id=1, source_target_pairs={{8,0},{16,8},{24,16},{32,24},{40,32},{48,40},{56,48},{64,56},{72,6... | collective-permute-start | bytes 196616 | tf_op jit(solution)/shard_map/ppermute | solution.py:18
  80.8 6.5 %collective-permute-done.6 = bf16[256,128]{1,0:T(8,128)(2,1)S(1)} collective-permute-done((bf16[256,128]{1,0:T(8,128)(2,1)S(1)}, bf16[256,128]{1,0:T(8,128)(2,1)S(1)}, u32[]{:S(2)}, u32[]{:S(2)}) %collective-permute-start.6) | collective-permute-done | bytes 65568 | tf_op jit(solution)/shard_map/ppermute | solution.py:18
  87.3 0.0 copy-done.4
  87.3 0.0 collective-permute-done.5
  87.4 2.1 %gather_fusion.3 = bf16[64,128,128]{2,1,0:T(8,128)(2,1)} fusion(bf16[16,128,128]{2,1,0:T(8,128)(2,1)S(1)} %bitcast.110, s32[1024]{0:T(1024)S(1)} %pad_clamp_fusion), kind=kCustom, calls=%fused_computation.3 | custom fusion | bytes 4194560 | tf_op jit(solution)/shard_map/gather | solution.py:26
  89.5 0.0 copy-start.3
  89.5 0.0 copy-start.5
  89.5 2.4 %fusion.14 = f32[8,128,128,1]{1,2,3,0:T(8,128)S(1)} fusion(bf16[8,8,128,128]{3,2,1,0:T(8,128)(2,1)S(1)} %copy-done, bf16[8,8,128,128]{3,2,1,0:T(8,128)(2,1)} %bitcast.106), kind=kOutput, calls=%fused_computation.35 | convolution fusion | flops 268435456 | bytes 4718592 | tf_op jit(solution)/shard_map/bjrc,bjcv->brv/dot_general | solution.py:27
  91.9 0.0 copy-done.3
  91.9 0.0 copy-done.5
  91.9 1.0 %fusion.6 = bf16[1024,128]{1,0:T(8,128)(2,1)} fusion(f32[8,128,128,1]{1,2,3,0:T(8,128)S(1)} %fusion.14, bf16[1,8,128,128]{3,2,1,0:T(8,128)(2,1)S(1)} %get-tuple-element.6, f32[8,128,128,1]{1,2,3,0:T(8,128)S(1)} %fusion.11, f32[8,128,128,1]{1,2,3,0:T(8,128)S(1)} %copy-done.5, f32[8,128,128,1]{1,2,3,0:T(8,128)S(1)} %copy-done.3), kind=kLoop, calls=%fused_computation.18 | loop fusion | flops 1835008 | bytes 2621440 | tf_op jit(solution)/shard_map/convert_element_type | solution.py:42
  (14 shorter events, 0.2 us)
Async XLA Ops:
  0.0 40.5 %copy-start = (bf16[8,8,128,128]{3,2,1,0:T(8,128)(2,1)S(1)}, bf16[8,8,128,128]{3,2,1,0:T(8,128)(2,1)}, u32[]{:S(2)}) copy-start(bf16[8,8,128,128]{3,2,1,0:T(8,128)(2,1)} %param.6) | copy-start | bytes 6291460
  0.0 11.3 %collective-permute-start = (bf16[128,1024]{1,0:T(8,128)(2,1)}, bf16[128,1024]{1,0:T(8,128)(2,1)S(1)}, u32[]{:S(2)}, u32[]{:S(2)}) collective-permute-start(bf16[128,1024]{1,0:T(8,128)(2,1)} %param.4), channel_id=1, source_target_pairs={{2,10},{3,11},{4,12},{5,13},{6,14},{7,15},{8,0},{9,1},{10,18},{11,... | collective-permute-start | bytes 786440 | tf_op jit(solution)/shard_map/ppermute | solution.py:52
  13.8 7.2 %copy-start.6 = (s32[8,8]{1,0:T(8,128)S(1)}, s32[8,8]{1,0:T(8,128)}, u32[]{:S(2)}) copy-start(s32[8,8]{1,0:T(8,128)} %param.7) | copy-start | bytes 772
  14.8 23.3 %all-to-all-start = ((bf16[2,128,8,128]{3,1,0,2:T(8,128)(2,1)}), bf16[2,128,8,128]{3,1,0,2:T(8,128)(2,1)S(1)}, u32[]{:S(2)}, u32[]{:S(2)}) async-start(bf16[2,128,8,128]{3,1,0,2:T(8,128)(2,1)} %copy.8), calls=%async_computation | async-start | bytes 1048576 | tf_op jit(solution)/shard_map/all_to_all | solution.py:63
  43.0 13.2 %collective-permute-start.1 = (bf16[768,128]{1,0:T(8,128)(2,1)S(1)}, bf16[768,128]{1,0:T(8,128)(2,1)S(1)}, u32[]{:S(2)}, u32[]{:S(2)}) collective-permute-start(bf16[768,128]{1,0:T(8,128)(2,1)S(1)} %slice.48), channel_id=1, source_target_pairs={{0,8},{8,16},{16,24},{24,32},{32,40},{40,48},{48,56},{56,64},{64,7... | collective-permute-start | bytes 589832 | tf_op jit(solution)/shard_map/ppermute | solution.py:13
  47.2 8.9 %collective-permute-start.2 = (bf16[256,128]{1,0:T(8,128)(2,1)S(1)}, bf16[256,128]{1,0:T(8,128)(2,1)S(1)}, u32[]{:S(2)}, u32[]{:S(2)}) collective-permute-start(bf16[256,128]{1,0:T(8,128)(2,1)S(1)} %slice.49), channel_id=1, source_target_pairs={{8,0},{16,8},{24,16},{32,24},{40,32},{48,40},{56,48},{64,56},{72,6... | collective-permute-start | bytes 196616 | tf_op jit(solution)/shard_map/ppermute | solution.py:18
  60.6 11.0 %copy-start.1 = (f32[8,128,128,1]{1,2,3,0:T(8,128)}, f32[8,128,128,1]{1,2,3,0:T(8,128)S(1)}, u32[]{:S(2)}) copy-start(f32[8,128,128,1]{1,2,3,0:T(8,128)S(1)} %fusion.12) | copy-start | bytes 1572868
  60.8 10.9 %collective-permute-start.3 = (bf16[768,128]{1,0:T(8,128)(2,1)S(1)}, bf16[768,128]{1,0:T(8,128)(2,1)S(1)}, u32[]{:S(2)}, u32[]{:S(2)}) collective-permute-start(bf16[768,128]{1,0:T(8,128)(2,1)S(1)} %slice.50), channel_id=1, source_target_pairs={{0,8},{8,16},{16,24},{24,32},{32,40},{40,48},{48,56},{56,64},{64,7... | collective-permute-start | bytes 589832 | tf_op jit(solution)/shard_map/ppermute | solution.py:13
  62.7 8.9 %collective-permute-start.4 = (bf16[256,128]{1,0:T(8,128)(2,1)S(1)}, bf16[256,128]{1,0:T(8,128)(2,1)S(1)}, u32[]{:S(2)}, u32[]{:S(2)}) collective-permute-start(bf16[256,128]{1,0:T(8,128)(2,1)S(1)} %slice.51), channel_id=1, source_target_pairs={{8,0},{16,8},{24,16},{32,24},{40,32},{48,40},{56,48},{64,56},{72,6... | collective-permute-start | bytes 196616 | tf_op jit(solution)/shard_map/ppermute | solution.py:18
  73.8 2.4 %copy-start.2 = (f32[8,128,128,1]{1,2,3,0:T(8,128)S(1)}, f32[8,128,128,1]{1,2,3,0:T(8,128)}, u32[]{:S(2)}) copy-start(f32[8,128,128,1]{1,2,3,0:T(8,128)} %copy-done.1) | copy-start | bytes 1572868
  76.2 11.1 %copy-start.4 = (f32[8,128,128,1]{1,2,3,0:T(8,128)}, f32[8,128,128,1]{1,2,3,0:T(8,128)S(1)}, u32[]{:S(2)}) copy-start(f32[8,128,128,1]{1,2,3,0:T(8,128)S(1)} %fusion.13) | copy-start | bytes 1572868
  76.5 10.9 %collective-permute-start.5 = (bf16[768,128]{1,0:T(8,128)(2,1)S(1)}, bf16[768,128]{1,0:T(8,128)(2,1)S(1)}, u32[]{:S(2)}, u32[]{:S(2)}) collective-permute-start(bf16[768,128]{1,0:T(8,128)(2,1)S(1)} %slice.52), channel_id=1, source_target_pairs={{0,8},{8,16},{16,24},{24,32},{32,40},{40,48},{48,56},{56,64},{64,7... | collective-permute-start | bytes 589832 | tf_op jit(solution)/shard_map/ppermute | solution.py:13
  78.4 8.9 %collective-permute-start.6 = (bf16[256,128]{1,0:T(8,128)(2,1)S(1)}, bf16[256,128]{1,0:T(8,128)(2,1)S(1)}, u32[]{:S(2)}, u32[]{:S(2)}) collective-permute-start(bf16[256,128]{1,0:T(8,128)(2,1)S(1)} %slice.53), channel_id=1, source_target_pairs={{8,0},{16,8},{24,16},{32,24},{40,32},{48,40},{56,48},{64,56},{72,6... | collective-permute-start | bytes 196616 | tf_op jit(solution)/shard_map/ppermute | solution.py:18
  89.5 2.4 %copy-start.3 = (f32[8,128,128,1]{1,2,3,0:T(8,128)S(1)}, f32[8,128,128,1]{1,2,3,0:T(8,128)}, u32[]{:S(2)}) copy-start(f32[8,128,128,1]{1,2,3,0:T(8,128)} %copy-done.1) | copy-start | bytes 1572868
  89.5 2.4 %copy-start.5 = (f32[8,128,128,1]{1,2,3,0:T(8,128)S(1)}, f32[8,128,128,1]{1,2,3,0:T(8,128)}, u32[]{:S(2)}) copy-start(f32[8,128,128,1]{1,2,3,0:T(8,128)} %copy-done.4) | copy-start | bytes 1572868

commit v7 on v4

--- a/solution.py
+++ b/solution.py
@@ -41,9 +41,23 @@
     return cur.astype(jnp.bfloat16)
 
 
+def exchange_groups(rotated, axis):
+    count = lax.axis_size(axis)
+    v = lax.axis_index(axis)
+    width = rotated.shape[1] // count
+    rows = rotated.shape[0]
+    got = [lax.dynamic_slice_in_dim(rotated, v * width, width, axis=1)]
+    for s in range(1, count):
+        piece = lax.dynamic_slice_in_dim(rotated, ((v + s) % count) * width, width, axis=1)
+        got.append(lax.ppermute(piece, axis, [(i, (i + s) % count) for i in range(count)]))
+    by_shift = jnp.stack(got)
+    order = (v - jnp.arange(count)) % count
+    return by_shift[order].reshape(count * rows, width)
+
+
 def per_device(vectors, rotation, blocks, columns):
     rotated = jnp.dot(vectors, rotation, preferred_element_type=jnp.float32).astype(jnp.bfloat16)
-    panel = lax.all_to_all(rotated, "vec", split_axis=1, concat_axis=0, tiled=True)
+    panel = exchange_groups(rotated, "vec")
     local_blocks = blocks.shape[0]
     n_tiles = local_blocks + REACH_LO + REACH_HI
     first_block = lax.axis_index("row") * local_blocks

time: 90.7 us -> 114 us (1.26)
  starting transfers between devices: 30.5 us -> 50.1 us
  waiting for transfers between devices: 36.8 us -> 40.4 us
    ppermute x0 -> x7, starting transfers between devices: none -> 24.2 us  [exchange_groups(): lax.ppermute(piece, axis, [(i, (i + s) % count) for i in range(count)])]
    ppermute x0 -> x7, waiting for transfers between devices: none -> 13.9 us  [exchange_groups(): lax.ppermute(piece, axis, [(i, (i + s) % count) for i in range(count)])]
    all_to_all x1 -> x0, waiting for transfers between devices: 10.4 us -> none  [per_device(): lax.all_to_all(rotated, 'vec', split_axis=1, concat_axis=0, tiled=True)]
    all_to_all x1 -> x0, starting transfers between devices: 7.27 us -> none  [per_device(): lax.all_to_all(rotated, 'vec', split_axis=1, concat_axis=0, tiled=True)]
    ppermute x4, starting transfers between devices: 14 us -> 16.8 us  [shift_up(): return lax.ppermute(cells, axis, [(i, i + 1) for i in range(count - 1)])]
  transfers between devices with their start and end apart: 9 -> 15, of which waited for: 5 -> 7; matrix products, arithmetic and copies ran while one was open for 0% -> 0% of each run, Pallas kernels for 0% -> 0%
where the time goes in v7:
time: 114 us
  starting transfers between devices  50.1 us (44%)
  waiting for transfers between devices  40.4 us (35%)
  matrix products  11.6 us (10%)
  local copies, waits for them, and re-layouts  9.53 us (8%)
  other arithmetic  1.64 us (1%)
    ppermute x4, waiting for transfers between devices, shift_down(): return lax.ppermute(cells, axis, [(i + 1, i) for i in range(count - 1)])  26.4 us
    ppermute x7, starting transfers between devices, exchange_groups(): lax.ppermute(piece, axis, [(i, (i + s) % count) for i in range(count)])  24.2 us
    ppermute x4, starting transfers between devices, shift_up(): return lax.ppermute(cells, axis, [(i, i + 1) for i in range(count - 1)])  16.8 us
    ppermute x7, waiting for transfers between devices, exchange_groups(): lax.ppermute(piece, axis, [(i, (i + s) % count) for i in range(count)])  13.9 us
    dot_general x4, matrix products, apply_operator(): jnp.einsum('bjrc,bjcv->brv', blocks, picked, preferred_element_type=jnp.f...  9.29 us
    ppermute x4, starting transfers between devices, shift_down(): return lax.ppermute(cells, axis, [(i + 1, i) for i in range(count - 1)])  9.14 us
    gather x4, local copies, waits for them, and re-layouts, apply_operator(): picked = tiles[local_index]  8.57 us
  transfers between devices with their start and end apart: 15, of which 7 were waited for; matrix products, arithmetic and copies ran while one was open for 0% of the time, Pallas kernels for 0%

profile of v7, /device:TPU:399, one launch (start us, length us, event | category | flops | bytes accessed | tf_op | source)
XLA Modules:
  0.0 113.7 jit_solution(9720137254872201885)
XLA Ops:
  0.0 0.0 copy-start
  0.0 0.0 copy-start.6
  0.0 2.3 %convolution_convert_fusion = bf16[128,1024]{1,0:T(8,128)(2,1)S(1)} fusion(bf16[128,1024]{1,0:T(8,128)(2,1)} %param.4, bf16[1024,1024]{1,0:T(8,128)(2,1)} %param.5), kind=kOutput, calls=%fused_computation.5 | convolution fusion | flops 268566528 | bytes 2621440 | tf_op jit(solution)/shard_map/dot_general | solution.py:59
  2.3 0.1 constant_dynamic-slice_fusion
  2.4 5.9 %collective-permute-start.6 = (bf16[128,128]{1,0:T(8,128)(2,1)S(1)}, bf16[128,128]{1,0:T(8,128)(2,1)S(1)}, u32[]{:S(2)}, u32[]{:S(2)}) collective-permute-start(bf16[128,128]{1,0:T(8,128)(2,1)S(1)} %get-tuple-element.5), channel_id=1, source_target_pairs={{0,7},{1,0},{2,1},{3,2},{4,3},{5,4},{6,5},{7,6},{8,15},{9,8},{10,9... | collective-permute-start | bytes 98312 | tf_op jit(solution)/shard_map/ppermute | solution.py:52
  8.3 3.5 %collective-permute-start.5 = (bf16[128,128]{1,0:T(8,128)(2,1)S(1)}, bf16[128,128]{1,0:T(8,128)(2,1)S(1)}, u32[]{:S(2)}, u32[]{:S(2)}) collective-permute-start(bf16[128,128]{1,0:T(8,128)(2,1)S(1)} %get-tuple-element.6), channel_id=1, source_target_pairs={{0,6},{1,7},{2,0},{3,1},{4,2},{5,3},{6,4},{7,5},{8,14},{9,15},{10,... | collective-permute-start | bytes 98312 | tf_op jit(solution)/shard_map/ppermute | solution.py:52
  11.8 2.6 %collective-permute-start.4 = (bf16[128,128]{1,0:T(8,128)(2,1)S(1)}, bf16[128,128]{1,0:T(8,128)(2,1)S(1)}, u32[]{:S(2)}, u32[]{:S(2)}) collective-permute-start(bf16[128,128]{1,0:T(8,128)(2,1)S(1)} %get-tuple-element.7), channel_id=1, source_target_pairs={{0,5},{1,6},{2,7},{3,0},{4,1},{5,2},{6,3},{7,4},{8,13},{9,14},{10,... | collective-permute-start | bytes 98312 | tf_op jit(solution)/shard_map/ppermute | solution.py:52
  14.4 5.9 %collective-permute-start.3 = (bf16[128,128]{1,0:T(8,128)(2,1)S(1)}, bf16[128,128]{1,0:T(8,128)(2,1)S(1)}, u32[]{:S(2)}, u32[]{:S(2)}) collective-permute-start(bf16[128,128]{1,0:T(8,128)(2,1)S(1)} %get-tuple-element.8), channel_id=1, source_target_pairs={{0,4},{1,5},{2,6},{3,7},{4,0},{5,1},{6,2},{7,3},{8,12},{9,13},{10,... | collective-permute-start | bytes 98312 | tf_op jit(solution)/shard_map/ppermute | solution.py:52
  20.4 2.4 %collective-permute-start = (bf16[128,128]{1,0:T(8,128)(2,1)S(1)}, bf16[128,128]{1,0:T(8,128)(2,1)S(1)}, u32[]{:S(2)}, u32[]{:S(2)}) collective-permute-start(bf16[128,128]{1,0:T(8,128)(2,1)S(1)} %get-tuple-element.11), channel_id=1, source_target_pairs={{0,1},{1,2},{2,3},{3,4},{4,5},{5,6},{6,7},{7,0},{8,9},{9,10},{10,1... | collective-permute-start | bytes 98312 | tf_op jit(solution)/shard_map/ppermute | solution.py:52
  22.8 3.4 %collective-permute-done = bf16[128,128]{1,0:T(8,128)(2,1)S(1)} collective-permute-done((bf16[128,128]{1,0:T(8,128)(2,1)S(1)}, bf16[128,128]{1,0:T(8,128)(2,1)S(1)}, u32[]{:S(2)}, u32[]{:S(2)}) %collective-permute-start) | collective-permute-done | bytes 32800 | tf_op jit(solution)/shard_map/ppermute | solution.py:52
  26.2 1.9 %collective-permute-start.1 = (bf16[128,128]{1,0:T(8,128)(2,1)S(1)}, bf16[128,128]{1,0:T(8,128)(2,1)S(1)}, u32[]{:S(2)}, u32[]{:S(2)}) collective-permute-start(bf16[128,128]{1,0:T(8,128)(2,1)S(1)} %get-tuple-element.10), channel_id=1, source_target_pairs={{0,2},{1,3},{2,4},{3,5},{4,6},{5,7},{6,0},{7,1},{8,10},{9,11},{10,... | collective-permute-start | bytes 98312 | tf_op jit(solution)/shard_map/ppermute | solution.py:52
  28.2 4.8 %collective-permute-done.1 = bf16[128,128]{1,0:T(8,128)(2,1)S(1)} collective-permute-done((bf16[128,128]{1,0:T(8,128)(2,1)S(1)}, bf16[128,128]{1,0:T(8,128)(2,1)S(1)}, u32[]{:S(2)}, u32[]{:S(2)}) %collective-permute-start.1) | collective-permute-done | bytes 32800 | tf_op jit(solution)/shard_map/ppermute | solution.py:52
  33.0 1.9 %collective-permute-start.2 = (bf16[128,128]{1,0:T(8,128)(2,1)S(1)}, bf16[128,128]{1,0:T(8,128)(2,1)S(1)}, u32[]{:S(2)}, u32[]{:S(2)}) collective-permute-start(bf16[128,128]{1,0:T(8,128)(2,1)S(1)} %get-tuple-element.9), channel_id=1, source_target_pairs={{0,3},{1,4},{2,5},{3,6},{4,7},{5,0},{6,1},{7,2},{8,11},{9,12},{10,... | collective-permute-start | bytes 98312 | tf_op jit(solution)/shard_map/ppermute | solution.py:52
  34.9 5.7 %collective-permute-done.2 = bf16[128,128]{1,0:T(8,128)(2,1)S(1)} collective-permute-done((bf16[128,128]{1,0:T(8,128)(2,1)S(1)}, bf16[128,128]{1,0:T(8,128)(2,1)S(1)}, u32[]{:S(2)}, u32[]{:S(2)}) %collective-permute-start.2) | collective-permute-done | bytes 32800 | tf_op jit(solution)/shard_map/ppermute | solution.py:52
  40.6 0.0 collective-permute-done.3
  40.7 0.0 collective-permute-done.4
  40.7 0.0 collective-permute-done.5
  40.7 0.0 collective-permute-done.6
  40.7 0.6 gather_fusion
  41.4 11.1 %collective-permute-start.7 = (bf16[768,128]{1,0:T(8,128)(2,1)S(1)}, bf16[768,128]{1,0:T(8,128)(2,1)S(1)}, u32[]{:S(2)}, u32[]{:S(2)}) collective-permute-start(bf16[768,128]{1,0:T(8,128)(2,1)S(1)} %bitcast.123), channel_id=1, source_target_pairs={{0,8},{8,16},{16,24},{24,32},{32,40},{40,48},{48,56},{56,64},{64,7... | collective-permute-start | bytes 589832 | tf_op jit(solution)/shard_map/ppermute | solution.py:14
  52.4 0.0 copy-done.6
  52.5 0.1 reshape.97
  52.5 1.9 %collective-permute-start.8 = (bf16[256,128]{1,0:T(8,128)(2,1)S(1)}, bf16[256,128]{1,0:T(8,128)(2,1)S(1)}, u32[]{:S(2)}, u32[]{:S(2)}) collective-permute-start(bf16[256,128]{1,0:T(8,128)(2,1)S(1)} %bitcast.124), channel_id=1, source_target_pairs={{8,0},{16,8},{24,16},{32,24},{40,32},{48,40},{56,48},{64,56},{72,6... | collective-permute-start | bytes 196616 | tf_op jit(solution)/shard_map/ppermute | solution.py:19
  54.5 7.0 %collective-permute-done.8 = bf16[256,128]{1,0:T(8,128)(2,1)S(1)} collective-permute-done((bf16[256,128]{1,0:T(8,128)(2,1)S(1)}, bf16[256,128]{1,0:T(8,128)(2,1)S(1)}, u32[]{:S(2)}, u32[]{:S(2)}) %collective-permute-start.8) | collective-permute-done | bytes 65568 | tf_op jit(solution)/shard_map/ppermute | solution.py:19
  61.4 0.0 collective-permute-done.7
  61.5 2.1 %gather_fusion.1 = bf16[64,128,128]{2,1,0:T(8,128)(2,1)} fusion(bf16[16,128,128]{2,1,0:T(8,128)(2,1)S(1)} %bitcast.121, s32[1024]{0:T(1024)S(1)} %pad_clamp_fusion), kind=kCustom, calls=%fused_computation.1 | custom fusion | bytes 4194560 | tf_op jit(solution)/shard_map/gather | solution.py:30
  63.6 0.0 copy-done
  63.6 2.3 %fusion.8 = f32[8,128,128,1]{1,2,3,0:T(8,128)S(1)} fusion(bf16[8,8,128,128]{3,2,1,0:T(8,128)(2,1)S(1)} %copy-done, bf16[8,8,128,128]{3,2,1,0:T(8,128)(2,1)} %bitcast.115), kind=kOutput, calls=%fused_computation.46 | convolution fusion | flops 268435456 | bytes 4718592 | tf_op jit(solution)/shard_map/bjrc,bjcv->brv/dot_general | solution.py:31
  65.9 0.1 multiply_convert_fusion
  66.1 1.9 %collective-permute-start.9 = (bf16[768,128]{1,0:T(8,128)(2,1)S(1)}, bf16[768,128]{1,0:T(8,128)(2,1)S(1)}, u32[]{:S(2)}, u32[]{:S(2)}) collective-permute-start(bf16[768,128]{1,0:T(8,128)(2,1)S(1)} %slice.52), channel_id=1, source_target_pairs={{0,8},{8,16},{16,24},{24,32},{32,40},{40,48},{48,56},{56,64},{64,7... | collective-permute-start | bytes 589832 | tf_op jit(solution)/shard_map/ppermute | solution.py:14
  68.0 2.4 %collective-permute-start.10 = (bf16[256,128]{1,0:T(8,128)(2,1)S(1)}, bf16[256,128]{1,0:T(8,128)(2,1)S(1)}, u32[]{:S(2)}, u32[]{:S(2)}) collective-permute-start(bf16[256,128]{1,0:T(8,128)(2,1)S(1)} %slice.53), channel_id=1, source_target_pairs={{8,0},{16,8},{24,16},{32,24},{40,32},{48,40},{56,48},{64,56},{72,6... | collective-permute-start | bytes 196616 | tf_op jit(solution)/shard_map/ppermute | solution.py:19
  70.4 6.5 %collective-permute-done.10 = bf16[256,128]{1,0:T(8,128)(2,1)S(1)} collective-permute-done((bf16[256,128]{1,0:T(8,128)(2,1)S(1)}, bf16[256,128]{1,0:T(8,128)(2,1)S(1)}, u32[]{:S(2)}, u32[]{:S(2)}) %collective-permute-start.10) | collective-permute-done | bytes 65568 | tf_op jit(solution)/shard_map/ppermute | solution.py:19
  76.9 0.0 collective-permute-done.9
  77.0 2.1 %gather_fusion.2 = bf16[64,128,128]{2,1,0:T(8,128)(2,1)} fusion(bf16[16,128,128]{2,1,0:T(8,128)(2,1)S(1)} %bitcast.119, s32[1024]{0:T(1024)S(1)} %pad_clamp_fusion), kind=kCustom, calls=%fused_computation.2 | custom fusion | bytes 4194560 | tf_op jit(solution)/shard_map/gather | solution.py:30
  79.1 2.3 %fusion.9 = f32[8,128,128,1]{1,2,3,0:T(8,128)S(1)} fusion(bf16[8,8,128,128]{3,2,1,0:T(8,128)(2,1)S(1)} %copy-done, bf16[8,8,128,128]{3,2,1,0:T(8,128)(2,1)} %bitcast.116), kind=kOutput, calls=%fused_computation.47 | convolution fusion | flops 268435456 | bytes 4718592 | tf_op jit(solution)/shard_map/bjrc,bjcv->brv/dot_general | solution.py:31
  81.4 0.0 copy-start.1
  81.4 0.1 fusion.7
  81.6 1.9 %collective-permute-start.11 = (bf16[768,128]{1,0:T(8,128)(2,1)S(1)}, bf16[768,128]{1,0:T(8,128)(2,1)S(1)}, u32[]{:S(2)}, u32[]{:S(2)}) collective-permute-start(bf16[768,128]{1,0:T(8,128)(2,1)S(1)} %slice.54), channel_id=1, source_target_pairs={{0,8},{8,16},{16,24},{24,32},{32,40},{40,48},{48,56},{56,64},{64,7... | collective-permute-start | bytes 589832 | tf_op jit(solution)/shard_map/ppermute | solution.py:14
  83.5 2.4 %collective-permute-start.12 = (bf16[256,128]{1,0:T(8,128)(2,1)S(1)}, bf16[256,128]{1,0:T(8,128)(2,1)S(1)}, u32[]{:S(2)}, u32[]{:S(2)}) collective-permute-start(bf16[256,128]{1,0:T(8,128)(2,1)S(1)} %slice.55), channel_id=1, source_target_pairs={{8,0},{16,8},{24,16},{32,24},{40,32},{48,40},{56,48},{64,56},{72,6... | collective-permute-start | bytes 196616 | tf_op jit(solution)/shard_map/ppermute | solution.py:19
  85.9 6.5 %collective-permute-done.12 = bf16[256,128]{1,0:T(8,128)(2,1)S(1)} collective-permute-done((bf16[256,128]{1,0:T(8,128)(2,1)S(1)}, bf16[256,128]{1,0:T(8,128)(2,1)S(1)}, u32[]{:S(2)}, u32[]{:S(2)}) %collective-permute-start.12) | collective-permute-done | bytes 65568 | tf_op jit(solution)/shard_map/ppermute | solution.py:19
  92.4 0.0 copy-done.1
  92.4 0.0 collective-permute-done.11
  92.5 2.1 %gather_fusion.3 = bf16[64,128,128]{2,1,0:T(8,128)(2,1)} fusion(bf16[16,128,128]{2,1,0:T(8,128)(2,1)S(1)} %bitcast.120, s32[1024]{0:T(1024)S(1)} %pad_clamp_fusion), kind=kCustom, calls=%fused_computation.3 | custom fusion | bytes 4194560 | tf_op jit(solution)/shard_map/gather | solution.py:30
  94.6 0.0 copy-start.2
  94.6 2.3 %fusion.10 = f32[8,128,128,1]{1,2,3,0:T(8,128)S(1)} fusion(bf16[8,8,128,128]{3,2,1,0:T(8,128)(2,1)S(1)} %copy-done, bf16[8,8,128,128]{3,2,1,0:T(8,128)(2,1)} %bitcast.117), kind=kOutput, calls=%fused_computation.48 | convolution fusion | flops 268435456 | bytes 4718592 | tf_op jit(solution)/shard_map/bjrc,bjcv->brv/dot_general | solution.py:31
  97.0 0.0 copy-done.2
  97.0 0.0 copy-start.4
  97.0 0.2 fusion.6
  97.2 1.9 %collective-permute-start.13 = (bf16[768,128]{1,0:T(8,128)(2,1)S(1)}, bf16[768,128]{1,0:T(8,128)(2,1)S(1)}, u32[]{:S(2)}, u32[]{:S(2)}) collective-permute-start(bf16[768,128]{1,0:T(8,128)(2,1)S(1)} %slice.56), channel_id=1, source_target_pairs={{0,8},{8,16},{16,24},{24,32},{32,40},{40,48},{48,56},{56,64},{64,7... | collective-permute-start | bytes 589832 | tf_op jit(solution)/shard_map/ppermute | solution.py:14
  99.2 2.4 %collective-permute-start.14 = (bf16[256,128]{1,0:T(8,128)(2,1)S(1)}, bf16[256,128]{1,0:T(8,128)(2,1)S(1)}, u32[]{:S(2)}, u32[]{:S(2)}) collective-permute-start(bf16[256,128]{1,0:T(8,128)(2,1)S(1)} %slice.57), channel_id=1, source_target_pairs={{8,0},{16,8},{24,16},{32,24},{40,32},{48,40},{56,48},{64,56},{72,6... | collective-permute-start | bytes 196616 | tf_op jit(solution)/shard_map/ppermute | solution.py:19
  101.6 6.5 %collective-permute-done.14 = bf16[256,128]{1,0:T(8,128)(2,1)S(1)} collective-permute-done((bf16[256,128]{1,0:T(8,128)(2,1)S(1)}, bf16[256,128]{1,0:T(8,128)(2,1)S(1)}, u32[]{:S(2)}, u32[]{:S(2)}) %collective-permute-start.14) | collective-permute-done | bytes 65568 | tf_op jit(solution)/shard_map/ppermute | solution.py:19
  108.1 0.0 copy-done.4
  108.1 0.0 collective-permute-done.13
  108.1 2.1 %gather_fusion.4 = bf16[64,128,128]{2,1,0:T(8,128)(2,1)} fusion(bf16[16,128,128]{2,1,0:T(8,128)(2,1)S(1)} %bitcast.118, s32[1024]{0:T(1024)S(1)} %pad_clamp_fusion), kind=kCustom, calls=%fused_computation.4 | custom fusion | bytes 4194560 | tf_op jit(solution)/shard_map/gather | solution.py:30
  110.3 0.0 copy-start.3
  110.3 0.0 copy-start.5
  110.3 2.4 %fusion.11 = f32[8,128,128,1]{1,2,3,0:T(8,128)S(1)} fusion(bf16[8,8,128,128]{3,2,1,0:T(8,128)(2,1)S(1)} %copy-done, bf16[8,8,128,128]{3,2,1,0:T(8,128)(2,1)} %bitcast.114), kind=kOutput, calls=%fused_computation.49 | convolution fusion | flops 268435456 | bytes 4718592 | tf_op jit(solution)/shard_map/bjrc,bjcv->brv/dot_general | solution.py:31
  112.7 0.0 copy-done.3
  112.7 0.0 copy-done.5
  112.7 1.0 fusion.2
  (24 shorter events, 0.4 us)
Async XLA Ops:
  0.0 63.6 %copy-start = (bf16[8,8,128,128]{3,2,1,0:T(8,128)(2,1)S(1)}, bf16[8,8,128,128]{3,2,1,0:T(8,128)(2,1)}, u32[]{:S(2)}) copy-start(bf16[8,8,128,128]{3,2,1,0:T(8,128)(2,1)} %param.6) | copy-start | bytes 6291460
  0.0 52.4 %copy-start.6 = (s32[8,8]{1,0:T(8,128)S(1)}, s32[8,8]{1,0:T(8,128)}, u32[]{:S(2)}) copy-start(s32[8,8]{1,0:T(8,128)} %param.7) | copy-start | bytes 772
  2.4 38.3 %collective-permute-start.6 = (bf16[128,128]{1,0:T(8,128)(2,1)S(1)}, bf16[128,128]{1,0:T(8,128)(2,1)S(1)}, u32[]{:S(2)}, u32[]{:S(2)}) collective-permute-start(bf16[128,128]{1,0:T(8,128)(2,1)S(1)} %get-tuple-element.5), channel_id=1, source_target_pairs={{0,7},{1,0},{2,1},{3,2},{4,3},{5,4},{6,5},{7,6},{8,15},{9,8},{10,9... | collective-permute-start | bytes 98312 | tf_op jit(solution)/shard_map/ppermute | solution.py:52
  8.3 32.4 %collective-permute-start.5 = (bf16[128,128]{1,0:T(8,128)(2,1)S(1)}, bf16[128,128]{1,0:T(8,128)(2,1)S(1)}, u32[]{:S(2)}, u32[]{:S(2)}) collective-permute-start(bf16[128,128]{1,0:T(8,128)(2,1)S(1)} %get-tuple-element.6), channel_id=1, source_target_pairs={{0,6},{1,7},{2,0},{3,1},{4,2},{5,3},{6,4},{7,5},{8,14},{9,15},{10,... | collective-permute-start | bytes 98312 | tf_op jit(solution)/shard_map/ppermute | solution.py:52
  11.8 28.8 %collective-permute-start.4 = (bf16[128,128]{1,0:T(8,128)(2,1)S(1)}, bf16[128,128]{1,0:T(8,128)(2,1)S(1)}, u32[]{:S(2)}, u32[]{:S(2)}) collective-permute-start(bf16[128,128]{1,0:T(8,128)(2,1)S(1)} %get-tuple-element.7), channel_id=1, source_target_pairs={{0,5},{1,6},{2,7},{3,0},{4,1},{5,2},{6,3},{7,4},{8,13},{9,14},{10,... | collective-permute-start | bytes 98312 | tf_op jit(solution)/shard_map/ppermute | solution.py:52
  14.4 26.2 %collective-permute-start.3 = (bf16[128,128]{1,0:T(8,128)(2,1)S(1)}, bf16[128,128]{1,0:T(8,128)(2,1)S(1)}, u32[]{:S(2)}, u32[]{:S(2)}) collective-permute-start(bf16[128,128]{1,0:T(8,128)(2,1)S(1)} %get-tuple-element.8), channel_id=1, source_target_pairs={{0,4},{1,5},{2,6},{3,7},{4,0},{5,1},{6,2},{7,3},{8,12},{9,13},{10,... | collective-permute-start | bytes 98312 | tf_op jit(solution)/shard_map/ppermute | solution.py:52
  20.4 5.9 %collective-permute-start = (bf16[128,128]{1,0:T(8,128)(2,1)S(1)}, bf16[128,128]{1,0:T(8,128)(2,1)S(1)}, u32[]{:S(2)}, u32[]{:S(2)}) collective-permute-start(bf16[128,128]{1,0:T(8,128)(2,1)S(1)} %get-tuple-element.11), channel_id=1, source_target_pairs={{0,1},{1,2},{2,3},{3,4},{4,5},{5,6},{6,7},{7,0},{8,9},{9,10},{10,1... | collective-permute-start | bytes 98312 | tf_op jit(solution)/shard_map/ppermute | solution.py:52
  26.2 6.8 %collective-permute-start.1 = (bf16[128,128]{1,0:T(8,128)(2,1)S(1)}, bf16[128,128]{1,0:T(8,128)(2,1)S(1)}, u32[]{:S(2)}, u32[]{:S(2)}) collective-permute-start(bf16[128,128]{1,0:T(8,128)(2,1)S(1)} %get-tuple-element.10), channel_id=1, source_target_pairs={{0,2},{1,3},{2,4},{3,5},{4,6},{5,7},{6,0},{7,1},{8,10},{9,11},{10,... | collective-permute-start | bytes 98312 | tf_op jit(solution)/shard_map/ppermute | solution.py:52
  33.0 7.7 %collective-permute-start.2 = (bf16[128,128]{1,0:T(8,128)(2,1)S(1)}, bf16[128,128]{1,0:T(8,128)(2,1)S(1)}, u32[]{:S(2)}, u32[]{:S(2)}) collective-permute-start(bf16[128,128]{1,0:T(8,128)(2,1)S(1)} %get-tuple-element.9), channel_id=1, source_target_pairs={{0,3},{1,4},{2,5},{3,6},{4,7},{5,0},{6,1},{7,2},{8,11},{9,12},{10,... | collective-permute-start | bytes 98312 | tf_op jit(solution)/shard_map/ppermute | solution.py:52
  41.4 20.1 %collective-permute-start.7 = (bf16[768,128]{1,0:T(8,128)(2,1)S(1)}, bf16[768,128]{1,0:T(8,128)(2,1)S(1)}, u32[]{:S(2)}, u32[]{:S(2)}) collective-permute-start(bf16[768,128]{1,0:T(8,128)(2,1)S(1)} %bitcast.123), channel_id=1, source_target_pairs={{0,8},{8,16},{16,24},{24,32},{32,40},{40,48},{48,56},{56,64},{64,7... | collective-permute-start | bytes 589832 | tf_op jit(solution)/shard_map/ppermute | solution.py:14
  52.5 8.9 %collective-permute-start.8 = (bf16[256,128]{1,0:T(8,128)(2,1)S(1)}, bf16[256,128]{1,0:T(8,128)(2,1)S(1)}, u32[]{:S(2)}, u32[]{:S(2)}) collective-permute-start(bf16[256,128]{1,0:T(8,128)(2,1)S(1)} %bitcast.124), channel_id=1, source_target_pairs={{8,0},{16,8},{24,16},{32,24},{40,32},{48,40},{56,48},{64,56},{72,6... | collective-permute-start | bytes 196616 | tf_op jit(solution)/shard_map/ppermute | solution.py:19
  66.1 10.9 %collective-permute-start.9 = (bf16[768,128]{1,0:T(8,128)(2,1)S(1)}, bf16[768,128]{1,0:T(8,128)(2,1)S(1)}, u32[]{:S(2)}, u32[]{:S(2)}) collective-permute-start(bf16[768,128]{1,0:T(8,128)(2,1)S(1)} %slice.52), channel_id=1, source_target_pairs={{0,8},{8,16},{16,24},{24,32},{32,40},{40,48},{48,56},{56,64},{64,7... | collective-permute-start | bytes 589832 | tf_op jit(solution)/shard_map/ppermute | solution.py:14
  68.0 8.9 %collective-permute-start.10 = (bf16[256,128]{1,0:T(8,128)(2,1)S(1)}, bf16[256,128]{1,0:T(8,128)(2,1)S(1)}, u32[]{:S(2)}, u32[]{:S(2)}) collective-permute-start(bf16[256,128]{1,0:T(8,128)(2,1)S(1)} %slice.53), channel_id=1, source_target_pairs={{8,0},{16,8},{24,16},{32,24},{40,32},{48,40},{56,48},{64,56},{72,6... | collective-permute-start | bytes 196616 | tf_op jit(solution)/shard_map/ppermute | solution.py:19
  81.4 11.0 %copy-start.1 = (f32[8,128,128,1]{1,2,3,0:T(8,128)}, f32[8,128,128,1]{1,2,3,0:T(8,128)S(1)}, u32[]{:S(2)}) copy-start(f32[8,128,128,1]{1,2,3,0:T(8,128)S(1)} %fusion.9) | copy-start | bytes 1572868
  81.6 10.9 %collective-permute-start.11 = (bf16[768,128]{1,0:T(8,128)(2,1)S(1)}, bf16[768,128]{1,0:T(8,128)(2,1)S(1)}, u32[]{:S(2)}, u32[]{:S(2)}) collective-permute-start(bf16[768,128]{1,0:T(8,128)(2,1)S(1)} %slice.54), channel_id=1, source_target_pairs={{0,8},{8,16},{16,24},{24,32},{32,40},{40,48},{48,56},{56,64},{64,7... | collective-permute-start | bytes 589832 | tf_op jit(solution)/shard_map/ppermute | solution.py:14
  83.5 8.9 %collective-permute-start.12 = (bf16[256,128]{1,0:T(8,128)(2,1)S(1)}, bf16[256,128]{1,0:T(8,128)(2,1)S(1)}, u32[]{:S(2)}, u32[]{:S(2)}) collective-permute-start(bf16[256,128]{1,0:T(8,128)(2,1)S(1)} %slice.55), channel_id=1, source_target_pairs={{8,0},{16,8},{24,16},{32,24},{40,32},{48,40},{56,48},{64,56},{72,6... | collective-permute-start | bytes 196616 | tf_op jit(solution)/shard_map/ppermute | solution.py:19
  94.6 2.4 %copy-start.2 = (f32[8,128,128,1]{1,2,3,0:T(8,128)S(1)}, f32[8,128,128,1]{1,2,3,0:T(8,128)}, u32[]{:S(2)}) copy-start(f32[8,128,128,1]{1,2,3,0:T(8,128)} %copy-done.1) | copy-start | bytes 1572868
  97.0 11.1 %copy-start.4 = (f32[8,128,128,1]{1,2,3,0:T(8,128)}, f32[8,128,128,1]{1,2,3,0:T(8,128)S(1)}, u32[]{:S(2)}) copy-start(f32[8,128,128,1]{1,2,3,0:T(8,128)S(1)} %fusion.10) | copy-start | bytes 1572868
  97.2 10.9 %collective-permute-start.13 = (bf16[768,128]{1,0:T(8,128)(2,1)S(1)}, bf16[768,128]{1,0:T(8,128)(2,1)S(1)}, u32[]{:S(2)}, u32[]{:S(2)}) collective-permute-start(bf16[768,128]{1,0:T(8,128)(2,1)S(1)} %slice.56), channel_id=1, source_target_pairs={{0,8},{8,16},{16,24},{24,32},{32,40},{40,48},{48,56},{56,64},{64,7... | collective-permute-start | bytes 589832 | tf_op jit(solution)/shard_map/ppermute | solution.py:14
  99.2 8.9 %collective-permute-start.14 = (bf16[256,128]{1,0:T(8,128)(2,1)S(1)}, bf16[256,128]{1,0:T(8,128)(2,1)S(1)}, u32[]{:S(2)}, u32[]{:S(2)}) collective-permute-start(bf16[256,128]{1,0:T(8,128)(2,1)S(1)} %slice.57), channel_id=1, source_target_pairs={{8,0},{16,8},{24,16},{32,24},{40,32},{48,40},{56,48},{64,56},{72,6... | collective-permute-start | bytes 196616 | tf_op jit(solution)/shard_map/ppermute | solution.py:19
  110.3 2.4 %copy-start.3 = (f32[8,128,128,1]{1,2,3,0:T(8,128)S(1)}, f32[8,128,128,1]{1,2,3,0:T(8,128)}, u32[]{:S(2)}) copy-start(f32[8,128,128,1]{1,2,3,0:T(8,128)} %copy-done.1) | copy-start | bytes 1572868
  110.3 2.4 %copy-start.5 = (f32[8,128,128,1]{1,2,3,0:T(8,128)S(1)}, f32[8,128,128,1]{1,2,3,0:T(8,128)}, u32[]{:S(2)}) copy-start(f32[8,128,128,1]{1,2,3,0:T(8,128)} %copy-done.4) | copy-start | bytes 1572868

commit v8 on v4

--- a/solution.py
+++ b/solution.py
@@ -23,12 +23,25 @@
     local_blocks, nnz, block_rows, _ = blocks.shape
     width = panel.shape[1]
 
+    row = lax.axis_index("row")
+    rows = lax.axis_size("row")
+    fixed_blocks = blocks[:, :3]
+    free_blocks = blocks[:, 3:]
+    free_index = local_index[:, 3:]
+
     def apply_operator(state_bf):
         lo = shift_up(state_bf[state_bf.shape[0] - REACH_LO * block_rows:], "row")
         hi = shift_down(state_bf[: REACH_HI * block_rows], "row")
+        lo = jnp.where(row == 0, jnp.tile(state_bf[:block_rows], (REACH_LO, 1)), lo)
+        hi = jnp.where(row == rows - 1, jnp.tile(state_bf[state_bf.shape[0] - block_rows:], (REACH_HI, 1)), hi)
         tiles = jnp.concatenate([lo, state_bf, hi], axis=0).reshape(-1, block_rows, width)
-        picked = tiles[local_index]
-        result = jnp.einsum("bjrc,bjcv->brv", blocks, picked, preferred_element_type=jnp.float32)
+        own = tiles[REACH_LO:REACH_LO + local_blocks]
+        below = tiles[:local_blocks]
+        above = tiles[REACH_LO + REACH_HI:REACH_LO + REACH_HI + local_blocks]
+        fixed = jnp.stack([own, below, above], axis=1)
+        result = jnp.einsum("bjrc,bjcv->brv", fixed_blocks, fixed, preferred_element_type=jnp.float32)
+        picked = tiles[free_index]
+        result = result + jnp.einsum("bjrc,bjcv->brv", free_blocks, picked, preferred_element_type=jnp.float32)
         return result.reshape(local_blocks * block_rows, width)
 
     prev = panel.astype(jnp.float32)

time: 90.7 us -> 100 us (1.10)
  the two profiles are of different devices: /device:TPU:399 before, /device:TPU:512 now
where the time goes in v8:
time: 100 us; the launch traced here: 99.7 us
  waiting for transfers between devices  40.6 us (41%)
  starting transfers between devices  24.9 us (25%)
  local copies, waits for them, and re-layouts  14.3 us (14%)
  matrix products  11.2 us (11%)
  other arithmetic  8.47 us (8%)
    ppermute x4, waiting for transfers between devices, shift_up(): return lax.ppermute(cells, axis, [(i, i + 1) for i in range(count - 1)])  28.9 us
    all_to_all x1, waiting for transfers between devices, per_device(): lax.all_to_all(rotated, 'vec', split_axis=1, concat_axis=0, tiled=True)  11.7 us
    ppermute x4, starting transfers between devices, shift_up(): return lax.ppermute(cells, axis, [(i, i + 1) for i in range(count - 1)])  9.63 us
    gather x4, local copies, waits for them, and re-layouts, apply_operator(): picked = tiles[free_index]  9.56 us
    ppermute x4, starting transfers between devices, shift_down(): return lax.ppermute(cells, axis, [(i + 1, i) for i in range(count - 1)])  7.68 us
    all_to_all x1, starting transfers between devices, per_device(): lax.all_to_all(rotated, 'vec', split_axis=1, concat_axis=0, tiled=True)  7.55 us
    dot_general x4, matrix products, apply_operator(): jnp.einsum('bjrc,bjcv->brv', fixed_blocks, fixed, preferred_element_type=...  5.92 us
    concatenate x8, other arithmetic, apply_operator(): jnp.concatenate([lo, state_bf, hi], axis=0).reshape(-1, block_rows, width)  4.31 us
  transfers between devices with their start and end apart: 9, of which 5 were waited for; matrix products, arithmetic and copies ran while one was open for 3% of the time, Pallas kernels for 0%

profile of v8, /device:TPU:512, one launch (start us, length us, event | category | flops | bytes accessed | tf_op | source)
XLA Modules:
  0.0 99.7 jit_solution(8865805528726294761)
XLA Ops:
  0.0 0.0 copy-start
  0.0 0.0 copy-start.10
  0.0 1.6 %copy-done = bf16[1024,1024]{1,0:T(8,128)(2,1)S(1)} copy-done((bf16[1024,1024]{1,0:T(8,128)(2,1)S(1)}, bf16[1024,1024]{1,0:T(8,128)(2,1)}, u32[]{:S(2)}) %copy-start) | copy-done | bytes 2097176
  1.6 1.4 %fusion.4 = bf16[16,8,8,128]{3,2,1,0:T(8,128)(2,1)S(1)} fusion(bf16[128,1024]{1,0:T(8,128)(2,1)} %param.4, bf16[1024,1024]{1,0:T(8,128)(2,1)S(1)} %copy-done), kind=kOutput, calls=%fused_computation.17 | convolution fusion | flops 268566528 | bytes 2621440 | tf_op jit(solution)/shard_map/dot_general | solution.py:58
  3.0 0.8 copy.26
  3.7 7.6 %all-to-all-start = ((bf16[128,8,128]{2,0,1:T(8,128)(2,1)}), bf16[128,8,128]{2,0,1:T(8,128)(2,1)S(1)}, u32[]{:S(2)}, u32[]{:S(2)}) async-start(bf16[128,8,128]{2,0,1:T(8,128)(2,1)} %bitcast.194), calls=%async_computation | async-start | bytes 524288 | tf_op jit(solution)/shard_map/all_to_all | solution.py:59
  11.3 0.0 copy-done.10
  11.3 0.1 compare_select_fusion
  11.4 0.1 reshape.122
  11.5 11.7 %all-to-all-done = bf16[128,8,128]{2,0,1:T(8,128)(2,1)S(1)} async-done(((bf16[128,8,128]{2,0,1:T(8,128)(2,1)}), bf16[128,8,128]{2,0,1:T(8,128)(2,1)S(1)}, u32[]{:S(2)}, u32[]{:S(2)}) %all-to-all-start) | async-done | bytes 262176 | tf_op jit(solution)/shard_map/all_to_all | solution.py:59
  23.2 1.9 %collective-permute-start.1 = (bf16[256,128]{1,0:T(8,128)(2,1)S(1)}, bf16[256,128]{1,0:T(8,128)(2,1)S(1)}, u32[]{:S(2)}, u32[]{:S(2)}) collective-permute-start(bf16[256,128]{1,0:T(8,128)(2,1)S(1)} %bitcast.218), channel_id=1, source_target_pairs={{8,0},{16,8},{24,16},{32,24},{40,32},{48,40},{56,48},{64,56},{72,6... | collective-permute-start | bytes 196616 | tf_op jit(solution)/shard_map/ppermute | solution.py:19
  25.1 2.4 %collective-permute-start = (bf16[768,128]{1,0:T(8,128)(2,1)S(1)}, bf16[768,128]{1,0:T(8,128)(2,1)S(1)}, u32[]{:S(2)}, u32[]{:S(2)}) collective-permute-start(bf16[768,128]{1,0:T(8,128)(2,1)S(1)} %bitcast.217), channel_id=1, source_target_pairs={{0,8},{8,16},{16,24},{24,32},{32,40},{40,48},{48,56},{56,64},{64,7... | collective-permute-start | bytes 589832 | tf_op jit(solution)/shard_map/ppermute | solution.py:14
  27.6 0.0 collective-permute-done.1
  27.6 7.9 %collective-permute-done = bf16[768,128]{1,0:T(8,128)(2,1)S(1)} collective-permute-done((bf16[768,128]{1,0:T(8,128)(2,1)S(1)}, bf16[768,128]{1,0:T(8,128)(2,1)S(1)}, u32[]{:S(2)}, u32[]{:S(2)}) %collective-permute-start) | collective-permute-done | bytes 196640 | tf_op jit(solution)/shard_map/ppermute | solution.py:14
  35.6 1.9 %gather_fusion = bf16[40,128,128]{2,1,0:T(8,128)(2,1)} fusion(bf16[16,128,128]{2,1,0:T(8,128)(2,1)S(1)} %bitcast.204, s32[1024]{0:T(1024)S(1)} %pad_clamp_fusion), kind=kCustom, calls=%fused_computation | custom fusion | bytes 2621600 | tf_op jit(solution)/shard_map/gather | solution.py:43
  37.4 0.0 copy-start.1
  37.4 2.4 %convolution_bitcast_fusion.3 = f32[8,128,128]{1,2,0:T(8,128)S(1)} fusion(bf16[8,8,128,128]{3,2,1,0:T(8,128)(2,1)} %param.6, bf16[8,5,128,128]{3,2,1,0:T(8,128)(2,1)} %bitcast.208), kind=kOutput, calls=%fused_computation.7 | convolution fusion | flops 167772160 | bytes 3932160 | tf_op jit(solution)/shard_map/bjrc,bjcv->brv/dot_general | solution.py:44
  39.8 0.0 copy-done.1
  39.8 0.4 fusion
  40.2 0.1 multiply_convert_fusion
  40.3 1.9 %collective-permute-start.3 = (bf16[256,128]{1,0:T(8,128)(2,1)S(1)}, bf16[256,128]{1,0:T(8,128)(2,1)S(1)}, u32[]{:S(2)}, u32[]{:S(2)}) collective-permute-start(bf16[256,128]{1,0:T(8,128)(2,1)S(1)} %slice.157), channel_id=1, source_target_pairs={{8,0},{16,8},{24,16},{32,24},{40,32},{48,40},{56,48},{64,56},{72,6... | collective-permute-start | bytes 196616 | tf_op jit(solution)/shard_map/ppermute | solution.py:19
  42.2 2.4 %collective-permute-start.2 = (bf16[768,128]{1,0:T(8,128)(2,1)S(1)}, bf16[768,128]{1,0:T(8,128)(2,1)S(1)}, u32[]{:S(2)}, u32[]{:S(2)}) collective-permute-start(bf16[768,128]{1,0:T(8,128)(2,1)S(1)} %slice.155), channel_id=1, source_target_pairs={{0,8},{8,16},{16,24},{24,32},{32,40},{40,48},{48,56},{56,64},{64,7... | collective-permute-start | bytes 589832 | tf_op jit(solution)/shard_map/ppermute | solution.py:14
  44.7 0.8 fusion.37
  45.5 0.0 collective-permute-done.3
  45.5 7.0 %collective-permute-done.2 = bf16[768,128]{1,0:T(8,128)(2,1)S(1)} collective-permute-done((bf16[768,128]{1,0:T(8,128)(2,1)S(1)}, bf16[768,128]{1,0:T(8,128)(2,1)S(1)}, u32[]{:S(2)}, u32[]{:S(2)}) %collective-permute-start.2) | collective-permute-done | bytes 196640 | tf_op jit(solution)/shard_map/ppermute | solution.py:14
  52.6 0.8 pad_maximum_fusion.9
  53.5 1.9 %gather_fusion.1 = bf16[40,128,128]{2,1,0:T(8,128)(2,1)} fusion(bf16[16,128,128]{2,1,0:T(8,128)(2,1)S(1)} %bitcast.202, s32[1024]{0:T(1024)S(1)} %pad_clamp_fusion), kind=kCustom, calls=%fused_computation.1 | custom fusion | bytes 2621600 | tf_op jit(solution)/shard_map/gather | solution.py:43
  55.3 0.0 copy-start.2
  55.3 0.0 copy-start.8
  55.3 1.9 %convolution_bitcast_fusion.7 = f32[8,128,128]{1,2,0:T(8,128)S(1)} fusion(bf16[8,1,128,128]{3,2,0,1:T(8,128)(2,1)} %bitcast.214, bf16[8,1,128,128]{3,2,0,1:T(8,128)(2,1)} %bitcast.213, bf16[8,1,128,128]{3,2,0,1:T(8,128)(2,1)} %fusion.37, bf16[8,8,128,128]{3,2,1,0:T(8,128)(2,1)} %param.6), kind=kOutput, calls=%fused_computation.11 | convolution fusion | flops 103022592 | bytes 2097152 | tf_op jit(solution)/shard_map/bjrc,bjcv->brv/dot_general | solution.py:42
  57.2 0.2 copy-done.2
  57.4 0.4 copy-done.8
  57.7 0.5 fusion.1
  58.2 0.1 fusion.44
  58.4 1.9 %collective-permute-start.5 = (bf16[256,128]{1,0:T(8,128)(2,1)S(1)}, bf16[256,128]{1,0:T(8,128)(2,1)S(1)}, u32[]{:S(2)}, u32[]{:S(2)}) collective-permute-start(bf16[256,128]{1,0:T(8,128)(2,1)S(1)} %slice.161), channel_id=1, source_target_pairs={{8,0},{16,8},{24,16},{32,24},{40,32},{48,40},{56,48},{64,56},{72,6... | collective-permute-start | bytes 196616 | tf_op jit(solution)/shard_map/ppermute | solution.py:19
  60.4 2.4 %collective-permute-start.4 = (bf16[768,128]{1,0:T(8,128)(2,1)S(1)}, bf16[768,128]{1,0:T(8,128)(2,1)S(1)}, u32[]{:S(2)}, u32[]{:S(2)}) collective-permute-start(bf16[768,128]{1,0:T(8,128)(2,1)S(1)} %slice.159), channel_id=1, source_target_pairs={{0,8},{8,16},{16,24},{24,32},{32,40},{40,48},{48,56},{56,64},{64,7... | collective-permute-start | bytes 589832 | tf_op jit(solution)/shard_map/ppermute | solution.py:14
  62.8 0.8 fusion.36
  63.6 0.0 collective-permute-done.5
  63.6 7.1 %collective-permute-done.4 = bf16[768,128]{1,0:T(8,128)(2,1)S(1)} collective-permute-done((bf16[768,128]{1,0:T(8,128)(2,1)S(1)}, bf16[768,128]{1,0:T(8,128)(2,1)S(1)}, u32[]{:S(2)}, u32[]{:S(2)}) %collective-permute-start.4) | collective-permute-done | bytes 196640 | tf_op jit(solution)/shard_map/ppermute | solution.py:14
  70.7 0.8 pad_maximum_fusion.2
  71.5 0.8 pad_maximum_fusion.7
  72.4 2.9 %gather_fusion.2 = bf16[40,128,128]{2,1,0:T(8,128)(2,1)} fusion(bf16[16,128,128]{2,1,0:T(8,128)(2,1)} %bitcast.203, s32[1024]{0:T(1024)S(1)} %pad_clamp_fusion), kind=kCustom, calls=%fused_computation.2 | custom fusion | bytes 2621600 | tf_op jit(solution)/shard_map/gather | solution.py:43
  75.3 0.0 copy-start.3
  75.3 1.9 %convolution_bitcast_fusion.6 = f32[8,128,128]{1,2,0:T(8,128)S(1)} fusion(bf16[8,1,128,128]{3,2,0,1:T(8,128)(2,1)} %bitcast.216, bf16[8,1,128,128]{3,2,0,1:T(8,128)(2,1)} %bitcast.215, bf16[8,1,128,128]{3,2,0,1:T(8,128)(2,1)} %fusion.36, bf16[8,8,128,128]{3,2,1,0:T(8,128)(2,1)} %param.6), kind=kOutput, calls=%fused_computation.10 | convolution fusion | flops 103022592 | bytes 2097152 | tf_op jit(solution)/shard_map/bjrc,bjcv->brv/dot_general | solution.py:42
  77.1 0.2 copy-done.3
  77.3 0.4 copy-done.9
  77.7 0.5 fusion.2
  78.2 0.0 copy-start.5
  78.2 0.2 fusion.43
  78.5 1.9 %collective-permute-start.7 = (bf16[256,128]{1,0:T(8,128)(2,1)S(1)}, bf16[256,128]{1,0:T(8,128)(2,1)S(1)}, u32[]{:S(2)}, u32[]{:S(2)}) collective-permute-start(bf16[256,128]{1,0:T(8,128)(2,1)S(1)} %slice.165), channel_id=1, source_target_pairs={{8,0},{16,8},{24,16},{32,24},{40,32},{48,40},{56,48},{64,56},{72,6... | collective-permute-start | bytes 196616 | tf_op jit(solution)/shard_map/ppermute | solution.py:19
  80.4 2.4 %collective-permute-start.6 = (bf16[768,128]{1,0:T(8,128)(2,1)S(1)}, bf16[768,128]{1,0:T(8,128)(2,1)S(1)}, u32[]{:S(2)}, u32[]{:S(2)}) collective-permute-start(bf16[768,128]{1,0:T(8,128)(2,1)S(1)} %slice.163), channel_id=1, source_target_pairs={{0,8},{8,16},{16,24},{24,32},{32,40},{40,48},{48,56},{56,64},{64,7... | collective-permute-start | bytes 589832 | tf_op jit(solution)/shard_map/ppermute | solution.py:14
  82.8 0.9 fusion.38
  83.7 0.0 copy-done.5
  83.7 0.0 collective-permute-done.7
  83.7 6.9 %collective-permute-done.6 = bf16[768,128]{1,0:T(8,128)(2,1)S(1)} collective-permute-done((bf16[768,128]{1,0:T(8,128)(2,1)S(1)}, bf16[768,128]{1,0:T(8,128)(2,1)S(1)}, u32[]{:S(2)}, u32[]{:S(2)}) %collective-permute-start.6) | collective-permute-done | bytes 196640 | tf_op jit(solution)/shard_map/ppermute | solution.py:14
  90.7 0.8 pad_maximum_fusion.3
  91.6 0.9 pad_maximum_fusion.5
  92.4 2.9 %gather_fusion.3 = bf16[40,128,128]{2,1,0:T(8,128)(2,1)} fusion(bf16[16,128,128]{2,1,0:T(8,128)(2,1)} %bitcast.201, s32[1024]{0:T(1024)S(1)} %pad_clamp_fusion), kind=kCustom, calls=%fused_computation.3 | custom fusion | bytes 2621600 | tf_op jit(solution)/shard_map/gather | solution.py:43
  95.3 1.9 %convolution_bitcast_fusion.5 = f32[8,128,128]{1,2,0:T(8,128)S(1)} fusion(bf16[8,1,128,128]{3,2,0,1:T(8,128)(2,1)} %bitcast.210, bf16[8,1,128,128]{3,2,0,1:T(8,128)(2,1)} %bitcast.209, bf16[8,1,128,128]{3,2,0,1:T(8,128)(2,1)} %fusion.38, bf16[8,8,128,128]{3,2,1,0:T(8,128)(2,1)} %param.6), kind=kOutput, calls=%fused_computation.9 | convolution fusion | flops 103022592 | bytes 2097152 | tf_op jit(solution)/shard_map/bjrc,bjcv->brv/dot_general | solution.py:42
  97.2 0.2 copy-done.4
  97.4 0.4 copy-done.7
  97.7 0.5 fusion.3
  98.2 0.5 copy-done.6
  98.8 1.0 fusion.31
  (29 shorter events, 0.4 us)
Async XLA Ops:
  0.0 1.6 %copy-start = (bf16[1024,1024]{1,0:T(8,128)(2,1)S(1)}, bf16[1024,1024]{1,0:T(8,128)(2,1)}, u32[]{:S(2)}) copy-start(bf16[1024,1024]{1,0:T(8,128)(2,1)} %param.5) | copy-start | bytes 6291460
  0.0 11.3 %copy-start.10 = (s32[8,8]{1,0:T(8,128)S(1)}, s32[8,8]{1,0:T(8,128)}, u32[]{:S(2)}) copy-start(s32[8,8]{1,0:T(8,128)} %param.7) | copy-start | bytes 772
  3.7 19.4 %all-to-all-start = ((bf16[128,8,128]{2,0,1:T(8,128)(2,1)}), bf16[128,8,128]{2,0,1:T(8,128)(2,1)S(1)}, u32[]{:S(2)}, u32[]{:S(2)}) async-start(bf16[128,8,128]{2,0,1:T(8,128)(2,1)} %bitcast.194), calls=%async_computation | async-start | bytes 524288 | tf_op jit(solution)/shard_map/all_to_all | solution.py:59
  23.2 4.4 %collective-permute-start.1 = (bf16[256,128]{1,0:T(8,128)(2,1)S(1)}, bf16[256,128]{1,0:T(8,128)(2,1)S(1)}, u32[]{:S(2)}, u32[]{:S(2)}) collective-permute-start(bf16[256,128]{1,0:T(8,128)(2,1)S(1)} %bitcast.218), channel_id=1, source_target_pairs={{8,0},{16,8},{24,16},{32,24},{40,32},{48,40},{56,48},{64,56},{72,6... | collective-permute-start | bytes 196616 | tf_op jit(solution)/shard_map/ppermute | solution.py:19
  25.1 10.3 %collective-permute-start = (bf16[768,128]{1,0:T(8,128)(2,1)S(1)}, bf16[768,128]{1,0:T(8,128)(2,1)S(1)}, u32[]{:S(2)}, u32[]{:S(2)}) collective-permute-start(bf16[768,128]{1,0:T(8,128)(2,1)S(1)} %bitcast.217), channel_id=1, source_target_pairs={{0,8},{8,16},{16,24},{24,32},{32,40},{40,48},{48,56},{56,64},{64,7... | collective-permute-start | bytes 589832 | tf_op jit(solution)/shard_map/ppermute | solution.py:14
  37.4 2.4 %copy-start.1 = (bf16[8,8,128,128]{3,2,1,0:T(8,128)(2,1)S(1)}, bf16[8,8,128,128]{3,2,1,0:T(8,128)(2,1)}, u32[]{:S(2)}) copy-start(bf16[8,8,128,128]{3,2,1,0:T(8,128)(2,1)} %param.6) | copy-start | bytes 6291460
  40.3 5.2 %collective-permute-start.3 = (bf16[256,128]{1,0:T(8,128)(2,1)S(1)}, bf16[256,128]{1,0:T(8,128)(2,1)S(1)}, u32[]{:S(2)}, u32[]{:S(2)}) collective-permute-start(bf16[256,128]{1,0:T(8,128)(2,1)S(1)} %slice.157), channel_id=1, source_target_pairs={{8,0},{16,8},{24,16},{32,24},{40,32},{48,40},{56,48},{64,56},{72,6... | collective-permute-start | bytes 196616 | tf_op jit(solution)/shard_map/ppermute | solution.py:19
  42.2 10.3 %collective-permute-start.2 = (bf16[768,128]{1,0:T(8,128)(2,1)S(1)}, bf16[768,128]{1,0:T(8,128)(2,1)S(1)}, u32[]{:S(2)}, u32[]{:S(2)}) collective-permute-start(bf16[768,128]{1,0:T(8,128)(2,1)S(1)} %slice.155), channel_id=1, source_target_pairs={{0,8},{8,16},{16,24},{24,32},{32,40},{40,48},{48,56},{56,64},{64,7... | collective-permute-start | bytes 589832 | tf_op jit(solution)/shard_map/ppermute | solution.py:14
  55.3 2.1 %copy-start.2 = (bf16[8,8,128,128]{3,2,1,0:T(8,128)(2,1)S(1)}, bf16[8,8,128,128]{3,2,1,0:T(8,128)(2,1)}, u32[]{:S(2)}) copy-start(bf16[8,8,128,128]{3,2,1,0:T(8,128)(2,1)} %param.6) | copy-start | bytes 6291460
  55.3 2.4 %copy-start.8 = (bf16[40,128,128]{2,1,0:T(8,128)(2,1)S(1)}, bf16[40,128,128]{2,1,0:T(8,128)(2,1)}, u32[]{:S(2)}) copy-start(bf16[40,128,128]{2,1,0:T(8,128)(2,1)} %gather_fusion.1) | copy-start | bytes 3932164
  58.4 5.2 %collective-permute-start.5 = (bf16[256,128]{1,0:T(8,128)(2,1)S(1)}, bf16[256,128]{1,0:T(8,128)(2,1)S(1)}, u32[]{:S(2)}, u32[]{:S(2)}) collective-permute-start(bf16[256,128]{1,0:T(8,128)(2,1)S(1)} %slice.161), channel_id=1, source_target_pairs={{8,0},{16,8},{24,16},{32,24},{40,32},{48,40},{56,48},{64,56},{72,6... | collective-permute-start | bytes 196616 | tf_op jit(solution)/shard_map/ppermute | solution.py:19
  60.4 10.3 %collective-permute-start.4 = (bf16[768,128]{1,0:T(8,128)(2,1)S(1)}, bf16[768,128]{1,0:T(8,128)(2,1)S(1)}, u32[]{:S(2)}, u32[]{:S(2)}) collective-permute-start(bf16[768,128]{1,0:T(8,128)(2,1)S(1)} %slice.159), channel_id=1, source_target_pairs={{0,8},{8,16},{16,24},{24,32},{32,40},{40,48},{48,56},{56,64},{64,7... | collective-permute-start | bytes 589832 | tf_op jit(solution)/shard_map/ppermute | solution.py:14
  75.3 2.1 %copy-start.3 = (bf16[8,8,128,128]{3,2,1,0:T(8,128)(2,1)S(1)}, bf16[8,8,128,128]{3,2,1,0:T(8,128)(2,1)}, u32[]{:S(2)}) copy-start(bf16[8,8,128,128]{3,2,1,0:T(8,128)(2,1)} %param.6) | copy-start | bytes 6291460
  75.3 2.4 %copy-start.9 = (bf16[40,128,128]{2,1,0:T(8,128)(2,1)S(1)}, bf16[40,128,128]{2,1,0:T(8,128)(2,1)}, u32[]{:S(2)}) copy-start(bf16[40,128,128]{2,1,0:T(8,128)(2,1)} %gather_fusion.2) | copy-start | bytes 3932164
  78.2 5.5 %copy-start.5 = (f32[8,128,128]{1,2,0:T(8,128)}, f32[8,128,128]{1,2,0:T(8,128)S(1)}, u32[]{:S(2)}) copy-start(f32[8,128,128]{1,2,0:T(8,128)S(1)} %fusion.2) | copy-start | bytes 1572868
  78.5 5.3 %collective-permute-start.7 = (bf16[256,128]{1,0:T(8,128)(2,1)S(1)}, bf16[256,128]{1,0:T(8,128)(2,1)S(1)}, u32[]{:S(2)}, u32[]{:S(2)}) collective-permute-start(bf16[256,128]{1,0:T(8,128)(2,1)S(1)} %slice.165), channel_id=1, source_target_pairs={{8,0},{16,8},{24,16},{32,24},{40,32},{48,40},{56,48},{64,56},{72,6... | collective-permute-start | bytes 196616 | tf_op jit(solution)/shard_map/ppermute | solution.py:19
  80.4 10.3 %collective-permute-start.6 = (bf16[768,128]{1,0:T(8,128)(2,1)S(1)}, bf16[768,128]{1,0:T(8,128)(2,1)S(1)}, u32[]{:S(2)}, u32[]{:S(2)}) collective-permute-start(bf16[768,128]{1,0:T(8,128)(2,1)S(1)} %slice.163), channel_id=1, source_target_pairs={{0,8},{8,16},{16,24},{24,32},{32,40},{40,48},{48,56},{56,64},{64,7... | collective-permute-start | bytes 589832 | tf_op jit(solution)/shard_map/ppermute | solution.py:14
  95.3 2.1 %copy-start.4 = (bf16[8,8,128,128]{3,2,1,0:T(8,128)(2,1)S(1)}, bf16[8,8,128,128]{3,2,1,0:T(8,128)(2,1)}, u32[]{:S(2)}) copy-start(bf16[8,8,128,128]{3,2,1,0:T(8,128)(2,1)} %param.6) | copy-start | bytes 6291460
  95.3 2.4 %copy-start.7 = (bf16[40,128,128]{2,1,0:T(8,128)(2,1)S(1)}, bf16[40,128,128]{2,1,0:T(8,128)(2,1)}, u32[]{:S(2)}) copy-start(bf16[40,128,128]{2,1,0:T(8,128)(2,1)} %gather_fusion.3) | copy-start | bytes 3932164
  97.7 1.0 %copy-start.6 = (f32[8,128,128]{1,2,0:T(8,128)S(1)}, f32[8,128,128]{1,2,0:T(8,128)}, u32[]{:S(2)}) copy-start(f32[8,128,128]{1,2,0:T(8,128)} %copy-done.5) | copy-start | bytes 1572868

commit v9 on v4

--- a/solution.py
+++ b/solution.py
@@ -19,7 +19,7 @@
     return lax.ppermute(cells, axis, [(i + 1, i) for i in range(count - 1)])
 
 
-def filter_chunk(panel, blocks, local_index):
+def filter_chunk(panel, blocks, offset):
     local_blocks, nnz, block_rows, _ = blocks.shape
     width = panel.shape[1]
 
@@ -27,7 +27,10 @@
         lo = shift_up(state_bf[state_bf.shape[0] - REACH_LO * block_rows:], "row")
         hi = shift_down(state_bf[: REACH_HI * block_rows], "row")
         tiles = jnp.concatenate([lo, state_bf, hi], axis=0).reshape(-1, block_rows, width)
-        picked = tiles[local_index]
+        picked = jnp.broadcast_to(tiles[None, :local_blocks].transpose(1, 0, 2, 3), (local_blocks, nnz, block_rows, width))
+        for w in range(1, REACH_LO + REACH_HI + 1):
+            window = tiles[w:w + local_blocks][:, None]
+            picked = jnp.where((offset == w)[:, :, None, None], window, picked)
         result = jnp.einsum("bjrc,bjcv->brv", blocks, picked, preferred_element_type=jnp.float32)
         return result.reshape(local_blocks * block_rows, width)
 
@@ -47,9 +50,9 @@
     local_blocks = blocks.shape[0]
     n_tiles = local_blocks + REACH_LO + REACH_HI
     first_block = lax.axis_index("row") * local_blocks
-    local_index = jnp.clip(columns - first_block + REACH_LO, 0, n_tiles - 1)
+    offset = jnp.clip(columns - first_block + REACH_LO - jnp.arange(local_blocks)[:, None], 0, REACH_LO + REACH_HI)
     width = panel.shape[1] // CHUNKS
-    outs = [filter_chunk(panel[:, k * width:(k + 1) * width], blocks, local_index) for k in range(CHUNKS)]
+    outs = [filter_chunk(panel[:, k * width:(k + 1) * width], blocks, offset) for k in range(CHUNKS)]
     return outs[0] if CHUNKS == 1 else jnp.concatenate(outs, axis=1)
 
 

time: 90.7 us -> 88.6 us (0.977)
  local copies, waits for them, and re-layouts: 9.52 us -> 0.84 us
  starting transfers between devices: 30.5 us -> 35.8 us
  matrix products: 11.6 us -> 15.8 us
  waiting for transfers between devices: 36.8 us -> 32.9 us
  other arithmetic: 1.62 us -> 2.64 us
    gather x4 -> x0, local copies, waits for them, and re-layouts: 8.58 us -> none  [apply_operator(): picked = tiles[local_index]]
    ppermute x4, waiting for transfers between devices: 26.4 us -> 20 us  [shift_down(): return lax.ppermute(cells, axis, [(i + 1, i) for i in range(count - 1)])]
    dot_general x4, matrix products: 9.29 us -> 13.5 us  [apply_operator(): jnp.einsum('bjrc,bjcv->brv', blocks, picked, preferred_element_type=jnp.f...]
    ppermute x4, starting transfers between devices: 14 us -> 17.4 us  [shift_up(): return lax.ppermute(cells, axis, [(i, i + 1) for i in range(count - 1)])]
    ppermute x4, waiting for transfers between devices: 0.01 us -> 2.56 us  [shift_up(): return lax.ppermute(cells, axis, [(i, i + 1) for i in range(count - 1)])]
    ppermute x4, starting transfers between devices: 9.14 us -> 11.1 us  [shift_down(): return lax.ppermute(cells, axis, [(i + 1, i) for i in range(count - 1)])]
    concatenate x4, other arithmetic: 0.14 us -> 1.18 us  [apply_operator(): jnp.concatenate([lo, state_bf, hi], axis=0).reshape(-1, block_rows, width)]
where the time goes in v9:
time: 88.6 us; the launch traced here: 88.1 us
  starting transfers between devices  35.8 us (40%)
  waiting for transfers between devices  32.9 us (37%)
  matrix products  15.8 us (18%)
  other arithmetic  2.64 us (3%)
    ppermute x4, waiting for transfers between devices, shift_down(): return lax.ppermute(cells, axis, [(i + 1, i) for i in range(count - 1)])  20 us
    ppermute x4, starting transfers between devices, shift_up(): return lax.ppermute(cells, axis, [(i, i + 1) for i in range(count - 1)])  17.4 us
    dot_general x4, matrix products, apply_operator(): jnp.einsum('bjrc,bjcv->brv', blocks, picked, preferred_element_type=jnp.f...  13.5 us
    ppermute x4, starting transfers between devices, shift_down(): return lax.ppermute(cells, axis, [(i + 1, i) for i in range(count - 1)])  11.1 us
    all_to_all x1, waiting for transfers between devices, per_device(): lax.all_to_all(rotated, 'vec', split_axis=1, concat_axis=0, tiled=True)  10.4 us
    all_to_all x1, starting transfers between devices, per_device(): lax.all_to_all(rotated, 'vec', split_axis=1, concat_axis=0, tiled=True)  7.27 us
    ppermute x4, waiting for transfers between devices, shift_up(): return lax.ppermute(cells, axis, [(i, i + 1) for i in range(count - 1)])  2.56 us
    dot_general x1, matrix products, per_device(): jnp.dot(vectors, rotation, preferred_element_type=jnp.float32)  2.28 us
  transfers between devices with their start and end apart: 9, of which 5 were waited for; matrix products, arithmetic and copies ran while one was open for 0% of the time, Pallas kernels for 0%

profile of v9, /device:TPU:399, one launch (start us, length us, event | category | flops | bytes accessed | tf_op | source)
XLA Modules:
  0.0 88.1 jit_solution(3857735125684571450)
XLA Ops:
  0.0 0.0 copy-start
  0.0 0.0 copy-start.1
  0.0 2.3 %fusion.68 = bf16[16,8,8,128]{3,2,1,0:T(8,128)(2,1)S(1)} fusion(bf16[128,1024]{1,0:T(8,128)(2,1)} %param.4, bf16[1024,1024]{1,0:T(8,128)(2,1)} %param.5), kind=kOutput, calls=%fused_computation.69 | convolution fusion | flops 268566528 | bytes 2621440 | tf_op jit(solution)/shard_map/dot_general | solution.py:48
  2.3 0.8 copy.12
  3.0 7.3 %all-to-all-start = ((bf16[128,8,128]{2,0,1:T(8,128)(2,1)}), bf16[128,8,128]{2,0,1:T(8,128)(2,1)S(1)}, u32[]{:S(2)}, u32[]{:S(2)}) async-start(bf16[128,8,128]{2,0,1:T(8,128)(2,1)} %bitcast.148), calls=%async_computation | async-start | bytes 524288 | tf_op jit(solution)/shard_map/all_to_all | solution.py:49
  10.3 10.4 %all-to-all-done = bf16[128,8,128]{2,0,1:T(8,128)(2,1)S(1)} async-done(((bf16[128,8,128]{2,0,1:T(8,128)(2,1)}), bf16[128,8,128]{2,0,1:T(8,128)(2,1)S(1)}, u32[]{:S(2)}, u32[]{:S(2)}) %all-to-all-start) | async-done | bytes 262176 | tf_op jit(solution)/shard_map/all_to_all | solution.py:49
  20.7 4.4 %collective-permute-start = (bf16[256,128]{1,0:T(8,128)(2,1)S(1)}, bf16[256,128]{1,0:T(8,128)(2,1)S(1)}, u32[]{:S(2)}, u32[]{:S(2)}) collective-permute-start(bf16[256,128]{1,0:T(8,128)(2,1)S(1)} %bitcast.186), channel_id=1, source_target_pairs={{8,0},{16,8},{24,16},{32,24},{40,32},{48,40},{56,48},{64,56},{72,6... | collective-permute-start | bytes 196616 | tf_op jit(solution)/shard_map/ppermute | solution.py:19
  25.1 5.8 %collective-permute-start.1 = (bf16[768,128]{1,0:T(8,128)(2,1)S(1)}, bf16[768,128]{1,0:T(8,128)(2,1)S(1)}, u32[]{:S(2)}, u32[]{:S(2)}) collective-permute-start(bf16[768,128]{1,0:T(8,128)(2,1)S(1)} %bitcast.185), channel_id=1, source_target_pairs={{0,8},{8,16},{16,24},{24,32},{32,40},{40,48},{48,56},{56,64},{64,7... | collective-permute-start | bytes 589832 | tf_op jit(solution)/shard_map/ppermute | solution.py:14
  30.9 0.0 copy-done.1
  30.9 0.0 collective-permute-done
  31.0 2.5 %collective-permute-done.1 = bf16[768,128]{1,0:T(8,128)(2,1)S(1)} collective-permute-done((bf16[768,128]{1,0:T(8,128)(2,1)S(1)}, bf16[768,128]{1,0:T(8,128)(2,1)S(1)}, u32[]{:S(2)}, u32[]{:S(2)}) %collective-permute-start.1) | collective-permute-done | bytes 196640 | tf_op jit(solution)/shard_map/ppermute | solution.py:14
  33.5 0.3 fusion.116
  33.8 0.0 copy-done
  33.8 3.4 %multiply_convert_fusion = (bf16[8,128,128]{2,1,0:T(8,128)(2,1)S(1)}, f32[8,128,128,1]{1,2,3,0:T(8,128)S(1)}) fusion(bf16[128,8,128]{2,0,1:T(8,128)(2,1)S(1)} %all-to-all-done, bf16[8,8,128,128]{3,2,1,0:T(8,128)(2,1)S(1)} %copy-done, pred[8,8]{1,0:T(8,128)(4,1)S(1)} %get-tuple-element.68, pred[8,8]{1,0:T(8,128)(4,1)S(1)} %get-tuple-element.67, ...), kind=kOutput, calls=%fused_computation.162 | convolution fusion | flops 277479424 | bytes 5505536 | tf_op jit(solution)/shard_map/bjrc,bjcv->brv/dot_general | solution.py:34
  37.2 0.1 multiply_convert_fusion.1
  37.4 7.7 %collective-permute-start.3 = (bf16[768,128]{1,0:T(8,128)(2,1)S(1)}, bf16[768,128]{1,0:T(8,128)(2,1)S(1)}, u32[]{:S(2)}, u32[]{:S(2)}) collective-permute-start(bf16[768,128]{1,0:T(8,128)(2,1)S(1)} %slice.257), channel_id=1, source_target_pairs={{0,8},{8,16},{16,24},{24,32},{32,40},{40,48},{48,56},{56,64},{64,7... | collective-permute-start | bytes 589832 | tf_op jit(solution)/shard_map/ppermute | solution.py:14
  45.1 1.9 %collective-permute-start.2 = (bf16[256,128]{1,0:T(8,128)(2,1)S(1)}, bf16[256,128]{1,0:T(8,128)(2,1)S(1)}, u32[]{:S(2)}, u32[]{:S(2)}) collective-permute-start(bf16[256,128]{1,0:T(8,128)(2,1)S(1)} %slice.254), channel_id=1, source_target_pairs={{8,0},{16,8},{24,16},{32,24},{40,32},{48,40},{56,48},{64,56},{72,6... | collective-permute-start | bytes 196616 | tf_op jit(solution)/shard_map/ppermute | solution.py:19
  47.0 7.0 %collective-permute-done.2 = bf16[256,128]{1,0:T(8,128)(2,1)S(1)} collective-permute-done((bf16[256,128]{1,0:T(8,128)(2,1)S(1)}, bf16[256,128]{1,0:T(8,128)(2,1)S(1)}, u32[]{:S(2)}, u32[]{:S(2)}) %collective-permute-start.2) | collective-permute-done | bytes 65568 | tf_op jit(solution)/shard_map/ppermute | solution.py:19
  54.0 0.0 collective-permute-done.3
  54.0 0.3 fusion.115
  54.3 3.4 %fusion.112 = (bf16[8,128,128]{2,1,0:T(8,128)(2,1)S(1)}, f32[8,128,128,1]{1,2,3,0:T(8,128)S(1)}) fusion(f32[8,128,128,1]{1,2,3,0:T(8,128)S(1)} %get-tuple-element.70, bf16[128,8,128]{2,0,1:T(8,128)(2,1)S(1)} %all-to-all-done, bf16[8,8,128,128]{3,2,1,0:T(8,128)(2,1)S(1)} %copy-done, pred[8,8]{1,0:T(8,128)(4,1)S(1)} %get-tuple-element.68, ...), kind=kOutput, calls=%fused_computation.172 | convolution fusion | flops 277741568 | bytes 6029824 | tf_op jit(solution)/shard_map/bjrc,bjcv->brv/dot_general | solution.py:34
  57.7 0.1 fusion.138
  57.8 1.9 %collective-permute-start.5 = (bf16[768,128]{1,0:T(8,128)(2,1)S(1)}, bf16[768,128]{1,0:T(8,128)(2,1)S(1)}, u32[]{:S(2)}, u32[]{:S(2)}) collective-permute-start(bf16[768,128]{1,0:T(8,128)(2,1)S(1)} %slice.271), channel_id=1, source_target_pairs={{0,8},{8,16},{16,24},{24,32},{32,40},{40,48},{48,56},{56,64},{64,7... | collective-permute-start | bytes 589832 | tf_op jit(solution)/shard_map/ppermute | solution.py:14
  59.8 2.4 %collective-permute-start.4 = (bf16[256,128]{1,0:T(8,128)(2,1)S(1)}, bf16[256,128]{1,0:T(8,128)(2,1)S(1)}, u32[]{:S(2)}, u32[]{:S(2)}) collective-permute-start(bf16[256,128]{1,0:T(8,128)(2,1)S(1)} %slice.268), channel_id=1, source_target_pairs={{8,0},{16,8},{24,16},{32,24},{40,32},{48,40},{56,48},{64,56},{72,6... | collective-permute-start | bytes 196616 | tf_op jit(solution)/shard_map/ppermute | solution.py:19
  62.2 6.5 %collective-permute-done.4 = bf16[256,128]{1,0:T(8,128)(2,1)S(1)} collective-permute-done((bf16[256,128]{1,0:T(8,128)(2,1)S(1)}, bf16[256,128]{1,0:T(8,128)(2,1)S(1)}, u32[]{:S(2)}, u32[]{:S(2)}) %collective-permute-start.4) | collective-permute-done | bytes 65568 | tf_op jit(solution)/shard_map/ppermute | solution.py:19
  68.7 0.0 collective-permute-done.5
  68.7 0.3 fusion.114
  69.0 3.4 %fusion.111 = (bf16[8,128,128]{2,1,0:T(8,128)(2,1)S(1)}, f32[8,128,128,1]{1,2,3,0:T(8,128)S(1)}) fusion(f32[8,128,128,1]{1,2,3,0:T(8,128)S(1)} %get-tuple-element.70, f32[8,128,128,1]{1,2,3,0:T(8,128)S(1)} %get-tuple-element.72, bf16[128,8,128]{2,0,1:T(8,128)(2,1)S(1)} %all-to-all-done, bf16[8,8,128,128]{3,2,1,0:T(8,128)(2,1)S(1)} %copy-done, ...), kind=kOutput, calls=%fused_computation.160 | convolution fusion | flops 278265856 | bytes 6554112 | tf_op jit(solution)/shard_map/bjrc,bjcv->brv/dot_general | solution.py:34
  72.4 0.2 fusion.137
  72.6 1.9 %collective-permute-start.7 = (bf16[768,128]{1,0:T(8,128)(2,1)S(1)}, bf16[768,128]{1,0:T(8,128)(2,1)S(1)}, u32[]{:S(2)}, u32[]{:S(2)}) collective-permute-start(bf16[768,128]{1,0:T(8,128)(2,1)S(1)} %slice.285), channel_id=1, source_target_pairs={{0,8},{8,16},{16,24},{24,32},{32,40},{40,48},{48,56},{56,64},{64,7... | collective-permute-start | bytes 589832 | tf_op jit(solution)/shard_map/ppermute | solution.py:14
  74.6 2.4 %collective-permute-start.6 = (bf16[256,128]{1,0:T(8,128)(2,1)S(1)}, bf16[256,128]{1,0:T(8,128)(2,1)S(1)}, u32[]{:S(2)}, u32[]{:S(2)}) collective-permute-start(bf16[256,128]{1,0:T(8,128)(2,1)S(1)} %slice.282), channel_id=1, source_target_pairs={{8,0},{16,8},{24,16},{32,24},{40,32},{48,40},{56,48},{64,56},{72,6... | collective-permute-start | bytes 196616 | tf_op jit(solution)/shard_map/ppermute | solution.py:19
  77.0 6.5 %collective-permute-done.6 = bf16[256,128]{1,0:T(8,128)(2,1)S(1)} collective-permute-done((bf16[256,128]{1,0:T(8,128)(2,1)S(1)}, bf16[256,128]{1,0:T(8,128)(2,1)S(1)}, u32[]{:S(2)}, u32[]{:S(2)}) %collective-permute-start.6) | collective-permute-done | bytes 65568 | tf_op jit(solution)/shard_map/ppermute | solution.py:19
  83.5 0.0 collective-permute-done.7
  83.5 0.3 fusion.113
  83.8 3.4 %fusion = f32[8,128,128,1]{1,2,3,0:T(8,128)S(1)} fusion(bf16[8,8,128,128]{3,2,1,0:T(8,128)(2,1)S(1)} %copy-done, pred[8,8]{1,0:T(8,128)(4,1)S(1)} %get-tuple-element.68, pred[8,8]{1,0:T(8,128)(4,1)S(1)} %get-tuple-element.67, pred[8,8]{1,0:T(8,128)(4,1)S(1)} %get-tuple-element.66, pred[8,8]{1,0:T(8,128)(4,1)S(1)} %get-tuple-element.65, ...), kind=kOutput, calls=%fused_computation | convolution fusion | flops 276824064 | bytes 4981248 | tf_op jit(solution)/shard_map/bjrc,bjcv->brv/dot_general | solution.py:34
  87.2 1.0 %fusion.108 = bf16[1024,128]{1,0:T(8,128)(2,1)} fusion(f32[8,128,128,1]{1,2,3,0:T(8,128)S(1)} %fusion, bf16[128,8,128]{2,0,1:T(8,128)(2,1)S(1)} %all-to-all-done, f32[8,128,128,1]{1,2,3,0:T(8,128)S(1)} %get-tuple-element.70, f32[8,128,128,1]{1,2,3,0:T(8,128)S(1)} %get-tuple-element.74, f32[8,128,128,1]{1,2,3,0:T(8,128)S(1)} %get-tuple-element.72), kind=kLoop, calls=%fused_computation.154 | loop fusion | flops 1835008 | bytes 2621440 | tf_op jit(solution)/shard_map/convert_element_type | solution.py:44
  (9 shorter events, 0.1 us)
Async XLA Ops:
  0.0 33.8 %copy-start = (bf16[8,8,128,128]{3,2,1,0:T(8,128)(2,1)S(1)}, bf16[8,8,128,128]{3,2,1,0:T(8,128)(2,1)}, u32[]{:S(2)}) copy-start(bf16[8,8,128,128]{3,2,1,0:T(8,128)(2,1)} %param.6) | copy-start | bytes 6291460
  0.0 30.9 %copy-start.1 = (s32[8,8]{1,0:T(8,128)S(1)}, s32[8,8]{1,0:T(8,128)}, u32[]{:S(2)}) copy-start(s32[8,8]{1,0:T(8,128)} %param.7) | copy-start | bytes 772
  3.0 17.6 %all-to-all-start = ((bf16[128,8,128]{2,0,1:T(8,128)(2,1)}), bf16[128,8,128]{2,0,1:T(8,128)(2,1)S(1)}, u32[]{:S(2)}, u32[]{:S(2)}) async-start(bf16[128,8,128]{2,0,1:T(8,128)(2,1)} %bitcast.148), calls=%async_computation | async-start | bytes 524288 | tf_op jit(solution)/shard_map/all_to_all | solution.py:49
  20.7 10.3 %collective-permute-start = (bf16[256,128]{1,0:T(8,128)(2,1)S(1)}, bf16[256,128]{1,0:T(8,128)(2,1)S(1)}, u32[]{:S(2)}, u32[]{:S(2)}) collective-permute-start(bf16[256,128]{1,0:T(8,128)(2,1)S(1)} %bitcast.186), channel_id=1, source_target_pairs={{8,0},{16,8},{24,16},{32,24},{40,32},{48,40},{56,48},{64,56},{72,6... | collective-permute-start | bytes 196616 | tf_op jit(solution)/shard_map/ppermute | solution.py:19
  25.1 8.4 %collective-permute-start.1 = (bf16[768,128]{1,0:T(8,128)(2,1)S(1)}, bf16[768,128]{1,0:T(8,128)(2,1)S(1)}, u32[]{:S(2)}, u32[]{:S(2)}) collective-permute-start(bf16[768,128]{1,0:T(8,128)(2,1)S(1)} %bitcast.185), channel_id=1, source_target_pairs={{0,8},{8,16},{16,24},{24,32},{32,40},{40,48},{48,56},{56,64},{64,7... | collective-permute-start | bytes 589832 | tf_op jit(solution)/shard_map/ppermute | solution.py:14
  37.4 16.6 %collective-permute-start.3 = (bf16[768,128]{1,0:T(8,128)(2,1)S(1)}, bf16[768,128]{1,0:T(8,128)(2,1)S(1)}, u32[]{:S(2)}, u32[]{:S(2)}) collective-permute-start(bf16[768,128]{1,0:T(8,128)(2,1)S(1)} %slice.257), channel_id=1, source_target_pairs={{0,8},{8,16},{16,24},{24,32},{32,40},{40,48},{48,56},{56,64},{64,7... | collective-permute-start | bytes 589832 | tf_op jit(solution)/shard_map/ppermute | solution.py:14
  45.1 8.9 %collective-permute-start.2 = (bf16[256,128]{1,0:T(8,128)(2,1)S(1)}, bf16[256,128]{1,0:T(8,128)(2,1)S(1)}, u32[]{:S(2)}, u32[]{:S(2)}) collective-permute-start(bf16[256,128]{1,0:T(8,128)(2,1)S(1)} %slice.254), channel_id=1, source_target_pairs={{8,0},{16,8},{24,16},{32,24},{40,32},{48,40},{56,48},{64,56},{72,6... | collective-permute-start | bytes 196616 | tf_op jit(solution)/shard_map/ppermute | solution.py:19
  57.8 10.9 %collective-permute-start.5 = (bf16[768,128]{1,0:T(8,128)(2,1)S(1)}, bf16[768,128]{1,0:T(8,128)(2,1)S(1)}, u32[]{:S(2)}, u32[]{:S(2)}) collective-permute-start(bf16[768,128]{1,0:T(8,128)(2,1)S(1)} %slice.271), channel_id=1, source_target_pairs={{0,8},{8,16},{16,24},{24,32},{32,40},{40,48},{48,56},{56,64},{64,7... | collective-permute-start | bytes 589832 | tf_op jit(solution)/shard_map/ppermute | solution.py:14
  59.8 8.9 %collective-permute-start.4 = (bf16[256,128]{1,0:T(8,128)(2,1)S(1)}, bf16[256,128]{1,0:T(8,128)(2,1)S(1)}, u32[]{:S(2)}, u32[]{:S(2)}) collective-permute-start(bf16[256,128]{1,0:T(8,128)(2,1)S(1)} %slice.268), channel_id=1, source_target_pairs={{8,0},{16,8},{24,16},{32,24},{40,32},{48,40},{56,48},{64,56},{72,6... | collective-permute-start | bytes 196616 | tf_op jit(solution)/shard_map/ppermute | solution.py:19
  72.6 10.9 %collective-permute-start.7 = (bf16[768,128]{1,0:T(8,128)(2,1)S(1)}, bf16[768,128]{1,0:T(8,128)(2,1)S(1)}, u32[]{:S(2)}, u32[]{:S(2)}) collective-permute-start(bf16[768,128]{1,0:T(8,128)(2,1)S(1)} %slice.285), channel_id=1, source_target_pairs={{0,8},{8,16},{16,24},{24,32},{32,40},{40,48},{48,56},{56,64},{64,7... | collective-permute-start | bytes 589832 | tf_op jit(solution)/shard_map/ppermute | solution.py:14
  74.6 8.9 %collective-permute-start.6 = (bf16[256,128]{1,0:T(8,128)(2,1)S(1)}, bf16[256,128]{1,0:T(8,128)(2,1)S(1)}, u32[]{:S(2)}, u32[]{:S(2)}) collective-permute-start(bf16[256,128]{1,0:T(8,128)(2,1)S(1)} %slice.282), channel_id=1, source_target_pairs={{8,0},{16,8},{24,16},{32,24},{40,32},{48,40},{56,48},{64,56},{72,6... | collective-permute-start | bytes 196616 | tf_op jit(solution)/shard_map/ppermute | solution.py:19

commit v10 on v4

--- a/solution.py
+++ b/solution.py
@@ -27,7 +27,9 @@
         lo = shift_up(state_bf[state_bf.shape[0] - REACH_LO * block_rows:], "row")
         hi = shift_down(state_bf[: REACH_HI * block_rows], "row")
         tiles = jnp.concatenate([lo, state_bf, hi], axis=0).reshape(-1, block_rows, width)
-        picked = tiles[local_index]
+        pieces = [lax.dynamic_index_in_dim(tiles, local_index[b, j], axis=0, keepdims=False)
+                  for b in range(local_blocks) for j in range(nnz)]
+        picked = jnp.stack(pieces).reshape(local_blocks, nnz, block_rows, width)
         result = jnp.einsum("bjrc,bjcv->brv", blocks, picked, preferred_element_type=jnp.float32)
         return result.reshape(local_blocks * block_rows, width)
 

time: 90.7 us -> 192 us (2.12)
  the two profiles are of different devices: /device:TPU:399 before, /device:TPU:415 now
where the time goes in v10:
time: 192 us; the launch traced here: 190 us
  between operations  121 us (63%)
  starting transfers between devices  33.8 us (18%)
  waiting for transfers between devices  20 us (10%)
  local copies, waits for them, and re-layouts  8.1 us (4%)
  matrix products  5.21 us (3%)
    ppermute x4, waiting for transfers between devices, shift_down(): return lax.ppermute(cells, axis, [(i + 1, i) for i in range(count - 1)])  20 us
    ppermute x4, starting transfers between devices, shift_up(): return lax.ppermute(cells, axis, [(i, i + 1) for i in range(count - 1)])  17.8 us
    ppermute x4, starting transfers between devices, shift_down(): return lax.ppermute(cells, axis, [(i + 1, i) for i in range(count - 1)])  8.65 us
    all_to_all x1, starting transfers between devices, per_device(): lax.all_to_all(rotated, 'vec', split_axis=1, concat_axis=0, tiled=True)  7.33 us
    unnamed x256, local copies, waits for them, and re-layouts  4.36 us
  transfers between devices with their start and end apart: 9, of which 3 were waited for; matrix products, arithmetic and copies ran while one was open for 2% of the time, Pallas kernels for 0%

profile of v10, /device:TPU:415, one launch (start us, length us, event | category | flops | bytes accessed | tf_op | source)
XLA Modules:
  0.0 189.9 jit_solution(14414099172104230586)
XLA Ops:
  0.0 0.0 copy-start
  0.0 0.0 copy-start.1
  0.0 2.3 %fusion = bf16[16,8,8,128]{3,2,1,0:T(8,128)(2,1)S(1)} fusion(bf16[128,1024]{1,0:T(8,128)(2,1)} %param.4, bf16[1024,1024]{1,0:T(8,128)(2,1)} %param.5), kind=kOutput, calls=%fused_computation.1 | convolution fusion | flops 268566528 | bytes 2621440 | tf_op jit(solution)/shard_map/dot_general | solution.py:47
  2.3 0.8 copy.15
  3.0 7.3 %all-to-all-start = ((bf16[128,8,128]{2,0,1:T(8,128)(2,1)}), bf16[128,8,128]{2,0,1:T(8,128)(2,1)S(1)}, u32[]{:S(2)}, u32[]{:S(2)}) async-start(bf16[128,8,128]{2,0,1:T(8,128)(2,1)} %bitcast.166), calls=%async_computation | async-start | bytes 524288 | tf_op jit(solution)/shard_map/all_to_all | solution.py:48
  10.4 0.0 copy-done.1
  10.4 0.7 fusion.10
  19.8 0.7 fusion.9
  44.4 0.0 all-to-all-done
  44.5 7.0 %collective-permute-start = (bf16[768,128]{1,0:T(8,128)(2,1)S(1)}, bf16[768,128]{1,0:T(8,128)(2,1)S(1)}, u32[]{:S(2)}, u32[]{:S(2)}) collective-permute-start(bf16[768,128]{1,0:T(8,128)(2,1)S(1)} %bitcast.430), channel_id=1, source_target_pairs={{0,8},{8,16},{16,24},{24,32},{32,40},{40,48},{48,56},{56,64},{64,7... | collective-permute-start | bytes 589832 | tf_op jit(solution)/shard_map/ppermute | solution.py:14
  51.5 0.7 fusion.7
  75.8 1.9 %collective-permute-start.1 = (bf16[256,128]{1,0:T(8,128)(2,1)S(1)}, bf16[256,128]{1,0:T(8,128)(2,1)S(1)}, u32[]{:S(2)}, u32[]{:S(2)}) collective-permute-start(bf16[256,128]{1,0:T(8,128)(2,1)S(1)} %bitcast.431), channel_id=1, source_target_pairs={{8,0},{16,8},{24,16},{32,24},{40,32},{48,40},{56,48},{64,56},{72,6... | collective-permute-start | bytes 196616 | tf_op jit(solution)/shard_map/ppermute | solution.py:19
  77.8 0.7 fusion.8
  141.9 0.0 collective-permute-done.1
  141.9 0.0 collective-permute-done
  143.4 0.0 copy-done
  143.4 0.7 fusion.11
  144.1 0.1 multiply_convert_fusion
  144.3 7.0 %collective-permute-start.2 = (bf16[768,128]{1,0:T(8,128)(2,1)S(1)}, bf16[768,128]{1,0:T(8,128)(2,1)S(1)}, u32[]{:S(2)}, u32[]{:S(2)}) collective-permute-start(bf16[768,128]{1,0:T(8,128)(2,1)S(1)} %slice.226), channel_id=1, source_target_pairs={{0,8},{8,16},{16,24},{24,32},{32,40},{40,48},{48,56},{56,64},{64,7... | collective-permute-start | bytes 589832 | tf_op jit(solution)/shard_map/ppermute | solution.py:14
  151.3 1.9 %collective-permute-start.3 = (bf16[256,128]{1,0:T(8,128)(2,1)S(1)}, bf16[256,128]{1,0:T(8,128)(2,1)S(1)}, u32[]{:S(2)}, u32[]{:S(2)}) collective-permute-start(bf16[256,128]{1,0:T(8,128)(2,1)S(1)} %slice.227), channel_id=1, source_target_pairs={{8,0},{16,8},{24,16},{32,24},{40,32},{48,40},{56,48},{64,56},{72,6... | collective-permute-start | bytes 196616 | tf_op jit(solution)/shard_map/ppermute | solution.py:19
  153.2 7.0 %collective-permute-done.3 = bf16[256,128]{1,0:T(8,128)(2,1)S(1)} collective-permute-done((bf16[256,128]{1,0:T(8,128)(2,1)S(1)}, bf16[256,128]{1,0:T(8,128)(2,1)S(1)}, u32[]{:S(2)}, u32[]{:S(2)}) %collective-permute-start.3) | collective-permute-done | bytes 65568 | tf_op jit(solution)/shard_map/ppermute | solution.py:19
  160.2 0.0 collective-permute-done.2
  161.6 0.7 fusion.12
  162.4 0.1 fusion.6
  162.5 1.9 %collective-permute-start.4 = (bf16[768,128]{1,0:T(8,128)(2,1)S(1)}, bf16[768,128]{1,0:T(8,128)(2,1)S(1)}, u32[]{:S(2)}, u32[]{:S(2)}) collective-permute-start(bf16[768,128]{1,0:T(8,128)(2,1)S(1)} %slice.228), channel_id=1, source_target_pairs={{0,8},{8,16},{16,24},{24,32},{32,40},{40,48},{48,56},{56,64},{64,7... | collective-permute-start | bytes 589832 | tf_op jit(solution)/shard_map/ppermute | solution.py:14
  164.5 2.4 %collective-permute-start.5 = (bf16[256,128]{1,0:T(8,128)(2,1)S(1)}, bf16[256,128]{1,0:T(8,128)(2,1)S(1)}, u32[]{:S(2)}, u32[]{:S(2)}) collective-permute-start(bf16[256,128]{1,0:T(8,128)(2,1)S(1)} %slice.229), channel_id=1, source_target_pairs={{8,0},{16,8},{24,16},{32,24},{40,32},{48,40},{56,48},{64,56},{72,6... | collective-permute-start | bytes 196616 | tf_op jit(solution)/shard_map/ppermute | solution.py:19
  166.9 6.5 %collective-permute-done.5 = bf16[256,128]{1,0:T(8,128)(2,1)S(1)} collective-permute-done((bf16[256,128]{1,0:T(8,128)(2,1)S(1)}, bf16[256,128]{1,0:T(8,128)(2,1)S(1)}, u32[]{:S(2)}, u32[]{:S(2)}) %collective-permute-start.5) | collective-permute-done | bytes 65568 | tf_op jit(solution)/shard_map/ppermute | solution.py:19
  173.4 0.0 collective-permute-done.4
  174.8 0.7 fusion.13
  175.6 0.2 fusion.5
  175.8 1.9 %collective-permute-start.6 = (bf16[768,128]{1,0:T(8,128)(2,1)S(1)}, bf16[768,128]{1,0:T(8,128)(2,1)S(1)}, u32[]{:S(2)}, u32[]{:S(2)}) collective-permute-start(bf16[768,128]{1,0:T(8,128)(2,1)S(1)} %slice.230), channel_id=1, source_target_pairs={{0,8},{8,16},{16,24},{24,32},{32,40},{40,48},{48,56},{56,64},{64,7... | collective-permute-start | bytes 589832 | tf_op jit(solution)/shard_map/ppermute | solution.py:14
  177.8 2.4 %collective-permute-start.7 = (bf16[256,128]{1,0:T(8,128)(2,1)S(1)}, bf16[256,128]{1,0:T(8,128)(2,1)S(1)}, u32[]{:S(2)}, u32[]{:S(2)}) collective-permute-start(bf16[256,128]{1,0:T(8,128)(2,1)S(1)} %slice.231), channel_id=1, source_target_pairs={{8,0},{16,8},{24,16},{32,24},{40,32},{48,40},{56,48},{64,56},{72,6... | collective-permute-start | bytes 196616 | tf_op jit(solution)/shard_map/ppermute | solution.py:19
  180.2 6.5 %collective-permute-done.7 = bf16[256,128]{1,0:T(8,128)(2,1)S(1)} collective-permute-done((bf16[256,128]{1,0:T(8,128)(2,1)S(1)}, bf16[256,128]{1,0:T(8,128)(2,1)S(1)}, u32[]{:S(2)}, u32[]{:S(2)}) %collective-permute-start.7) | collective-permute-done | bytes 65568 | tf_op jit(solution)/shard_map/ppermute | solution.py:19
  186.7 0.0 collective-permute-done.6
  188.1 0.7 fusion.14
  188.9 1.0 fusion.3
  (269 shorter events, 4.7 us)
Async XLA Ops:
  0.0 143.4 %copy-start = (bf16[8,8,128,128]{3,2,1,0:T(8,128)(2,1)S(1)}, bf16[8,8,128,128]{3,2,1,0:T(8,128)(2,1)}, u32[]{:S(2)}) copy-start(bf16[8,8,128,128]{3,2,1,0:T(8,128)(2,1)} %param.6) | copy-start | bytes 6291460
  0.0 10.4 %copy-start.1 = (s32[8,8]{1,0:T(8,128)S(1)}, s32[8,8]{1,0:T(8,128)}, u32[]{:S(2)}) copy-start(s32[8,8]{1,0:T(8,128)} %param.7) | copy-start | bytes 772
  3.0 41.4 %all-to-all-start = ((bf16[128,8,128]{2,0,1:T(8,128)(2,1)}), bf16[128,8,128]{2,0,1:T(8,128)(2,1)S(1)}, u32[]{:S(2)}, u32[]{:S(2)}) async-start(bf16[128,8,128]{2,0,1:T(8,128)(2,1)} %bitcast.166), calls=%async_computation | async-start | bytes 524288 | tf_op jit(solution)/shard_map/all_to_all | solution.py:48
  44.5 97.5 %collective-permute-start = (bf16[768,128]{1,0:T(8,128)(2,1)S(1)}, bf16[768,128]{1,0:T(8,128)(2,1)S(1)}, u32[]{:S(2)}, u32[]{:S(2)}) collective-permute-start(bf16[768,128]{1,0:T(8,128)(2,1)S(1)} %bitcast.430), channel_id=1, source_target_pairs={{0,8},{8,16},{16,24},{24,32},{32,40},{40,48},{48,56},{56,64},{64,7... | collective-permute-start | bytes 589832 | tf_op jit(solution)/shard_map/ppermute | solution.py:14
  75.8 66.1 %collective-permute-start.1 = (bf16[256,128]{1,0:T(8,128)(2,1)S(1)}, bf16[256,128]{1,0:T(8,128)(2,1)S(1)}, u32[]{:S(2)}, u32[]{:S(2)}) collective-permute-start(bf16[256,128]{1,0:T(8,128)(2,1)S(1)} %bitcast.431), channel_id=1, source_target_pairs={{8,0},{16,8},{24,16},{32,24},{40,32},{48,40},{56,48},{64,56},{72,6... | collective-permute-start | bytes 196616 | tf_op jit(solution)/shard_map/ppermute | solution.py:19
  144.3 15.9 %collective-permute-start.2 = (bf16[768,128]{1,0:T(8,128)(2,1)S(1)}, bf16[768,128]{1,0:T(8,128)(2,1)S(1)}, u32[]{:S(2)}, u32[]{:S(2)}) collective-permute-start(bf16[768,128]{1,0:T(8,128)(2,1)S(1)} %slice.226), channel_id=1, source_target_pairs={{0,8},{8,16},{16,24},{24,32},{32,40},{40,48},{48,56},{56,64},{64,7... | collective-permute-start | bytes 589832 | tf_op jit(solution)/shard_map/ppermute | solution.py:14
  151.3 8.9 %collective-permute-start.3 = (bf16[256,128]{1,0:T(8,128)(2,1)S(1)}, bf16[256,128]{1,0:T(8,128)(2,1)S(1)}, u32[]{:S(2)}, u32[]{:S(2)}) collective-permute-start(bf16[256,128]{1,0:T(8,128)(2,1)S(1)} %slice.227), channel_id=1, source_target_pairs={{8,0},{16,8},{24,16},{32,24},{40,32},{48,40},{56,48},{64,56},{72,6... | collective-permute-start | bytes 196616 | tf_op jit(solution)/shard_map/ppermute | solution.py:19
  162.5 10.9 %collective-permute-start.4 = (bf16[768,128]{1,0:T(8,128)(2,1)S(1)}, bf16[768,128]{1,0:T(8,128)(2,1)S(1)}, u32[]{:S(2)}, u32[]{:S(2)}) collective-permute-start(bf16[768,128]{1,0:T(8,128)(2,1)S(1)} %slice.228), channel_id=1, source_target_pairs={{0,8},{8,16},{16,24},{24,32},{32,40},{40,48},{48,56},{56,64},{64,7... | collective-permute-start | bytes 589832 | tf_op jit(solution)/shard_map/ppermute | solution.py:14
  164.5 8.9 %collective-permute-start.5 = (bf16[256,128]{1,0:T(8,128)(2,1)S(1)}, bf16[256,128]{1,0:T(8,128)(2,1)S(1)}, u32[]{:S(2)}, u32[]{:S(2)}) collective-permute-start(bf16[256,128]{1,0:T(8,128)(2,1)S(1)} %slice.229), channel_id=1, source_target_pairs={{8,0},{16,8},{24,16},{32,24},{40,32},{48,40},{56,48},{64,56},{72,6... | collective-permute-start | bytes 196616 | tf_op jit(solution)/shard_map/ppermute | solution.py:19
  175.8 10.9 %collective-permute-start.6 = (bf16[768,128]{1,0:T(8,128)(2,1)S(1)}, bf16[768,128]{1,0:T(8,128)(2,1)S(1)}, u32[]{:S(2)}, u32[]{:S(2)}) collective-permute-start(bf16[768,128]{1,0:T(8,128)(2,1)S(1)} %slice.230), channel_id=1, source_target_pairs={{0,8},{8,16},{16,24},{24,32},{32,40},{40,48},{48,56},{56,64},{64,7... | collective-permute-start | bytes 589832 | tf_op jit(solution)/shard_map/ppermute | solution.py:14
  177.8 8.9 %collective-permute-start.7 = (bf16[256,128]{1,0:T(8,128)(2,1)S(1)}, bf16[256,128]{1,0:T(8,128)(2,1)S(1)}, u32[]{:S(2)}, u32[]{:S(2)}) collective-permute-start(bf16[256,128]{1,0:T(8,128)(2,1)S(1)} %slice.231), channel_id=1, source_target_pairs={{8,0},{16,8},{24,16},{32,24},{40,32},{48,40},{56,48},{64,56},{72,6... | collective-permute-start | bytes 196616 | tf_op jit(solution)/shard_map/ppermute | solution.py:19

commit v11 on v9

--- a/solution.py
+++ b/solution.py
@@ -27,10 +27,21 @@
         lo = shift_up(state_bf[state_bf.shape[0] - REACH_LO * block_rows:], "row")
         hi = shift_down(state_bf[: REACH_HI * block_rows], "row")
         tiles = jnp.concatenate([lo, state_bf, hi], axis=0).reshape(-1, block_rows, width)
-        picked = jnp.broadcast_to(tiles[None, :local_blocks].transpose(1, 0, 2, 3), (local_blocks, nnz, block_rows, width))
-        for w in range(1, REACH_LO + REACH_HI + 1):
-            window = tiles[w:w + local_blocks][:, None]
-            picked = jnp.where((offset == w)[:, :, None, None], window, picked)
+        windows = [tiles[w:w + local_blocks][:, None] for w in range(REACH_LO + REACH_HI + 1)]
+
+        def pick(first, count, candidates):
+            part = offset[:, first:first + count, None, None]
+            got = jnp.broadcast_to(windows[candidates[0]], (local_blocks, count, block_rows, width))
+            for w in candidates[1:]:
+                got = jnp.where(part == w, windows[w], got)
+            return got
+
+        picked = jnp.concatenate([
+            pick(0, 1, [REACH_LO]),
+            pick(1, 1, list(range(REACH_LO + 1))),
+            pick(2, 1, list(range(REACH_LO, REACH_LO + REACH_HI + 1))),
+            pick(3, nnz - 3, list(range(REACH_LO + REACH_HI + 1))),
+        ], axis=1)
         result = jnp.einsum("bjrc,bjcv->brv", blocks, picked, preferred_element_type=jnp.float32)
         return result.reshape(local_blocks * block_rows, width)
 

time: 88.6 us -> 82.4 us (0.930)
  matrix products: 15.8 us -> 5.95 us
  starting transfers between devices: 35.8 us -> 30.5 us
  other arithmetic: 2.64 us -> 7.91 us
  waiting for transfers between devices: 32.9 us -> 36.5 us
    dot_general x4, matrix products: 13.5 us -> 3.67 us  [apply_operator(): jnp.einsum('bjrc,bjcv->brv', blocks, picked, preferred_element_type=jnp.f...]
    ppermute x4, waiting for transfers between devices: 20 us -> 26.2 us  [shift_down(): return lax.ppermute(cells, axis, [(i + 1, i) for i in range(count - 1)])]
    select_n x0 -> x11, other arithmetic: none -> 4.91 us  [pick(): got = jnp.where(part == w, windows[w], got)]
    ppermute x4, starting transfers between devices: 17.4 us -> 14 us  [shift_up(): return lax.ppermute(cells, axis, [(i, i + 1) for i in range(count - 1)])]
    ppermute x4, waiting for transfers between devices: 2.56 us -> 0.01 us  [shift_up(): return lax.ppermute(cells, axis, [(i, i + 1) for i in range(count - 1)])]
    ppermute x4, starting transfers between devices: 11.1 us -> 9.14 us  [shift_down(): return lax.ppermute(cells, axis, [(i + 1, i) for i in range(count - 1)])]
where the time goes in v11:
time: 82.4 us; the launch traced here: 82 us
  waiting for transfers between devices  36.5 us (44%)
  starting transfers between devices  30.5 us (37%)
  other arithmetic  7.91 us (10%)
  matrix products  5.95 us (7%)
  local copies, waits for them, and re-layouts  0.84 us (1%)
    ppermute x4, waiting for transfers between devices, shift_down(): return lax.ppermute(cells, axis, [(i + 1, i) for i in range(count - 1)])  26.2 us
    ppermute x4, starting transfers between devices, shift_up(): return lax.ppermute(cells, axis, [(i, i + 1) for i in range(count - 1)])  14 us
    all_to_all x1, waiting for transfers between devices, per_device(): lax.all_to_all(rotated, 'vec', split_axis=1, concat_axis=0, tiled=True)  10.3 us
    ppermute x4, starting transfers between devices, shift_down(): return lax.ppermute(cells, axis, [(i + 1, i) for i in range(count - 1)])  9.14 us
    all_to_all x1, starting transfers between devices, per_device(): lax.all_to_all(rotated, 'vec', split_axis=1, concat_axis=0, tiled=True)  7.27 us
    select_n x11, other arithmetic, pick(): got = jnp.where(part == w, windows[w], got)  4.91 us
    dot_general x4, matrix products, apply_operator(): jnp.einsum('bjrc,bjcv->brv', blocks, picked, preferred_element_type=jnp.f...  3.67 us
    dot_general x1, matrix products, per_device(): jnp.dot(vectors, rotation, preferred_element_type=jnp.float32)  2.28 us
  transfers between devices with their start and end apart: 9, of which 5 were waited for; matrix products, arithmetic and copies ran while one was open for 0% of the time, Pallas kernels for 0%

profile of v11, /device:TPU:399, one launch (start us, length us, event | category | flops | bytes accessed | tf_op | source)
XLA Modules:
  0.0 82.0 jit_solution(13981838797630592618)
XLA Ops:
  0.0 0.0 copy-start
  0.0 0.0 copy-start.1
  0.0 2.3 %fusion.32 = bf16[16,8,8,128]{3,2,1,0:T(8,128)(2,1)S(1)} fusion(bf16[128,1024]{1,0:T(8,128)(2,1)} %param.4, bf16[1024,1024]{1,0:T(8,128)(2,1)} %param.5), kind=kOutput, calls=%fused_computation.37 | convolution fusion | flops 268566528 | bytes 2621440 | tf_op jit(solution)/shard_map/dot_general | solution.py:59
  2.3 0.8 copy.23
  3.0 7.3 %all-to-all-start = ((bf16[128,8,128]{2,0,1:T(8,128)(2,1)}), bf16[128,8,128]{2,0,1:T(8,128)(2,1)S(1)}, u32[]{:S(2)}, u32[]{:S(2)}) async-start(bf16[128,8,128]{2,0,1:T(8,128)(2,1)} %bitcast.202), calls=%async_computation | async-start | bytes 524288 | tf_op jit(solution)/shard_map/all_to_all | solution.py:60
  10.3 0.0 copy-done.1
  10.3 10.3 %all-to-all-done = bf16[128,8,128]{2,0,1:T(8,128)(2,1)S(1)} async-done(((bf16[128,8,128]{2,0,1:T(8,128)(2,1)}), bf16[128,8,128]{2,0,1:T(8,128)(2,1)S(1)}, u32[]{:S(2)}, u32[]{:S(2)}) %all-to-all-start) | async-done | bytes 262176 | tf_op jit(solution)/shard_map/all_to_all | solution.py:60
  20.7 8.3 %collective-permute-start = (bf16[768,128]{1,0:T(8,128)(2,1)S(1)}, bf16[768,128]{1,0:T(8,128)(2,1)S(1)}, u32[]{:S(2)}, u32[]{:S(2)}) collective-permute-start(bf16[768,128]{1,0:T(8,128)(2,1)S(1)} %bitcast.275), channel_id=1, source_target_pairs={{0,8},{8,16},{16,24},{24,32},{32,40},{40,48},{48,56},{56,64},{64,7... | collective-permute-start | bytes 589832 | tf_op jit(solution)/shard_map/ppermute | solution.py:14
  29.0 0.1 slice_compare_fusion.7
  29.1 1.9 %collective-permute-start.1 = (bf16[256,128]{1,0:T(8,128)(2,1)S(1)}, bf16[256,128]{1,0:T(8,128)(2,1)S(1)}, u32[]{:S(2)}, u32[]{:S(2)}) collective-permute-start(bf16[256,128]{1,0:T(8,128)(2,1)S(1)} %bitcast.276), channel_id=1, source_target_pairs={{8,0},{16,8},{24,16},{32,24},{40,32},{48,40},{56,48},{64,56},{72,6... | collective-permute-start | bytes 196616 | tf_op jit(solution)/shard_map/ppermute | solution.py:19
  31.0 0.3 compare_reduce_fusion.7
  31.3 6.7 %collective-permute-done.1 = bf16[256,128]{1,0:T(8,128)(2,1)S(1)} collective-permute-done((bf16[256,128]{1,0:T(8,128)(2,1)S(1)}, bf16[256,128]{1,0:T(8,128)(2,1)S(1)}, u32[]{:S(2)}, u32[]{:S(2)}) %collective-permute-start.1) | collective-permute-done | bytes 65568 | tf_op jit(solution)/shard_map/ppermute | solution.py:19
  38.0 0.0 collective-permute-done
  38.0 0.3 fusion.44
  38.3 0.8 select_select_fusion.3
  39.0 0.2 select_bitcast_fusion.7
  39.3 0.0 copy-done
  39.3 0.9 %fusion = f32[8,128,128,1]{1,2,3,0:T(8,128)S(1)} fusion(bf16[8,8,128,128]{3,2,1,0:T(8,128)(2,1)S(1)} %copy-done, bf16[8,5,128,128]{3,2,1,0:T(8,128)(2,1)S(1)} %select_select_fusion.3, bf16[8,1,128,128]{3,2,1,0:T(8,128)(2,1)S(1)} %get-tuple-element.70, bf16[8,1,128,128]{3,2,1,0:T(8,128)(2,1)S(1)} %get-tuple-element.69, bf16[8,1,128,128]{3,2,1,0:T(8,128)(2,1)S(1)} %bitcast.207), kind=kOutput, calls=%fused_computation | convolution fusion | flops 276824064 | bytes 4718592 | tf_op jit(solution)/shard_map/bjrc,bjcv->brv/dot_general | solution.py:45
  40.2 0.1 multiply_convert_fusion
  40.4 1.9 %collective-permute-start.2 = (bf16[768,128]{1,0:T(8,128)(2,1)S(1)}, bf16[768,128]{1,0:T(8,128)(2,1)S(1)}, u32[]{:S(2)}, u32[]{:S(2)}) collective-permute-start(bf16[768,128]{1,0:T(8,128)(2,1)S(1)} %slice.275), channel_id=1, source_target_pairs={{0,8},{8,16},{16,24},{24,32},{32,40},{40,48},{48,56},{56,64},{64,7... | collective-permute-start | bytes 589832 | tf_op jit(solution)/shard_map/ppermute | solution.py:14
  42.3 2.4 %collective-permute-start.3 = (bf16[256,128]{1,0:T(8,128)(2,1)S(1)}, bf16[256,128]{1,0:T(8,128)(2,1)S(1)}, u32[]{:S(2)}, u32[]{:S(2)}) collective-permute-start(bf16[256,128]{1,0:T(8,128)(2,1)S(1)} %slice.286), channel_id=1, source_target_pairs={{8,0},{16,8},{24,16},{32,24},{40,32},{48,40},{56,48},{64,56},{72,6... | collective-permute-start | bytes 196616 | tf_op jit(solution)/shard_map/ppermute | solution.py:19
  44.7 6.5 %collective-permute-done.3 = bf16[256,128]{1,0:T(8,128)(2,1)S(1)} collective-permute-done((bf16[256,128]{1,0:T(8,128)(2,1)S(1)}, bf16[256,128]{1,0:T(8,128)(2,1)S(1)}, u32[]{:S(2)}, u32[]{:S(2)}) %collective-permute-start.3) | collective-permute-done | bytes 65568 | tf_op jit(solution)/shard_map/ppermute | solution.py:19
  51.2 0.0 collective-permute-done.2
  51.2 0.3 fusion.43
  51.5 0.2 select_bitcast_fusion.5
  51.8 0.8 select_select_fusion.2
  52.5 0.1 select_bitcast_fusion.4
  52.7 0.9 %fusion.8 = f32[8,128,128,1]{1,2,3,0:T(8,128)S(1)} fusion(bf16[8,8,128,128]{3,2,1,0:T(8,128)(2,1)S(1)} %copy-done, bf16[8,5,128,128]{3,2,1,0:T(8,128)(2,1)S(1)} %select_select_fusion.2, bf16[8,1,128,128]{3,2,1,0:T(8,128)(2,1)S(1)} %select_bitcast_fusion.4, bf16[8,1,128,128]{3,2,1,0:T(8,128)(2,1)S(1)} %get-tuple-element.17, ...), kind=kOutput, calls=%fused_computation.8 | convolution fusion | flops 276824064 | bytes 4718592 | tf_op jit(solution)/shard_map/bjrc,bjcv->brv/dot_general | solution.py:45
  53.6 0.1 fusion.70
  53.7 1.9 %collective-permute-start.4 = (bf16[768,128]{1,0:T(8,128)(2,1)S(1)}, bf16[768,128]{1,0:T(8,128)(2,1)S(1)}, u32[]{:S(2)}, u32[]{:S(2)}) collective-permute-start(bf16[768,128]{1,0:T(8,128)(2,1)S(1)} %slice.289), channel_id=1, source_target_pairs={{0,8},{8,16},{16,24},{24,32},{32,40},{40,48},{48,56},{56,64},{64,7... | collective-permute-start | bytes 589832 | tf_op jit(solution)/shard_map/ppermute | solution.py:14
  55.7 2.4 %collective-permute-start.5 = (bf16[256,128]{1,0:T(8,128)(2,1)S(1)}, bf16[256,128]{1,0:T(8,128)(2,1)S(1)}, u32[]{:S(2)}, u32[]{:S(2)}) collective-permute-start(bf16[256,128]{1,0:T(8,128)(2,1)S(1)} %slice.300), channel_id=1, source_target_pairs={{8,0},{16,8},{24,16},{32,24},{40,32},{48,40},{56,48},{64,56},{72,6... | collective-permute-start | bytes 196616 | tf_op jit(solution)/shard_map/ppermute | solution.py:19
  58.1 6.5 %collective-permute-done.5 = bf16[256,128]{1,0:T(8,128)(2,1)S(1)} collective-permute-done((bf16[256,128]{1,0:T(8,128)(2,1)S(1)}, bf16[256,128]{1,0:T(8,128)(2,1)S(1)}, u32[]{:S(2)}, u32[]{:S(2)}) %collective-permute-start.5) | collective-permute-done | bytes 65568 | tf_op jit(solution)/shard_map/ppermute | solution.py:19
  64.6 0.0 collective-permute-done.4
  64.6 0.3 fusion.42
  64.9 0.5 select_bitcast_fusion.3
  65.4 0.8 select_select_fusion.1
  66.2 0.1 select_bitcast_fusion.2
  66.3 0.9 %fusion.16 = f32[8,128,128,1]{1,2,3,0:T(8,128)S(1)} fusion(bf16[8,8,128,128]{3,2,1,0:T(8,128)(2,1)S(1)} %copy-done, bf16[8,5,128,128]{3,2,1,0:T(8,128)(2,1)S(1)} %select_select_fusion.1, bf16[8,1,128,128]{3,2,1,0:T(8,128)(2,1)S(1)} %select_bitcast_fusion.2, bf16[8,1,128,128]{3,2,1,0:T(8,128)(2,1)S(1)} %get-tuple-element.15, ...), kind=kOutput, calls=%fused_computation.16 | convolution fusion | flops 276824064 | bytes 4718592 | tf_op jit(solution)/shard_map/bjrc,bjcv->brv/dot_general | solution.py:45
  67.2 0.2 fusion.69
  67.5 1.9 %collective-permute-start.6 = (bf16[768,128]{1,0:T(8,128)(2,1)S(1)}, bf16[768,128]{1,0:T(8,128)(2,1)S(1)}, u32[]{:S(2)}, u32[]{:S(2)}) collective-permute-start(bf16[768,128]{1,0:T(8,128)(2,1)S(1)} %slice.303), channel_id=1, source_target_pairs={{0,8},{8,16},{16,24},{24,32},{32,40},{40,48},{48,56},{56,64},{64,7... | collective-permute-start | bytes 589832 | tf_op jit(solution)/shard_map/ppermute | solution.py:14
  69.4 2.4 %collective-permute-start.7 = (bf16[256,128]{1,0:T(8,128)(2,1)S(1)}, bf16[256,128]{1,0:T(8,128)(2,1)S(1)}, u32[]{:S(2)}, u32[]{:S(2)}) collective-permute-start(bf16[256,128]{1,0:T(8,128)(2,1)S(1)} %slice.314), channel_id=1, source_target_pairs={{8,0},{16,8},{24,16},{32,24},{40,32},{48,40},{56,48},{64,56},{72,6... | collective-permute-start | bytes 196616 | tf_op jit(solution)/shard_map/ppermute | solution.py:19
  71.8 6.5 %collective-permute-done.7 = bf16[256,128]{1,0:T(8,128)(2,1)S(1)} collective-permute-done((bf16[256,128]{1,0:T(8,128)(2,1)S(1)}, bf16[256,128]{1,0:T(8,128)(2,1)S(1)}, u32[]{:S(2)}, u32[]{:S(2)}) %collective-permute-start.7) | collective-permute-done | bytes 65568 | tf_op jit(solution)/shard_map/ppermute | solution.py:19
  78.3 0.0 collective-permute-done.6
  78.3 0.3 fusion.41
  78.6 0.5 select_bitcast_fusion.1
  79.2 0.8 select_select_fusion
  80.0 0.1 select_bitcast_fusion
  80.1 0.9 %fusion.24 = f32[8,128,128,1]{1,2,3,0:T(8,128)S(1)} fusion(bf16[8,8,128,128]{3,2,1,0:T(8,128)(2,1)S(1)} %copy-done, bf16[8,5,128,128]{3,2,1,0:T(8,128)(2,1)S(1)} %select_select_fusion, bf16[8,1,128,128]{3,2,1,0:T(8,128)(2,1)S(1)} %select_bitcast_fusion, bf16[8,1,128,128]{3,2,1,0:T(8,128)(2,1)S(1)} %get-tuple-element.13, ...), kind=kOutput, calls=%fused_computation.24 | convolution fusion | flops 276824064 | bytes 4718592 | tf_op jit(solution)/shard_map/bjrc,bjcv->brv/dot_general | solution.py:45
  81.0 1.0 %fusion.36 = bf16[1024,128]{1,0:T(8,128)(2,1)} fusion(f32[8,128,128,1]{1,2,3,0:T(8,128)S(1)} %fusion.24, bf16[128,8,128]{2,0,1:T(8,128)(2,1)S(1)} %all-to-all-done, f32[8,128,128,1]{1,2,3,0:T(8,128)S(1)} %fusion, f32[8,128,128,1]{1,2,3,0:T(8,128)S(1)} %fusion.16, f32[8,128,128,1]{1,2,3,0:T(8,128)S(1)} %fusion.8), kind=kLoop, calls=%fused_computation.86 | loop fusion | flops 1835008 | bytes 2621440 | tf_op jit(solution)/shard_map/convert_element_type | solution.py:55
  (9 shorter events, 0.1 us)
Async XLA Ops:
  0.0 39.3 %copy-start = (bf16[8,8,128,128]{3,2,1,0:T(8,128)(2,1)S(1)}, bf16[8,8,128,128]{3,2,1,0:T(8,128)(2,1)}, u32[]{:S(2)}) copy-start(bf16[8,8,128,128]{3,2,1,0:T(8,128)(2,1)} %param.6) | copy-start | bytes 6291460
  0.0 10.3 %copy-start.1 = (s32[8,8]{1,0:T(8,128)S(1)}, s32[8,8]{1,0:T(8,128)}, u32[]{:S(2)}) copy-start(s32[8,8]{1,0:T(8,128)} %param.7) | copy-start | bytes 772
  3.0 17.6 %all-to-all-start = ((bf16[128,8,128]{2,0,1:T(8,128)(2,1)}), bf16[128,8,128]{2,0,1:T(8,128)(2,1)S(1)}, u32[]{:S(2)}, u32[]{:S(2)}) async-start(bf16[128,8,128]{2,0,1:T(8,128)(2,1)} %bitcast.202), calls=%async_computation | async-start | bytes 524288 | tf_op jit(solution)/shard_map/all_to_all | solution.py:60
  20.7 17.3 %collective-permute-start = (bf16[768,128]{1,0:T(8,128)(2,1)S(1)}, bf16[768,128]{1,0:T(8,128)(2,1)S(1)}, u32[]{:S(2)}, u32[]{:S(2)}) collective-permute-start(bf16[768,128]{1,0:T(8,128)(2,1)S(1)} %bitcast.275), channel_id=1, source_target_pairs={{0,8},{8,16},{16,24},{24,32},{32,40},{40,48},{48,56},{56,64},{64,7... | collective-permute-start | bytes 589832 | tf_op jit(solution)/shard_map/ppermute | solution.py:14
  29.1 8.9 %collective-permute-start.1 = (bf16[256,128]{1,0:T(8,128)(2,1)S(1)}, bf16[256,128]{1,0:T(8,128)(2,1)S(1)}, u32[]{:S(2)}, u32[]{:S(2)}) collective-permute-start(bf16[256,128]{1,0:T(8,128)(2,1)S(1)} %bitcast.276), channel_id=1, source_target_pairs={{8,0},{16,8},{24,16},{32,24},{40,32},{48,40},{56,48},{64,56},{72,6... | collective-permute-start | bytes 196616 | tf_op jit(solution)/shard_map/ppermute | solution.py:19
  40.4 10.9 %collective-permute-start.2 = (bf16[768,128]{1,0:T(8,128)(2,1)S(1)}, bf16[768,128]{1,0:T(8,128)(2,1)S(1)}, u32[]{:S(2)}, u32[]{:S(2)}) collective-permute-start(bf16[768,128]{1,0:T(8,128)(2,1)S(1)} %slice.275), channel_id=1, source_target_pairs={{0,8},{8,16},{16,24},{24,32},{32,40},{40,48},{48,56},{56,64},{64,7... | collective-permute-start | bytes 589832 | tf_op jit(solution)/shard_map/ppermute | solution.py:14
  42.3 8.9 %collective-permute-start.3 = (bf16[256,128]{1,0:T(8,128)(2,1)S(1)}, bf16[256,128]{1,0:T(8,128)(2,1)S(1)}, u32[]{:S(2)}, u32[]{:S(2)}) collective-permute-start(bf16[256,128]{1,0:T(8,128)(2,1)S(1)} %slice.286), channel_id=1, source_target_pairs={{8,0},{16,8},{24,16},{32,24},{40,32},{48,40},{56,48},{64,56},{72,6... | collective-permute-start | bytes 196616 | tf_op jit(solution)/shard_map/ppermute | solution.py:19
  53.7 10.9 %collective-permute-start.4 = (bf16[768,128]{1,0:T(8,128)(2,1)S(1)}, bf16[768,128]{1,0:T(8,128)(2,1)S(1)}, u32[]{:S(2)}, u32[]{:S(2)}) collective-permute-start(bf16[768,128]{1,0:T(8,128)(2,1)S(1)} %slice.289), channel_id=1, source_target_pairs={{0,8},{8,16},{16,24},{24,32},{32,40},{40,48},{48,56},{56,64},{64,7... | collective-permute-start | bytes 589832 | tf_op jit(solution)/shard_map/ppermute | solution.py:14
  55.7 8.9 %collective-permute-start.5 = (bf16[256,128]{1,0:T(8,128)(2,1)S(1)}, bf16[256,128]{1,0:T(8,128)(2,1)S(1)}, u32[]{:S(2)}, u32[]{:S(2)}) collective-permute-start(bf16[256,128]{1,0:T(8,128)(2,1)S(1)} %slice.300), channel_id=1, source_target_pairs={{8,0},{16,8},{24,16},{32,24},{40,32},{48,40},{56,48},{64,56},{72,6... | collective-permute-start | bytes 196616 | tf_op jit(solution)/shard_map/ppermute | solution.py:19
  67.5 10.9 %collective-permute-start.6 = (bf16[768,128]{1,0:T(8,128)(2,1)S(1)}, bf16[768,128]{1,0:T(8,128)(2,1)S(1)}, u32[]{:S(2)}, u32[]{:S(2)}) collective-permute-start(bf16[768,128]{1,0:T(8,128)(2,1)S(1)} %slice.303), channel_id=1, source_target_pairs={{0,8},{8,16},{16,24},{24,32},{32,40},{40,48},{48,56},{56,64},{64,7... | collective-permute-start | bytes 589832 | tf_op jit(solution)/shard_map/ppermute | solution.py:14
  69.4 8.9 %collective-permute-start.7 = (bf16[256,128]{1,0:T(8,128)(2,1)S(1)}, bf16[256,128]{1,0:T(8,128)(2,1)S(1)}, u32[]{:S(2)}, u32[]{:S(2)}) collective-permute-start(bf16[256,128]{1,0:T(8,128)(2,1)S(1)} %slice.314), channel_id=1, source_target_pairs={{8,0},{16,8},{24,16},{32,24},{40,32},{48,40},{56,48},{64,56},{72,6... | collective-permute-start | bytes 196616 | tf_op jit(solution)/shard_map/ppermute | solution.py:19

commit v12 on v11

--- a/solution.py
+++ b/solution.py
@@ -19,13 +19,31 @@
     return lax.ppermute(cells, axis, [(i + 1, i) for i in range(count - 1)])
 
 
+def swap_halos(state_bf, block_rows):
+    count = lax.axis_size("row")
+    r = lax.axis_index("row")
+    tail = state_bf[state_bf.shape[0] - REACH_LO * block_rows:]
+    head = state_bf[: REACH_LO * block_rows]
+    even = r % 2 == 0
+    pairs_in = []
+    pairs_across = []
+    for k in range(0, count - 1, 2):
+        pairs_in += [(k, k + 1), (k + 1, k)]
+    for k in range(1, count - 1, 2):
+        pairs_across += [(k, k + 1), (k + 1, k)]
+    got_in = lax.ppermute(jnp.where(even, tail, head), "row", pairs_in)
+    got_across = lax.ppermute(jnp.where(even, head, tail), "row", pairs_across)
+    lo = jnp.where(even, got_across, got_in)
+    hi = jnp.where(even, got_in, got_across)[: REACH_HI * block_rows]
+    return lo, hi
+
+
 def filter_chunk(panel, blocks, offset):
     local_blocks, nnz, block_rows, _ = blocks.shape
     width = panel.shape[1]
 
     def apply_operator(state_bf):
-        lo = shift_up(state_bf[state_bf.shape[0] - REACH_LO * block_rows:], "row")
-        hi = shift_down(state_bf[: REACH_HI * block_rows], "row")
+        lo, hi = swap_halos(state_bf, block_rows)
         tiles = jnp.concatenate([lo, state_bf, hi], axis=0).reshape(-1, block_rows, width)
         windows = [tiles[w:w + local_blocks][:, None] for w in range(REACH_LO + REACH_HI + 1)]
 

time: 82.4 us -> 81.6 us (level)
  the two profiles are of different devices: /device:TPU:399 before, /device:TPU:512 now
where the time goes in v12:
time: 81.6 us; the launch traced here: 81.2 us
  waiting for transfers between devices  41.1 us (50%)
  starting transfers between devices  24.9 us (31%)
  other arithmetic  8.18 us (10%)
  matrix products  5.95 us (7%)
    ppermute x4, waiting for transfers between devices, swap_halos(): got_across = lax.ppermute(jnp.where(even, head, tail), 'row', pairs_across)  29.5 us
    all_to_all x1, waiting for transfers between devices, per_device(): lax.all_to_all(rotated, 'vec', split_axis=1, concat_axis=0, tiled=True)  11.6 us
    ppermute x4, starting transfers between devices, swap_halos(): got_in = lax.ppermute(jnp.where(even, tail, head), 'row', pairs_in)  9.27 us
    ppermute x4, starting transfers between devices, swap_halos(): got_across = lax.ppermute(jnp.where(even, head, tail), 'row', pairs_across)  8.04 us
    all_to_all x1, starting transfers between devices, per_device(): lax.all_to_all(rotated, 'vec', split_axis=1, concat_axis=0, tiled=True)  7.56 us
    select_n x11, other arithmetic, pick(): got = jnp.where(part == w, windows[w], got)  4.91 us
    dot_general x4, matrix products, apply_operator(): jnp.einsum('bjrc,bjcv->brv', blocks, picked, preferred_element_type=jnp.f...  3.67 us
    dot_general x1, matrix products, per_device(): jnp.dot(vectors, rotation, preferred_element_type=jnp.float32)  2.28 us
  transfers between devices with their start and end apart: 9, of which 5 were waited for; matrix products, arithmetic and copies ran while one was open for 0% of the time, Pallas kernels for 0%

profile of v12, /device:TPU:512, one launch (start us, length us, event | category | flops | bytes accessed | tf_op | source)
XLA Modules:
  0.0 81.2 jit_solution(16669908502896987179)
XLA Ops:
  0.0 0.0 copy-start
  0.0 0.0 copy-start.1
  0.0 2.3 %fusion.32 = bf16[16,8,8,128]{3,2,1,0:T(8,128)(2,1)S(1)} fusion(bf16[128,1024]{1,0:T(8,128)(2,1)} %param.4, bf16[1024,1024]{1,0:T(8,128)(2,1)} %param.5), kind=kOutput, calls=%fused_computation.37 | convolution fusion | flops 268566528 | bytes 2621440 | tf_op jit(solution)/shard_map/dot_general | solution.py:77
  2.3 0.8 copy.23
  3.0 7.6 %all-to-all-start = ((bf16[128,8,128]{2,0,1:T(8,128)(2,1)}), bf16[128,8,128]{2,0,1:T(8,128)(2,1)S(1)}, u32[]{:S(2)}, u32[]{:S(2)}) async-start(bf16[128,8,128]{2,0,1:T(8,128)(2,1)} %bitcast.202), calls=%async_computation | async-start | bytes 524288 | tf_op jit(solution)/shard_map/all_to_all | solution.py:78
  10.6 0.0 copy-done.1
  10.6 0.3 compare_reduce_fusion.7
  10.9 11.6 %all-to-all-done = bf16[128,8,128]{2,0,1:T(8,128)(2,1)S(1)} async-done(((bf16[128,8,128]{2,0,1:T(8,128)(2,1)}), bf16[128,8,128]{2,0,1:T(8,128)(2,1)S(1)}, u32[]{:S(2)}, u32[]{:S(2)}) %all-to-all-start) | async-done | bytes 262176 | tf_op jit(solution)/shard_map/all_to_all | solution.py:78
  22.5 1.9 %collective-permute-start = (bf16[768,128]{1,0:T(8,128)(2,1)S(1)}, bf16[768,128]{1,0:T(8,128)(2,1)S(1)}, u32[]{:S(2)}, u32[]{:S(2)}) collective-permute-start(bf16[768,128]{1,0:T(8,128)(2,1)S(1)} %bitcast.275), channel_id=1, source_target_pairs={{8,16},{16,8},{24,32},{32,24},{40,48},{48,40},{56,64},{64,56},{72,... | collective-permute-start | bytes 589832 | tf_op jit(solution)/shard_map/ppermute | solution.py:35
  24.4 3.5 %collective-permute-start.1 = (bf16[768,128]{1,0:T(8,128)(2,1)S(1)}, bf16[768,128]{1,0:T(8,128)(2,1)S(1)}, u32[]{:S(2)}, u32[]{:S(2)}) collective-permute-start(bf16[768,128]{1,0:T(8,128)(2,1)S(1)} %bitcast.274), channel_id=1, source_target_pairs={{0,8},{8,0},{16,24},{24,16},{32,40},{40,32},{48,56},{56,48},{64,72... | collective-permute-start | bytes 589832 | tf_op jit(solution)/shard_map/ppermute | solution.py:34
  27.9 0.1 slice_compare_fusion.7
  28.0 4.8 %collective-permute-done = bf16[768,128]{1,0:T(8,128)(2,1)S(1)} collective-permute-done((bf16[768,128]{1,0:T(8,128)(2,1)S(1)}, bf16[768,128]{1,0:T(8,128)(2,1)S(1)}, u32[]{:S(2)}, u32[]{:S(2)}) %collective-permute-start) | collective-permute-done | bytes 196640 | tf_op jit(solution)/shard_map/ppermute | solution.py:35
  32.8 0.0 collective-permute-done.1
  32.9 0.3 fusion.44
  33.2 0.8 select_select_fusion.3
  33.9 0.2 select_bitcast_fusion.7
  34.2 0.0 copy-done
  34.2 0.9 %fusion = f32[8,128,128,1]{1,2,3,0:T(8,128)S(1)} fusion(bf16[8,8,128,128]{3,2,1,0:T(8,128)(2,1)S(1)} %copy-done, bf16[8,5,128,128]{3,2,1,0:T(8,128)(2,1)S(1)} %select_select_fusion.3, bf16[8,1,128,128]{3,2,1,0:T(8,128)(2,1)S(1)} %get-tuple-element.76, bf16[8,1,128,128]{3,2,1,0:T(8,128)(2,1)S(1)} %get-tuple-element.75, bf16[8,1,128,128]{3,2,1,0:T(8,128)(2,1)S(1)} %bitcast.206), kind=kOutput, calls=%fused_computation | convolution fusion | flops 276824064 | bytes 4718592 | tf_op jit(solution)/shard_map/bjrc,bjcv->brv/dot_general | solution.py:63
  35.1 0.1 multiply_convert_fusion
  35.3 1.9 %collective-permute-start.3 = (bf16[768,128]{1,0:T(8,128)(2,1)S(1)}, bf16[768,128]{1,0:T(8,128)(2,1)S(1)}, u32[]{:S(2)}, u32[]{:S(2)}) collective-permute-start(bf16[768,128]{1,0:T(8,128)(2,1)S(1)} %get-tuple-element.73), channel_id=1, source_target_pairs={{0,8},{8,0},{16,24},{24,16},{32,40},{40,32},{48,56},{56,48},{64,72... | collective-permute-start | bytes 589832 | tf_op jit(solution)/shard_map/ppermute | solution.py:34
  37.2 2.0 %collective-permute-start.2 = (bf16[768,128]{1,0:T(8,128)(2,1)S(1)}, bf16[768,128]{1,0:T(8,128)(2,1)S(1)}, u32[]{:S(2)}, u32[]{:S(2)}) collective-permute-start(bf16[768,128]{1,0:T(8,128)(2,1)S(1)} %get-tuple-element.74), channel_id=1, source_target_pairs={{8,16},{16,8},{24,32},{32,24},{40,48},{48,40},{56,64},{64,56},{72,... | collective-permute-start | bytes 589832 | tf_op jit(solution)/shard_map/ppermute | solution.py:35
  39.2 0.0 collective-permute-done.3
  39.3 8.3 %collective-permute-done.2 = bf16[768,128]{1,0:T(8,128)(2,1)S(1)} collective-permute-done((bf16[768,128]{1,0:T(8,128)(2,1)S(1)}, bf16[768,128]{1,0:T(8,128)(2,1)S(1)}, u32[]{:S(2)}, u32[]{:S(2)}) %collective-permute-start.2) | collective-permute-done | bytes 196640 | tf_op jit(solution)/shard_map/ppermute | solution.py:35
  47.5 0.3 fusion.43
  47.9 0.2 select_bitcast_fusion.5
  48.1 0.8 select_select_fusion.2
  48.9 0.1 select_bitcast_fusion.4
  49.0 0.9 %fusion.8 = f32[8,128,128,1]{1,2,3,0:T(8,128)S(1)} fusion(bf16[8,8,128,128]{3,2,1,0:T(8,128)(2,1)S(1)} %copy-done, bf16[8,5,128,128]{3,2,1,0:T(8,128)(2,1)S(1)} %select_select_fusion.2, bf16[8,1,128,128]{3,2,1,0:T(8,128)(2,1)S(1)} %select_bitcast_fusion.4, bf16[8,1,128,128]{3,2,1,0:T(8,128)(2,1)S(1)} %get-tuple-element.17, ...), kind=kOutput, calls=%fused_computation.8 | convolution fusion | flops 276824064 | bytes 4718592 | tf_op jit(solution)/shard_map/bjrc,bjcv->brv/dot_general | solution.py:63
  49.9 0.1 fusion.70
  50.1 1.9 %collective-permute-start.5 = (bf16[768,128]{1,0:T(8,128)(2,1)S(1)}, bf16[768,128]{1,0:T(8,128)(2,1)S(1)}, u32[]{:S(2)}, u32[]{:S(2)}) collective-permute-start(bf16[768,128]{1,0:T(8,128)(2,1)S(1)} %get-tuple-element.65), channel_id=1, source_target_pairs={{0,8},{8,0},{16,24},{24,16},{32,40},{40,32},{48,56},{56,48},{64,72... | collective-permute-start | bytes 589832 | tf_op jit(solution)/shard_map/ppermute | solution.py:34
  52.0 2.0 %collective-permute-start.4 = (bf16[768,128]{1,0:T(8,128)(2,1)S(1)}, bf16[768,128]{1,0:T(8,128)(2,1)S(1)}, u32[]{:S(2)}, u32[]{:S(2)}) collective-permute-start(bf16[768,128]{1,0:T(8,128)(2,1)S(1)} %get-tuple-element.66), channel_id=1, source_target_pairs={{8,16},{16,8},{24,32},{32,24},{40,48},{48,40},{56,64},{64,56},{72,... | collective-permute-start | bytes 589832 | tf_op jit(solution)/shard_map/ppermute | solution.py:35
  54.1 0.0 collective-permute-done.5
  54.1 8.3 %collective-permute-done.4 = bf16[768,128]{1,0:T(8,128)(2,1)S(1)} collective-permute-done((bf16[768,128]{1,0:T(8,128)(2,1)S(1)}, bf16[768,128]{1,0:T(8,128)(2,1)S(1)}, u32[]{:S(2)}, u32[]{:S(2)}) %collective-permute-start.4) | collective-permute-done | bytes 196640 | tf_op jit(solution)/shard_map/ppermute | solution.py:35
  62.4 0.3 fusion.42
  62.7 0.5 select_bitcast_fusion.3
  63.2 0.8 select_select_fusion.1
  64.0 0.1 select_bitcast_fusion.2
  64.1 0.9 %fusion.16 = f32[8,128,128,1]{1,2,3,0:T(8,128)S(1)} fusion(bf16[8,8,128,128]{3,2,1,0:T(8,128)(2,1)S(1)} %copy-done, bf16[8,5,128,128]{3,2,1,0:T(8,128)(2,1)S(1)} %select_select_fusion.1, bf16[8,1,128,128]{3,2,1,0:T(8,128)(2,1)S(1)} %select_bitcast_fusion.2, bf16[8,1,128,128]{3,2,1,0:T(8,128)(2,1)S(1)} %get-tuple-element.15, ...), kind=kOutput, calls=%fused_computation.16 | convolution fusion | flops 276824064 | bytes 4718592 | tf_op jit(solution)/shard_map/bjrc,bjcv->brv/dot_general | solution.py:63
  65.0 0.2 fusion.69
  65.3 1.9 %collective-permute-start.7 = (bf16[768,128]{1,0:T(8,128)(2,1)S(1)}, bf16[768,128]{1,0:T(8,128)(2,1)S(1)}, u32[]{:S(2)}, u32[]{:S(2)}) collective-permute-start(bf16[768,128]{1,0:T(8,128)(2,1)S(1)} %get-tuple-element.57), channel_id=1, source_target_pairs={{0,8},{8,0},{16,24},{24,16},{32,40},{40,32},{48,56},{56,48},{64,72... | collective-permute-start | bytes 589832 | tf_op jit(solution)/shard_map/ppermute | solution.py:34
  67.2 2.0 %collective-permute-start.6 = (bf16[768,128]{1,0:T(8,128)(2,1)S(1)}, bf16[768,128]{1,0:T(8,128)(2,1)S(1)}, u32[]{:S(2)}, u32[]{:S(2)}) collective-permute-start(bf16[768,128]{1,0:T(8,128)(2,1)S(1)} %get-tuple-element.58), channel_id=1, source_target_pairs={{8,16},{16,8},{24,32},{32,24},{40,48},{48,40},{56,64},{64,56},{72,... | collective-permute-start | bytes 589832 | tf_op jit(solution)/shard_map/ppermute | solution.py:35
  69.3 0.0 collective-permute-done.7
  69.3 8.3 %collective-permute-done.6 = bf16[768,128]{1,0:T(8,128)(2,1)S(1)} collective-permute-done((bf16[768,128]{1,0:T(8,128)(2,1)S(1)}, bf16[768,128]{1,0:T(8,128)(2,1)S(1)}, u32[]{:S(2)}, u32[]{:S(2)}) %collective-permute-start.6) | collective-permute-done | bytes 196640 | tf_op jit(solution)/shard_map/ppermute | solution.py:35
  77.6 0.3 fusion.41
  77.9 0.5 select_bitcast_fusion.1
  78.4 0.8 select_select_fusion
  79.2 0.1 select_bitcast_fusion
  79.3 0.9 %fusion.24 = f32[8,128,128,1]{1,2,3,0:T(8,128)S(1)} fusion(bf16[8,8,128,128]{3,2,1,0:T(8,128)(2,1)S(1)} %copy-done, bf16[8,5,128,128]{3,2,1,0:T(8,128)(2,1)S(1)} %select_select_fusion, bf16[8,1,128,128]{3,2,1,0:T(8,128)(2,1)S(1)} %select_bitcast_fusion, bf16[8,1,128,128]{3,2,1,0:T(8,128)(2,1)S(1)} %get-tuple-element.13, ...), kind=kOutput, calls=%fused_computation.24 | convolution fusion | flops 276824064 | bytes 4718592 | tf_op jit(solution)/shard_map/bjrc,bjcv->brv/dot_general | solution.py:63
  80.2 1.0 %fusion.36 = bf16[1024,128]{1,0:T(8,128)(2,1)} fusion(f32[8,128,128,1]{1,2,3,0:T(8,128)S(1)} %fusion.24, bf16[128,8,128]{2,0,1:T(8,128)(2,1)S(1)} %all-to-all-done, f32[8,128,128,1]{1,2,3,0:T(8,128)S(1)} %fusion, f32[8,128,128,1]{1,2,3,0:T(8,128)S(1)} %fusion.16, f32[8,128,128,1]{1,2,3,0:T(8,128)S(1)} %fusion.8), kind=kLoop, calls=%fused_computation.86 | loop fusion | flops 1835008 | bytes 2621440 | tf_op jit(solution)/shard_map/convert_element_type | solution.py:73
  (13 shorter events, 0.3 us)
Async XLA Ops:
  0.0 34.2 %copy-start = (bf16[8,8,128,128]{3,2,1,0:T(8,128)(2,1)S(1)}, bf16[8,8,128,128]{3,2,1,0:T(8,128)(2,1)}, u32[]{:S(2)}) copy-start(bf16[8,8,128,128]{3,2,1,0:T(8,128)(2,1)} %param.6) | copy-start | bytes 6291460
  0.0 10.6 %copy-start.1 = (s32[8,8]{1,0:T(8,128)S(1)}, s32[8,8]{1,0:T(8,128)}, u32[]{:S(2)}) copy-start(s32[8,8]{1,0:T(8,128)} %param.7) | copy-start | bytes 772
  3.0 19.4 %all-to-all-start = ((bf16[128,8,128]{2,0,1:T(8,128)(2,1)}), bf16[128,8,128]{2,0,1:T(8,128)(2,1)S(1)}, u32[]{:S(2)}, u32[]{:S(2)}) async-start(bf16[128,8,128]{2,0,1:T(8,128)(2,1)} %bitcast.202), calls=%async_computation | async-start | bytes 524288 | tf_op jit(solution)/shard_map/all_to_all | solution.py:78
  22.5 10.3 %collective-permute-start = (bf16[768,128]{1,0:T(8,128)(2,1)S(1)}, bf16[768,128]{1,0:T(8,128)(2,1)S(1)}, u32[]{:S(2)}, u32[]{:S(2)}) collective-permute-start(bf16[768,128]{1,0:T(8,128)(2,1)S(1)} %bitcast.275), channel_id=1, source_target_pairs={{8,16},{16,8},{24,32},{32,24},{40,48},{48,40},{56,64},{64,56},{72,... | collective-permute-start | bytes 589832 | tf_op jit(solution)/shard_map/ppermute | solution.py:35
  24.4 8.4 %collective-permute-start.1 = (bf16[768,128]{1,0:T(8,128)(2,1)S(1)}, bf16[768,128]{1,0:T(8,128)(2,1)S(1)}, u32[]{:S(2)}, u32[]{:S(2)}) collective-permute-start(bf16[768,128]{1,0:T(8,128)(2,1)S(1)} %bitcast.274), channel_id=1, source_target_pairs={{0,8},{8,0},{16,24},{24,16},{32,40},{40,32},{48,56},{56,48},{64,72... | collective-permute-start | bytes 589832 | tf_op jit(solution)/shard_map/ppermute | solution.py:34
  35.3 4.0 %collective-permute-start.3 = (bf16[768,128]{1,0:T(8,128)(2,1)S(1)}, bf16[768,128]{1,0:T(8,128)(2,1)S(1)}, u32[]{:S(2)}, u32[]{:S(2)}) collective-permute-start(bf16[768,128]{1,0:T(8,128)(2,1)S(1)} %get-tuple-element.73), channel_id=1, source_target_pairs={{0,8},{8,0},{16,24},{24,16},{32,40},{40,32},{48,56},{56,48},{64,72... | collective-permute-start | bytes 589832 | tf_op jit(solution)/shard_map/ppermute | solution.py:34
  37.2 10.3 %collective-permute-start.2 = (bf16[768,128]{1,0:T(8,128)(2,1)S(1)}, bf16[768,128]{1,0:T(8,128)(2,1)S(1)}, u32[]{:S(2)}, u32[]{:S(2)}) collective-permute-start(bf16[768,128]{1,0:T(8,128)(2,1)S(1)} %get-tuple-element.74), channel_id=1, source_target_pairs={{8,16},{16,8},{24,32},{32,24},{40,48},{48,40},{56,64},{64,56},{72,... | collective-permute-start | bytes 589832 | tf_op jit(solution)/shard_map/ppermute | solution.py:35
  50.1 4.0 %collective-permute-start.5 = (bf16[768,128]{1,0:T(8,128)(2,1)S(1)}, bf16[768,128]{1,0:T(8,128)(2,1)S(1)}, u32[]{:S(2)}, u32[]{:S(2)}) collective-permute-start(bf16[768,128]{1,0:T(8,128)(2,1)S(1)} %get-tuple-element.65), channel_id=1, source_target_pairs={{0,8},{8,0},{16,24},{24,16},{32,40},{40,32},{48,56},{56,48},{64,72... | collective-permute-start | bytes 589832 | tf_op jit(solution)/shard_map/ppermute | solution.py:34
  52.0 10.3 %collective-permute-start.4 = (bf16[768,128]{1,0:T(8,128)(2,1)S(1)}, bf16[768,128]{1,0:T(8,128)(2,1)S(1)}, u32[]{:S(2)}, u32[]{:S(2)}) collective-permute-start(bf16[768,128]{1,0:T(8,128)(2,1)S(1)} %get-tuple-element.66), channel_id=1, source_target_pairs={{8,16},{16,8},{24,32},{32,24},{40,48},{48,40},{56,64},{64,56},{72,... | collective-permute-start | bytes 589832 | tf_op jit(solution)/shard_map/ppermute | solution.py:35
  65.3 4.0 %collective-permute-start.7 = (bf16[768,128]{1,0:T(8,128)(2,1)S(1)}, bf16[768,128]{1,0:T(8,128)(2,1)S(1)}, u32[]{:S(2)}, u32[]{:S(2)}) collective-permute-start(bf16[768,128]{1,0:T(8,128)(2,1)S(1)} %get-tuple-element.57), channel_id=1, source_target_pairs={{0,8},{8,0},{16,24},{24,16},{32,40},{40,32},{48,56},{56,48},{64,72... | collective-permute-start | bytes 589832 | tf_op jit(solution)/shard_map/ppermute | solution.py:34
  67.2 10.3 %collective-permute-start.6 = (bf16[768,128]{1,0:T(8,128)(2,1)S(1)}, bf16[768,128]{1,0:T(8,128)(2,1)S(1)}, u32[]{:S(2)}, u32[]{:S(2)}) collective-permute-start(bf16[768,128]{1,0:T(8,128)(2,1)S(1)} %get-tuple-element.58), channel_id=1, source_target_pairs={{8,16},{16,8},{24,32},{32,24},{40,48},{48,40},{56,64},{64,56},{72,... | collective-permute-start | bytes 589832 | tf_op jit(solution)/shard_map/ppermute | solution.py:35

commit v13 on v11

v13 whole, which is shorter than its diff:
```python
import jax
import jax.numpy as jnp
from jax import lax
from jax.sharding import PartitionSpec as P

DEG = 4
REACH_LO = 6
REACH_HI = 2


def shift_up(cells, axis):
    count = lax.axis_size(axis)
    return lax.ppermute(cells, axis, [(i, i + 1) for i in range(count - 1)])


def shift_down(cells, axis):
    count = lax.axis_size(axis)
    return lax.ppermute(cells, axis, [(i + 1, i) for i in range(count - 1)])


def filter_chunk(panel, blocks, offset):
    _, nnz, block_rows, _ = blocks.shape
    width = panel.shape[1]
    local_blocks = panel.shape[0] // block_rows - REACH_LO - REACH_HI

    def apply_operator(state_bf, n_rows):
        lo = shift_up(state_bf[(local_blocks - REACH_LO) * block_rows:local_blocks * block_rows], "row")
        tiles = jnp.concatenate([lo, state_bf], axis=0).reshape(-1, block_rows, width)
        windows = [tiles[w:w + n_rows][:, None] for w in range(REACH_LO + REACH_HI + 1)]

        def pick(first, count, candidates):
            part = offset[:n_rows, first:first + count, None, None]
            got = jnp.broadcast_to(windows[candidates[0]], (n_rows, count, block_rows, width))
            for w in candidates[1:]:
                got = jnp.where(part == w, windows[w], got)
            return got

        picked = jnp.concatenate([
            pick(0, 1, [REACH_LO]),
            pick(1, 1, list(range(REACH_LO + 1))),
            pick(2, 1, list(range(REACH_LO, REACH_LO + REACH_HI + 1))),
            pick(3, nnz - 3, list(range(REACH_LO + REACH_HI + 1))),
        ], axis=1)
        result = jnp.einsum("bjrc,bjcv->brv", blocks[:n_rows], picked, preferred_element_type=jnp.float32)
        return result.reshape(n_rows * block_rows, width)

    counts = [local_blocks + REACH_HI * (DEG - 1 - k) for k in range(DEG)]
    n0 = counts[0]
    prev = panel[: n0 * block_rows].astype(jnp.float32)
    cur = (apply_operator(panel, n0) - 0.25 * prev) / 2.0
    for degree in range(DEG - 1):
        n = counts[degree + 1] * block_rows
        sent = cur.astype(jnp.bfloat16)
        nxt = 2.0 * (apply_operator(sent, counts[degree + 1]) - 0.25 * cur[:n]) / 2.0 - prev[:n]
        prev = cur[:n]
        cur = nxt
    return cur.astype(jnp.bfloat16)


def per_device(vectors, rotation, blocks, columns):
    rotated = jnp.dot(vectors, rotation, preferred_element_type=jnp.float32).astype(jnp.bfloat16)
    panel = lax.all_to_all(rotated, "vec", split_axis=1, concat_axis=0, tiled=True)
    local_blocks, _, block_rows, _ = blocks.shape
    extra = REACH_HI * (DEG - 1)
    blocks_ext = jnp.concatenate([blocks, shift_down(blocks[:extra], "row")], axis=0)
    columns_ext = jnp.concatenate([columns, shift_down(columns[:extra], "row")], axis=0)
    panel_ext = jnp.concatenate([panel, shift_down(panel, "row")], axis=0)
    first_block = lax.axis_index("row") * local_blocks
    own = jnp.arange(local_blocks + extra)[:, None]
    offset = jnp.clip(columns_ext - first_block + REACH_LO - own, 0, REACH_LO + REACH_HI)
    return filter_chunk(panel_ext, blocks_ext, offset)


def solution(mesh):
    return jax.shard_map(
        per_device,
        mesh=mesh,
        in_specs=(P(("row", "vec"), None), P(), P("row", None, None, None), P("row", None)),
        out_specs=P("row", "vec"),
        check_vma=False,
    )
```

time: 82.4 us -> 101 us (1.23)
  the two profiles are of different devices: /device:TPU:399 before, /device:TPU:528 now
where the time goes in v13:
time: 101 us
  waiting for transfers between devices  46.8 us (46%)
  starting transfers between devices  27.7 us (27%)
  local copies, waits for them, and re-layouts  11 us (11%)
  other arithmetic  9.41 us (9%)
  matrix products  5.45 us (5%)
    ppermute x4, waiting for transfers between devices, shift_up(): return lax.ppermute(cells, axis, [(i, i + 1) for i in range(count - 1)])  33.2 us
    ppermute x3, waiting for transfers between devices, shift_down(): return lax.ppermute(cells, axis, [(i + 1, i) for i in range(count - 1)])  13.7 us
    ppermute x3, starting transfers between devices, shift_down(): return lax.ppermute(cells, axis, [(i + 1, i) for i in range(count - 1)])  12.1 us
    all_to_all x1, starting transfers between devices, per_device(): lax.all_to_all(rotated, 'vec', split_axis=1, concat_axis=0, tiled=True)  7.89 us
    ppermute x4, starting transfers between devices, shift_up(): return lax.ppermute(cells, axis, [(i, i + 1) for i in range(count - 1)])  7.68 us
    unnamed x11, local copies, waits for them, and re-layouts  5.27 us
    select_n x8, other arithmetic, pick(): got = jnp.where(part == w, windows[w], got)  5.05 us
    dot_general x4, matrix products, apply_operator(): jnp.einsum('bjrc,bjcv->brv', blocks[:n_rows], picked, preferred_element_t...  4.06 us
  transfers between devices with their start and end apart: 8, of which 5 were waited for; matrix products, arithmetic and copies ran while one was open for 8% of the time, Pallas kernels for 0%

profile of v13, /device:TPU:528, one launch (start us, length us, event | category | flops | bytes accessed | tf_op | source)
XLA Modules:
  0.0 100.7 jit_solution(16504950227694902755)
XLA Ops:
  0.0 0.0 copy-start
  0.0 1.6 %copy-done = bf16[1024,1024]{1,0:T(8,128)(2,1)S(1)} copy-done((bf16[1024,1024]{1,0:T(8,128)(2,1)S(1)}, bf16[1024,1024]{1,0:T(8,128)(2,1)}, u32[]{:S(2)}) %copy-start) | copy-done | bytes 2097176
  1.6 1.4 %fusion.32 = bf16[16,8,8,128]{3,2,1,0:T(8,128)(2,1)S(1)} fusion(bf16[128,1024]{1,0:T(8,128)(2,1)} %param.4, bf16[1024,1024]{1,0:T(8,128)(2,1)S(1)} %copy-done), kind=kOutput, calls=%fused_computation.42 | convolution fusion | flops 268566528 | bytes 2621440 | tf_op jit(solution)/shard_map/dot_general | solution.py:61
  3.0 0.0 copy-start.4
  3.0 0.8 copy.16
  3.8 7.9 %all-to-all-start = ((bf16[128,8,128]{2,0,1:T(8,128)(2,1)}), bf16[128,8,128]{2,0,1:T(8,128)(2,1)S(1)}, u32[]{:S(2)}, u32[]{:S(2)}) async-start(bf16[128,8,128]{2,0,1:T(8,128)(2,1)} %bitcast.113), calls=%async_computation | async-start | bytes 524288 | tf_op jit(solution)/shard_map/all_to_all | solution.py:62
  11.6 0.0 copy-start.2
  11.6 2.9 %slice.241 = bf16[6,8,128,128]{3,2,1,0:T(8,128)(2,1)} slice(bf16[8,8,128,128]{3,2,1,0:T(8,128)(2,1)} %param.6), slice={[0:6], [0:8], [0:128], [0:128]} | slice | bytes 3145728 | tf_op jit(solution)/shard_map/slice | solution.py:65
  14.6 1.9 %collective-permute-start = (bf16[6,8,128,128]{3,2,1,0:T(8,128)(2,1)}, bf16[6,8,128,128]{3,2,1,0:T(8,128)(2,1)}, u32[]{:S(2)}, u32[]{:S(2)}) collective-permute-start(bf16[6,8,128,128]{3,2,1,0:T(8,128)(2,1)} %slice.241), channel_id=1, source_target_pairs={{8,0},{16,8},{24,16},{32,24},{40,32},{48,40},{56,48},{64,56},{72,6... | collective-permute-start | bytes 4718600 | tf_op jit(solution)/shard_map/ppermute | solution.py:18
  16.5 0.0 copy-done.4
  16.5 3.1 %collective-permute-start.2 = (s32[6,8]{1,0:T(8,128)S(1)}, s32[6,8]{1,0:T(8,128)S(1)}, u32[]{:S(2)}, u32[]{:S(2)}) collective-permute-start(s32[6,8]{1,0:T(8,128)S(1)} %bitcast.196), channel_id=1, source_target_pairs={{8,0},{16,8},{24,16},{32,24},{40,32},{48,40},{56,48},{64,56},{72,6... | collective-permute-start | bytes 584 | tf_op jit(solution)/shard_map/ppermute | solution.py:18
  19.6 0.0 copy-done.2
  19.6 1.5 %constant_dynamic-update-slice_fusion.1 = bf16[14,8,128,128]{3,2,1,0:T(8,128)(2,1)} fusion(bf16[8,8,128,128]{3,2,1,0:T(8,128)(2,1)S(1)} %copy-done.2), kind=kLoop, calls=%fused_computation.145 | loop fusion | bytes 4194304
  21.1 13.7 %collective-permute-done.2 = s32[6,8]{1,0:T(8,128)S(1)} collective-permute-done((s32[6,8]{1,0:T(8,128)S(1)}, s32[6,8]{1,0:T(8,128)S(1)}, u32[]{:S(2)}, u32[]{:S(2)}) %collective-permute-start.2) | collective-permute-done | bytes 224 | tf_op jit(solution)/shard_map/ppermute | solution.py:18
  34.7 0.3 compare_reduce_fusion.23
  35.0 0.3 compare_reduce_fusion.15
  35.3 0.3 compare_reduce_fusion.7
  35.6 0.0 all-to-all-done
  35.6 7.1 %collective-permute-start.1 = (bf16[1024,128]{1,0:T(8,128)(2,1)S(1)}, bf16[1024,128]{1,0:T(8,128)(2,1)S(1)}, u32[]{:S(2)}, u32[]{:S(2)}) collective-permute-start(bf16[1024,128]{1,0:T(8,128)(2,1)S(1)} %bitcast.137), channel_id=1, source_target_pairs={{8,0},{16,8},{24,16},{32,24},{40,32},{48,40},{56,48},{64,56},{72,6... | collective-permute-start | bytes 786440 | tf_op jit(solution)/shard_map/ppermute | solution.py:18
  42.8 0.3 compare_reduce_fusion.31
  43.1 1.9 %collective-permute-start.3 = (bf16[768,128]{1,0:T(8,128)(2,1)S(1)}, bf16[768,128]{1,0:T(8,128)(2,1)S(1)}, u32[]{:S(2)}, u32[]{:S(2)}) collective-permute-start(bf16[768,128]{1,0:T(8,128)(2,1)S(1)} %bitcast.195), channel_id=1, source_target_pairs={{0,8},{8,16},{16,24},{24,32},{32,40},{40,48},{48,56},{56,64},{64,7... | collective-permute-start | bytes 589832 | tf_op jit(solution)/shard_map/ppermute | solution.py:13
  45.0 0.1 slice_compare_fusion.23
  45.1 8.3 %collective-permute-done.3 = bf16[768,128]{1,0:T(8,128)(2,1)S(1)} collective-permute-done((bf16[768,128]{1,0:T(8,128)(2,1)S(1)}, bf16[768,128]{1,0:T(8,128)(2,1)S(1)}, u32[]{:S(2)}, u32[]{:S(2)}) %collective-permute-start.3) | collective-permute-done | bytes 196640 | tf_op jit(solution)/shard_map/ppermute | solution.py:13
  53.4 0.0 collective-permute-done.1
  53.4 0.3 fusion.66
  53.8 0.3 fusion.68
  54.1 0.3 select_select_fusion.5
  54.4 0.0 copy-start.1
  54.4 1.2 %select_select_fusion = bf16[14,5,128,128]{3,2,1,0:T(8,128)(2,1)S(1)} fusion(pred[14,5]{1,0:T(8,128)(4,1)S(1)} %get-tuple-element.118, pred[14,5]{1,0:T(8,128)(4,1)S(1)} %get-tuple-element.117, pred[14,5]{1,0:T(8,128)(4,1)S(1)} %get-tuple-element.116, pred[14,5]{1,0:T(8,128)(4,1)S(1)} %get-tuple-element.115, pred[14,5]{1,0:T(8,128)(4,1)S(1)} %get-tuple-element.114, ...), kind=kLoop, calls=%fused_computation.24 | loop fusion | flops 9175040 | bytes 6423088 | tf_op jit(solution)/shard_map/jit(_where)/select_n | solution.py:35
  55.6 0.0 collective-permute-done
  55.6 0.8 copy-done.1
  56.4 1.7 %constant_dynamic-update-slice_fusion = bf16[14,8,128,128]{3,2,1,0:T(8,128)(2,1)S(1)} fusion(bf16[14,8,128,128]{3,2,1,0:T(8,128)(2,1)S(1)} %copy-done.1, bf16[6,8,128,128]{3,2,1,0:T(8,128)(2,1)} %collective-permute-done), kind=kLoop, calls=%fused_computation.144 | loop fusion | bytes 3145728 | tf_op jit(solution)/shard_map/concatenate | solution.py:65
  58.1 1.4 %fusion = f32[14,128,128,1]{2,1,3,0:T(8,128)S(1)} fusion(bf16[14,8,128,128]{3,2,1,0:T(8,128)(2,1)S(1)} %constant_dynamic-update-slice_fusion, bf16[14,5,128,128]{3,2,1,0:T(8,128)(2,1)S(1)} %select_select_fusion, bf16[14,1,128,128]{3,2,1,0:T(8,128)(2,1)S(1)} %get-tuple-element.74, bf16[14,1,128,128]{3,2,1,0:T(8,128)(2,1)S(1)} %get-tuple-element.73, ...), kind=kOutput, calls=%fused_computation | convolution fusion | flops 475267072 | bytes 8257536 | tf_op jit(solution)/shard_map/bjrc,bjcv->brv/dot_general | solution.py:44
  59.5 0.2 fusion.64
  59.7 1.9 %collective-permute-start.4 = (bf16[768,128]{1,0:T(8,128)(2,1)S(1)}, bf16[768,128]{1,0:T(8,128)(2,1)S(1)}, u32[]{:S(2)}, u32[]{:S(2)}) collective-permute-start(bf16[768,128]{1,0:T(8,128)(2,1)S(1)} %slice.318), channel_id=1, source_target_pairs={{0,8},{8,16},{16,24},{24,32},{32,40},{40,48},{48,56},{56,64},{64,7... | collective-permute-start | bytes 589832 | tf_op jit(solution)/shard_map/ppermute | solution.py:13
  61.6 0.1 slice_compare_fusion.15
  61.7 8.3 %collective-permute-done.4 = bf16[768,128]{1,0:T(8,128)(2,1)S(1)} collective-permute-done((bf16[768,128]{1,0:T(8,128)(2,1)S(1)}, bf16[768,128]{1,0:T(8,128)(2,1)S(1)}, u32[]{:S(2)}, u32[]{:S(2)}) %collective-permute-start.4) | collective-permute-done | bytes 196640 | tf_op jit(solution)/shard_map/ppermute | solution.py:13
  70.0 0.5 fusion.41
  70.5 1.1 %select_select_fusion.1 = bf16[12,5,128,128]{3,2,1,0:T(8,128)(2,1)S(1)} fusion(pred[12,5]{1,0:T(8,128)(4,1)S(1)} %get-tuple-element.110, pred[12,5]{1,0:T(8,128)(4,1)S(1)} %get-tuple-element.109, pred[12,5]{1,0:T(8,128)(4,1)S(1)} %get-tuple-element.108, pred[12,5]{1,0:T(8,128)(4,1)S(1)} %get-tuple-element.107, pred[12,5]{1,0:T(8,128)(4,1)S(1)} %get-tuple-element.106, ...), kind=kLoop, calls=%fused_computation.33 | loop fusion | flops 7864320 | bytes 5505504 | tf_op jit(solution)/shard_map/jit(_where)/select_n | solution.py:35
  71.7 0.3 select_select_fusion.7
  71.9 1.0 fusion.8
  72.9 0.1 fusion.63
  73.1 1.9 %collective-permute-start.5 = (bf16[768,128]{1,0:T(8,128)(2,1)S(1)}, bf16[768,128]{1,0:T(8,128)(2,1)S(1)}, u32[]{:S(2)}, u32[]{:S(2)}) collective-permute-start(bf16[768,128]{1,0:T(8,128)(2,1)S(1)} %slice.337), channel_id=1, source_target_pairs={{0,8},{8,16},{16,24},{24,32},{32,40},{40,48},{48,56},{56,64},{64,7... | collective-permute-start | bytes 589832 | tf_op jit(solution)/shard_map/ppermute | solution.py:13
  75.0 0.1 slice_compare_fusion.7
  75.1 8.3 %collective-permute-done.5 = bf16[768,128]{1,0:T(8,128)(2,1)S(1)} collective-permute-done((bf16[768,128]{1,0:T(8,128)(2,1)S(1)}, bf16[768,128]{1,0:T(8,128)(2,1)S(1)}, u32[]{:S(2)}, u32[]{:S(2)}) %collective-permute-start.5) | collective-permute-done | bytes 196640 | tf_op jit(solution)/shard_map/ppermute | solution.py:13
  83.4 0.4 fusion.46
  83.8 0.9 select_select_fusion.2
  84.7 0.2 select_select_fusion.9
  85.0 0.9 fusion.16
  85.8 0.1 fusion.62
  86.0 1.9 %collective-permute-start.6 = (bf16[768,128]{1,0:T(8,128)(2,1)S(1)}, bf16[768,128]{1,0:T(8,128)(2,1)S(1)}, u32[]{:S(2)}, u32[]{:S(2)}) collective-permute-start(bf16[768,128]{1,0:T(8,128)(2,1)S(1)} %slice.356), channel_id=1, source_target_pairs={{0,8},{8,16},{16,24},{24,32},{32,40},{40,48},{48,56},{56,64},{64,7... | collective-permute-start | bytes 589832 | tf_op jit(solution)/shard_map/ppermute | solution.py:13
  87.9 0.1 slice_compare_fusion.31
  88.0 8.3 %collective-permute-done.6 = bf16[768,128]{1,0:T(8,128)(2,1)S(1)} collective-permute-done((bf16[768,128]{1,0:T(8,128)(2,1)S(1)}, bf16[768,128]{1,0:T(8,128)(2,1)S(1)}, u32[]{:S(2)}, u32[]{:S(2)}) %collective-permute-start.6) | collective-permute-done | bytes 196640 | tf_op jit(solution)/shard_map/ppermute | solution.py:13
  96.3 0.4 fusion.51
  96.7 0.8 select_select_fusion.3
  97.4 0.0 copy-start.3
  97.5 0.2 select_select_fusion.11
  97.7 1.3 %copy-done.3 = bf16[8,8,128,128]{3,2,1,0:T(8,128)(2,1)S(1)} copy-done((bf16[8,8,128,128]{3,2,1,0:T(8,128)(2,1)S(1)}, bf16[8,8,128,128]{3,2,1,0:T(8,128)(2,1)}, u32[]{:S(2)}) %copy-start.3) | copy-done | bytes 2097176
  99.0 0.9 fusion.24
  99.9 0.8 fusion.36
  (6 shorter events, 0.1 us)
Async XLA Ops:
  0.0 1.6 %copy-start = (bf16[1024,1024]{1,0:T(8,128)(2,1)S(1)}, bf16[1024,1024]{1,0:T(8,128)(2,1)}, u32[]{:S(2)}) copy-start(bf16[1024,1024]{1,0:T(8,128)(2,1)} %param.5) | copy-start | bytes 6291460
  3.0 13.5 %copy-start.4 = (s32[8,8]{1,0:T(8,128)S(1)}, s32[8,8]{1,0:T(8,128)}, u32[]{:S(2)}) copy-start(s32[8,8]{1,0:T(8,128)} %param.7) | copy-start | bytes 772
  3.8 31.9 %all-to-all-start = ((bf16[128,8,128]{2,0,1:T(8,128)(2,1)}), bf16[128,8,128]{2,0,1:T(8,128)(2,1)S(1)}, u32[]{:S(2)}, u32[]{:S(2)}) async-start(bf16[128,8,128]{2,0,1:T(8,128)(2,1)} %bitcast.113), calls=%async_computation | async-start | bytes 524288 | tf_op jit(solution)/shard_map/all_to_all | solution.py:62
  11.6 7.9 %copy-start.2 = (bf16[8,8,128,128]{3,2,1,0:T(8,128)(2,1)S(1)}, bf16[8,8,128,128]{3,2,1,0:T(8,128)(2,1)}, u32[]{:S(2)}) copy-start(bf16[8,8,128,128]{3,2,1,0:T(8,128)(2,1)} %param.6) | copy-start | bytes 6291460
  14.6 41.0 %collective-permute-start = (bf16[6,8,128,128]{3,2,1,0:T(8,128)(2,1)}, bf16[6,8,128,128]{3,2,1,0:T(8,128)(2,1)}, u32[]{:S(2)}, u32[]{:S(2)}) collective-permute-start(bf16[6,8,128,128]{3,2,1,0:T(8,128)(2,1)} %slice.241), channel_id=1, source_target_pairs={{8,0},{16,8},{24,16},{32,24},{40,32},{48,40},{56,48},{64,56},{72,6... | collective-permute-start | bytes 4718600 | tf_op jit(solution)/shard_map/ppermute | solution.py:18
  16.5 18.2 %collective-permute-start.2 = (s32[6,8]{1,0:T(8,128)S(1)}, s32[6,8]{1,0:T(8,128)S(1)}, u32[]{:S(2)}, u32[]{:S(2)}) collective-permute-start(s32[6,8]{1,0:T(8,128)S(1)} %bitcast.196), channel_id=1, source_target_pairs={{8,0},{16,8},{24,16},{32,24},{40,32},{48,40},{56,48},{64,56},{72,6... | collective-permute-start | bytes 584 | tf_op jit(solution)/shard_map/ppermute | solution.py:18
  35.6 17.8 %collective-permute-start.1 = (bf16[1024,128]{1,0:T(8,128)(2,1)S(1)}, bf16[1024,128]{1,0:T(8,128)(2,1)S(1)}, u32[]{:S(2)}, u32[]{:S(2)}) collective-permute-start(bf16[1024,128]{1,0:T(8,128)(2,1)S(1)} %bitcast.137), channel_id=1, source_target_pairs={{8,0},{16,8},{24,16},{32,24},{40,32},{48,40},{56,48},{64,56},{72,6... | collective-permute-start | bytes 786440 | tf_op jit(solution)/shard_map/ppermute | solution.py:18
  43.1 10.3 %collective-permute-start.3 = (bf16[768,128]{1,0:T(8,128)(2,1)S(1)}, bf16[768,128]{1,0:T(8,128)(2,1)S(1)}, u32[]{:S(2)}, u32[]{:S(2)}) collective-permute-start(bf16[768,128]{1,0:T(8,128)(2,1)S(1)} %bitcast.195), channel_id=1, source_target_pairs={{0,8},{8,16},{16,24},{24,32},{32,40},{40,48},{48,56},{56,64},{64,7... | collective-permute-start | bytes 589832 | tf_op jit(solution)/shard_map/ppermute | solution.py:13
  54.4 2.0 %copy-start.1 = (bf16[14,8,128,128]{3,2,1,0:T(8,128)(2,1)S(1)}, bf16[14,8,128,128]{3,2,1,0:T(8,128)(2,1)}, u32[]{:S(2)}) copy-start(bf16[14,8,128,128]{3,2,1,0:T(8,128)(2,1)} %constant_dynamic-update-slice_fusion.1) | copy-start | bytes 11010052
  59.7 10.3 %collective-permute-start.4 = (bf16[768,128]{1,0:T(8,128)(2,1)S(1)}, bf16[768,128]{1,0:T(8,128)(2,1)S(1)}, u32[]{:S(2)}, u32[]{:S(2)}) collective-permute-start(bf16[768,128]{1,0:T(8,128)(2,1)S(1)} %slice.318), channel_id=1, source_target_pairs={{0,8},{8,16},{16,24},{24,32},{32,40},{40,48},{48,56},{56,64},{64,7... | collective-permute-start | bytes 589832 | tf_op jit(solution)/shard_map/ppermute | solution.py:13
  73.1 10.3 %collective-permute-start.5 = (bf16[768,128]{1,0:T(8,128)(2,1)S(1)}, bf16[768,128]{1,0:T(8,128)(2,1)S(1)}, u32[]{:S(2)}, u32[]{:S(2)}) collective-permute-start(bf16[768,128]{1,0:T(8,128)(2,1)S(1)} %slice.337), channel_id=1, source_target_pairs={{0,8},{8,16},{16,24},{24,32},{32,40},{40,48},{48,56},{56,64},{64,7... | collective-permute-start | bytes 589832 | tf_op jit(solution)/shard_map/ppermute | solution.py:13
  86.0 10.3 %collective-permute-start.6 = (bf16[768,128]{1,0:T(8,128)(2,1)S(1)}, bf16[768,128]{1,0:T(8,128)(2,1)S(1)}, u32[]{:S(2)}, u32[]{:S(2)}) collective-permute-start(bf16[768,128]{1,0:T(8,128)(2,1)S(1)} %slice.356), channel_id=1, source_target_pairs={{0,8},{8,16},{16,24},{24,32},{32,40},{40,48},{48,56},{56,64},{64,7... | collective-permute-start | bytes 589832 | tf_op jit(solution)/shard_map/ppermute | solution.py:13
  97.4 1.6 %copy-start.3 = (bf16[8,8,128,128]{3,2,1,0:T(8,128)(2,1)S(1)}, bf16[8,8,128,128]{3,2,1,0:T(8,128)(2,1)}, u32[]{:S(2)}) copy-start(bf16[8,8,128,128]{3,2,1,0:T(8,128)(2,1)} %param.6) | copy-start | bytes 6291460

commit v14 on v11

--- a/solution.py
+++ b/solution.py
@@ -22,16 +22,14 @@
 def filter_chunk(panel, blocks, offset):
     local_blocks, nnz, block_rows, _ = blocks.shape
     width = panel.shape[1]
+    split = REACH_HI
 
-    def apply_operator(state_bf):
-        lo = shift_up(state_bf[state_bf.shape[0] - REACH_LO * block_rows:], "row")
-        hi = shift_down(state_bf[: REACH_HI * block_rows], "row")
-        tiles = jnp.concatenate([lo, state_bf, hi], axis=0).reshape(-1, block_rows, width)
-        windows = [tiles[w:w + local_blocks][:, None] for w in range(REACH_LO + REACH_HI + 1)]
+    def product(tiles, first, n_rows):
+        windows = [tiles[first + w:first + w + n_rows][:, None] for w in range(REACH_LO + REACH_HI + 1)]
 
-        def pick(first, count, candidates):
-            part = offset[:, first:first + count, None, None]
-            got = jnp.broadcast_to(windows[candidates[0]], (local_blocks, count, block_rows, width))
+        def pick(entry, count, candidates):
+            part = offset[first:first + n_rows, entry:entry + count, None, None]
+            got = jnp.broadcast_to(windows[candidates[0]], (n_rows, count, block_rows, width))
             for w in candidates[1:]:
                 got = jnp.where(part == w, windows[w], got)
             return got
@@ -42,17 +40,32 @@
             pick(2, 1, list(range(REACH_LO, REACH_LO + REACH_HI + 1))),
             pick(3, nnz - 3, list(range(REACH_LO + REACH_HI + 1))),
         ], axis=1)
-        result = jnp.einsum("bjrc,bjcv->brv", blocks, picked, preferred_element_type=jnp.float32)
-        return result.reshape(local_blocks * block_rows, width)
+        result = jnp.einsum("bjrc,bjcv->brv", blocks[first:first + n_rows], picked, preferred_element_type=jnp.float32)
+        return result.reshape(n_rows * block_rows, width)
 
-    prev = panel.astype(jnp.float32)
-    cur = (apply_operator(panel) - 0.25 * prev) / 2.0
+    def apply_operator(head, rest):
+        lo = shift_up(rest, "row")
+        hi = shift_down(head, "row")
+        part = jnp.concatenate([lo, head, rest], axis=0).reshape(-1, block_rows, width)
+        new_head = product(part, 0, split)
+        tiles = jnp.concatenate([lo, head, rest, hi], axis=0).reshape(-1, block_rows, width)
+        new_rest = product(tiles, split, local_blocks - split)
+        return new_head, new_rest
+
+    cut = split * block_rows
+    p_head, p_rest = panel[:cut], panel[cut:]
+    prev = (p_head.astype(jnp.float32), p_rest.astype(jnp.float32))
+    a_head, a_rest = apply_operator(p_head, p_rest)
+    cur = ((a_head - 0.25 * prev[0]) / 2.0, (a_rest - 0.25 * prev[1]) / 2.0)
     for degree in range(DEG - 1):
-        sent = cur.astype(jnp.bfloat16)
-        nxt = 2.0 * (apply_operator(sent) - 0.25 * cur) / 2.0 - prev
+        a_head, a_rest = apply_operator(cur[0].astype(jnp.bfloat16), cur[1].astype(jnp.bfloat16))
+        nxt = (
+            2.0 * (a_head - 0.25 * cur[0]) / 2.0 - prev[0],
+            2.0 * (a_rest - 0.25 * cur[1]) / 2.0 - prev[1],
+        )
         prev = cur
         cur = nxt
-    return cur.astype(jnp.bfloat16)
+    return jnp.concatenate([cur[0], cur[1]], axis=0).astype(jnp.bfloat16)
 
 
 def per_device(vectors, rotation, blocks, columns):

time: 82.4 us -> 83.4 us (1.012)
  local copies, waits for them, and re-layouts: 0.84 us -> 3.48 us
  waiting for transfers between devices: 36.5 us -> 34 us
  other arithmetic: 7.91 us -> 9.02 us
    ppermute x4, waiting for transfers between devices: 26.2 us -> 23.7 us  [shift_down(): return lax.ppermute(cells, axis, [(i + 1, i) for i in range(count - 1)])]
    unnamed x4 -> x6, local copies, waits for them, and re-layouts: 0.01 us -> 2.4 us
    convert_element_type x4 -> x6, other arithmetic: 1.44 us -> 0.5 us  [the longest x3 0.36 us: filter_chunk(): cur[1].astype(jnp.bfloat16)]
    dot_general x1, matrix products: 2.28 us -> 1.39 us  [per_device(): jnp.dot(vectors, rotation, preferred_element_type=jnp.float32)]
    select_n x11 -> x20, other arithmetic: 4.91 us -> 5.6 us  [pick(): got = jnp.where(part == w, windows[w], got)]
    dot_general x4 -> x8, matrix products: 3.67 us -> 4.15 us  [product(): jnp.einsum('bjrc,bjcv->brv', blocks[first:first + n_rows], picked, prefer...]
  transfers between devices with their start and end apart: 9 -> 9, of which waited for: 5 -> 6; matrix products, arithmetic and copies ran while one was open for 0% -> 5% of each run, Pallas kernels for 0% -> 0%
where the time goes in v14:
time: 83.4 us; the launch traced here: 82.9 us
  waiting for transfers between devices  34 us (41%)
  starting transfers between devices  30.4 us (36%)
  other arithmetic  9.02 us (11%)
  matrix products  5.54 us (7%)
  local copies, waits for them, and re-layouts  3.48 us (4%)
    ppermute x4, waiting for transfers between devices, shift_down(): return lax.ppermute(cells, axis, [(i + 1, i) for i in range(count - 1)])  23.7 us
    ppermute x4, starting transfers between devices, shift_up(): return lax.ppermute(cells, axis, [(i, i + 1) for i in range(count - 1)])  14 us
    all_to_all x1, waiting for transfers between devices, per_device(): lax.all_to_all(rotated, 'vec', split_axis=1, concat_axis=0, tiled=True)  9.6 us
    ppermute x4, starting transfers between devices, shift_down(): return lax.ppermute(cells, axis, [(i + 1, i) for i in range(count - 1)])  9.14 us
    all_to_all x1, starting transfers between devices, per_device(): lax.all_to_all(rotated, 'vec', split_axis=1, concat_axis=0, tiled=True)  7.28 us
    select_n x20, other arithmetic, pick(): got = jnp.where(part == w, windows[w], got)  5.6 us
    dot_general x8, matrix products, product(): jnp.einsum('bjrc,bjcv->brv', blocks[first:first + n_rows], picked, prefer...  4.15 us
    unnamed x6, local copies, waits for them, and re-layouts  2.4 us
  transfers between devices with their start and end apart: 9, of which 6 were waited for; matrix products, arithmetic and copies ran while one was open for 5% of the time, Pallas kernels for 0%

profile of v14, /device:TPU:399, one launch (start us, length us, event | category | flops | bytes accessed | tf_op | source)
XLA Modules:
  0.0 82.9 jit_solution(17208738105230145977)
XLA Ops:
  0.0 1.6 %copy-done = bf16[1024,1024]{1,0:T(8,128)(2,1)S(1)} copy-done((bf16[1024,1024]{1,0:T(8,128)(2,1)S(1)}, bf16[1024,1024]{1,0:T(8,128)(2,1)}, u32[]{:S(2)}) %copy-start) | copy-done | bytes 2097176
  1.6 1.4 %fusion.32 = bf16[16,8,8,128]{3,2,1,0:T(8,128)(2,1)S(1)} fusion(bf16[128,1024]{1,0:T(8,128)(2,1)} %param.4, bf16[1024,1024]{1,0:T(8,128)(2,1)S(1)} %copy-done), kind=kOutput, calls=%fused_computation.33 | convolution fusion | flops 268566528 | bytes 2621440 | tf_op jit(solution)/shard_map/dot_general | solution.py:72
  3.0 0.8 copy.39
  3.7 7.3 %all-to-all-start = ((bf16[128,8,128]{2,0,1:T(8,128)(2,1)}), bf16[128,8,128]{2,0,1:T(8,128)(2,1)S(1)}, u32[]{:S(2)}, u32[]{:S(2)}) async-start(bf16[128,8,128]{2,0,1:T(8,128)(2,1)} %bitcast.368), calls=%async_computation | async-start | bytes 524288 | tf_op jit(solution)/shard_map/all_to_all | solution.py:73
  11.0 0.3 compare_reduce_fusion.7
  11.3 0.3 compare_reduce_fusion.15
  11.7 0.1 slice_compare_fusion.7
  11.8 9.6 %all-to-all-done = bf16[128,8,128]{2,0,1:T(8,128)(2,1)S(1)} async-done(((bf16[128,8,128]{2,0,1:T(8,128)(2,1)}), bf16[128,8,128]{2,0,1:T(8,128)(2,1)S(1)}, u32[]{:S(2)}, u32[]{:S(2)}) %all-to-all-start) | async-done | bytes 262176 | tf_op jit(solution)/shard_map/all_to_all | solution.py:73
  21.4 8.3 %collective-permute-start = (bf16[768,128]{1,0:T(8,128)(2,1)S(1)}, bf16[768,128]{1,0:T(8,128)(2,1)S(1)}, u32[]{:S(2)}, u32[]{:S(2)}) collective-permute-start(bf16[768,128]{1,0:T(8,128)(2,1)S(1)} %bitcast.369), channel_id=1, source_target_pairs={{0,8},{8,16},{16,24},{24,32},{32,40},{40,48},{48,56},{56,64},{64,7... | collective-permute-start | bytes 589832 | tf_op jit(solution)/shard_map/ppermute | solution.py:14
  29.7 1.9 %collective-permute-start.1 = (bf16[256,128]{1,0:T(8,128)(2,1)S(1)}, bf16[256,128]{1,0:T(8,128)(2,1)S(1)}, u32[]{:S(2)}, u32[]{:S(2)}) collective-permute-start(bf16[256,128]{1,0:T(8,128)(2,1)S(1)} %bitcast.383), channel_id=1, source_target_pairs={{8,0},{16,8},{24,16},{32,24},{40,32},{48,40},{56,48},{64,56},{72,6... | collective-permute-start | bytes 196616 | tf_op jit(solution)/shard_map/ppermute | solution.py:19
  31.6 0.6 collective-permute-done
  32.4 6.2 %collective-permute-done.1 = bf16[256,128]{1,0:T(8,128)(2,1)S(1)} collective-permute-done((bf16[256,128]{1,0:T(8,128)(2,1)S(1)}, bf16[256,128]{1,0:T(8,128)(2,1)S(1)}, u32[]{:S(2)}, u32[]{:S(2)}) %collective-permute-start.1) | collective-permute-done | bytes 65568 | tf_op jit(solution)/shard_map/ppermute | solution.py:19
  38.6 0.1 fusion.87
  38.7 0.2 slice_bitcast_fusion.1
  38.9 0.6 select_select_fusion.3
  39.5 0.8 copy-done.2
  40.3 0.7 fusion
  41.1 0.1 multiply_convert_fusion.1
  41.2 1.9 %collective-permute-start.2 = (bf16[768,128]{1,0:T(8,128)(2,1)S(1)}, bf16[768,128]{1,0:T(8,128)(2,1)S(1)}, u32[]{:S(2)}, u32[]{:S(2)}) collective-permute-start(bf16[768,128]{1,0:T(8,128)(2,1)S(1)} %multiply_convert_fusion.1), channel_id=1, source_target_pairs={{0,8},{8,16},{16,24},{24,32},{32,40},{40,48},{48,56},{56,64},{64,7... | collective-permute-start | bytes 589832 | tf_op jit(solution)/shard_map/ppermute | solution.py:14
  43.2 0.1 slice_bitcast_fusion
  43.3 0.2 select_select_fusion.7
  43.5 0.3 fusion.37
  43.8 2.4 %collective-permute-start.3 = (bf16[256,128]{1,0:T(8,128)(2,1)S(1)}, bf16[256,128]{1,0:T(8,128)(2,1)S(1)}, u32[]{:S(2)}, u32[]{:S(2)}) collective-permute-start(bf16[256,128]{1,0:T(8,128)(2,1)S(1)} %multiply_convert_fusion.2), channel_id=1, source_target_pairs={{8,0},{16,8},{24,16},{32,24},{40,32},{48,40},{56,48},{64,56},{72,6... | collective-permute-start | bytes 196616 | tf_op jit(solution)/shard_map/ppermute | solution.py:19
  46.4 0.1 fusion.120
  46.5 0.1 select_bitcast_fusion.13
  46.6 0.2 select_select_fusion.6
  46.8 0.1 select_bitcast_fusion.12
  46.9 5.8 %collective-permute-done.3 = bf16[256,128]{1,0:T(8,128)(2,1)S(1)} collective-permute-done((bf16[256,128]{1,0:T(8,128)(2,1)S(1)}, bf16[256,128]{1,0:T(8,128)(2,1)S(1)}, u32[]{:S(2)}, u32[]{:S(2)}) %collective-permute-start.3) | collective-permute-done | bytes 65568 | tf_op jit(solution)/shard_map/ppermute | solution.py:19
  52.7 0.1 fusion.85
  52.9 0.2 select_bitcast_fusion.5
  53.1 0.6 select_select_fusion.2
  53.7 0.1 select_bitcast_fusion.4
  53.8 0.8 fusion.8
  54.5 0.1 fusion.108
  54.7 1.9 %collective-permute-start.4 = (bf16[768,128]{1,0:T(8,128)(2,1)S(1)}, bf16[768,128]{1,0:T(8,128)(2,1)S(1)}, u32[]{:S(2)}, u32[]{:S(2)}) collective-permute-start(bf16[768,128]{1,0:T(8,128)(2,1)S(1)} %fusion.108), channel_id=1, source_target_pairs={{0,8},{8,16},{16,24},{24,32},{32,40},{40,48},{48,56},{56,64},{64,7... | collective-permute-start | bytes 589832 | tf_op jit(solution)/shard_map/ppermute | solution.py:14
  56.6 0.3 fusion.45
  56.9 2.4 %collective-permute-start.5 = (bf16[256,128]{1,0:T(8,128)(2,1)S(1)}, bf16[256,128]{1,0:T(8,128)(2,1)S(1)}, u32[]{:S(2)}, u32[]{:S(2)}) collective-permute-start(bf16[256,128]{1,0:T(8,128)(2,1)S(1)} %fusion.107), channel_id=1, source_target_pairs={{8,0},{16,8},{24,16},{32,24},{40,32},{48,40},{56,48},{64,56},{72,6... | collective-permute-start | bytes 196616 | tf_op jit(solution)/shard_map/ppermute | solution.py:19
  59.5 0.1 select_bitcast_fusion.11
  59.7 0.2 select_select_fusion.5
  59.9 0.1 select_bitcast_fusion.10
  60.0 5.8 %collective-permute-done.5 = bf16[256,128]{1,0:T(8,128)(2,1)S(1)} collective-permute-done((bf16[256,128]{1,0:T(8,128)(2,1)S(1)}, bf16[256,128]{1,0:T(8,128)(2,1)S(1)}, u32[]{:S(2)}, u32[]{:S(2)}) %collective-permute-start.5) | collective-permute-done | bytes 65568 | tf_op jit(solution)/shard_map/ppermute | solution.py:19
  65.8 0.1 fusion.83
  65.9 0.6 select_bitcast_fusion.3
  66.5 0.6 select_select_fusion.1
  67.1 0.1 select_bitcast_fusion.2
  67.2 0.8 fusion.16
  68.0 0.2 fusion.106
  68.2 1.9 %collective-permute-start.6 = (bf16[768,128]{1,0:T(8,128)(2,1)S(1)}, bf16[768,128]{1,0:T(8,128)(2,1)S(1)}, u32[]{:S(2)}, u32[]{:S(2)}) collective-permute-start(bf16[768,128]{1,0:T(8,128)(2,1)S(1)} %fusion.106), channel_id=1, source_target_pairs={{0,8},{8,16},{16,24},{24,32},{32,40},{40,48},{48,56},{56,64},{64,7... | collective-permute-start | bytes 589832 | tf_op jit(solution)/shard_map/ppermute | solution.py:14
  70.1 0.3 fusion.53
  70.5 2.4 %collective-permute-start.7 = (bf16[256,128]{1,0:T(8,128)(2,1)S(1)}, bf16[256,128]{1,0:T(8,128)(2,1)S(1)}, u32[]{:S(2)}, u32[]{:S(2)}) collective-permute-start(bf16[256,128]{1,0:T(8,128)(2,1)S(1)} %fusion.105), channel_id=1, source_target_pairs={{8,0},{16,8},{24,16},{32,24},{40,32},{48,40},{56,48},{64,56},{72,6... | collective-permute-start | bytes 196616 | tf_op jit(solution)/shard_map/ppermute | solution.py:19
  73.0 0.1 fusion.118
  73.1 0.2 select_bitcast_fusion.9
  73.3 0.2 select_select_fusion.4
  73.5 0.1 select_bitcast_fusion.8
  73.6 5.8 %collective-permute-done.7 = bf16[256,128]{1,0:T(8,128)(2,1)S(1)} collective-permute-done((bf16[256,128]{1,0:T(8,128)(2,1)S(1)}, bf16[256,128]{1,0:T(8,128)(2,1)S(1)}, u32[]{:S(2)}, u32[]{:S(2)}) %collective-permute-start.7) | collective-permute-done | bytes 65568 | tf_op jit(solution)/shard_map/ppermute | solution.py:19
  79.4 0.1 fusion.81
  79.5 0.6 select_bitcast_fusion.1
  80.1 0.6 select_select_fusion
  80.7 0.1 select_bitcast_fusion
  80.8 0.3 fusion.61
  81.1 0.1 fusion.92
  81.2 0.8 fusion.24
  82.0 0.2 fusion.72
  82.2 0.7 pad_maximum_fusion.4
  (24 shorter events, 0.8 us)
Async XLA Ops:
  0.0 1.6 %copy-start = (bf16[1024,1024]{1,0:T(8,128)(2,1)S(1)}, bf16[1024,1024]{1,0:T(8,128)(2,1)}, u32[]{:S(2)}) copy-start(bf16[1024,1024]{1,0:T(8,128)(2,1)} %param.5) | copy-start | bytes 6291460
  0.0 11.0 %copy-start.1 = (s32[8,8]{1,0:T(8,128)S(1)}, s32[8,8]{1,0:T(8,128)}, u32[]{:S(2)}) copy-start(s32[8,8]{1,0:T(8,128)} %param.7) | copy-start | bytes 772
  3.7 17.7 %all-to-all-start = ((bf16[128,8,128]{2,0,1:T(8,128)(2,1)}), bf16[128,8,128]{2,0,1:T(8,128)(2,1)S(1)}, u32[]{:S(2)}, u32[]{:S(2)}) async-start(bf16[128,8,128]{2,0,1:T(8,128)(2,1)} %bitcast.368), calls=%async_computation | async-start | bytes 524288 | tf_op jit(solution)/shard_map/all_to_all | solution.py:73
  21.4 10.9 %collective-permute-start = (bf16[768,128]{1,0:T(8,128)(2,1)S(1)}, bf16[768,128]{1,0:T(8,128)(2,1)S(1)}, u32[]{:S(2)}, u32[]{:S(2)}) collective-permute-start(bf16[768,128]{1,0:T(8,128)(2,1)S(1)} %bitcast.369), channel_id=1, source_target_pairs={{0,8},{8,16},{16,24},{24,32},{32,40},{40,48},{48,56},{56,64},{64,7... | collective-permute-start | bytes 589832 | tf_op jit(solution)/shard_map/ppermute | solution.py:14
  29.7 8.9 %collective-permute-start.1 = (bf16[256,128]{1,0:T(8,128)(2,1)S(1)}, bf16[256,128]{1,0:T(8,128)(2,1)S(1)}, u32[]{:S(2)}, u32[]{:S(2)}) collective-permute-start(bf16[256,128]{1,0:T(8,128)(2,1)S(1)} %bitcast.383), channel_id=1, source_target_pairs={{8,0},{16,8},{24,16},{32,24},{40,32},{48,40},{56,48},{64,56},{72,6... | collective-permute-start | bytes 196616 | tf_op jit(solution)/shard_map/ppermute | solution.py:19
  38.7 1.6 %copy-start.2 = (bf16[8,8,128,128]{3,2,1,0:T(8,128)(2,1)S(1)}, bf16[8,8,128,128]{3,2,1,0:T(8,128)(2,1)}, u32[]{:S(2)}) copy-start(bf16[8,8,128,128]{3,2,1,0:T(8,128)(2,1)} %param.6) | copy-start | bytes 6291460
  41.2 5.1 %collective-permute-start.2 = (bf16[768,128]{1,0:T(8,128)(2,1)S(1)}, bf16[768,128]{1,0:T(8,128)(2,1)S(1)}, u32[]{:S(2)}, u32[]{:S(2)}) collective-permute-start(bf16[768,128]{1,0:T(8,128)(2,1)S(1)} %multiply_convert_fusion.1), channel_id=1, source_target_pairs={{0,8},{8,16},{16,24},{24,32},{32,40},{40,48},{48,56},{56,64},{64,7... | collective-permute-start | bytes 589832 | tf_op jit(solution)/shard_map/ppermute | solution.py:14
  43.8 8.9 %collective-permute-start.3 = (bf16[256,128]{1,0:T(8,128)(2,1)S(1)}, bf16[256,128]{1,0:T(8,128)(2,1)S(1)}, u32[]{:S(2)}, u32[]{:S(2)}) collective-permute-start(bf16[256,128]{1,0:T(8,128)(2,1)S(1)} %multiply_convert_fusion.2), channel_id=1, source_target_pairs={{8,0},{16,8},{24,16},{32,24},{40,32},{48,40},{56,48},{64,56},{72,6... | collective-permute-start | bytes 196616 | tf_op jit(solution)/shard_map/ppermute | solution.py:19
  54.7 4.7 %collective-permute-start.4 = (bf16[768,128]{1,0:T(8,128)(2,1)S(1)}, bf16[768,128]{1,0:T(8,128)(2,1)S(1)}, u32[]{:S(2)}, u32[]{:S(2)}) collective-permute-start(bf16[768,128]{1,0:T(8,128)(2,1)S(1)} %fusion.108), channel_id=1, source_target_pairs={{0,8},{8,16},{16,24},{24,32},{32,40},{40,48},{48,56},{56,64},{64,7... | collective-permute-start | bytes 589832 | tf_op jit(solution)/shard_map/ppermute | solution.py:14
  56.9 8.9 %collective-permute-start.5 = (bf16[256,128]{1,0:T(8,128)(2,1)S(1)}, bf16[256,128]{1,0:T(8,128)(2,1)S(1)}, u32[]{:S(2)}, u32[]{:S(2)}) collective-permute-start(bf16[256,128]{1,0:T(8,128)(2,1)S(1)} %fusion.107), channel_id=1, source_target_pairs={{8,0},{16,8},{24,16},{32,24},{40,32},{48,40},{56,48},{64,56},{72,6... | collective-permute-start | bytes 196616 | tf_op jit(solution)/shard_map/ppermute | solution.py:19
  68.2 4.7 %collective-permute-start.6 = (bf16[768,128]{1,0:T(8,128)(2,1)S(1)}, bf16[768,128]{1,0:T(8,128)(2,1)S(1)}, u32[]{:S(2)}, u32[]{:S(2)}) collective-permute-start(bf16[768,128]{1,0:T(8,128)(2,1)S(1)} %fusion.106), channel_id=1, source_target_pairs={{0,8},{8,16},{16,24},{24,32},{32,40},{40,48},{48,56},{56,64},{64,7... | collective-permute-start | bytes 589832 | tf_op jit(solution)/shard_map/ppermute | solution.py:14
  70.5 8.9 %collective-permute-start.7 = (bf16[256,128]{1,0:T(8,128)(2,1)S(1)}, bf16[256,128]{1,0:T(8,128)(2,1)S(1)}, u32[]{:S(2)}, u32[]{:S(2)}) collective-permute-start(bf16[256,128]{1,0:T(8,128)(2,1)S(1)} %fusion.105), channel_id=1, source_target_pairs={{8,0},{16,8},{24,16},{32,24},{40,32},{48,40},{56,48},{64,56},{72,6... | collective-permute-start | bytes 196616 | tf_op jit(solution)/shard_map/ppermute | solution.py:19

commit v15 on v12

--- a/solution.py
+++ b/solution.py
@@ -74,8 +74,9 @@
 
 
 def per_device(vectors, rotation, blocks, columns):
-    rotated = jnp.dot(vectors, rotation, preferred_element_type=jnp.float32).astype(jnp.bfloat16)
-    panel = lax.all_to_all(rotated, "vec", split_axis=1, concat_axis=0, tiled=True)
+    rotated_t = lax.dot_general(rotation, vectors, (((0,), (1,)), ((), ())), preferred_element_type=jnp.float32)
+    panel_t = lax.all_to_all(rotated_t.astype(jnp.bfloat16), "vec", split_axis=0, concat_axis=1, tiled=True)
+    panel = panel_t.T
     local_blocks = blocks.shape[0]
     n_tiles = local_blocks + REACH_LO + REACH_HI
     first_block = lax.axis_index("row") * local_blocks

time: 81.6 us -> 75.2 us (0.922)
  waiting for transfers between devices: 41.1 us -> 35.7 us
  other arithmetic: 8.18 us -> 7.21 us
  matrix products: 5.95 us -> 6.89 us
    ppermute x4, waiting for transfers between devices: 29.5 us -> 24.1 us  [swap_halos(): got_across = lax.ppermute(jnp.where(even, head, tail), 'row', pairs_across)]
    select_n x11 -> x8, other arithmetic: 4.91 us -> 3.94 us  [pick(): got = jnp.where(part == w, windows[w], got)]
    dot_general x1, matrix products: 2.28 us -> 3.22 us  [per_device(): lax.dot_general(rotation, vectors, (((0,), (1,)), ((), ())), preferred_el...]
  transfers between devices with their start and end apart: 9 -> 9, of which waited for: 5 -> 5; matrix products, arithmetic and copies ran while one was open for 0% -> 1% of each run, Pallas kernels for 0% -> 0%
where the time goes in v15:
time: 75.2 us; the launch traced here: 74.8 us
  waiting for transfers between devices  35.7 us (47%)
  starting transfers between devices  24.5 us (33%)
  other arithmetic  7.21 us (10%)
  matrix products  6.89 us (9%)
    ppermute x4, waiting for transfers between devices, swap_halos(): got_across = lax.ppermute(jnp.where(even, head, tail), 'row', pairs_across)  24.1 us
    all_to_all x1, waiting for transfers between devices, per_device(): lax.all_to_all(rotated_t.astype(jnp.bfloat16), 'vec', split_axis=0, conca...  11.6 us
    ppermute x4, starting transfers between devices, swap_halos(): got_in = lax.ppermute(jnp.where(even, tail, head), 'row', pairs_in)  9.27 us
    ppermute x4, starting transfers between devices, swap_halos(): got_across = lax.ppermute(jnp.where(even, head, tail), 'row', pairs_across)  7.68 us
    all_to_all x1, starting transfers between devices, per_device(): lax.all_to_all(rotated_t.astype(jnp.bfloat16), 'vec', split_axis=0, conca...  7.56 us
    select_n x8, other arithmetic, pick(): got = jnp.where(part == w, windows[w], got)  3.94 us
    dot_general x4, matrix products, apply_operator(): jnp.einsum('bjrc,bjcv->brv', blocks, picked, preferred_element_type=jnp.f...  3.67 us
    dot_general x1, matrix products, per_device(): lax.dot_general(rotation, vectors, (((0,), (1,)), ((), ())), preferred_el...  3.22 us
  transfers between devices with their start and end apart: 9, of which 5 were waited for; matrix products, arithmetic and copies ran while one was open for 1% of the time, Pallas kernels for 0%

profile of v15, /device:TPU:512, one launch (start us, length us, event | category | flops | bytes accessed | tf_op | source)
XLA Modules:
  0.0 74.8 jit_solution(8664362119887141742)
XLA Ops:
  0.0 0.0 copy-start
  0.0 0.0 copy-start.1
  0.0 3.2 %convolution_convert_fusion = bf16[1024,128]{1,0:T(8,128)(2,1)} fusion(bf16[1024,1024]{1,0:T(8,128)(2,1)} %param.5, bf16[128,1024]{1,0:T(8,128)(2,1)} %param.4), kind=kOutput, calls=%fused_computation.36 | convolution fusion | flops 268566528 | bytes 2621440 | tf_op jit(solution)/shard_map/dot_general | solution.py:77
  3.2 7.6 %all-to-all-start = ((bf16[8,128,128]{2,1,0:T(8,128)(2,1)}), bf16[8,128,128]{2,1,0:T(8,128)(2,1)S(1)}, u32[]{:S(2)}, u32[]{:S(2)}) async-start(bf16[8,128,128]{2,1,0:T(8,128)(2,1)} %bitcast), calls=%async_computation | async-start | bytes 524288 | tf_op jit(solution)/shard_map/all_to_all | solution.py:78
  10.8 0.0 copy-done.1
  10.8 0.3 compare_reduce_fusion.7
  11.1 11.6 %all-to-all-done = bf16[8,128,128]{2,1,0:T(8,128)(2,1)S(1)} async-done(((bf16[8,128,128]{2,1,0:T(8,128)(2,1)}), bf16[8,128,128]{2,1,0:T(8,128)(2,1)S(1)}, u32[]{:S(2)}, u32[]{:S(2)}) %all-to-all-start) | async-done | bytes 262176 | tf_op jit(solution)/shard_map/all_to_all | solution.py:78
  22.7 0.2 copy.5
  22.9 1.9 %collective-permute-start = (bf16[768,128]{1,0:T(8,128)(2,1)S(1)}, bf16[768,128]{1,0:T(8,128)(2,1)S(1)}, u32[]{:S(2)}, u32[]{:S(2)}) collective-permute-start(bf16[768,128]{1,0:T(8,128)(2,1)S(1)} %get-tuple-element.84), channel_id=1, source_target_pairs={{8,16},{16,8},{24,32},{32,24},{40,48},{48,40},{56,64},{64,56},{72,... | collective-permute-start | bytes 589832 | tf_op jit(solution)/shard_map/ppermute | solution.py:35
  24.8 3.5 %collective-permute-start.1 = (bf16[768,128]{1,0:T(8,128)(2,1)S(1)}, bf16[768,128]{1,0:T(8,128)(2,1)S(1)}, u32[]{:S(2)}, u32[]{:S(2)}) collective-permute-start(bf16[768,128]{1,0:T(8,128)(2,1)S(1)} %get-tuple-element.83), channel_id=1, source_target_pairs={{0,8},{8,0},{16,24},{24,16},{32,40},{40,32},{48,56},{56,48},{64,72... | collective-permute-start | bytes 589832 | tf_op jit(solution)/shard_map/ppermute | solution.py:34
  28.3 0.1 slice_compare_fusion.7
  28.4 4.8 %collective-permute-done = bf16[768,128]{1,0:T(8,128)(2,1)S(1)} collective-permute-done((bf16[768,128]{1,0:T(8,128)(2,1)S(1)}, bf16[768,128]{1,0:T(8,128)(2,1)S(1)}, u32[]{:S(2)}, u32[]{:S(2)}) %collective-permute-start) | collective-permute-done | bytes 196640 | tf_op jit(solution)/shard_map/ppermute | solution.py:35
  33.2 0.0 collective-permute-done.1
  33.2 0.3 fusion.39
  33.5 0.2 select_select_fusion.11
  33.8 0.8 %select_select_fusion.3 = bf16[8,5,128,128]{3,2,1,0:T(8,128)(2,1)S(1)} fusion(pred[8,5]{1,0:T(8,128)(4,1)S(1)} %get-tuple-element.92, pred[8,5]{1,0:T(8,128)(4,1)S(1)} %get-tuple-element.91, pred[8,5]{1,0:T(8,128)(4,1)S(1)} %get-tuple-element.90, pred[8,5]{1,0:T(8,128)(4,1)S(1)} %get-tuple-element.89, pred[8,5]{1,0:T(8,128)(4,1)S(1)} %get-tuple-element.88, ...), kind=kLoop, calls=%fused_computation.35 | loop fusion | flops 5242880 | bytes 3670336 | tf_op jit(solution)/shard_map/jit(_where)/select_n | solution.py:54
  34.5 0.0 copy-done
  34.6 0.9 %fusion = f32[8,128,128,1]{1,2,3,0:T(8,128)S(1)} fusion(bf16[8,8,128,128]{3,2,1,0:T(8,128)(2,1)S(1)} %copy-done, bf16[8,5,128,128]{3,2,1,0:T(8,128)(2,1)S(1)} %select_select_fusion.3, bf16[8,1,128,128]{3,2,1,0:T(8,128)(2,1)S(1)} %get-tuple-element.76, bf16[8,1,128,128]{3,2,1,0:T(8,128)(2,1)S(1)} %get-tuple-element.75, bf16[8,1,128,128]{3,2,1,0:T(8,128)(2,1)S(1)} %bitcast.165), kind=kOutput, calls=%fused_computation | convolution fusion | flops 276824064 | bytes 4718592 | tf_op jit(solution)/shard_map/bjrc,bjcv->brv/dot_general | solution.py:63
  35.5 0.1 multiply_convert_fusion
  35.6 1.9 %collective-permute-start.2 = (bf16[768,128]{1,0:T(8,128)(2,1)S(1)}, bf16[768,128]{1,0:T(8,128)(2,1)S(1)}, u32[]{:S(2)}, u32[]{:S(2)}) collective-permute-start(bf16[768,128]{1,0:T(8,128)(2,1)S(1)} %get-tuple-element.74), channel_id=1, source_target_pairs={{8,16},{16,8},{24,32},{32,24},{40,48},{48,40},{56,64},{64,56},{72,... | collective-permute-start | bytes 589832 | tf_op jit(solution)/shard_map/ppermute | solution.py:35
  37.6 1.9 %collective-permute-start.3 = (bf16[768,128]{1,0:T(8,128)(2,1)S(1)}, bf16[768,128]{1,0:T(8,128)(2,1)S(1)}, u32[]{:S(2)}, u32[]{:S(2)}) collective-permute-start(bf16[768,128]{1,0:T(8,128)(2,1)S(1)} %get-tuple-element.73), channel_id=1, source_target_pairs={{0,8},{8,0},{16,24},{24,16},{32,40},{40,32},{48,56},{56,48},{64,72... | collective-permute-start | bytes 589832 | tf_op jit(solution)/shard_map/ppermute | solution.py:34
  39.5 6.5 %collective-permute-done.2 = bf16[768,128]{1,0:T(8,128)(2,1)S(1)} collective-permute-done((bf16[768,128]{1,0:T(8,128)(2,1)S(1)}, bf16[768,128]{1,0:T(8,128)(2,1)S(1)}, u32[]{:S(2)}, u32[]{:S(2)}) %collective-permute-start.2) | collective-permute-done | bytes 196640 | tf_op jit(solution)/shard_map/ppermute | solution.py:35
  45.9 0.0 collective-permute-done.3
  46.0 0.3 fusion.38
  46.3 0.8 %select_select_fusion.2 = bf16[8,5,128,128]{3,2,1,0:T(8,128)(2,1)S(1)} fusion(pred[8,5]{1,0:T(8,128)(4,1)S(1)} %get-tuple-element.92, pred[8,5]{1,0:T(8,128)(4,1)S(1)} %get-tuple-element.91, pred[8,5]{1,0:T(8,128)(4,1)S(1)} %get-tuple-element.90, pred[8,5]{1,0:T(8,128)(4,1)S(1)} %get-tuple-element.89, pred[8,5]{1,0:T(8,128)(4,1)S(1)} %get-tuple-element.88, ...), kind=kLoop, calls=%fused_computation.34 | loop fusion | flops 5242880 | bytes 3670336 | tf_op jit(solution)/shard_map/jit(_where)/select_n | solution.py:54
  47.1 0.2 select_select_fusion.9
  47.3 0.9 %fusion.8 = f32[8,128,128,1]{1,2,3,0:T(8,128)S(1)} fusion(bf16[8,8,128,128]{3,2,1,0:T(8,128)(2,1)S(1)} %copy-done, bf16[8,5,128,128]{3,2,1,0:T(8,128)(2,1)S(1)} %select_select_fusion.2, bf16[8,1,128,128]{3,2,1,0:T(8,128)(2,1)S(1)} %get-tuple-element.66, bf16[8,1,128,128]{3,2,1,0:T(8,128)(2,1)S(1)} %get-tuple-element.65, ...), kind=kOutput, calls=%fused_computation.8 | convolution fusion | flops 276824064 | bytes 4718592 | tf_op jit(solution)/shard_map/bjrc,bjcv->brv/dot_general | solution.py:63
  48.2 0.1 fusion.65
  48.4 1.9 %collective-permute-start.4 = (bf16[768,128]{1,0:T(8,128)(2,1)S(1)}, bf16[768,128]{1,0:T(8,128)(2,1)S(1)}, u32[]{:S(2)}, u32[]{:S(2)}) collective-permute-start(bf16[768,128]{1,0:T(8,128)(2,1)S(1)} %get-tuple-element.64), channel_id=1, source_target_pairs={{8,16},{16,8},{24,32},{32,24},{40,48},{48,40},{56,64},{64,56},{72,... | collective-permute-start | bytes 589832 | tf_op jit(solution)/shard_map/ppermute | solution.py:35
  50.3 1.9 %collective-permute-start.5 = (bf16[768,128]{1,0:T(8,128)(2,1)S(1)}, bf16[768,128]{1,0:T(8,128)(2,1)S(1)}, u32[]{:S(2)}, u32[]{:S(2)}) collective-permute-start(bf16[768,128]{1,0:T(8,128)(2,1)S(1)} %get-tuple-element.63), channel_id=1, source_target_pairs={{0,8},{8,0},{16,24},{24,16},{32,40},{40,32},{48,56},{56,48},{64,72... | collective-permute-start | bytes 589832 | tf_op jit(solution)/shard_map/ppermute | solution.py:34
  52.3 6.5 %collective-permute-done.4 = bf16[768,128]{1,0:T(8,128)(2,1)S(1)} collective-permute-done((bf16[768,128]{1,0:T(8,128)(2,1)S(1)}, bf16[768,128]{1,0:T(8,128)(2,1)S(1)}, u32[]{:S(2)}, u32[]{:S(2)}) %collective-permute-start.4) | collective-permute-done | bytes 196640 | tf_op jit(solution)/shard_map/ppermute | solution.py:35
  58.7 0.0 collective-permute-done.5
  58.8 0.3 fusion.37
  59.1 0.8 %select_select_fusion.1 = bf16[8,5,128,128]{3,2,1,0:T(8,128)(2,1)S(1)} fusion(pred[8,5]{1,0:T(8,128)(4,1)S(1)} %get-tuple-element.92, pred[8,5]{1,0:T(8,128)(4,1)S(1)} %get-tuple-element.91, pred[8,5]{1,0:T(8,128)(4,1)S(1)} %get-tuple-element.90, pred[8,5]{1,0:T(8,128)(4,1)S(1)} %get-tuple-element.89, pred[8,5]{1,0:T(8,128)(4,1)S(1)} %get-tuple-element.88, ...), kind=kLoop, calls=%fused_computation.33 | loop fusion | flops 5242880 | bytes 3670336 | tf_op jit(solution)/shard_map/jit(_where)/select_n | solution.py:54
  59.8 0.2 select_select_fusion.7
  60.1 0.9 %fusion.16 = f32[8,128,128,1]{1,2,3,0:T(8,128)S(1)} fusion(bf16[8,8,128,128]{3,2,1,0:T(8,128)(2,1)S(1)} %copy-done, bf16[8,5,128,128]{3,2,1,0:T(8,128)(2,1)S(1)} %select_select_fusion.1, bf16[8,1,128,128]{3,2,1,0:T(8,128)(2,1)S(1)} %get-tuple-element.56, bf16[8,1,128,128]{3,2,1,0:T(8,128)(2,1)S(1)} %get-tuple-element.55, ...), kind=kOutput, calls=%fused_computation.16 | convolution fusion | flops 276824064 | bytes 4718592 | tf_op jit(solution)/shard_map/bjrc,bjcv->brv/dot_general | solution.py:63
  61.0 0.2 fusion.64
  61.3 1.9 %collective-permute-start.6 = (bf16[768,128]{1,0:T(8,128)(2,1)S(1)}, bf16[768,128]{1,0:T(8,128)(2,1)S(1)}, u32[]{:S(2)}, u32[]{:S(2)}) collective-permute-start(bf16[768,128]{1,0:T(8,128)(2,1)S(1)} %get-tuple-element.54), channel_id=1, source_target_pairs={{8,16},{16,8},{24,32},{32,24},{40,48},{48,40},{56,64},{64,56},{72,... | collective-permute-start | bytes 589832 | tf_op jit(solution)/shard_map/ppermute | solution.py:35
  63.2 1.9 %collective-permute-start.7 = (bf16[768,128]{1,0:T(8,128)(2,1)S(1)}, bf16[768,128]{1,0:T(8,128)(2,1)S(1)}, u32[]{:S(2)}, u32[]{:S(2)}) collective-permute-start(bf16[768,128]{1,0:T(8,128)(2,1)S(1)} %get-tuple-element.53), channel_id=1, source_target_pairs={{0,8},{8,0},{16,24},{24,16},{32,40},{40,32},{48,56},{56,48},{64,72... | collective-permute-start | bytes 589832 | tf_op jit(solution)/shard_map/ppermute | solution.py:34
  65.1 6.5 %collective-permute-done.6 = bf16[768,128]{1,0:T(8,128)(2,1)S(1)} collective-permute-done((bf16[768,128]{1,0:T(8,128)(2,1)S(1)}, bf16[768,128]{1,0:T(8,128)(2,1)S(1)}, u32[]{:S(2)}, u32[]{:S(2)}) %collective-permute-start.6) | collective-permute-done | bytes 196640 | tf_op jit(solution)/shard_map/ppermute | solution.py:35
  71.6 0.0 collective-permute-done.7
  71.6 0.3 fusion.36
  71.9 0.8 %select_select_fusion = bf16[8,5,128,128]{3,2,1,0:T(8,128)(2,1)S(1)} fusion(pred[8,5]{1,0:T(8,128)(4,1)S(1)} %get-tuple-element.92, pred[8,5]{1,0:T(8,128)(4,1)S(1)} %get-tuple-element.91, pred[8,5]{1,0:T(8,128)(4,1)S(1)} %get-tuple-element.90, pred[8,5]{1,0:T(8,128)(4,1)S(1)} %get-tuple-element.89, pred[8,5]{1,0:T(8,128)(4,1)S(1)} %get-tuple-element.88, ...), kind=kLoop, calls=%fused_computation.32 | loop fusion | flops 5242880 | bytes 3670336 | tf_op jit(solution)/shard_map/jit(_where)/select_n | solution.py:54
  72.7 0.2 select_select_fusion.5
  72.9 0.9 %fusion.24 = f32[8,128,128,1]{1,2,3,0:T(8,128)S(1)} fusion(bf16[8,8,128,128]{3,2,1,0:T(8,128)(2,1)S(1)} %copy-done, bf16[8,5,128,128]{3,2,1,0:T(8,128)(2,1)S(1)} %select_select_fusion, bf16[8,1,128,128]{3,2,1,0:T(8,128)(2,1)S(1)} %get-tuple-element.46, bf16[8,1,128,128]{3,2,1,0:T(8,128)(2,1)S(1)} %get-tuple-element.45, ...), kind=kOutput, calls=%fused_computation.24 | convolution fusion | flops 276824064 | bytes 4718592 | tf_op jit(solution)/shard_map/bjrc,bjcv->brv/dot_general | solution.py:63
  73.8 1.0 %fusion.34 = bf16[1024,128]{1,0:T(8,128)(2,1)} fusion(f32[8,128,128,1]{1,2,3,0:T(8,128)S(1)} %fusion.24, bf16[128,8,128]{0,2,1:T(8,128)(2,1)S(1)} %copy.5, f32[8,128,128,1]{1,2,3,0:T(8,128)S(1)} %fusion, f32[8,128,128,1]{1,2,3,0:T(8,128)S(1)} %fusion.16, f32[8,128,128,1]{1,2,3,0:T(8,128)S(1)} %fusion.8), kind=kLoop, calls=%fused_computation.82 | loop fusion | flops 1835008 | bytes 2621440 | tf_op jit(solution)/shard_map/convert_element_type | solution.py:73
  (13 shorter events, 0.3 us)
Async XLA Ops:
  0.0 34.5 %copy-start = (bf16[8,8,128,128]{3,2,1,0:T(8,128)(2,1)S(1)}, bf16[8,8,128,128]{3,2,1,0:T(8,128)(2,1)}, u32[]{:S(2)}) copy-start(bf16[8,8,128,128]{3,2,1,0:T(8,128)(2,1)} %param.6) | copy-start | bytes 6291460
  0.0 10.8 %copy-start.1 = (s32[8,8]{1,0:T(8,128)S(1)}, s32[8,8]{1,0:T(8,128)}, u32[]{:S(2)}) copy-start(s32[8,8]{1,0:T(8,128)} %param.7) | copy-start | bytes 772
  3.2 19.4 %all-to-all-start = ((bf16[8,128,128]{2,1,0:T(8,128)(2,1)}), bf16[8,128,128]{2,1,0:T(8,128)(2,1)S(1)}, u32[]{:S(2)}, u32[]{:S(2)}) async-start(bf16[8,128,128]{2,1,0:T(8,128)(2,1)} %bitcast), calls=%async_computation | async-start | bytes 524288 | tf_op jit(solution)/shard_map/all_to_all | solution.py:78
  22.9 10.3 %collective-permute-start = (bf16[768,128]{1,0:T(8,128)(2,1)S(1)}, bf16[768,128]{1,0:T(8,128)(2,1)S(1)}, u32[]{:S(2)}, u32[]{:S(2)}) collective-permute-start(bf16[768,128]{1,0:T(8,128)(2,1)S(1)} %get-tuple-element.84), channel_id=1, source_target_pairs={{8,16},{16,8},{24,32},{32,24},{40,48},{48,40},{56,64},{64,56},{72,... | collective-permute-start | bytes 589832 | tf_op jit(solution)/shard_map/ppermute | solution.py:35
  24.8 8.4 %collective-permute-start.1 = (bf16[768,128]{1,0:T(8,128)(2,1)S(1)}, bf16[768,128]{1,0:T(8,128)(2,1)S(1)}, u32[]{:S(2)}, u32[]{:S(2)}) collective-permute-start(bf16[768,128]{1,0:T(8,128)(2,1)S(1)} %get-tuple-element.83), channel_id=1, source_target_pairs={{0,8},{8,0},{16,24},{24,16},{32,40},{40,32},{48,56},{56,48},{64,72... | collective-permute-start | bytes 589832 | tf_op jit(solution)/shard_map/ppermute | solution.py:34
  35.6 10.3 %collective-permute-start.2 = (bf16[768,128]{1,0:T(8,128)(2,1)S(1)}, bf16[768,128]{1,0:T(8,128)(2,1)S(1)}, u32[]{:S(2)}, u32[]{:S(2)}) collective-permute-start(bf16[768,128]{1,0:T(8,128)(2,1)S(1)} %get-tuple-element.74), channel_id=1, source_target_pairs={{8,16},{16,8},{24,32},{32,24},{40,48},{48,40},{56,64},{64,56},{72,... | collective-permute-start | bytes 589832 | tf_op jit(solution)/shard_map/ppermute | solution.py:35
  37.6 8.4 %collective-permute-start.3 = (bf16[768,128]{1,0:T(8,128)(2,1)S(1)}, bf16[768,128]{1,0:T(8,128)(2,1)S(1)}, u32[]{:S(2)}, u32[]{:S(2)}) collective-permute-start(bf16[768,128]{1,0:T(8,128)(2,1)S(1)} %get-tuple-element.73), channel_id=1, source_target_pairs={{0,8},{8,0},{16,24},{24,16},{32,40},{40,32},{48,56},{56,48},{64,72... | collective-permute-start | bytes 589832 | tf_op jit(solution)/shard_map/ppermute | solution.py:34
  48.4 10.3 %collective-permute-start.4 = (bf16[768,128]{1,0:T(8,128)(2,1)S(1)}, bf16[768,128]{1,0:T(8,128)(2,1)S(1)}, u32[]{:S(2)}, u32[]{:S(2)}) collective-permute-start(bf16[768,128]{1,0:T(8,128)(2,1)S(1)} %get-tuple-element.64), channel_id=1, source_target_pairs={{8,16},{16,8},{24,32},{32,24},{40,48},{48,40},{56,64},{64,56},{72,... | collective-permute-start | bytes 589832 | tf_op jit(solution)/shard_map/ppermute | solution.py:35
  50.3 8.4 %collective-permute-start.5 = (bf16[768,128]{1,0:T(8,128)(2,1)S(1)}, bf16[768,128]{1,0:T(8,128)(2,1)S(1)}, u32[]{:S(2)}, u32[]{:S(2)}) collective-permute-start(bf16[768,128]{1,0:T(8,128)(2,1)S(1)} %get-tuple-element.63), channel_id=1, source_target_pairs={{0,8},{8,0},{16,24},{24,16},{32,40},{40,32},{48,56},{56,48},{64,72... | collective-permute-start | bytes 589832 | tf_op jit(solution)/shard_map/ppermute | solution.py:34
  61.3 10.3 %collective-permute-start.6 = (bf16[768,128]{1,0:T(8,128)(2,1)S(1)}, bf16[768,128]{1,0:T(8,128)(2,1)S(1)}, u32[]{:S(2)}, u32[]{:S(2)}) collective-permute-start(bf16[768,128]{1,0:T(8,128)(2,1)S(1)} %get-tuple-element.54), channel_id=1, source_target_pairs={{8,16},{16,8},{24,32},{32,24},{40,48},{48,40},{56,64},{64,56},{72,... | collective-permute-start | bytes 589832 | tf_op jit(solution)/shard_map/ppermute | solution.py:35
  63.2 8.4 %collective-permute-start.7 = (bf16[768,128]{1,0:T(8,128)(2,1)S(1)}, bf16[768,128]{1,0:T(8,128)(2,1)S(1)}, u32[]{:S(2)}, u32[]{:S(2)}) collective-permute-start(bf16[768,128]{1,0:T(8,128)(2,1)S(1)} %get-tuple-element.53), channel_id=1, source_target_pairs={{0,8},{8,0},{16,24},{24,16},{32,40},{40,32},{48,56},{56,48},{64,72... | collective-permute-start | bytes 589832 | tf_op jit(solution)/shard_map/ppermute | solution.py:34

commit v16 on v15

--- a/solution.py
+++ b/solution.py
@@ -44,8 +44,18 @@
 
     def apply_operator(state_bf):
         lo, hi = swap_halos(state_bf, block_rows)
-        tiles = jnp.concatenate([lo, state_bf, hi], axis=0).reshape(-1, block_rows, width)
-        windows = [tiles[w:w + local_blocks][:, None] for w in range(REACH_LO + REACH_HI + 1)]
+        lo_t = lo.reshape(-1, block_rows, width)
+        own_t = state_bf.reshape(-1, block_rows, width)
+        hi_t = hi.reshape(-1, block_rows, width)
+
+        def window(w):
+            parts = [lo_t[w:], own_t[:max(w + local_blocks - REACH_LO, 0)]] if w < REACH_LO else [own_t[w - REACH_LO:]]
+            if w + local_blocks > REACH_LO + local_blocks:
+                parts.append(hi_t[:w + local_blocks - REACH_LO - local_blocks])
+            parts = [p for p in parts if p.shape[0] > 0]
+            return jnp.concatenate(parts, axis=0)[:, None]
+
+        windows = [window(w) for w in range(REACH_LO + REACH_HI + 1)]
 
         def pick(first, count, candidates):
             part = offset[:, first:first + count, None, None]

time: 75.2 us -> 76.5 us (1.017)
    select_n x8 -> x12, other arithmetic: 3.94 us -> 4.54 us  [pick(): got = jnp.where(part == w, windows[w], got)]
where the time goes in v16:
time: 76.5 us; the launch traced here: 76.1 us
  waiting for transfers between devices  35.6 us (47%)
  starting transfers between devices  24.5 us (32%)
  other arithmetic  7.57 us (10%)
  matrix products  6.89 us (9%)
  between operations  0.86 us (1%)
    ppermute x4, waiting for transfers between devices, swap_halos(): got_across = lax.ppermute(jnp.where(even, head, tail), 'row', pairs_across)  24.1 us
    all_to_all x1, waiting for transfers between devices, per_device(): lax.all_to_all(rotated_t.astype(jnp.bfloat16), 'vec', split_axis=0, conca...  11.5 us
    ppermute x4, starting transfers between devices, swap_halos(): got_in = lax.ppermute(jnp.where(even, tail, head), 'row', pairs_in)  9.27 us
    ppermute x4, starting transfers between devices, swap_halos(): got_across = lax.ppermute(jnp.where(even, head, tail), 'row', pairs_across)  7.68 us
    all_to_all x1, starting transfers between devices, per_device(): lax.all_to_all(rotated_t.astype(jnp.bfloat16), 'vec', split_axis=0, conca...  7.56 us
    select_n x12, other arithmetic, pick(): got = jnp.where(part == w, windows[w], got)  4.54 us
    dot_general x4, matrix products, apply_operator(): jnp.einsum('bjrc,bjcv->brv', blocks, picked, preferred_element_type=jnp.f...  3.67 us
    dot_general x1, matrix products, per_device(): lax.dot_general(rotation, vectors, (((0,), (1,)), ((), ())), preferred_el...  3.22 us
  transfers between devices with their start and end apart: 9, of which 5 were waited for; matrix products, arithmetic and copies ran while one was open for 1% of the time, Pallas kernels for 0%

profile of v16, /device:TPU:512, one launch (start us, length us, event | category | flops | bytes accessed | tf_op | source)
XLA Modules:
  0.0 76.1 jit_solution(398385966813254329)
XLA Ops:
  0.0 0.0 copy-start
  0.0 0.0 copy-start.1
  0.0 3.2 %convolution_convert_fusion = bf16[1024,128]{1,0:T(8,128)(2,1)} fusion(bf16[1024,1024]{1,0:T(8,128)(2,1)} %param.5, bf16[128,1024]{1,0:T(8,128)(2,1)} %param.4), kind=kOutput, calls=%fused_computation.36 | convolution fusion | flops 268566528 | bytes 2621440 | tf_op jit(solution)/shard_map/dot_general | solution.py:87
  3.2 7.6 %all-to-all-start = ((bf16[8,128,128]{2,1,0:T(8,128)(2,1)}), bf16[8,128,128]{2,1,0:T(8,128)(2,1)S(1)}, u32[]{:S(2)}, u32[]{:S(2)}) async-start(bf16[8,128,128]{2,1,0:T(8,128)(2,1)} %bitcast), calls=%async_computation | async-start | bytes 524288 | tf_op jit(solution)/shard_map/all_to_all | solution.py:88
  10.8 0.0 copy-done.1
  10.8 0.3 compare_reduce_fusion.7
  11.1 0.1 slice_compare_fusion.7
  11.2 11.5 %all-to-all-done = bf16[8,128,128]{2,1,0:T(8,128)(2,1)S(1)} async-done(((bf16[8,128,128]{2,1,0:T(8,128)(2,1)}), bf16[8,128,128]{2,1,0:T(8,128)(2,1)S(1)}, u32[]{:S(2)}, u32[]{:S(2)}) %all-to-all-start) | async-done | bytes 262176 | tf_op jit(solution)/shard_map/all_to_all | solution.py:88
  22.7 0.2 copy.5
  22.9 0.1 fusion.52
  23.0 1.9 %collective-permute-start = (bf16[768,128]{1,0:T(8,128)(2,1)S(1)}, bf16[768,128]{1,0:T(8,128)(2,1)S(1)}, u32[]{:S(2)}, u32[]{:S(2)}) collective-permute-start(bf16[768,128]{1,0:T(8,128)(2,1)S(1)} %get-tuple-element.40), channel_id=1, source_target_pairs={{8,16},{16,8},{24,32},{32,24},{40,48},{48,40},{56,64},{64,56},{72,... | collective-permute-start | bytes 589832 | tf_op jit(solution)/shard_map/ppermute | solution.py:35
  24.9 3.5 %collective-permute-start.1 = (bf16[768,128]{1,0:T(8,128)(2,1)S(1)}, bf16[768,128]{1,0:T(8,128)(2,1)S(1)}, u32[]{:S(2)}, u32[]{:S(2)}) collective-permute-start(bf16[768,128]{1,0:T(8,128)(2,1)S(1)} %get-tuple-element.41), channel_id=1, source_target_pairs={{0,8},{8,0},{16,24},{24,16},{32,40},{40,32},{48,56},{56,48},{64,72... | collective-permute-start | bytes 589832 | tf_op jit(solution)/shard_map/ppermute | solution.py:34
  28.4 4.8 %collective-permute-done = bf16[768,128]{1,0:T(8,128)(2,1)S(1)} collective-permute-done((bf16[768,128]{1,0:T(8,128)(2,1)S(1)}, bf16[768,128]{1,0:T(8,128)(2,1)S(1)}, u32[]{:S(2)}, u32[]{:S(2)}) %collective-permute-start) | collective-permute-done | bytes 196640 | tf_op jit(solution)/shard_map/ppermute | solution.py:35
  33.3 0.0 collective-permute-done.1
  33.6 0.1 pad_maximum_fusion.4
  33.7 0.1 maximum_select_fusion.5
  33.8 0.8 %select_select_fusion.3 = bf16[8,5,128,128]{3,2,1,0:T(8,128)(2,1)S(1)} fusion(pred[8,5]{1,0:T(8,128)(4,1)S(1)} %get-tuple-element.68, pred[8,5]{1,0:T(8,128)(4,1)S(1)} %get-tuple-element.67, pred[8,5]{1,0:T(8,128)(4,1)S(1)} %get-tuple-element.66, pred[8,5]{1,0:T(8,128)(4,1)S(1)} %get-tuple-element.65, pred[8,5]{1,0:T(8,128)(4,1)S(1)} %get-tuple-element.64, ...), kind=kLoop, calls=%fused_computation.35 | loop fusion | flops 5242880 | bytes 3670336 | tf_op jit(solution)/shard_map/jit(_where)/select_n | solution.py:64
  34.6 0.3 fusion.36
  34.8 0.0 copy-done
  34.8 0.9 %fusion = f32[8,128,128,1]{1,2,3,0:T(8,128)S(1)} fusion(bf16[8,8,128,128]{3,2,1,0:T(8,128)(2,1)S(1)} %copy-done, bf16[8,5,128,128]{3,2,1,0:T(8,128)(2,1)S(1)} %select_select_fusion.3, bf16[8,1,128,128]{3,2,1,0:T(8,128)(2,1)S(1)} %maximum_select_fusion.5, bf16[8,1,128,128]{3,2,1,0:T(8,128)(2,1)S(1)} %fusion.36, bf16[8,1,128,128]{3,2,1,0:T(8,128)(2,1)S(1)} %bitcast.333), kind=kOutput, calls=%fused_computation | convolution fusion | flops 276824064 | bytes 4718592 | tf_op jit(solution)/shard_map/bjrc,bjcv->brv/dot_general | solution.py:73
  35.8 0.1 multiply_convert_fusion
  35.9 0.1 fusion.50
  36.0 1.9 %collective-permute-start.2 = (bf16[768,128]{1,0:T(8,128)(2,1)S(1)}, bf16[768,128]{1,0:T(8,128)(2,1)S(1)}, u32[]{:S(2)}, u32[]{:S(2)}) collective-permute-start(bf16[768,128]{1,0:T(8,128)(2,1)S(1)} %get-tuple-element.34), channel_id=1, source_target_pairs={{8,16},{16,8},{24,32},{32,24},{40,48},{48,40},{56,64},{64,56},{72,... | collective-permute-start | bytes 589832 | tf_op jit(solution)/shard_map/ppermute | solution.py:35
  37.9 1.9 %collective-permute-start.3 = (bf16[768,128]{1,0:T(8,128)(2,1)S(1)}, bf16[768,128]{1,0:T(8,128)(2,1)S(1)}, u32[]{:S(2)}, u32[]{:S(2)}) collective-permute-start(bf16[768,128]{1,0:T(8,128)(2,1)S(1)} %get-tuple-element.35), channel_id=1, source_target_pairs={{0,8},{8,0},{16,24},{24,16},{32,40},{40,32},{48,56},{56,48},{64,72... | collective-permute-start | bytes 589832 | tf_op jit(solution)/shard_map/ppermute | solution.py:34
  39.9 6.4 %collective-permute-done.2 = bf16[768,128]{1,0:T(8,128)(2,1)S(1)} collective-permute-done((bf16[768,128]{1,0:T(8,128)(2,1)S(1)}, bf16[768,128]{1,0:T(8,128)(2,1)S(1)}, u32[]{:S(2)}, u32[]{:S(2)}) %collective-permute-start.2) | collective-permute-done | bytes 196640 | tf_op jit(solution)/shard_map/ppermute | solution.py:35
  46.3 0.0 collective-permute-done.3
  46.8 0.1 maximum_select_fusion.12
  46.9 0.8 select_select_fusion.2
  47.7 0.2 fusion.37
  47.9 0.9 %fusion.8 = f32[8,128,128,1]{1,2,3,0:T(8,128)S(1)} fusion(bf16[8,8,128,128]{3,2,1,0:T(8,128)(2,1)S(1)} %copy-done, bf16[8,5,128,128]{3,2,1,0:T(8,128)(2,1)S(1)} %select_select_fusion.2, bf16[8,1,128,128]{3,2,1,0:T(8,128)(2,1)S(1)} %maximum_select_fusion.12, bf16[8,1,128,128]{3,2,1,0:T(8,128)(2,1)S(1)} %fusion.37, bf16[8,1,128,128]{3,2,1,0:T(8,128)(2,1)S(1)} %bitcast.337), kind=kOutput, calls=%fused_computation.8 | convolution fusion | flops 276824064 | bytes 4718592 | tf_op jit(solution)/shard_map/bjrc,bjcv->brv/dot_general | solution.py:73
  48.8 0.1 fusion.45
  49.0 0.1 fusion.48
  49.1 1.9 %collective-permute-start.4 = (bf16[768,128]{1,0:T(8,128)(2,1)S(1)}, bf16[768,128]{1,0:T(8,128)(2,1)S(1)}, u32[]{:S(2)}, u32[]{:S(2)}) collective-permute-start(bf16[768,128]{1,0:T(8,128)(2,1)S(1)} %get-tuple-element.28), channel_id=1, source_target_pairs={{8,16},{16,8},{24,32},{32,24},{40,48},{48,40},{56,64},{64,56},{72,... | collective-permute-start | bytes 589832 | tf_op jit(solution)/shard_map/ppermute | solution.py:35
  51.0 1.9 %collective-permute-start.5 = (bf16[768,128]{1,0:T(8,128)(2,1)S(1)}, bf16[768,128]{1,0:T(8,128)(2,1)S(1)}, u32[]{:S(2)}, u32[]{:S(2)}) collective-permute-start(bf16[768,128]{1,0:T(8,128)(2,1)S(1)} %get-tuple-element.29), channel_id=1, source_target_pairs={{0,8},{8,0},{16,24},{24,16},{32,40},{40,32},{48,56},{56,48},{64,72... | collective-permute-start | bytes 589832 | tf_op jit(solution)/shard_map/ppermute | solution.py:34
  53.0 6.4 %collective-permute-done.4 = bf16[768,128]{1,0:T(8,128)(2,1)S(1)} collective-permute-done((bf16[768,128]{1,0:T(8,128)(2,1)S(1)}, bf16[768,128]{1,0:T(8,128)(2,1)S(1)}, u32[]{:S(2)}, u32[]{:S(2)}) %collective-permute-start.4) | collective-permute-done | bytes 196640 | tf_op jit(solution)/shard_map/ppermute | solution.py:35
  59.4 0.0 collective-permute-done.5
  59.9 0.1 maximum_select_fusion.19
  60.0 0.8 select_select_fusion.1
  60.8 0.2 fusion.38
  61.0 0.9 %fusion.16 = f32[8,128,128,1]{1,2,3,0:T(8,128)S(1)} fusion(bf16[8,8,128,128]{3,2,1,0:T(8,128)(2,1)S(1)} %copy-done, bf16[8,5,128,128]{3,2,1,0:T(8,128)(2,1)S(1)} %select_select_fusion.1, bf16[8,1,128,128]{3,2,1,0:T(8,128)(2,1)S(1)} %maximum_select_fusion.19, bf16[8,1,128,128]{3,2,1,0:T(8,128)(2,1)S(1)} %fusion.38, bf16[8,1,128,128]{3,2,1,0:T(8,128)(2,1)S(1)} %bitcast.341), kind=kOutput, calls=%fused_computation.16 | convolution fusion | flops 276824064 | bytes 4718592 | tf_op jit(solution)/shard_map/bjrc,bjcv->brv/dot_general | solution.py:73
  61.9 0.2 fusion.44
  62.2 0.1 fusion.46
  62.3 1.9 %collective-permute-start.6 = (bf16[768,128]{1,0:T(8,128)(2,1)S(1)}, bf16[768,128]{1,0:T(8,128)(2,1)S(1)}, u32[]{:S(2)}, u32[]{:S(2)}) collective-permute-start(bf16[768,128]{1,0:T(8,128)(2,1)S(1)} %get-tuple-element.22), channel_id=1, source_target_pairs={{8,16},{16,8},{24,32},{32,24},{40,48},{48,40},{56,64},{64,56},{72,... | collective-permute-start | bytes 589832 | tf_op jit(solution)/shard_map/ppermute | solution.py:35
  64.2 1.9 %collective-permute-start.7 = (bf16[768,128]{1,0:T(8,128)(2,1)S(1)}, bf16[768,128]{1,0:T(8,128)(2,1)S(1)}, u32[]{:S(2)}, u32[]{:S(2)}) collective-permute-start(bf16[768,128]{1,0:T(8,128)(2,1)S(1)} %get-tuple-element.23), channel_id=1, source_target_pairs={{0,8},{8,0},{16,24},{24,16},{32,40},{40,32},{48,56},{56,48},{64,72... | collective-permute-start | bytes 589832 | tf_op jit(solution)/shard_map/ppermute | solution.py:34
  66.2 6.4 %collective-permute-done.6 = bf16[768,128]{1,0:T(8,128)(2,1)S(1)} collective-permute-done((bf16[768,128]{1,0:T(8,128)(2,1)S(1)}, bf16[768,128]{1,0:T(8,128)(2,1)S(1)}, u32[]{:S(2)}, u32[]{:S(2)}) %collective-permute-start.6) | collective-permute-done | bytes 196640 | tf_op jit(solution)/shard_map/ppermute | solution.py:35
  72.6 0.0 collective-permute-done.7
  73.0 0.1 maximum_select_fusion.26
  73.2 0.8 select_select_fusion
  73.9 0.2 fusion.39
  74.2 0.9 %fusion.24 = f32[8,128,128,1]{1,2,3,0:T(8,128)S(1)} fusion(bf16[8,8,128,128]{3,2,1,0:T(8,128)(2,1)S(1)} %copy-done, bf16[8,5,128,128]{3,2,1,0:T(8,128)(2,1)S(1)} %select_select_fusion, bf16[8,1,128,128]{3,2,1,0:T(8,128)(2,1)S(1)} %maximum_select_fusion.26, bf16[8,1,128,128]{3,2,1,0:T(8,128)(2,1)S(1)} %fusion.39, bf16[8,1,128,128]{3,2,1,0:T(8,128)(2,1)S(1)} %bitcast.345), kind=kOutput, calls=%fused_computation.24 | convolution fusion | flops 276824064 | bytes 4718592 | tf_op jit(solution)/shard_map/bjrc,bjcv->brv/dot_general | solution.py:73
  75.1 1.0 %fusion.34 = bf16[1024,128]{1,0:T(8,128)(2,1)} fusion(f32[8,128,128,1]{1,2,3,0:T(8,128)S(1)} %fusion.24, bf16[128,8,128]{0,2,1:T(8,128)(2,1)S(1)} %copy.5, f32[8,128,128,1]{1,2,3,0:T(8,128)S(1)} %fusion, f32[8,128,128,1]{1,2,3,0:T(8,128)S(1)} %fusion.16, f32[8,128,128,1]{1,2,3,0:T(8,128)S(1)} %fusion.8), kind=kLoop, calls=%fused_computation.42 | loop fusion | flops 1835008 | bytes 2621440 | tf_op jit(solution)/shard_map/convert_element_type | solution.py:83
  (80 shorter events, 1.5 us)
Async XLA Ops:
  0.0 34.8 %copy-start = (bf16[8,8,128,128]{3,2,1,0:T(8,128)(2,1)S(1)}, bf16[8,8,128,128]{3,2,1,0:T(8,128)(2,1)}, u32[]{:S(2)}) copy-start(bf16[8,8,128,128]{3,2,1,0:T(8,128)(2,1)} %param.6) | copy-start | bytes 6291460
  0.0 10.8 %copy-start.1 = (s32[8,8]{1,0:T(8,128)S(1)}, s32[8,8]{1,0:T(8,128)}, u32[]{:S(2)}) copy-start(s32[8,8]{1,0:T(8,128)} %param.7) | copy-start | bytes 772
  3.2 19.4 %all-to-all-start = ((bf16[8,128,128]{2,1,0:T(8,128)(2,1)}), bf16[8,128,128]{2,1,0:T(8,128)(2,1)S(1)}, u32[]{:S(2)}, u32[]{:S(2)}) async-start(bf16[8,128,128]{2,1,0:T(8,128)(2,1)} %bitcast), calls=%async_computation | async-start | bytes 524288 | tf_op jit(solution)/shard_map/all_to_all | solution.py:88
  23.0 10.3 %collective-permute-start = (bf16[768,128]{1,0:T(8,128)(2,1)S(1)}, bf16[768,128]{1,0:T(8,128)(2,1)S(1)}, u32[]{:S(2)}, u32[]{:S(2)}) collective-permute-start(bf16[768,128]{1,0:T(8,128)(2,1)S(1)} %get-tuple-element.40), channel_id=1, source_target_pairs={{8,16},{16,8},{24,32},{32,24},{40,48},{48,40},{56,64},{64,56},{72,... | collective-permute-start | bytes 589832 | tf_op jit(solution)/shard_map/ppermute | solution.py:35
  24.9 8.4 %collective-permute-start.1 = (bf16[768,128]{1,0:T(8,128)(2,1)S(1)}, bf16[768,128]{1,0:T(8,128)(2,1)S(1)}, u32[]{:S(2)}, u32[]{:S(2)}) collective-permute-start(bf16[768,128]{1,0:T(8,128)(2,1)S(1)} %get-tuple-element.41), channel_id=1, source_target_pairs={{0,8},{8,0},{16,24},{24,16},{32,40},{40,32},{48,56},{56,48},{64,72... | collective-permute-start | bytes 589832 | tf_op jit(solution)/shard_map/ppermute | solution.py:34
  36.0 10.3 %collective-permute-start.2 = (bf16[768,128]{1,0:T(8,128)(2,1)S(1)}, bf16[768,128]{1,0:T(8,128)(2,1)S(1)}, u32[]{:S(2)}, u32[]{:S(2)}) collective-permute-start(bf16[768,128]{1,0:T(8,128)(2,1)S(1)} %get-tuple-element.34), channel_id=1, source_target_pairs={{8,16},{16,8},{24,32},{32,24},{40,48},{48,40},{56,64},{64,56},{72,... | collective-permute-start | bytes 589832 | tf_op jit(solution)/shard_map/ppermute | solution.py:35
  37.9 8.4 %collective-permute-start.3 = (bf16[768,128]{1,0:T(8,128)(2,1)S(1)}, bf16[768,128]{1,0:T(8,128)(2,1)S(1)}, u32[]{:S(2)}, u32[]{:S(2)}) collective-permute-start(bf16[768,128]{1,0:T(8,128)(2,1)S(1)} %get-tuple-element.35), channel_id=1, source_target_pairs={{0,8},{8,0},{16,24},{24,16},{32,40},{40,32},{48,56},{56,48},{64,72... | collective-permute-start | bytes 589832 | tf_op jit(solution)/shard_map/ppermute | solution.py:34
  49.1 10.3 %collective-permute-start.4 = (bf16[768,128]{1,0:T(8,128)(2,1)S(1)}, bf16[768,128]{1,0:T(8,128)(2,1)S(1)}, u32[]{:S(2)}, u32[]{:S(2)}) collective-permute-start(bf16[768,128]{1,0:T(8,128)(2,1)S(1)} %get-tuple-element.28), channel_id=1, source_target_pairs={{8,16},{16,8},{24,32},{32,24},{40,48},{48,40},{56,64},{64,56},{72,... | collective-permute-start | bytes 589832 | tf_op jit(solution)/shard_map/ppermute | solution.py:35
  51.0 8.4 %collective-permute-start.5 = (bf16[768,128]{1,0:T(8,128)(2,1)S(1)}, bf16[768,128]{1,0:T(8,128)(2,1)S(1)}, u32[]{:S(2)}, u32[]{:S(2)}) collective-permute-start(bf16[768,128]{1,0:T(8,128)(2,1)S(1)} %get-tuple-element.29), channel_id=1, source_target_pairs={{0,8},{8,0},{16,24},{24,16},{32,40},{40,32},{48,56},{56,48},{64,72... | collective-permute-start | bytes 589832 | tf_op jit(solution)/shard_map/ppermute | solution.py:34
  62.3 10.3 %collective-permute-start.6 = (bf16[768,128]{1,0:T(8,128)(2,1)S(1)}, bf16[768,128]{1,0:T(8,128)(2,1)S(1)}, u32[]{:S(2)}, u32[]{:S(2)}) collective-permute-start(bf16[768,128]{1,0:T(8,128)(2,1)S(1)} %get-tuple-element.22), channel_id=1, source_target_pairs={{8,16},{16,8},{24,32},{32,24},{40,48},{48,40},{56,64},{64,56},{72,... | collective-permute-start | bytes 589832 | tf_op jit(solution)/shard_map/ppermute | solution.py:35
  64.2 8.4 %collective-permute-start.7 = (bf16[768,128]{1,0:T(8,128)(2,1)S(1)}, bf16[768,128]{1,0:T(8,128)(2,1)S(1)}, u32[]{:S(2)}, u32[]{:S(2)}) collective-permute-start(bf16[768,128]{1,0:T(8,128)(2,1)S(1)} %get-tuple-element.23), channel_id=1, source_target_pairs={{0,8},{8,0},{16,24},{24,16},{32,40},{40,32},{48,56},{56,48},{64,72... | collective-permute-start | bytes 589832 | tf_op jit(solution)/shard_map/ppermute | solution.py:34

commit v17 on v11

--- a/solution.py
+++ b/solution.py
@@ -56,8 +56,9 @@
 
 
 def per_device(vectors, rotation, blocks, columns):
-    rotated = jnp.dot(vectors, rotation, preferred_element_type=jnp.float32).astype(jnp.bfloat16)
-    panel = lax.all_to_all(rotated, "vec", split_axis=1, concat_axis=0, tiled=True)
+    rotated_t = lax.dot_general(rotation, vectors, (((0,), (1,)), ((), ())), preferred_element_type=jnp.float32)
+    panel_t = lax.all_to_all(rotated_t.astype(jnp.bfloat16), "vec", split_axis=0, concat_axis=1, tiled=True)
+    panel = panel_t.T
     local_blocks = blocks.shape[0]
     n_tiles = local_blocks + REACH_LO + REACH_HI
     first_block = lax.axis_index("row") * local_blocks

time: 82.4 us -> 81.7 us (level)
  other arithmetic: 7.91 us -> 6.94 us
  matrix products: 5.95 us -> 6.89 us
    select_n x11 -> x8, other arithmetic: 4.91 us -> 3.94 us  [pick(): got = jnp.where(part == w, windows[w], got)]
    dot_general x1, matrix products: 2.28 us -> 3.22 us  [per_device(): lax.dot_general(rotation, vectors, (((0,), (1,)), ((), ())), preferred_el...]
where the time goes in v17:
time: 81.7 us; the launch traced here: 81.4 us
  waiting for transfers between devices  36.5 us (45%)
  starting transfers between devices  30.5 us (37%)
  other arithmetic  6.94 us (8%)
  matrix products  6.89 us (8%)
    ppermute x4, waiting for transfers between devices, shift_down(): return lax.ppermute(cells, axis, [(i + 1, i) for i in range(count - 1)])  26.2 us
    ppermute x4, starting transfers between devices, shift_up(): return lax.ppermute(cells, axis, [(i, i + 1) for i in range(count - 1)])  14.1 us
    all_to_all x1, waiting for transfers between devices, per_device(): lax.all_to_all(rotated_t.astype(jnp.bfloat16), 'vec', split_axis=0, conca...  10.3 us
    ppermute x4, starting transfers between devices, shift_down(): return lax.ppermute(cells, axis, [(i + 1, i) for i in range(count - 1)])  9.14 us
    all_to_all x1, starting transfers between devices, per_device(): lax.all_to_all(rotated_t.astype(jnp.bfloat16), 'vec', split_axis=0, conca...  7.27 us
    select_n x8, other arithmetic, pick(): got = jnp.where(part == w, windows[w], got)  3.94 us
    dot_general x4, matrix products, apply_operator(): jnp.einsum('bjrc,bjcv->brv', blocks, picked, preferred_element_type=jnp.f...  3.67 us
    dot_general x1, matrix products, per_device(): lax.dot_general(rotation, vectors, (((0,), (1,)), ((), ())), preferred_el...  3.22 us
  transfers between devices with their start and end apart: 9, of which 5 were waited for; matrix products, arithmetic and copies ran while one was open for 0% of the time, Pallas kernels for 0%

profile of v17, /device:TPU:399, one launch (start us, length us, event | category | flops | bytes accessed | tf_op | source)
XLA Modules:
  0.0 81.4 jit_solution(5042766895321104417)
XLA Ops:
  0.0 0.0 copy-start
  0.0 0.0 copy-start.1
  0.0 3.2 %convolution_convert_fusion = bf16[1024,128]{1,0:T(8,128)(2,1)} fusion(bf16[1024,1024]{1,0:T(8,128)(2,1)} %param.5, bf16[128,1024]{1,0:T(8,128)(2,1)} %param.4), kind=kOutput, calls=%fused_computation.36 | convolution fusion | flops 268566528 | bytes 2621440 | tf_op jit(solution)/shard_map/dot_general | solution.py:59
  3.2 7.3 %all-to-all-start = ((bf16[8,128,128]{2,1,0:T(8,128)(2,1)}), bf16[8,128,128]{2,1,0:T(8,128)(2,1)S(1)}, u32[]{:S(2)}, u32[]{:S(2)}) async-start(bf16[8,128,128]{2,1,0:T(8,128)(2,1)} %bitcast), calls=%async_computation | async-start | bytes 524288 | tf_op jit(solution)/shard_map/all_to_all | solution.py:60
  10.5 0.0 copy-done.1
  10.5 10.3 %all-to-all-done = bf16[8,128,128]{2,1,0:T(8,128)(2,1)S(1)} async-done(((bf16[8,128,128]{2,1,0:T(8,128)(2,1)}), bf16[8,128,128]{2,1,0:T(8,128)(2,1)S(1)}, u32[]{:S(2)}, u32[]{:S(2)}) %all-to-all-start) | async-done | bytes 262176 | tf_op jit(solution)/shard_map/all_to_all | solution.py:60
  20.8 0.2 copy.5
  21.0 8.3 %collective-permute-start = (bf16[768,128]{1,0:T(8,128)(2,1)S(1)}, bf16[768,128]{1,0:T(8,128)(2,1)S(1)}, u32[]{:S(2)}, u32[]{:S(2)}) collective-permute-start(bf16[768,128]{1,0:T(8,128)(2,1)S(1)} %slice.253), channel_id=1, source_target_pairs={{0,8},{8,16},{16,24},{24,32},{32,40},{40,48},{48,56},{56,64},{64,7... | collective-permute-start | bytes 589832 | tf_op jit(solution)/shard_map/ppermute | solution.py:14
  29.3 0.1 slice_compare_fusion.7
  29.4 1.9 %collective-permute-start.1 = (bf16[256,128]{1,0:T(8,128)(2,1)S(1)}, bf16[256,128]{1,0:T(8,128)(2,1)S(1)}, u32[]{:S(2)}, u32[]{:S(2)}) collective-permute-start(bf16[256,128]{1,0:T(8,128)(2,1)S(1)} %slice.264), channel_id=1, source_target_pairs={{8,0},{16,8},{24,16},{32,24},{40,32},{48,40},{56,48},{64,56},{72,6... | collective-permute-start | bytes 196616 | tf_op jit(solution)/shard_map/ppermute | solution.py:19
  31.4 0.3 compare_reduce_fusion.7
  31.7 6.7 %collective-permute-done.1 = bf16[256,128]{1,0:T(8,128)(2,1)S(1)} collective-permute-done((bf16[256,128]{1,0:T(8,128)(2,1)S(1)}, bf16[256,128]{1,0:T(8,128)(2,1)S(1)}, u32[]{:S(2)}, u32[]{:S(2)}) %collective-permute-start.1) | collective-permute-done | bytes 65568 | tf_op jit(solution)/shard_map/ppermute | solution.py:19
  38.3 0.0 collective-permute-done
  38.3 0.3 fusion.39
  38.6 0.2 select_select_fusion.11
  38.9 0.8 select_select_fusion.3
  39.7 0.0 copy-done
  39.7 0.9 %fusion = f32[8,128,128,1]{1,2,3,0:T(8,128)S(1)} fusion(bf16[8,8,128,128]{3,2,1,0:T(8,128)(2,1)S(1)} %copy-done, bf16[8,5,128,128]{3,2,1,0:T(8,128)(2,1)S(1)} %select_select_fusion.3, bf16[8,1,128,128]{3,2,1,0:T(8,128)(2,1)S(1)} %get-tuple-element.70, bf16[8,1,128,128]{3,2,1,0:T(8,128)(2,1)S(1)} %get-tuple-element.69, bf16[8,1,128,128]{3,2,1,0:T(8,128)(2,1)S(1)} %bitcast.166), kind=kOutput, calls=%fused_computation | convolution fusion | flops 276824064 | bytes 4718592 | tf_op jit(solution)/shard_map/bjrc,bjcv->brv/dot_general | solution.py:45
  40.6 0.1 multiply_convert_fusion
  40.7 1.9 %collective-permute-start.2 = (bf16[768,128]{1,0:T(8,128)(2,1)S(1)}, bf16[768,128]{1,0:T(8,128)(2,1)S(1)}, u32[]{:S(2)}, u32[]{:S(2)}) collective-permute-start(bf16[768,128]{1,0:T(8,128)(2,1)S(1)} %slice.267), channel_id=1, source_target_pairs={{0,8},{8,16},{16,24},{24,32},{32,40},{40,48},{48,56},{56,64},{64,7... | collective-permute-start | bytes 589832 | tf_op jit(solution)/shard_map/ppermute | solution.py:14
  42.7 2.4 %collective-permute-start.3 = (bf16[256,128]{1,0:T(8,128)(2,1)S(1)}, bf16[256,128]{1,0:T(8,128)(2,1)S(1)}, u32[]{:S(2)}, u32[]{:S(2)}) collective-permute-start(bf16[256,128]{1,0:T(8,128)(2,1)S(1)} %slice.278), channel_id=1, source_target_pairs={{8,0},{16,8},{24,16},{32,24},{40,32},{48,40},{56,48},{64,56},{72,6... | collective-permute-start | bytes 196616 | tf_op jit(solution)/shard_map/ppermute | solution.py:19
  45.1 6.5 %collective-permute-done.3 = bf16[256,128]{1,0:T(8,128)(2,1)S(1)} collective-permute-done((bf16[256,128]{1,0:T(8,128)(2,1)S(1)}, bf16[256,128]{1,0:T(8,128)(2,1)S(1)}, u32[]{:S(2)}, u32[]{:S(2)}) %collective-permute-start.3) | collective-permute-done | bytes 65568 | tf_op jit(solution)/shard_map/ppermute | solution.py:19
  51.6 0.0 collective-permute-done.2
  51.6 0.3 fusion.38
  51.9 0.8 select_select_fusion.2
  52.6 0.2 select_select_fusion.9
  52.9 0.9 %fusion.8 = f32[8,128,128,1]{1,2,3,0:T(8,128)S(1)} fusion(bf16[8,8,128,128]{3,2,1,0:T(8,128)(2,1)S(1)} %copy-done, bf16[8,5,128,128]{3,2,1,0:T(8,128)(2,1)S(1)} %select_select_fusion.2, bf16[8,1,128,128]{3,2,1,0:T(8,128)(2,1)S(1)} %get-tuple-element.62, bf16[8,1,128,128]{3,2,1,0:T(8,128)(2,1)S(1)} %get-tuple-element.61, ...), kind=kOutput, calls=%fused_computation.8 | convolution fusion | flops 276824064 | bytes 4718592 | tf_op jit(solution)/shard_map/bjrc,bjcv->brv/dot_general | solution.py:45
  53.8 0.1 fusion.65
  54.0 1.9 %collective-permute-start.4 = (bf16[768,128]{1,0:T(8,128)(2,1)S(1)}, bf16[768,128]{1,0:T(8,128)(2,1)S(1)}, u32[]{:S(2)}, u32[]{:S(2)}) collective-permute-start(bf16[768,128]{1,0:T(8,128)(2,1)S(1)} %slice.281), channel_id=1, source_target_pairs={{0,8},{8,16},{16,24},{24,32},{32,40},{40,48},{48,56},{56,64},{64,7... | collective-permute-start | bytes 589832 | tf_op jit(solution)/shard_map/ppermute | solution.py:14
  55.9 2.4 %collective-permute-start.5 = (bf16[256,128]{1,0:T(8,128)(2,1)S(1)}, bf16[256,128]{1,0:T(8,128)(2,1)S(1)}, u32[]{:S(2)}, u32[]{:S(2)}) collective-permute-start(bf16[256,128]{1,0:T(8,128)(2,1)S(1)} %slice.292), channel_id=1, source_target_pairs={{8,0},{16,8},{24,16},{32,24},{40,32},{48,40},{56,48},{64,56},{72,6... | collective-permute-start | bytes 196616 | tf_op jit(solution)/shard_map/ppermute | solution.py:19
  58.3 6.5 %collective-permute-done.5 = bf16[256,128]{1,0:T(8,128)(2,1)S(1)} collective-permute-done((bf16[256,128]{1,0:T(8,128)(2,1)S(1)}, bf16[256,128]{1,0:T(8,128)(2,1)S(1)}, u32[]{:S(2)}, u32[]{:S(2)}) %collective-permute-start.5) | collective-permute-done | bytes 65568 | tf_op jit(solution)/shard_map/ppermute | solution.py:19
  64.8 0.0 collective-permute-done.4
  64.8 0.3 fusion.37
  65.1 0.8 select_select_fusion.1
  65.9 0.2 select_select_fusion.7
  66.1 0.9 %fusion.16 = f32[8,128,128,1]{1,2,3,0:T(8,128)S(1)} fusion(bf16[8,8,128,128]{3,2,1,0:T(8,128)(2,1)S(1)} %copy-done, bf16[8,5,128,128]{3,2,1,0:T(8,128)(2,1)S(1)} %select_select_fusion.1, bf16[8,1,128,128]{3,2,1,0:T(8,128)(2,1)S(1)} %get-tuple-element.54, bf16[8,1,128,128]{3,2,1,0:T(8,128)(2,1)S(1)} %get-tuple-element.53, ...), kind=kOutput, calls=%fused_computation.16 | convolution fusion | flops 276824064 | bytes 4718592 | tf_op jit(solution)/shard_map/bjrc,bjcv->brv/dot_general | solution.py:45
  67.1 0.2 fusion.64
  67.3 1.9 %collective-permute-start.6 = (bf16[768,128]{1,0:T(8,128)(2,1)S(1)}, bf16[768,128]{1,0:T(8,128)(2,1)S(1)}, u32[]{:S(2)}, u32[]{:S(2)}) collective-permute-start(bf16[768,128]{1,0:T(8,128)(2,1)S(1)} %slice.295), channel_id=1, source_target_pairs={{0,8},{8,16},{16,24},{24,32},{32,40},{40,48},{48,56},{56,64},{64,7... | collective-permute-start | bytes 589832 | tf_op jit(solution)/shard_map/ppermute | solution.py:14
  69.2 2.4 %collective-permute-start.7 = (bf16[256,128]{1,0:T(8,128)(2,1)S(1)}, bf16[256,128]{1,0:T(8,128)(2,1)S(1)}, u32[]{:S(2)}, u32[]{:S(2)}) collective-permute-start(bf16[256,128]{1,0:T(8,128)(2,1)S(1)} %slice.306), channel_id=1, source_target_pairs={{8,0},{16,8},{24,16},{32,24},{40,32},{48,40},{56,48},{64,56},{72,6... | collective-permute-start | bytes 196616 | tf_op jit(solution)/shard_map/ppermute | solution.py:19
  71.7 6.5 %collective-permute-done.7 = bf16[256,128]{1,0:T(8,128)(2,1)S(1)} collective-permute-done((bf16[256,128]{1,0:T(8,128)(2,1)S(1)}, bf16[256,128]{1,0:T(8,128)(2,1)S(1)}, u32[]{:S(2)}, u32[]{:S(2)}) %collective-permute-start.7) | collective-permute-done | bytes 65568 | tf_op jit(solution)/shard_map/ppermute | solution.py:19
  78.1 0.0 collective-permute-done.6
  78.1 0.3 fusion.36
  78.5 0.8 select_select_fusion
  79.2 0.2 select_select_fusion.5
  79.5 0.9 %fusion.24 = f32[8,128,128,1]{1,2,3,0:T(8,128)S(1)} fusion(bf16[8,8,128,128]{3,2,1,0:T(8,128)(2,1)S(1)} %copy-done, bf16[8,5,128,128]{3,2,1,0:T(8,128)(2,1)S(1)} %select_select_fusion, bf16[8,1,128,128]{3,2,1,0:T(8,128)(2,1)S(1)} %get-tuple-element.46, bf16[8,1,128,128]{3,2,1,0:T(8,128)(2,1)S(1)} %get-tuple-element.45, ...), kind=kOutput, calls=%fused_computation.24 | convolution fusion | flops 276824064 | bytes 4718592 | tf_op jit(solution)/shard_map/bjrc,bjcv->brv/dot_general | solution.py:45
  80.4 1.0 %fusion.34 = bf16[1024,128]{1,0:T(8,128)(2,1)} fusion(f32[8,128,128,1]{1,2,3,0:T(8,128)S(1)} %fusion.24, bf16[128,8,128]{0,2,1:T(8,128)(2,1)S(1)} %copy.5, f32[8,128,128,1]{1,2,3,0:T(8,128)S(1)} %fusion, f32[8,128,128,1]{1,2,3,0:T(8,128)S(1)} %fusion.16, f32[8,128,128,1]{1,2,3,0:T(8,128)S(1)} %fusion.8), kind=kLoop, calls=%fused_computation.82 | loop fusion | flops 1835008 | bytes 2621440 | tf_op jit(solution)/shard_map/convert_element_type | solution.py:55
  (9 shorter events, 0.1 us)
Async XLA Ops:
  0.0 39.7 %copy-start = (bf16[8,8,128,128]{3,2,1,0:T(8,128)(2,1)S(1)}, bf16[8,8,128,128]{3,2,1,0:T(8,128)(2,1)}, u32[]{:S(2)}) copy-start(bf16[8,8,128,128]{3,2,1,0:T(8,128)(2,1)} %param.6) | copy-start | bytes 6291460
  0.0 10.5 %copy-start.1 = (s32[8,8]{1,0:T(8,128)S(1)}, s32[8,8]{1,0:T(8,128)}, u32[]{:S(2)}) copy-start(s32[8,8]{1,0:T(8,128)} %param.7) | copy-start | bytes 772
  3.2 17.6 %all-to-all-start = ((bf16[8,128,128]{2,1,0:T(8,128)(2,1)}), bf16[8,128,128]{2,1,0:T(8,128)(2,1)S(1)}, u32[]{:S(2)}, u32[]{:S(2)}) async-start(bf16[8,128,128]{2,1,0:T(8,128)(2,1)} %bitcast), calls=%async_computation | async-start | bytes 524288 | tf_op jit(solution)/shard_map/all_to_all | solution.py:60
  21.0 17.3 %collective-permute-start = (bf16[768,128]{1,0:T(8,128)(2,1)S(1)}, bf16[768,128]{1,0:T(8,128)(2,1)S(1)}, u32[]{:S(2)}, u32[]{:S(2)}) collective-permute-start(bf16[768,128]{1,0:T(8,128)(2,1)S(1)} %slice.253), channel_id=1, source_target_pairs={{0,8},{8,16},{16,24},{24,32},{32,40},{40,48},{48,56},{56,64},{64,7... | collective-permute-start | bytes 589832 | tf_op jit(solution)/shard_map/ppermute | solution.py:14
  29.4 8.9 %collective-permute-start.1 = (bf16[256,128]{1,0:T(8,128)(2,1)S(1)}, bf16[256,128]{1,0:T(8,128)(2,1)S(1)}, u32[]{:S(2)}, u32[]{:S(2)}) collective-permute-start(bf16[256,128]{1,0:T(8,128)(2,1)S(1)} %slice.264), channel_id=1, source_target_pairs={{8,0},{16,8},{24,16},{32,24},{40,32},{48,40},{56,48},{64,56},{72,6... | collective-permute-start | bytes 196616 | tf_op jit(solution)/shard_map/ppermute | solution.py:19
  40.7 10.9 %collective-permute-start.2 = (bf16[768,128]{1,0:T(8,128)(2,1)S(1)}, bf16[768,128]{1,0:T(8,128)(2,1)S(1)}, u32[]{:S(2)}, u32[]{:S(2)}) collective-permute-start(bf16[768,128]{1,0:T(8,128)(2,1)S(1)} %slice.267), channel_id=1, source_target_pairs={{0,8},{8,16},{16,24},{24,32},{32,40},{40,48},{48,56},{56,64},{64,7... | collective-permute-start | bytes 589832 | tf_op jit(solution)/shard_map/ppermute | solution.py:14
  42.7 8.9 %collective-permute-start.3 = (bf16[256,128]{1,0:T(8,128)(2,1)S(1)}, bf16[256,128]{1,0:T(8,128)(2,1)S(1)}, u32[]{:S(2)}, u32[]{:S(2)}) collective-permute-start(bf16[256,128]{1,0:T(8,128)(2,1)S(1)} %slice.278), channel_id=1, source_target_pairs={{8,0},{16,8},{24,16},{32,24},{40,32},{48,40},{56,48},{64,56},{72,6... | collective-permute-start | bytes 196616 | tf_op jit(solution)/shard_map/ppermute | solution.py:19
  54.0 10.9 %collective-permute-start.4 = (bf16[768,128]{1,0:T(8,128)(2,1)S(1)}, bf16[768,128]{1,0:T(8,128)(2,1)S(1)}, u32[]{:S(2)}, u32[]{:S(2)}) collective-permute-start(bf16[768,128]{1,0:T(8,128)(2,1)S(1)} %slice.281), channel_id=1, source_target_pairs={{0,8},{8,16},{16,24},{24,32},{32,40},{40,48},{48,56},{56,64},{64,7... | collective-permute-start | bytes 589832 | tf_op jit(solution)/shard_map/ppermute | solution.py:14
  55.9 8.9 %collective-permute-start.5 = (bf16[256,128]{1,0:T(8,128)(2,1)S(1)}, bf16[256,128]{1,0:T(8,128)(2,1)S(1)}, u32[]{:S(2)}, u32[]{:S(2)}) collective-permute-start(bf16[256,128]{1,0:T(8,128)(2,1)S(1)} %slice.292), channel_id=1, source_target_pairs={{8,0},{16,8},{24,16},{32,24},{40,32},{48,40},{56,48},{64,56},{72,6... | collective-permute-start | bytes 196616 | tf_op jit(solution)/shard_map/ppermute | solution.py:19
  67.3 10.9 %collective-permute-start.6 = (bf16[768,128]{1,0:T(8,128)(2,1)S(1)}, bf16[768,128]{1,0:T(8,128)(2,1)S(1)}, u32[]{:S(2)}, u32[]{:S(2)}) collective-permute-start(bf16[768,128]{1,0:T(8,128)(2,1)S(1)} %slice.295), channel_id=1, source_target_pairs={{0,8},{8,16},{16,24},{24,32},{32,40},{40,48},{48,56},{56,64},{64,7... | collective-permute-start | bytes 589832 | tf_op jit(solution)/shard_map/ppermute | solution.py:14
  69.2 8.9 %collective-permute-start.7 = (bf16[256,128]{1,0:T(8,128)(2,1)S(1)}, bf16[256,128]{1,0:T(8,128)(2,1)S(1)}, u32[]{:S(2)}, u32[]{:S(2)}) collective-permute-start(bf16[256,128]{1,0:T(8,128)(2,1)S(1)} %slice.306), channel_id=1, source_target_pairs={{8,0},{16,8},{24,16},{32,24},{40,32},{48,40},{56,48},{64,56},{72,6... | collective-permute-start | bytes 196616 | tf_op jit(solution)/shard_map/ppermute | solution.py:19
